TPU v7x, 256 devices: a whole 4x4x8 slice. The times are simulated.
256 devices in a mesh: gx: 16 (over y, x), gy: 16 (over z, core).
Axes of the slice: x: 4, y: 4, z: 8, core: 2. Of those that a mesh axis runs over, the one named last changes fastest.
Arguments:
- state: float32 [6, 256, 49152], P(None, 'gx', 'gy'), as said below
- shock_height: float32 [256, 32], P('gx'), may hold values from 0.9 to 1.1
- wall_segment: int32 [256], P('gx'), may hold values from 0 to 15, never falling along the last dimension, each value on 1 to 32 neighbouring positions
- segment_level: int32 [16], replicated, may hold values from 0 to 15
- blow_table: float32 [16, 32], replicated, may hold values from 0.1 to 1.5
Outputs:
- state_new: float32 [6, 256, 49152], P(None, 'gx', 'gy')
- shock_new: float32 [256, 32], P('gx')
Inputs may be any that keep to these rules, and one draw needn't show every extreme that they name: `state`: each cell has density in [0.5, 2], p / density in [0.6, 2.5], q5 / density in [0.05, 0.6], u in [0, 2], v and w in [-1, 1]. `wall_segment`: segment numbers never fall along the stream; each segment covers 1 to 32 cells.
All inputs are finite; a program needn't handle non-finite values.
Results may differ from a plain program's by a relative error of at most 0.00002.
Values sent between devices are 32-bit elements; how exact they have to be, the bound alone decides.
No kernel may reach another device: no remote copies, remote signals or barrier semaphores. Data moves between devices by JAX's collectives and lax.ppermute only.
A program may use at most 64 MiB of HBM per device.

v0:
```python
import math

import jax
import jax.numpy as jnp
from jax import lax
from jax.sharding import PartitionSpec as P

HEAT_RATIO = 1.4
STREAM_STEP = 0.05
SPAN_STEP = 0.05
STRETCH_RATE = 2.0
CHARACTER_KELVIN = 3.0
WHITE_LAW_FACTOR = 1.0
LANDAU_TELLER = 0.002
FREE_PRESSURE = 0.1
FREE_MACH = 6.0
COURANT = 0.05


def padded(block, sides, width):
    for axis, dim in sides:
        count = lax.axis_size(axis)
        forward = [(i, i + 1) for i in range(count - 1)]
        backward = [(target, source) for source, target in forward]
        low = lax.ppermute(
            lax.slice_in_dim(block, block.shape[dim] - width, None, axis=dim), axis, forward
        )
        high = lax.ppermute(lax.slice_in_dim(block, 0, width, axis=dim), axis, backward)
        block = jnp.concatenate([low, block, high], axis=dim)
    return block


def broadcast(array, axis, root):
    mine = lax.axis_index(axis) == root
    return lax.psum(jnp.where(mine, array, jnp.zeros_like(array)), axis)


def zshift(values, offset, planes):
    length = values.shape[-1]
    plane_at = jnp.arange(length, dtype=jnp.int32) % planes
    if offset > 0:
        return jnp.where(
            plane_at >= offset,
            jnp.roll(values, offset, axis=-1),
            jnp.roll(values, offset - planes, axis=-1),
        )
    return jnp.where(
        plane_at < planes + offset,
        jnp.roll(values, offset, axis=-1),
        jnp.roll(values, offset + planes, axis=-1),
    )


def primitives(conserved):
    specific_volume_inverse = conserved[0]
    vel_x = conserved[1] / specific_volume_inverse
    vel_y = conserved[2] / specific_volume_inverse
    vel_z = conserved[3] / specific_volume_inverse
    thermodynamic_stress = (HEAT_RATIO - 1.0) * (
        conserved[4]
        - 0.5 * (conserved[1] * vel_x + conserved[2] * vel_y + conserved[3] * vel_z)
        - conserved[5]
    )
    sound_speed = jnp.sqrt(HEAT_RATIO * thermodynamic_stress / specific_volume_inverse)
    return (specific_volume_inverse, vel_x, vel_y, vel_z, thermodynamic_stress, sound_speed)


def face_difference(plus_flux, minus_flux, cells, axis_at, stride):

    def window(values, offset):
        return lax.slice_in_dim(
            values, offset * stride, (offset + cells + 1) * stride, axis=axis_at
        )

    upwind = (
        2.0 * window(plus_flux, 0)
        - 13.0 * window(plus_flux, 1)
        + 47.0 * window(plus_flux, 2)
        + 27.0 * window(plus_flux, 3)
        - 3.0 * window(plus_flux, 4)
    ) / 60.0
    downwind = (
        -3.0 * window(minus_flux, 1)
        + 27.0 * window(minus_flux, 2)
        + 47.0 * window(minus_flux, 3)
        - 13.0 * window(minus_flux, 4)
        + 2.0 * window(minus_flux, 5)
    ) / 60.0
    face_sum = upwind + downwind
    return lax.slice_in_dim(
        face_sum, stride, (cells + 1) * stride, axis=axis_at
    ) - lax.slice_in_dim(face_sum, 0, cells * stride, axis=axis_at)


def stretch(index_rows, total_rows):
    growth = jnp.exp(STRETCH_RATE * (index_rows + 0.5) / total_rows)
    denominator = math.exp(STRETCH_RATE) - 1.0
    return ((growth - 1.0) / denominator, STRETCH_RATE * growth / (total_rows * denominator))


def split_pair(fluxes, speeds, conserved):
    return (0.5 * (fluxes + speeds * conserved), 0.5 * (fluxes - speeds * conserved))


def stream_part(conserved_x, height_ext, spacing_rows, planes):
    columns = conserved_x.shape[1] - 6
    specific_volume_inverse, vel_x, vel_y, vel_z, thermodynamic_stress, sound_speed = primitives(
        conserved_x
    )
    metric = (
        SPAN_STEP
        * jnp.tile(height_ext, (1, conserved_x.shape[2] // planes))
        * spacing_rows[None, :]
    )
    fluxes = (
        jnp.stack(
            [
                conserved_x[1],
                conserved_x[1] * vel_x + thermodynamic_stress,
                conserved_x[2] * vel_x,
                conserved_x[3] * vel_x,
                (conserved_x[4] + thermodynamic_stress) * vel_x,
                conserved_x[5] * vel_x,
            ]
        )
        * metric
    )
    speeds = (jnp.abs(vel_x) + sound_speed) * metric
    plus_flux, minus_flux = split_pair(fluxes, speeds, conserved_x)
    return face_difference(plus_flux, minus_flux, columns, 1, 1)


def normal_part(conserved_y, slope_x, slope_z, shock_rate, eta_rows, planes):
    copies = conserved_y.shape[2] // planes
    row_count = copies - 6
    specific_volume_inverse, vel_x, vel_y, vel_z, thermodynamic_stress, sound_speed = primitives(
        conserved_y
    )
    face_area = STREAM_STEP * SPAN_STEP
    metric_x = -face_area * eta_rows[None, :] * jnp.tile(slope_x, (1, copies))
    metric_z = -face_area * eta_rows[None, :] * jnp.tile(slope_z, (1, copies))
    metric_t = -face_area * eta_rows[None, :] * jnp.tile(shock_rate, (1, copies))
    contra = metric_t + metric_x * vel_x + face_area * vel_y + metric_z * vel_z
    fluxes = jnp.stack(
        [
            conserved_y[0] * contra,
            conserved_y[1] * contra + metric_x * thermodynamic_stress,
            conserved_y[2] * contra + face_area * thermodynamic_stress,
            conserved_y[3] * contra + metric_z * thermodynamic_stress,
            (conserved_y[4] + thermodynamic_stress) * contra - metric_t * thermodynamic_stress,
            conserved_y[5] * contra,
        ]
    )
    speeds = jnp.abs(contra) + sound_speed * jnp.sqrt(
        metric_x * metric_x + face_area * face_area + metric_z * metric_z
    )
    plus_flux, minus_flux = split_pair(fluxes, speeds, conserved_y)
    return face_difference(plus_flux, minus_flux, row_count, 2, planes)


def span_part(conserved, height, spacing_rows, planes):
    specific_volume_inverse, vel_x, vel_y, vel_z, thermodynamic_stress, sound_speed = primitives(
        conserved
    )
    metric = (
        STREAM_STEP * jnp.tile(height, (1, conserved.shape[2] // planes)) * spacing_rows[None, :]
    )
    fluxes = (
        jnp.stack(
            [
                conserved[3],
                conserved[1] * vel_z,
                conserved[2] * vel_z,
                conserved[3] * vel_z + thermodynamic_stress,
                (conserved[4] + thermodynamic_stress) * vel_z,
                conserved[5] * vel_z,
            ]
        )
        * metric
    )
    speeds = (jnp.abs(vel_z) + sound_speed) * metric
    plus_flux, minus_flux = split_pair(fluxes, speeds, conserved)
    upwind = (
        2.0 * zshift(plus_flux, 2, planes)
        - 13.0 * zshift(plus_flux, 1, planes)
        + 47.0 * plus_flux
        + 27.0 * zshift(plus_flux, -1, planes)
        - 3.0 * zshift(plus_flux, -2, planes)
    ) / 60.0
    downwind = (
        -3.0 * zshift(minus_flux, 1, planes)
        + 27.0 * minus_flux
        + 47.0 * zshift(minus_flux, -1, planes)
        - 13.0 * zshift(minus_flux, -2, planes)
        + 2.0 * zshift(minus_flux, -3, planes)
    ) / 60.0
    face_sum = upwind + downwind
    return face_sum - zshift(face_sum, 1, planes)


def relaxation(conserved):
    specific_volume_inverse, vel_x, vel_y, vel_z, thermodynamic_stress, sound_speed = primitives(
        conserved
    )
    heavy_particle_kelvin = thermodynamic_stress / specific_volume_inverse
    oscillator_balanced_share = CHARACTER_KELVIN / (
        jnp.exp(CHARACTER_KELVIN / heavy_particle_kelvin) - 1.0
    )
    landau_teller_source = thermodynamic_stress / (
        LANDAU_TELLER * jnp.exp(WHITE_LAW_FACTOR * jnp.exp(-jnp.log(heavy_particle_kelvin) / 3.0))
    )
    return (
        specific_volume_inverse
        * (oscillator_balanced_share - conserved[5] / specific_volume_inverse)
        * landau_teller_source
    )


def slopes(height_ext, planes):
    columns = height_ext.shape[0] - 6
    slope_x = (
        height_ext[1 : columns + 1]
        - 8.0 * height_ext[2 : columns + 2]
        + 8.0 * height_ext[4 : columns + 4]
        - height_ext[5 : columns + 5]
    ) / (12.0 * STREAM_STEP)
    height = height_ext[3 : columns + 3]
    slope_z = (
        zshift(height, 2, planes)
        - 8.0 * zshift(height, 1, planes)
        + 8.0 * zshift(height, -1, planes)
        - zshift(height, -2, planes)
    ) / (12.0 * SPAN_STEP)
    return (slope_x, slope_z)


def shock_speed(top_row, slope_x, slope_z):
    specific_volume_inverse, vel_x, vel_y, vel_z, thermodynamic_stress, sound_speed = primitives(
        top_row
    )
    tilt_norm = jnp.sqrt(1.0 + slope_x * slope_x + slope_z * slope_z)
    normal = (vel_y - vel_x * slope_x - vel_z * slope_z) / tilt_norm
    sine_sq = slope_x * slope_x / (tilt_norm * tilt_norm)
    jump_pressure = FREE_PRESSURE * (
        1.0 + 2.0 * HEAT_RATIO / (HEAT_RATIO + 1.0) * (FREE_MACH * FREE_MACH * sine_sq - 1.0)
    )
    return tilt_norm * (
        normal + (jump_pressure - thermodynamic_stress) / (specific_volume_inverse * sound_speed)
    )


def wall_ghosts(first_rows, blowing, planes):
    mirror = jnp.concatenate(
        [
            first_rows[..., 2 * planes : 3 * planes],
            first_rows[..., planes : 2 * planes],
            first_rows[..., 0:planes],
        ],
        axis=-1,
    )
    blown_y = 2.0 * jnp.tile(blowing, (1, 3)) - mirror[2]
    stagnation_enthalpy_sum = (
        mirror[4] + 0.5 * (blown_y * blown_y - mirror[2] * mirror[2]) / mirror[0]
    )
    return jnp.stack([mirror[0], mirror[1], blown_y, mirror[3], stagnation_enthalpy_sum, mirror[5]])


def advance(
    conserved,
    conserved_x,
    conserved_y,
    height_ext,
    slope_x,
    slope_z,
    shock_rate,
    first_row,
    total_rows,
    planes,
):
    columns = conserved.shape[1]
    row_count = conserved.shape[2] // planes
    local_rows = (first_row + jnp.arange(row_count, dtype=jnp.int32)).astype(jnp.float32)
    eta_local, spacing_local = stretch(local_rows, total_rows)
    spacing_rows = jnp.repeat(spacing_local, planes)
    outer_rows = (first_row - 3 + jnp.arange(row_count + 6, dtype=jnp.int32)).astype(jnp.float32)
    eta_outer = stretch(outer_rows, total_rows)[0]
    eta_rows = jnp.repeat(eta_outer, planes)
    height = height_ext[3 : columns + 3]
    divergence = (
        stream_part(conserved_x, height_ext, spacing_rows, planes)
        + normal_part(conserved_y, slope_x, slope_z, shock_rate, eta_rows, planes)
        + span_part(conserved, height, spacing_rows, planes)
    )
    height_rows = jnp.tile(height, (1, row_count))
    rate_rows = jnp.tile(shock_rate, (1, row_count))
    volume = STREAM_STEP * SPAN_STEP * height_rows * spacing_rows[None, :]
    change = -divergence / volume - conserved * (rate_rows / height_rows)
    change = jnp.concatenate([change[:5], (change[5] + relaxation(conserved))[None]], axis=0)
    return conserved + COURANT / total_rows * change


def edge_fill(values, axis_at, cells, device_at, devices):
    positions = jnp.arange(cells + 6, dtype=jnp.int32)
    processor_arrangement = [1] * values.ndim
    processor_arrangement[axis_at] = cells + 6
    positions = positions.reshape(processor_arrangement)
    leading = lax.slice_in_dim(values, 3, 4, axis=axis_at)
    trailing = lax.slice_in_dim(values, cells + 2, cells + 3, axis=axis_at)
    values = jnp.where((device_at == 0) & (positions < 3), leading, values)
    return jnp.where((device_at == devices - 1) & (positions >= cells + 3), trailing, values)


def wall_flux(wall_segment, segment_level, blow_table):
    seg_hit = wall_segment[:, None] == jnp.arange(segment_level.shape[0], dtype=jnp.int32)[None, :]
    levels = jnp.sum(jnp.where(seg_hit, segment_level[None, :], 0), axis=1)
    level_hit = levels[:, None] == jnp.arange(blow_table.shape[0], dtype=jnp.int32)[None, :]
    return jnp.sum(jnp.where(level_hit[:, :, None], blow_table[None, :, :], 0.0), axis=1)


def shards(state, shock_height, wall_segment, segment_level, blow_table):
    planes = blow_table.shape[1]
    columns = state.shape[1]
    length = state.shape[2]
    row_count = length // planes
    col_devs = lax.axis_size("gx")
    row_devs = lax.axis_size("gy")
    col_dev = lax.axis_index("gx")
    row_dev = lax.axis_index("gy")
    total_rows = row_count * row_devs
    conserved_x = padded(state, (("gx", 1),), 3)
    height_ext = padded(shock_height, (("gx", 0),), 3)
    conserved_x = edge_fill(conserved_x, 1, columns, col_dev, col_devs)
    height_ext = edge_fill(height_ext, 0, columns, col_dev, col_devs)
    slope_x, slope_z = slopes(height_ext, planes)
    own_rate = shock_speed(state[:, :, length - planes :], slope_x, slope_z)
    shock_rate = broadcast(own_rate, "gy", row_devs - 1)
    blowing = wall_flux(wall_segment, segment_level, blow_table)
    halo_y = padded(state, (("gy", 2),), 3 * planes)
    ghost_below = jnp.where(
        row_dev == 0,
        wall_ghosts(state[..., : 3 * planes], blowing, planes),
        halo_y[..., : 3 * planes],
    )
    ghost_above = jnp.where(
        row_dev == row_devs - 1,
        jnp.tile(state[..., length - planes :], (1, 1, 3)),
        halo_y[..., length + 3 * planes :],
    )
    conserved_y = jnp.concatenate([ghost_below, state, ghost_above], axis=2)
    state_new = advance(
        state,
        conserved_x,
        conserved_y,
        height_ext,
        slope_x,
        slope_z,
        shock_rate,
        row_dev * row_count,
        total_rows,
        planes,
    )
    shock_new = shock_height + COURANT / total_rows * shock_rate
    return (state_new, shock_new)


def solution(mesh):
    in_specs = (P(None, "gx", "gy"), P("gx", None), P("gx"), P(), P())
    out_specs = (P(None, "gx", "gy"), P("gx", None))
    return jax.shard_map(shards, mesh=mesh, in_specs=in_specs, out_specs=out_specs, check_vma=False)
```

profile of v0, /device:TPU:8, one launch (start us, length us, event | category | flops | bytes accessed | tf_op | source)
XLA Modules:
  0.0 124.9 jit_solution(7692212084763646776)
XLA Ops:
  1.5 3.4 %collective-permute-start.2 = (f32[3,32]{1,0:T(4,128)S(1)}, f32[3,32]{1,0:T(4,128)S(1)}, u32[]{:S(2)}, u32[]{:S(2)}) collective-permute-start(f32[3,32]{1,0:T(4,128)S(1)} %get-tuple-element.71), channel_id=1, source_target_pairs={{0,16},{16,32},{32,48},{48,64},{64,80},{80,96},{96,112},{112,128},... | collective-permute-start | bytes 1160 | tf_op jit(solution)/shard_map/ppermute | solution.py:25
  4.9 4.6 %collective-permute-start.3 = (f32[3,32]{1,0:T(4,128)S(1)}, f32[3,32]{1,0:T(4,128)S(1)}, u32[]{:S(2)}, u32[]{:S(2)}) collective-permute-start(f32[3,32]{1,0:T(4,128)S(1)} %get-tuple-element.72), channel_id=1, source_target_pairs={{16,0},{32,16},{48,32},{64,48},{80,64},{96,80},{112,96},{128,112},... | collective-permute-start | bytes 1160 | tf_op jit(solution)/shard_map/ppermute | solution.py:28
  9.4 2.2 %fusion.97 = (f32[6,3,3072]{2,1,0:T(4,128)}, f32[6,3,3072]{2,1,0:T(4,128)}) fusion(f32[6,16,3072]{2,1,0:T(8,128)} %param.5), kind=kLoop, calls=%fused_computation.217 | loop fusion | bytes 884736 | tf_op jit(solution)/shard_map/slice | solution.py:26
  11.6 1.9 %collective-permute-start = (f32[6,3,3072]{2,1,0:T(4,128)}, f32[6,3,3072]{2,1,0:T(4,128)}, u32[]{:S(2)}, u32[]{:S(2)}) collective-permute-start(f32[6,3,3072]{2,1,0:T(4,128)} %get-tuple-element.50), channel_id=1, source_target_pairs={{0,16},{16,32},{32,48},{48,64},{64,80},{80,96},{96,112},{112,128},... | collective-permute-start | bytes 663560 | tf_op jit(solution)/shard_map/ppermute | solution.py:25
  13.5 6.0 %collective-permute-start.1 = (f32[6,3,3072]{2,1,0:T(4,128)}, f32[6,3,3072]{2,1,0:T(4,128)}, u32[]{:S(2)}, u32[]{:S(2)}) collective-permute-start(f32[6,3,3072]{2,1,0:T(4,128)} %get-tuple-element.51), channel_id=1, source_target_pairs={{16,0},{32,16},{48,32},{64,48},{80,64},{96,80},{112,96},{128,112},... | collective-permute-start | bytes 663560 | tf_op jit(solution)/shard_map/ppermute | solution.py:28
  20.3 1.9 %collective-permute-start.4 = (f32[6,16,96]{2,1,0:T(8,128)}, f32[6,16,96]{2,1,0:T(8,128)}, u32[]{:S(2)}, u32[]{:S(2)}) collective-permute-start(f32[6,16,96]{2,1,0:T(8,128)} %get-tuple-element.53), channel_id=1, source_target_pairs={{0,1},{1,2},{2,3},{3,4},{4,5},{5,6},{6,7},{7,8},{8,9},{9,10},{10,1... | collective-permute-start | bytes 110600 | tf_op jit(solution)/shard_map/ppermute | solution.py:25
  29.3 1.3 %collective-permute-start.5 = (f32[6,16,96]{2,1,0:T(8,128)}, f32[6,16,96]{2,1,0:T(8,128)}, u32[]{:S(2)}, u32[]{:S(2)}) collective-permute-start(f32[6,16,96]{2,1,0:T(8,128)} %get-tuple-element.52), channel_id=1, source_target_pairs={{1,0},{2,1},{3,2},{4,3},{5,4},{6,5},{7,6},{8,7},{9,8},{10,9},{11,1... | collective-permute-start | bytes 110600 | tf_op jit(solution)/shard_map/ppermute | solution.py:28
  33.4 1.1 tile.92
  34.5 1.0 tile.93
  35.5 1.5 %fusion.79 = (f32[16,32]{1,0:T(8,128)S(1)}, f32[16,32]{1,0:T(8,128)}, f32[16,32]{1,0:T(8,128)}) fusion(f32[6,16,3072]{2,1,0:T(8,128)S(1)} %copy-done, pred[]{:T(512)S(6)} %eq.69, f32[22,32]{1,0:T(8,128)S(1)} %fusion.56, f32[16,2]{1,0:T(8,128)} %get-tuple-element.62, f32[16,30]{1,0:T(8,128)} %get-tuple-element.64, f32[16,1]{1,0:T(8,128)} %get-tuple-element.66, ...), kind=kLoop, calls=%fused_computation.193 | loop fusion | flops 26624 | bytes 34817 | tf_op jit(solution)/shard_map/jit(_where)/select_n | solution.py:35
  37.0 31.8 %psum.7 = f32[16,32]{1,0:T(8,128)} all-reduce(f32[16,32]{1,0:T(8,128)S(1)} %get-tuple-element.12), channel_id=1, replica_groups=mesh['gx'=16,'gy'=16] {'gy'}, use_global_device_ids=true, to_apply=%region_2.3 | all-reduce | flops 512 | bytes 4096 | tf_op jit(solution)/shard_map/psum | solution.py:35
  69.6 1.1 tile.95
  70.7 1.1 multiply_dynamic-update-slice_fusion.7
  71.9 0.9 broadcast_multiply_fusion.3
  73.5 1.8 %fusion.85 = (f32[6,16,3041]{2,1,0:T(8,128)}, f32[6,16,3041]{2,1,0:T(8,128)}) fusion(f32[6,16,3072]{2,1,0:T(8,128)S(1)} %get-tuple-element.19), kind=kLoop, calls=%fused_computation.205 | loop fusion | bytes 4670976 | tf_op jit(solution)/shard_map/jit(_roll_static)/slice | solution.py:50
  75.2 1.8 %fusion.86 = (f32[6,16,3071]{2,1,0:T(8,128)}, f32[6,16,3071]{2,1,0:T(8,128)}) fusion(f32[6,16,3072]{2,1,0:T(8,128)S(1)} %get-tuple-element.19), kind=kLoop, calls=%fused_computation.206 | loop fusion | bytes 4717056 | tf_op jit(solution)/shard_map/jit(_roll_static)/slice | solution.py:49
  77.1 1.8 %fusion.89 = (f32[6,16,3042]{2,1,0:T(8,128)}, f32[6,16,3042]{2,1,0:T(8,128)}) fusion(f32[6,16,3072]{2,1,0:T(8,128)S(1)} %get-tuple-element.20), kind=kLoop, calls=%fused_computation.209 | loop fusion | bytes 4672512 | tf_op jit(solution)/shard_map/jit(_roll_static)/slice | solution.py:50
  78.9 1.8 %fusion.90 = (f32[6,16,3070]{2,1,0:T(8,128)}, f32[6,16,3070]{2,1,0:T(8,128)}) fusion(f32[6,16,3072]{2,1,0:T(8,128)S(1)} %get-tuple-element.20), kind=kLoop, calls=%fused_computation.210 | loop fusion | bytes 4715520 | tf_op jit(solution)/shard_map/jit(_roll_static)/slice | solution.py:49
  80.7 1.9 %fusion.93 = (f32[6,16,3041]{2,1,0:T(8,128)}, f32[6,16,3041]{2,1,0:T(8,128)}) fusion(f32[6,16,3072]{2,1,0:T(8,128)S(1)} %get-tuple-element.20), kind=kLoop, calls=%fused_computation.213 | loop fusion | bytes 4670976 | tf_op jit(solution)/shard_map/jit(_roll_static)/slice | solution.py:50
  82.5 1.8 %fusion.94 = (f32[6,16,3071]{2,1,0:T(8,128)}, f32[6,16,3071]{2,1,0:T(8,128)}) fusion(f32[6,16,3072]{2,1,0:T(8,128)S(1)} %get-tuple-element.20), kind=kLoop, calls=%fused_computation.214 | loop fusion | bytes 4717056 | tf_op jit(solution)/shard_map/jit(_roll_static)/slice | solution.py:49
  84.3 1.4 %slice.663 = f32[6,16,3070]{2,1,0:T(8,128)} slice(f32[6,16,3072]{2,1,0:T(8,128)S(1)} %get-tuple-element.19), slice={[0:6], [0:16], [2:3072]} | slice | bytes 2357760 | tf_op jit(solution)/shard_map/jit(_roll_static)/slice | solution.py:49
  85.7 1.4 %slice.667 = f32[6,16,3069]{2,1,0:T(8,128)} slice(f32[6,16,3072]{2,1,0:T(8,128)S(1)} %get-tuple-element.19), slice={[0:6], [0:16], [3:3072]} | slice | bytes 2356992 | tf_op jit(solution)/shard_map/jit(_roll_static)/slice | solution.py:49
  93.4 1.2 tile.35
  94.7 1.7 %broadcast_multiply_fusion.2 = f32[22,3072]{1,0:T(8,128)} fusion(f32[22,3072]{1,0:T(8,128)} %tile.35, f32[3072]{0:T(1024)S(1)} %copy-done.18), kind=kLoop, calls=%fused_computation.132 | loop fusion | flops 67584 | bytes 552960 | tf_op jit(solution)/shard_map/mul | solution.py:111
  96.4 8.5 %fusion.32 = f32[6,16,3072]{2,1,0:T(8,128)S(1)} fusion(f32[6,16,3070]{2,1,0:T(8,128)} %get-tuple-element.37, f32[6,16,2]{2,1,0:T(8,128)} %get-tuple-element.39, f32[6,16,30]{2,1,0:T(8,128)} %get-tuple-element.33, f32[6,16,3042]{2,1,0:T(8,128)} %get-tuple-element.35, f32[6,16,3071]{2,1,0:T(8,128)} %get-tuple-element.45, f32[6,16,1]{2,1,0:T(8,128)} %get-tuple-element.47, ...), kind=kLoop, calls=%fused_computation.60 | loop fusion | flops 14155776 | bytes 22821888 | tf_op jit(solution)/shard_map/add | solution.py:197
  105.6 1.4 %slice.673 = f32[6,16,3041]{2,1,0:T(8,128)} slice(f32[6,16,3072]{2,1,0:T(8,128)S(1)} %fusion.32), slice={[0:6], [0:16], [31:3072]} | slice | bytes 2335488 | tf_op jit(solution)/shard_map/jit(_roll_static)/slice | solution.py:45
  110.9 1.7 %concatenate.126 = f32[6,16,3264]{2,1,0:T(8,128)S(1)} concatenate(f32[6,16,96]{2,1,0:T(8,128)} %broadcast_select_fusion.1, f32[6,16,3072]{2,1,0:T(8,128)S(1)} %copy-done, f32[6,16,96]{2,1,0:T(8,128)S(1)} %broadcast_select_fusion), dimensions={2} | concatenate | bytes 2506752 | tf_op jit(solution)/shard_map/concatenate | solution.py:349
  113.6 2.3 %fusion.13 = f32[6,16,3104]{2,1,0:T(8,128)S(1)} fusion(f32[6,16,3264]{2,1,0:T(8,128)S(1)} %get-tuple-element.18, f32[6,16,3264]{2,1,0:T(8,128)S(1)} %get-tuple-element.17), kind=kLoop, calls=%fused_computation.29 | loop fusion | flops 5959680 | bytes 13111296 | tf_op jit(solution)/shard_map/add | solution.py:89
  115.9 1.4 %fusion.10 = f32[6,22,3072]{2,1,0:T(8,128)S(1)} fusion(f32[6,3,3072]{2,1,0:T(4,128)} %collective-permute-done.1, f32[6,16,3072]{2,1,0:T(8,128)S(1)} %copy-done, f32[6,3,3072]{2,1,0:T(4,128)} %collective-permute-done, f32[6,3072]{1,0:T(8,128)S(1)} %copy-done.15, f32[6,3072]{1,0:T(8,128)S(1)} %copy-done.16, pred[22]{0:T(512)(128)(4,1)S(1)} %copy-done.37, ...), kind=kLoop, calls=%fused_computation.21 | loop fusion | flops 1622016 | bytes 3391532 | tf_op jit(solution)/shard_map/jit(_where)/select_n | solution.py:310
  119.3 2.2 %fusion.2 = f32[6,17,3072]{2,1,0:T(8,128)S(1)} fusion(f32[6,22,3072]{2,1,0:T(8,128)S(1)} %get-tuple-element.16, f32[6,22,3072]{2,1,0:T(8,128)S(1)} %get-tuple-element.15), kind=kLoop, calls=%fused_computation.3 | loop fusion | flops 6266880 | bytes 13787136 | tf_op jit(solution)/shard_map/add | solution.py:89
  121.6 0.9 fusion.25
  123.7 1.2 fusion.45
  (176 shorter events, 27.4 us)
Async XLA Ops:
  0.6 21.5 %copy-start.24 = (f32[16,32]{1,0:T(8,128)S(1)}, f32[16,32]{1,0:T(8,128)}, u32[]{:S(2)}) copy-start(f32[16,32]{1,0:T(8,128)} %param.6) | copy-start | bytes 6148
  0.6 18.9 %copy-start = (f32[6,16,3072]{2,1,0:T(8,128)S(1)}, f32[6,16,3072]{2,1,0:T(8,128)}, u32[]{:S(2)}) copy-start(f32[6,16,3072]{2,1,0:T(8,128)} %param.5) | copy-start | bytes 3538948
  1.5 27.8 %collective-permute-start.2 = (f32[3,32]{1,0:T(4,128)S(1)}, f32[3,32]{1,0:T(4,128)S(1)}, u32[]{:S(2)}, u32[]{:S(2)}) collective-permute-start(f32[3,32]{1,0:T(4,128)S(1)} %get-tuple-element.71), channel_id=1, source_target_pairs={{0,16},{16,32},{32,48},{48,64},{64,80},{80,96},{96,112},{112,128},... | collective-permute-start | bytes 1160 | tf_op jit(solution)/shard_map/ppermute | solution.py:25
  4.9 25.7 %collective-permute-start.3 = (f32[3,32]{1,0:T(4,128)S(1)}, f32[3,32]{1,0:T(4,128)S(1)}, u32[]{:S(2)}, u32[]{:S(2)}) collective-permute-start(f32[3,32]{1,0:T(4,128)S(1)} %get-tuple-element.72), channel_id=1, source_target_pairs={{16,0},{32,16},{48,32},{64,48},{80,64},{96,80},{112,96},{128,112},... | collective-permute-start | bytes 1160 | tf_op jit(solution)/shard_map/ppermute | solution.py:28
  11.6 104.3 %collective-permute-start = (f32[6,3,3072]{2,1,0:T(4,128)}, f32[6,3,3072]{2,1,0:T(4,128)}, u32[]{:S(2)}, u32[]{:S(2)}) collective-permute-start(f32[6,3,3072]{2,1,0:T(4,128)} %get-tuple-element.50), channel_id=1, source_target_pairs={{0,16},{16,32},{32,48},{48,64},{64,80},{80,96},{96,112},{112,128},... | collective-permute-start | bytes 663560 | tf_op jit(solution)/shard_map/ppermute | solution.py:25
  13.5 102.4 %collective-permute-start.1 = (f32[6,3,3072]{2,1,0:T(4,128)}, f32[6,3,3072]{2,1,0:T(4,128)}, u32[]{:S(2)}, u32[]{:S(2)}) collective-permute-start(f32[6,3,3072]{2,1,0:T(4,128)} %get-tuple-element.51), channel_id=1, source_target_pairs={{16,0},{32,16},{48,32},{64,48},{80,64},{96,80},{112,96},{128,112},... | collective-permute-start | bytes 663560 | tf_op jit(solution)/shard_map/ppermute | solution.py:28
  20.3 90.0 %collective-permute-start.4 = (f32[6,16,96]{2,1,0:T(8,128)}, f32[6,16,96]{2,1,0:T(8,128)}, u32[]{:S(2)}, u32[]{:S(2)}) collective-permute-start(f32[6,16,96]{2,1,0:T(8,128)} %get-tuple-element.53), channel_id=1, source_target_pairs={{0,1},{1,2},{2,3},{3,4},{4,5},{5,6},{6,7},{7,8},{8,9},{9,10},{10,1... | collective-permute-start | bytes 110600 | tf_op jit(solution)/shard_map/ppermute | solution.py:25
  22.8 73.6 %copy-start.29 = (pred[3072]{0:T(1024)(128)(4,1)}, pred[3072]{0:T(1024)(128)(4,1)S(1)}, u32[]{:S(2)}) copy-start(pred[3072]{0:T(1024)(128)(4,1)S(1)} %get-tuple-element.82) | copy-start | bytes 9220
  25.2 45.5 %copy-start.7 = (f32[1,16,3072]{2,1,0:T(8,128)}, f32[1,16,3072]{2,1,0:T(8,128)S(1)}, u32[]{:S(2)}) copy-start(f32[1,16,3072]{2,1,0:T(8,128)S(1)} %get-tuple-element.3) | copy-start | bytes 589828
  26.2 7.1 %copy-start.22 = (f32[6,16,96]{2,1,0:T(8,128)}, f32[6,16,96]{2,1,0:T(8,128)S(1)}, u32[]{:S(2)}) copy-start(f32[6,16,96]{2,1,0:T(8,128)S(1)} %constant_dynamic-update-slice_fusion) | copy-start | bytes 110596
  26.3 7.1 %copy-start.36 = (pred[22]{0:T(512)(128)(4,1)}, pred[22]{0:T(512)(128)(4,1)S(1)}, u32[]{:S(2)}) copy-start(pred[22]{0:T(512)(128)(4,1)S(1)} %get-tuple-element.73) | copy-start | bytes 70
  26.3 7.1 %copy-start.38 = (pred[22]{0:T(512)(128)(4,1)}, pred[22]{0:T(512)(128)(4,1)S(1)}, u32[]{:S(2)}) copy-start(pred[22]{0:T(512)(128)(4,1)S(1)} %get-tuple-element.74) | copy-start | bytes 70
  29.3 79.7 %collective-permute-start.5 = (f32[6,16,96]{2,1,0:T(8,128)}, f32[6,16,96]{2,1,0:T(8,128)}, u32[]{:S(2)}, u32[]{:S(2)}) collective-permute-start(f32[6,16,96]{2,1,0:T(8,128)} %get-tuple-element.52), channel_id=1, source_target_pairs={{1,0},{2,1},{3,2},{4,3},{5,4},{6,5},{7,6},{8,7},{9,8},{10,9},{11,1... | collective-permute-start | bytes 110600 | tf_op jit(solution)/shard_map/ppermute | solution.py:28
  93.4 3.0 %copy-start.31 = (pred[3072]{0:T(1024)(128)(4,1)S(1)}, pred[3072]{0:T(1024)(128)(4,1)}, u32[]{:S(2)}) copy-start(pred[3072]{0:T(1024)(128)(4,1)} %get-tuple-element.81) | copy-start | bytes 9220
  93.4 3.0 %copy-start.32 = (pred[3072]{0:T(1024)(128)(4,1)S(1)}, pred[3072]{0:T(1024)(128)(4,1)}, u32[]{:S(2)}) copy-start(pred[3072]{0:T(1024)(128)(4,1)} %get-tuple-element.79) | copy-start | bytes 9220
  93.4 2.9 %copy-start.33 = (pred[3072]{0:T(1024)(128)(4,1)S(1)}, pred[3072]{0:T(1024)(128)(4,1)}, u32[]{:S(2)}) copy-start(pred[3072]{0:T(1024)(128)(4,1)} %get-tuple-element.80) | copy-start | bytes 9220
  93.4 2.9 %copy-start.34 = (pred[3072]{0:T(1024)(128)(4,1)S(1)}, pred[3072]{0:T(1024)(128)(4,1)}, u32[]{:S(2)}) copy-start(pred[3072]{0:T(1024)(128)(4,1)} %fusion.63) | copy-start | bytes 9220
  96.4 8.6 %copy-start.21 = (f32[16,32]{1,0:T(8,128)S(1)}, f32[16,32]{1,0:T(8,128)}, u32[]{:S(2)}) copy-start(f32[16,32]{1,0:T(8,128)} %psum.7) | copy-start | bytes 6148
  96.4 8.6 %copy-start.25 = (f32[16,32]{1,0:T(8,128)S(1)}, f32[16,32]{1,0:T(8,128)}, u32[]{:S(2)}) copy-start(f32[16,32]{1,0:T(8,128)} %param.6) | copy-start | bytes 6148
  105.0 2.1 %copy-start.1 = (f32[6,16,3072]{2,1,0:T(8,128)}, f32[6,16,3072]{2,1,0:T(8,128)S(1)}, u32[]{:S(2)}) copy-start(f32[6,16,3072]{2,1,0:T(8,128)S(1)} %fusion.32) | copy-start | bytes 3538948
  108.6 1.6 %copy-start.23 = (f32[6,16,96]{2,1,0:T(8,128)S(1)}, f32[6,16,96]{2,1,0:T(8,128)}, u32[]{:S(2)}) copy-start(f32[6,16,96]{2,1,0:T(8,128)} %copy-done.22) | copy-start | bytes 110596
  110.9 1.7 %copy-start.14 = (f32[3264]{0:T(1024)S(1)}, f32[3264]{0:T(1024)}, u32[]{:S(2)}) copy-start(f32[3264]{0:T(1024)} %mul.830) | copy-start | bytes 39172
  113.5 2.3 %copy-start.15 = (f32[6,3072]{1,0:T(8,128)S(1)}, f32[6,3072]{1,0:T(8,128)}, u32[]{:S(2)}) copy-start(f32[6,3072]{1,0:T(8,128)} %get-tuple-element.77) | copy-start | bytes 221188
  113.5 2.3 %copy-start.16 = (f32[6,3072]{1,0:T(8,128)S(1)}, f32[6,3072]{1,0:T(8,128)}, u32[]{:S(2)}) copy-start(f32[6,3072]{1,0:T(8,128)} %get-tuple-element.78) | copy-start | bytes 221188
  113.5 2.3 %copy-start.37 = (pred[22]{0:T(512)(128)(4,1)S(1)}, pred[22]{0:T(512)(128)(4,1)}, u32[]{:S(2)}) copy-start(pred[22]{0:T(512)(128)(4,1)} %copy-done.36) | copy-start | bytes 70
  113.6 2.3 %copy-start.39 = (pred[22]{0:T(512)(128)(4,1)S(1)}, pred[22]{0:T(512)(128)(4,1)}, u32[]{:S(2)}) copy-start(pred[22]{0:T(512)(128)(4,1)} %copy-done.38) | copy-start | bytes 70
  115.9 1.5 %copy-start.19 = (f32[3072]{0:T(1024)S(1)}, f32[3072]{0:T(1024)}, u32[]{:S(2)}) copy-start(f32[3072]{0:T(1024)} %mul.794) | copy-start | bytes 36868
  119.3 2.3 %copy-start.2 = (f32[6,16,3072]{2,1,0:T(8,128)S(1)}, f32[6,16,3072]{2,1,0:T(8,128)}, u32[]{:S(2)}) copy-start(f32[6,16,3072]{2,1,0:T(8,128)} %copy-done.1) | copy-start | bytes 3538948
  119.3 2.3 %copy-start.4 = (f32[6,16,3041]{2,1,0:T(8,128)S(1)}, f32[6,16,3041]{2,1,0:T(8,128)}, u32[]{:S(2)}) copy-start(f32[6,16,3041]{2,1,0:T(8,128)} %slice.673) | copy-start | bytes 3503236
  119.3 2.3 %copy-start.12 = (f32[16,3072]{1,0:T(8,128)S(1)}, f32[16,3072]{1,0:T(8,128)}, u32[]{:S(2)}) copy-start(f32[16,3072]{1,0:T(8,128)} %get-tuple-element.58) | copy-start | bytes 589828
  119.3 2.3 %copy-start.13 = (f32[16,3072]{1,0:T(8,128)S(1)}, f32[16,3072]{1,0:T(8,128)}, u32[]{:S(2)}) copy-start(f32[16,3072]{1,0:T(8,128)} %get-tuple-element.59) | copy-start | bytes 589828
  119.3 2.3 %copy-start.30 = (pred[3072]{0:T(1024)(128)(4,1)S(1)}, pred[3072]{0:T(1024)(128)(4,1)}, u32[]{:S(2)}) copy-start(pred[3072]{0:T(1024)(128)(4,1)} %copy-done.29) | copy-start | bytes 9220
  (16 other events, 15.4 us)
where the time goes:
time: 126 us; the launch traced here: 125 us
  local copies, waits for them, and re-layouts  43.7 us (35%)
  blocking collectives  31.8 us (25%)
  other arithmetic  28.7 us (23%)
  starting transfers between devices  19.1 us (15%)
  between operations  1.58 us (1%)
    psum x1, blocking collectives, broadcast(): return lax.psum(jnp.where(mine, array, jnp.zeros_like(array)), axis)  31.8 us
    slice x15, local copies, waits for them, and re-layouts, zshift(): jnp.roll(values, offset, axis=-1)  13.7 us
    ppermute x3, starting transfers between devices, padded(): lax.ppermute(lax.slice_in_dim(block, 0, width, axis=dim), axis, backward)  11.9 us
    slice x8, local copies, waits for them, and re-layouts, zshift(): jnp.roll(values, offset + planes, axis=-1)  8.92 us
    add x1, other arithmetic, span_part(): face_sum = upwind + downwind  8.53 us
    ppermute x3, starting transfers between devices, padded(): lax.ppermute(lax.slice_in_dim(block, block.shape[dim] - width, None, axis...  7.2 us
    add x2, other arithmetic, face_difference(): face_sum = upwind + downwind  4.5 us
    unnamed x87, local copies, waits for them, and re-layouts  3.51 us
  transfers between devices with their start and end apart: 6, of which 0 were waited for; matrix products, arithmetic and copies ran while one was open for 49% of the time, Pallas kernels for 0%

commit v1 on v0

--- a/solution.py
+++ b/solution.py
@@ -31,8 +31,19 @@
 
 
 def broadcast(array, axis, root):
-    mine = lax.axis_index(axis) == root
-    return lax.psum(jnp.where(mine, array, jnp.zeros_like(array)), axis)
+    count = lax.axis_size(axis)
+    index = lax.axis_index(axis)
+    holders = [root]
+    while len(holders) < count:
+        waiting = [i for i in range(count) if i not in holders]
+        pairs = list(zip(holders, waiting))
+        received = lax.ppermute(array, axis, pairs)
+        targets = jnp.zeros((), jnp.bool_)
+        for _, target in pairs:
+            targets = targets | (index == target)
+        array = jnp.where(targets, received, array)
+        holders = holders + [target for _, target in pairs]
+    return array
 
 
 def zshift(values, offset, planes):
@@ -332,8 +343,8 @@
     conserved_x = edge_fill(conserved_x, 1, columns, col_dev, col_devs)
     height_ext = edge_fill(height_ext, 0, columns, col_dev, col_devs)
     slope_x, slope_z = slopes(height_ext, planes)
-    own_rate = shock_speed(state[:, :, length - planes :], slope_x, slope_z)
-    shock_rate = broadcast(own_rate, "gy", row_devs - 1)
+    top_row = broadcast(state[:, :, length - planes :], "gy", row_devs - 1)
+    shock_rate = shock_speed(top_row, slope_x, slope_z)
     blowing = wall_flux(wall_segment, segment_level, blow_table)
     halo_y = padded(state, (("gy", 2),), 3 * planes)
     ghost_below = jnp.where(

time: 126 us -> 121 us (0.960)
  the two profiles are of different devices: /device:TPU:8 before, /device:TPU:25 now
where the time goes in v1:
time: 121 us; the launch traced here: 120 us
  local copies, waits for them, and re-layouts  54.2 us (45%)
  other arithmetic  29.9 us (25%)
  starting transfers between devices  27.2 us (22%)
  waiting for transfers between devices  7.14 us (6%)
  between operations  1.82 us (2%)
    slice x15, local copies, waits for them, and re-layouts, zshift(): jnp.roll(values, offset, axis=-1)  13.2 us
    ppermute x3, starting transfers between devices, padded(): lax.ppermute(lax.slice_in_dim(block, 0, width, axis=dim), axis, backward)  11.7 us
    ppermute x3, starting transfers between devices, padded(): lax.ppermute(lax.slice_in_dim(block, block.shape[dim] - width, None, axis...  10.2 us
    slice x8, local copies, waits for them, and re-layouts, zshift(): jnp.roll(values, offset + planes, axis=-1)  8.99 us
    ppermute x4, waiting for transfers between devices, broadcast(): received = lax.ppermute(array, axis, pairs)  7.12 us
    unnamed x149, local copies, waits for them, and re-layouts  6.51 us
    ppermute x4, starting transfers between devices, broadcast(): received = lax.ppermute(array, axis, pairs)  5.3 us
    add x1, other arithmetic, span_part(): face_sum = upwind + downwind  5.16 us
  transfers between devices with their start and end apart: 10, of which 2 were waited for; matrix products, arithmetic and copies ran while one was open for 58% of the time, Pallas kernels for 0%

profile of v1, /device:TPU:25, one launch (start us, length us, event | category | flops | bytes accessed | tf_op | source)
XLA Modules:
  0.0 120.2 jit_solution(2555888381047456505)
XLA Ops:
  0.7 1.6 %slice.495 = f32[6,16,32]{2,1,0:T(8,128)} slice(f32[6,16,3072]{2,1,0:T(8,128)} %param.5), slice={[0:6], [0:16], [3040:3072]} | slice | bytes 24576 | tf_op jit(solution)/shard_map/slice | solution.py:357
  4.2 3.1 %collective-permute-start.2 = (f32[3,32]{1,0:T(4,128)S(1)}, f32[3,32]{1,0:T(4,128)S(1)}, u32[]{:S(2)}, u32[]{:S(2)}) collective-permute-start(f32[3,32]{1,0:T(4,128)S(1)} %get-tuple-element.72), channel_id=1, source_target_pairs={{0,16},{16,32},{32,48},{48,64},{64,80},{80,96},{96,112},{112,128},... | collective-permute-start | bytes 1160 | tf_op jit(solution)/shard_map/ppermute | solution.py:25
  7.3 4.3 %collective-permute-start.3 = (f32[3,32]{1,0:T(4,128)S(1)}, f32[3,32]{1,0:T(4,128)S(1)}, u32[]{:S(2)}, u32[]{:S(2)}) collective-permute-start(f32[3,32]{1,0:T(4,128)S(1)} %get-tuple-element.73), channel_id=1, source_target_pairs={{16,0},{32,16},{48,32},{64,48},{80,64},{96,80},{112,96},{128,112},... | collective-permute-start | bytes 1160 | tf_op jit(solution)/shard_map/ppermute | solution.py:28
  11.6 2.2 %fusion.91 = (f32[6,3,3072]{2,1,0:T(4,128)}, f32[6,3,3072]{2,1,0:T(4,128)}) fusion(f32[6,16,3072]{2,1,0:T(8,128)} %param.5), kind=kLoop, calls=%fused_computation.212 | loop fusion | bytes 884736 | tf_op jit(solution)/shard_map/slice | solution.py:26
  13.8 1.9 %collective-permute-start = (f32[6,3,3072]{2,1,0:T(4,128)}, f32[6,3,3072]{2,1,0:T(4,128)}, u32[]{:S(2)}, u32[]{:S(2)}) collective-permute-start(f32[6,3,3072]{2,1,0:T(4,128)} %get-tuple-element.51), channel_id=1, source_target_pairs={{0,16},{16,32},{32,48},{48,64},{64,80},{80,96},{96,112},{112,128},... | collective-permute-start | bytes 663560 | tf_op jit(solution)/shard_map/ppermute | solution.py:25
  15.7 5.5 %collective-permute-start.1 = (f32[6,3,3072]{2,1,0:T(4,128)}, f32[6,3,3072]{2,1,0:T(4,128)}, u32[]{:S(2)}, u32[]{:S(2)}) collective-permute-start(f32[6,3,3072]{2,1,0:T(4,128)} %get-tuple-element.52), channel_id=1, source_target_pairs={{16,0},{32,16},{48,32},{64,48},{80,64},{96,80},{112,96},{128,112},... | collective-permute-start | bytes 663560 | tf_op jit(solution)/shard_map/ppermute | solution.py:28
  31.3 5.2 %collective-permute-start.4 = (f32[6,16,96]{2,1,0:T(8,128)}, f32[6,16,96]{2,1,0:T(8,128)}, u32[]{:S(2)}, u32[]{:S(2)}) collective-permute-start(f32[6,16,96]{2,1,0:T(8,128)} %get-tuple-element.54), channel_id=1, source_target_pairs={{0,1},{1,2},{2,3},{3,4},{4,5},{5,6},{6,7},{7,8},{8,9},{9,10},{10,1... | collective-permute-start | bytes 110600 | tf_op jit(solution)/shard_map/ppermute | solution.py:25
  36.5 1.9 %collective-permute-start.5 = (f32[6,16,96]{2,1,0:T(8,128)}, f32[6,16,96]{2,1,0:T(8,128)}, u32[]{:S(2)}, u32[]{:S(2)}) collective-permute-start(f32[6,16,96]{2,1,0:T(8,128)} %get-tuple-element.53), channel_id=1, source_target_pairs={{1,0},{2,1},{3,2},{4,3},{5,4},{6,5},{7,6},{8,7},{9,8},{10,9},{11,1... | collective-permute-start | bytes 110600 | tf_op jit(solution)/shard_map/ppermute | solution.py:28
  43.8 1.7 %broadcast_multiply_fusion.2 = f32[22,3072]{1,0:T(8,128)} fusion(f32[22,3072]{1,0:T(8,128)} %tile.35, f32[3072]{0:T(1024)S(1)} %mul.794), kind=kLoop, calls=%fused_computation.132 | loop fusion | flops 67584 | bytes 552960 | tf_op jit(solution)/shard_map/mul | solution.py:122
  47.9 1.3 %collective-permute-start.7 = (f32[6,16,32]{2,1,0:T(8,128)S(1)}, f32[6,16,32]{2,1,0:T(8,128)S(1)}, u32[]{:S(2)}, u32[]{:S(2)}) collective-permute-start(f32[6,16,32]{2,1,0:T(8,128)S(1)} %get-tuple-element.56), channel_id=1, source_target_pairs={{15,1},{0,2},{31,17},{16,18},{47,33},{32,34},{63,49},{48,50},{79,6... | collective-permute-start | bytes 36872 | tf_op jit(solution)/shard_map/ppermute | solution.py:40
  49.3 6.0 %collective-permute-done.7 = f32[6,16,32]{2,1,0:T(8,128)S(1)} collective-permute-done((f32[6,16,32]{2,1,0:T(8,128)S(1)}, f32[6,16,32]{2,1,0:T(8,128)S(1)}, u32[]{:S(2)}, u32[]{:S(2)}) %collective-permute-start.7) | collective-permute-done | bytes 12320 | tf_op jit(solution)/shard_map/ppermute | solution.py:40
  55.3 1.3 %collective-permute-start.8 = (f32[6,16,32]{2,1,0:T(8,128)S(1)}, f32[6,16,32]{2,1,0:T(8,128)S(1)}, u32[]{:S(2)}, u32[]{:S(2)}) collective-permute-start(f32[6,16,32]{2,1,0:T(8,128)S(1)} %broadcast_select_fusion.1), channel_id=1, source_target_pairs={{15,3},{0,4},{1,5},{2,6},{31,19},{16,20},{17,21},{18,22},{47,35},{... | collective-permute-start | bytes 36872 | tf_op jit(solution)/shard_map/ppermute | solution.py:40
  57.8 1.5 %collective-permute-start.9 = (f32[6,16,32]{2,1,0:T(8,128)S(1)}, f32[6,16,32]{2,1,0:T(8,128)S(1)}, u32[]{:S(2)}, u32[]{:S(2)}) collective-permute-start(f32[6,16,32]{2,1,0:T(8,128)S(1)} %broadcast_select_fusion.2), channel_id=1, source_target_pairs={{15,7},{0,8},{1,9},{2,10},{3,11},{4,12},{5,13},{6,14},{31,23},{16,... | collective-permute-start | bytes 36872 | tf_op jit(solution)/shard_map/ppermute | solution.py:40
  61.0 1.4 %concatenate.126 = f32[6,16,3264]{2,1,0:T(8,128)} concatenate(f32[6,16,96]{2,1,0:T(8,128)S(1)} %broadcast_select_fusion.5, f32[6,16,3072]{2,1,0:T(8,128)S(1)} %copy-done, f32[6,16,96]{2,1,0:T(8,128)S(1)} %broadcast_select_fusion.4), dimensions={2} | concatenate | bytes 2506752 | tf_op jit(solution)/shard_map/concatenate | solution.py:360
  64.5 1.6 %broadcast_multiply_fusion = (f32[6,16,3072]{2,1,0:T(8,128)S(1)}, f32[6,16,3072]{2,1,0:T(8,128)S(1)}) fusion(f32[6,16,3072]{2,1,0:T(8,128)S(1)} %copy-done, f32[16,3072]{1,0:T(8,128)S(1)} %copy-done.18, f32[6,16,3072]{2,1,0:T(8,128)} %multiply_dynamic-update-slice_fusion.6, f32[16,3072]{1,0:T(8,128)S(1)} %get-tuple-element.61), kind=kLoop, calls=%fused_computation.85 | loop fusion | flops 1769472 | bytes 5111808 | tf_op jit(solution)/shard_map/mul | solution.py:113
  66.1 1.8 %fusion.79 = (f32[6,16,3041]{2,1,0:T(8,128)}, f32[6,16,3041]{2,1,0:T(8,128)}) fusion(f32[6,16,3072]{2,1,0:T(8,128)S(1)} %get-tuple-element.20), kind=kLoop, calls=%fused_computation.200 | loop fusion | bytes 4670976 | tf_op jit(solution)/shard_map/jit(_roll_static)/slice | solution.py:61
  68.0 1.8 %fusion.80 = (f32[6,16,3071]{2,1,0:T(8,128)}, f32[6,16,3071]{2,1,0:T(8,128)}) fusion(f32[6,16,3072]{2,1,0:T(8,128)S(1)} %get-tuple-element.20), kind=kLoop, calls=%fused_computation.201 | loop fusion | bytes 4717056 | tf_op jit(solution)/shard_map/jit(_roll_static)/slice | solution.py:60
  69.7 1.8 %fusion.83 = (f32[6,16,3042]{2,1,0:T(8,128)}, f32[6,16,3042]{2,1,0:T(8,128)}) fusion(f32[6,16,3072]{2,1,0:T(8,128)S(1)} %get-tuple-element.21), kind=kLoop, calls=%fused_computation.204 | loop fusion | bytes 4672512 | tf_op jit(solution)/shard_map/jit(_roll_static)/slice | solution.py:61
  71.5 1.8 %fusion.84 = (f32[6,16,3070]{2,1,0:T(8,128)}, f32[6,16,3070]{2,1,0:T(8,128)}) fusion(f32[6,16,3072]{2,1,0:T(8,128)S(1)} %get-tuple-element.21), kind=kLoop, calls=%fused_computation.205 | loop fusion | bytes 4715520 | tf_op jit(solution)/shard_map/jit(_roll_static)/slice | solution.py:60
  73.4 1.9 %fusion.87 = (f32[6,16,3041]{2,1,0:T(8,128)}, f32[6,16,3041]{2,1,0:T(8,128)}) fusion(f32[6,16,3072]{2,1,0:T(8,128)S(1)} %get-tuple-element.21), kind=kLoop, calls=%fused_computation.208 | loop fusion | bytes 4670976 | tf_op jit(solution)/shard_map/jit(_roll_static)/slice | solution.py:61
  75.2 1.8 %fusion.88 = (f32[6,16,3071]{2,1,0:T(8,128)}, f32[6,16,3071]{2,1,0:T(8,128)}) fusion(f32[6,16,3072]{2,1,0:T(8,128)S(1)} %get-tuple-element.21), kind=kLoop, calls=%fused_computation.209 | loop fusion | bytes 4717056 | tf_op jit(solution)/shard_map/jit(_roll_static)/slice | solution.py:60
  77.4 1.4 %slice.667 = f32[6,16,3069]{2,1,0:T(8,128)} slice(f32[6,16,3072]{2,1,0:T(8,128)S(1)} %get-tuple-element.20), slice={[0:6], [0:16], [3:3072]} | slice | bytes 2356992 | tf_op jit(solution)/shard_map/jit(_roll_static)/slice | solution.py:60
  86.6 2.1 %tile.41 = f32[1,16,3264]{2,1,0:T(8,128)} reshape(f32[16,102,32]{2,1,0:T(8,128)} %tile.40) | data formatting | bytes 417792 | tf_op jit(solution)/shard_map/tile | solution.py:153
  88.6 1.6 %tile.42 = f32[16,102,32]{2,1,0:T(8,128)} broadcast(f32[16,32]{1,0:T(8,128)} %get-tuple-element.4), dimensions={0,2} | broadcast | bytes 210944 | tf_op jit(solution)/shard_map/tile | solution.py:151
  90.3 2.1 %tile.43 = f32[1,16,3264]{2,1,0:T(8,128)} reshape(f32[16,102,32]{2,1,0:T(8,128)} %tile.42) | data formatting | bytes 417792 | tf_op jit(solution)/shard_map/tile | solution.py:151
  92.3 1.6 %tile.44 = f32[16,102,32]{2,1,0:T(8,128)} broadcast(f32[16,32]{1,0:T(8,128)} %get-tuple-element.5), dimensions={0,2} | broadcast | bytes 210944 | tf_op jit(solution)/shard_map/tile | solution.py:152
  94.0 2.1 %tile.90 = f32[1,16,3264]{2,1,0:T(8,128)} reshape(f32[16,102,32]{2,1,0:T(8,128)} %tile.44) | data formatting | bytes 417792 | tf_op jit(solution)/shard_map/tile | solution.py:152
  96.1 2.0 %add_bitcast_fusion = (f32[16,3264]{1,0:T(8,128)S(1)}, f32[1,16,3264]{2,1,0:T(8,128)S(1)}, f32[1,16,3264]{2,1,0:T(8,128)S(1)}) fusion(f32[1,16,3264]{2,1,0:T(8,128)} %tile.90, f32[1,16,3264]{2,1,0:T(8,128)} %tile.43, f32[6,16,3264]{2,1,0:T(8,128)} %concatenate.126, f32[3264]{0:T(1024)S(1)} %mul.830, f32[1,16,3264]{2,1,0:T(8,128)} %tile.41), kind=kLoop, calls=%fused_computation.105 | loop fusion | flops 1514496 | bytes 2519808 | tf_op jit(solution)/shard_map/mul | solution.py:113
  99.9 2.3 %fusion.13 = f32[6,16,3104]{2,1,0:T(8,128)S(1)} fusion(f32[6,16,3264]{2,1,0:T(8,128)S(1)} %get-tuple-element.19, f32[6,16,3264]{2,1,0:T(8,128)S(1)} %get-tuple-element.18), kind=kLoop, calls=%fused_computation.29 | loop fusion | flops 5959680 | bytes 13111296 | tf_op jit(solution)/shard_map/add | solution.py:100
  105.0 5.2 %fusion.32 = f32[6,16,3072]{2,1,0:T(8,128)S(1)} fusion(f32[6,16,3070]{2,1,0:T(8,128)S(1)} %copy-done.10, f32[6,16,2]{2,1,0:T(8,128)S(1)} %copy-done.43, f32[6,16,30]{2,1,0:T(8,128)S(1)} %copy-done.41, f32[6,16,3042]{2,1,0:T(8,128)S(1)} %copy-done.8, f32[6,16,3071]{2,1,0:T(8,128)S(1)} %copy-done.14, f32[6,16,1]{2,1,0:T(8,128)S(1)} %copy-done.47, ...), kind=kLoop, calls=%fused_computation.60 | loop fusion | flops 14155776 | bytes 22821888 | tf_op jit(solution)/shard_map/add | solution.py:208
  111.1 1.5 %fusion.10 = f32[6,22,3072]{2,1,0:T(8,128)S(1)} fusion(f32[6,3,3072]{2,1,0:T(4,128)} %collective-permute-done.1, f32[6,16,3072]{2,1,0:T(8,128)S(1)} %copy-done, f32[6,3,3072]{2,1,0:T(4,128)} %collective-permute-done, f32[6,3072]{1,0:T(8,128)S(1)} %copy-done.28, f32[6,3072]{1,0:T(8,128)S(1)} %copy-done.29, pred[22]{0:T(512)(128)(4,1)} %copy-done.69, ...), kind=kLoop, calls=%fused_computation.21 | loop fusion | flops 1622016 | bytes 3391532 | tf_op jit(solution)/shard_map/jit(_where)/select_n | solution.py:321
  114.5 2.4 %fusion.2 = f32[6,17,3072]{2,1,0:T(8,128)S(1)} fusion(f32[6,22,3072]{2,1,0:T(8,128)S(1)} %get-tuple-element.17, f32[6,22,3072]{2,1,0:T(8,128)S(1)} %get-tuple-element.16), kind=kLoop, calls=%fused_computation.3 | loop fusion | flops 6266880 | bytes 13787136 | tf_op jit(solution)/shard_map/add | solution.py:100
  (248 shorter events, 42.9 us)
Async XLA Ops:
  0.6 20.6 %copy-start = (f32[6,16,3072]{2,1,0:T(8,128)S(1)}, f32[6,16,3072]{2,1,0:T(8,128)}, u32[]{:S(2)}) copy-start(f32[6,16,3072]{2,1,0:T(8,128)} %param.5) | copy-start | bytes 3538948
  0.6 20.6 %copy-start.52 = (f32[16,32]{1,0:T(8,128)S(1)}, f32[16,32]{1,0:T(8,128)}, u32[]{:S(2)}) copy-start(f32[16,32]{1,0:T(8,128)} %param.6) | copy-start | bytes 6148
  2.2 45.5 %collective-permute-start.6 = (f32[6,16,32]{2,1,0:T(8,128)}, f32[6,16,32]{2,1,0:T(8,128)}, u32[]{:S(2)}, u32[]{:S(2)}) collective-permute-start(f32[6,16,32]{2,1,0:T(8,128)} %slice.495), channel_id=1, source_target_pairs={{15,0},{31,16},{47,32},{63,48},{79,64},{95,80},{111,96},{127,112},... | collective-permute-start | bytes 36872 | tf_op jit(solution)/shard_map/ppermute | solution.py:40
  4.2 27.0 %collective-permute-start.2 = (f32[3,32]{1,0:T(4,128)S(1)}, f32[3,32]{1,0:T(4,128)S(1)}, u32[]{:S(2)}, u32[]{:S(2)}) collective-permute-start(f32[3,32]{1,0:T(4,128)S(1)} %get-tuple-element.72), channel_id=1, source_target_pairs={{0,16},{16,32},{32,48},{48,64},{64,80},{80,96},{96,112},{112,128},... | collective-permute-start | bytes 1160 | tf_op jit(solution)/shard_map/ppermute | solution.py:25
  7.3 29.2 %collective-permute-start.3 = (f32[3,32]{1,0:T(4,128)S(1)}, f32[3,32]{1,0:T(4,128)S(1)}, u32[]{:S(2)}, u32[]{:S(2)}) collective-permute-start(f32[3,32]{1,0:T(4,128)S(1)} %get-tuple-element.73), channel_id=1, source_target_pairs={{16,0},{32,16},{48,32},{64,48},{80,64},{96,80},{112,96},{128,112},... | collective-permute-start | bytes 1160 | tf_op jit(solution)/shard_map/ppermute | solution.py:28
  13.8 96.9 %collective-permute-start = (f32[6,3,3072]{2,1,0:T(4,128)}, f32[6,3,3072]{2,1,0:T(4,128)}, u32[]{:S(2)}, u32[]{:S(2)}) collective-permute-start(f32[6,3,3072]{2,1,0:T(4,128)} %get-tuple-element.51), channel_id=1, source_target_pairs={{0,16},{16,32},{32,48},{48,64},{64,80},{80,96},{96,112},{112,128},... | collective-permute-start | bytes 663560 | tf_op jit(solution)/shard_map/ppermute | solution.py:25
  15.7 95.0 %collective-permute-start.1 = (f32[6,3,3072]{2,1,0:T(4,128)}, f32[6,3,3072]{2,1,0:T(4,128)}, u32[]{:S(2)}, u32[]{:S(2)}) collective-permute-start(f32[6,3,3072]{2,1,0:T(4,128)} %get-tuple-element.52), channel_id=1, source_target_pairs={{16,0},{32,16},{48,32},{64,48},{80,64},{96,80},{112,96},{128,112},... | collective-permute-start | bytes 663560 | tf_op jit(solution)/shard_map/ppermute | solution.py:28
  24.7 39.0 %copy-start.30 = (f32[3072]{0:T(1024)}, f32[3072]{0:T(1024)S(1)}, u32[]{:S(2)}) copy-start(f32[3072]{0:T(1024)S(1)} %mul.794) | copy-start | bytes 36868
  27.7 13.3 %copy-start.22 = (f32[1,16,3072]{2,1,0:T(8,128)}, f32[1,16,3072]{2,1,0:T(8,128)S(1)}, u32[]{:S(2)}) copy-start(f32[1,16,3072]{2,1,0:T(8,128)S(1)} %get-tuple-element.7) | copy-start | bytes 589828
  30.5 10.0 %copy-start.69 = (pred[22]{0:T(512)(128)(4,1)}, pred[22]{0:T(512)(128)(4,1)S(1)}, u32[]{:S(2)}) copy-start(pred[22]{0:T(512)(128)(4,1)S(1)} %get-tuple-element.74) | copy-start | bytes 70
  30.6 10.0 %copy-start.70 = (pred[22]{0:T(512)(128)(4,1)}, pred[22]{0:T(512)(128)(4,1)S(1)}, u32[]{:S(2)}) copy-start(pred[22]{0:T(512)(128)(4,1)S(1)} %get-tuple-element.75) | copy-start | bytes 70
  31.3 28.0 %collective-permute-start.4 = (f32[6,16,96]{2,1,0:T(8,128)}, f32[6,16,96]{2,1,0:T(8,128)}, u32[]{:S(2)}, u32[]{:S(2)}) collective-permute-start(f32[6,16,96]{2,1,0:T(8,128)} %get-tuple-element.54), channel_id=1, source_target_pairs={{0,1},{1,2},{2,3},{3,4},{4,5},{5,6},{6,7},{7,8},{8,9},{9,10},{10,1... | collective-permute-start | bytes 110600 | tf_op jit(solution)/shard_map/ppermute | solution.py:25
  36.5 23.6 %collective-permute-start.5 = (f32[6,16,96]{2,1,0:T(8,128)}, f32[6,16,96]{2,1,0:T(8,128)}, u32[]{:S(2)}, u32[]{:S(2)}) collective-permute-start(f32[6,16,96]{2,1,0:T(8,128)} %get-tuple-element.53), channel_id=1, source_target_pairs={{1,0},{2,1},{3,2},{4,3},{5,4},{6,5},{7,6},{8,7},{9,8},{10,9},{11,1... | collective-permute-start | bytes 110600 | tf_op jit(solution)/shard_map/ppermute | solution.py:28
  46.5 13.5 %copy-start.48 = (f32[6,16,96]{2,1,0:T(8,128)S(1)}, f32[6,16,96]{2,1,0:T(8,128)}, u32[]{:S(2)}) copy-start(f32[6,16,96]{2,1,0:T(8,128)} %tile.39) | copy-start | bytes 110596
  47.9 7.4 %collective-permute-start.7 = (f32[6,16,32]{2,1,0:T(8,128)S(1)}, f32[6,16,32]{2,1,0:T(8,128)S(1)}, u32[]{:S(2)}, u32[]{:S(2)}) collective-permute-start(f32[6,16,32]{2,1,0:T(8,128)S(1)} %get-tuple-element.56), channel_id=1, source_target_pairs={{15,1},{0,2},{31,17},{16,18},{47,33},{32,34},{63,49},{48,50},{79,6... | collective-permute-start | bytes 36872 | tf_op jit(solution)/shard_map/ppermute | solution.py:40
  55.3 2.5 %collective-permute-start.8 = (f32[6,16,32]{2,1,0:T(8,128)S(1)}, f32[6,16,32]{2,1,0:T(8,128)S(1)}, u32[]{:S(2)}, u32[]{:S(2)}) collective-permute-start(f32[6,16,32]{2,1,0:T(8,128)S(1)} %broadcast_select_fusion.1), channel_id=1, source_target_pairs={{15,3},{0,4},{1,5},{2,6},{31,19},{16,20},{17,21},{18,22},{47,35},{... | collective-permute-start | bytes 36872 | tf_op jit(solution)/shard_map/ppermute | solution.py:40
  57.8 4.7 %collective-permute-start.9 = (f32[6,16,32]{2,1,0:T(8,128)S(1)}, f32[6,16,32]{2,1,0:T(8,128)S(1)}, u32[]{:S(2)}, u32[]{:S(2)}) collective-permute-start(f32[6,16,32]{2,1,0:T(8,128)S(1)} %broadcast_select_fusion.2), channel_id=1, source_target_pairs={{15,7},{0,8},{1,9},{2,10},{3,11},{4,12},{5,13},{6,14},{31,23},{16,... | collective-permute-start | bytes 36872 | tf_op jit(solution)/shard_map/ppermute | solution.py:40
  78.8 6.8 %copy-start.50 = (f32[16,32]{1,0:T(8,128)S(1)}, f32[16,32]{1,0:T(8,128)}, u32[]{:S(2)}) copy-start(f32[16,32]{1,0:T(8,128)} %copy-done.49) | copy-start | bytes 6148
  99.8 3.5 %copy-start.7 = (f32[6,16,3042]{2,1,0:T(8,128)S(1)}, f32[6,16,3042]{2,1,0:T(8,128)}, u32[]{:S(2)}) copy-start(f32[6,16,3042]{2,1,0:T(8,128)} %get-tuple-element.35) | copy-start | bytes 3504388
  99.8 3.8 %copy-start.8 = (f32[6,16,3042]{2,1,0:T(8,128)S(1)}, f32[6,16,3042]{2,1,0:T(8,128)}, u32[]{:S(2)}) copy-start(f32[6,16,3042]{2,1,0:T(8,128)} %get-tuple-element.36) | copy-start | bytes 3504388
  99.8 4.2 %copy-start.9 = (f32[6,16,3070]{2,1,0:T(8,128)S(1)}, f32[6,16,3070]{2,1,0:T(8,128)}, u32[]{:S(2)}) copy-start(f32[6,16,3070]{2,1,0:T(8,128)} %get-tuple-element.37) | copy-start | bytes 3536644
  99.8 4.5 %copy-start.10 = (f32[6,16,3070]{2,1,0:T(8,128)S(1)}, f32[6,16,3070]{2,1,0:T(8,128)}, u32[]{:S(2)}) copy-start(f32[6,16,3070]{2,1,0:T(8,128)} %get-tuple-element.38) | copy-start | bytes 3536644
  99.8 4.8 %copy-start.11 = (f32[6,16,3041]{2,1,0:T(8,128)S(1)}, f32[6,16,3041]{2,1,0:T(8,128)}, u32[]{:S(2)}) copy-start(f32[6,16,3041]{2,1,0:T(8,128)} %get-tuple-element.43) | copy-start | bytes 3503236
  99.8 5.1 %copy-start.12 = (f32[6,16,3041]{2,1,0:T(8,128)S(1)}, f32[6,16,3041]{2,1,0:T(8,128)}, u32[]{:S(2)}) copy-start(f32[6,16,3041]{2,1,0:T(8,128)} %get-tuple-element.44) | copy-start | bytes 3503236
  99.8 5.1 %copy-start.19 = (f32[16,3072]{1,0:T(8,128)S(1)}, f32[16,3072]{1,0:T(8,128)}, u32[]{:S(2)}) copy-start(f32[16,3072]{1,0:T(8,128)} %get-tuple-element.24) | copy-start | bytes 589828
  99.8 5.2 %copy-start.21 = (f32[16,3072]{1,0:T(8,128)S(1)}, f32[16,3072]{1,0:T(8,128)}, u32[]{:S(2)}) copy-start(f32[16,3072]{1,0:T(8,128)} %copy-done.20) | copy-start | bytes 589828
  99.8 5.1 %copy-start.32 = (f32[6,16,2]{2,1,0:T(8,128)S(1)}, f32[6,16,2]{2,1,0:T(8,128)}, u32[]{:S(2)}) copy-start(f32[6,16,2]{2,1,0:T(8,128)} %slice.664) | copy-start | bytes 2308
  99.9 5.1 %copy-start.33 = (f32[6,16,30]{2,1,0:T(8,128)S(1)}, f32[6,16,30]{2,1,0:T(8,128)}, u32[]{:S(2)}) copy-start(f32[6,16,30]{2,1,0:T(8,128)} %slice.665) | copy-start | bytes 34564
  99.9 5.1 %copy-start.34 = (f32[6,16,3]{2,1,0:T(8,128)S(1)}, f32[6,16,3]{2,1,0:T(8,128)}, u32[]{:S(2)}) copy-start(f32[6,16,3]{2,1,0:T(8,128)} %slice.668) | copy-start | bytes 3460
  99.9 5.1 %copy-start.35 = (f32[6,16,29]{2,1,0:T(8,128)S(1)}, f32[6,16,29]{2,1,0:T(8,128)}, u32[]{:S(2)}) copy-start(f32[6,16,29]{2,1,0:T(8,128)} %slice.669) | copy-start | bytes 33412
  99.9 5.1 %copy-start.63 = (pred[3072]{0:T(1024)(128)(4,1)S(1)}, pred[3072]{0:T(1024)(128)(4,1)}, u32[]{:S(2)}) copy-start(pred[3072]{0:T(1024)(128)(4,1)} %get-tuple-element.83) | copy-start | bytes 9220
  99.9 5.1 %copy-start.64 = (pred[3072]{0:T(1024)(128)(4,1)S(1)}, pred[3072]{0:T(1024)(128)(4,1)}, u32[]{:S(2)}) copy-start(pred[3072]{0:T(1024)(128)(4,1)} %get-tuple-element.82) | copy-start | bytes 9220
  (51 other events, 108.5 us)

commit v2 on v1

--- a/solution.py
+++ b/solution.py
@@ -3,6 +3,8 @@
 import jax
 import jax.numpy as jnp
 from jax import lax
+from jax.experimental import pallas as pl
+from jax.experimental.pallas import tpu as pltpu
 from jax.sharding import PartitionSpec as P
 
 HEAT_RATIO = 1.4
@@ -15,6 +17,149 @@
 FREE_PRESSURE = 0.1
 FREE_MACH = 6.0
 COURANT = 0.05
+
+
+PLUS_WEIGHTS = (-2.0, 15.0, -60.0, 20.0, 30.0, -3.0, 0.0)
+MINUS_WEIGHTS = (0.0, 3.0, -30.0, -20.0, 60.0, -15.0, 2.0)
+CHUNK = 256
+PAD = 128
+
+
+def kernel_primitives(q):
+    inverse = 1.0 / q[0]
+    vel_x = q[1] * inverse
+    vel_y = q[2] * inverse
+    vel_z = q[3] * inverse
+    stress = (HEAT_RATIO - 1.0) * (q[4] - 0.5 * (q[1] * vel_x + q[2] * vel_y + q[3] * vel_z) - q[5])
+    sound = jnp.sqrt(HEAT_RATIO * stress * inverse)
+    return inverse, vel_x, vel_y, vel_z, stress, sound
+
+
+def combined(plus, minus, t):
+    a = PLUS_WEIGHTS[t + 3]
+    b = MINUS_WEIGHTS[t + 3]
+    if a == 0.0:
+        return b * minus
+    if b == 0.0:
+        return a * plus
+    return a * plus + b * minus
+
+
+def make_kernel(columns, length, planes, dt):
+    width = CHUNK + 2 * PAD
+    face_area = STREAM_STEP * SPAN_STEP
+
+    def kernel(qx_ref, qy_ref, hx_ref, hz_ref, sx_ref, sz_ref, rt_ref, rh_ref, s_ref, eta_ref,
+               out_ref, px_ref, mx_ref):
+        lane = lax.broadcasted_iota(jnp.int32, (columns, CHUNK), 1) % planes
+
+        def body(k, carry):
+            o = pl.multiple_of(k * CHUNK, CHUNK)
+            spacing = s_ref[:, pl.ds(o, CHUNK)]
+            xa = [qx_ref[c, :, pl.ds(o, CHUNK)] for c in range(6)]
+            inverse, vel_x, vel_y, vel_z, stress, sound = kernel_primitives(xa)
+            metric = STREAM_STEP * hx_ref[...] * spacing
+            fluxes = [xa[1], xa[1] * vel_x + stress, xa[2] * vel_x, xa[3] * vel_x,
+                      (xa[4] + stress) * vel_x, xa[5] * vel_x]
+            speed = (jnp.abs(vel_x) + sound) * metric
+            for c in range(6):
+                f = fluxes[c] * metric
+                px_ref[c] = 0.5 * (f + speed * xa[c])
+                mx_ref[c] = 0.5 * (f - speed * xa[c])
+            div = []
+            for c in range(6):
+                acc = None
+                for t in range(-3, 4):
+                    term = None
+                    a = PLUS_WEIGHTS[t + 3]
+                    b = MINUS_WEIGHTS[t + 3]
+                    if a != 0.0:
+                        term = a * px_ref[c, pl.ds(t + 3, columns), :]
+                    if b != 0.0:
+                        mterm = b * mx_ref[c, pl.ds(t + 3, columns), :]
+                        term = mterm if term is None else term + mterm
+                    acc = term if acc is None else acc + term
+                div.append(acc)
+            ya = [qy_ref[c, :, pl.ds(o, width)] for c in range(6)]
+            inverse, vel_x, vel_y, vel_z, stress, sound = kernel_primitives(ya)
+            eta = eta_ref[:, pl.ds(o, width)]
+            scaled = -face_area * eta
+            metric_x = scaled * sx_ref[...]
+            metric_z = scaled * sz_ref[...]
+            metric_t = scaled * rt_ref[...]
+            contra = metric_t + metric_x * vel_x + face_area * vel_y + metric_z * vel_z
+            fluxes = [ya[0] * contra, ya[1] * contra + metric_x * stress,
+                      ya[2] * contra + face_area * stress, ya[3] * contra + metric_z * stress,
+                      (ya[4] + stress) * contra - metric_t * stress, ya[5] * contra]
+            speed = jnp.abs(contra) + sound * jnp.sqrt(
+                metric_x * metric_x + face_area * face_area + metric_z * metric_z)
+            for c in range(6):
+                plus = 0.5 * (fluxes[c] + speed * ya[c])
+                minus = 0.5 * (fluxes[c] - speed * ya[c])
+                acc = None
+                for t in range(-3, 4):
+                    term = combined(plus, minus, t)
+                    if t != 0:
+                        term = pltpu.roll(term, (-planes * t) % width, 1)
+                    acc = term if acc is None else acc + term
+                div[c] = div[c] + acc[:, PAD:PAD + CHUNK]
+            q = [v[:, PAD:PAD + CHUNK] for v in ya]
+            inverse = inverse[:, PAD:PAD + CHUNK]
+            vel_x = vel_x[:, PAD:PAD + CHUNK]
+            vel_z = vel_z[:, PAD:PAD + CHUNK]
+            stress = stress[:, PAD:PAD + CHUNK]
+            sound = sound[:, PAD:PAD + CHUNK]
+            height = hz_ref[...]
+            metric = STREAM_STEP * height * spacing
+            fluxes = [q[3], q[1] * vel_z, q[2] * vel_z, q[3] * vel_z + stress,
+                      (q[4] + stress) * vel_z, q[5] * vel_z]
+            speed = (jnp.abs(vel_z) + sound) * metric
+            for c in range(6):
+                f = fluxes[c] * metric
+                plus = 0.5 * (f + speed * q[c])
+                minus = 0.5 * (f - speed * q[c])
+                acc = None
+                for t in range(-3, 4):
+                    term = combined(plus, minus, t)
+                    if t > 0:
+                        term = jnp.where(lane < planes - t, pltpu.roll(term, CHUNK - t, 1),
+                                         pltpu.roll(term, planes - t, 1))
+                    elif t < 0:
+                        term = jnp.where(lane >= -t, pltpu.roll(term, -t, 1),
+                                         pltpu.roll(term, (CHUNK - planes - t) % CHUNK, 1))
+                    acc = term if acc is None else acc + term
+                div[c] = div[c] + acc
+            kelvin = stress * inverse
+            balanced = CHARACTER_KELVIN / (jnp.exp(CHARACTER_KELVIN / kelvin) - 1.0)
+            teller = stress / (LANDAU_TELLER * jnp.exp(
+                WHITE_LAW_FACTOR * jnp.exp(-jnp.log(kelvin) / 3.0)))
+            source = q[0] * (balanced - q[5] * inverse) * teller
+            volume = face_area * height * spacing
+            ratio = rh_ref[...]
+            for c in range(6):
+                change = -(div[c] * (1.0 / 60.0)) / volume - q[c] * ratio
+                if c == 5:
+                    change = change + source
+                out_ref[c, :, pl.ds(o, CHUNK)] = q[c] + dt * change
+            return carry
+
+        lax.fori_loop(0, length // CHUNK, body, 0)
+
+    return kernel
+
+
+def update(qx, qy, hx, hz, sx, sz, rt, rh, s_lane, eta_lane, planes, dt, interpret=False):
+    columns = hz.shape[0]
+    length = s_lane.shape[1]
+    kern = make_kernel(columns, length, planes, dt)
+    rows_x = qx.shape[1]
+    return pl.pallas_call(
+        kern,
+        out_shape=jax.ShapeDtypeStruct((6, columns, length), jnp.float32),
+        scratch_shapes=[pltpu.VMEM((6, rows_x, CHUNK), jnp.float32),
+                        pltpu.VMEM((6, rows_x, CHUNK), jnp.float32)],
+        interpret=interpret,
+    )(qx, qy, hx, hz, sx, sz, rt, rh, s_lane, eta_lane)
 
 
 def padded(block, sides, width):
@@ -357,18 +502,31 @@
         jnp.tile(state[..., length - planes :], (1, 1, 3)),
         halo_y[..., length + 3 * planes :],
     )
-    conserved_y = jnp.concatenate([ghost_below, state, ghost_above], axis=2)
-    state_new = advance(
-        state,
+    conserved_y = jnp.concatenate(
+        [ghost_below[..., :planes], ghost_below, state, ghost_above, ghost_above[..., -planes:]], axis=2
+    )
+    conserved_x = jnp.concatenate([conserved_x, conserved_x[:, -2:]], axis=1)
+    width = CHUNK + 2 * PAD
+    height = height_ext[3 : columns + 3]
+    first_row = row_dev * row_count
+    local_rows = (first_row + jnp.arange(row_count, dtype=jnp.int32)).astype(jnp.float32)
+    spacing_lane = jnp.repeat(stretch(local_rows, total_rows)[1], planes)[None, :]
+    outer_rows = (first_row - 4 + jnp.arange(row_count + 8, dtype=jnp.int32)).astype(jnp.float32)
+    eta_lane = jnp.repeat(stretch(outer_rows, total_rows)[0], planes)[None, :]
+    height_x = jnp.tile(jnp.concatenate([height_ext, height_ext[-2:]], axis=0), (1, CHUNK // planes))
+    state_new = update(
         conserved_x,
         conserved_y,
-        height_ext,
-        slope_x,
-        slope_z,
-        shock_rate,
-        row_dev * row_count,
-        total_rows,
+        height_x,
+        jnp.tile(height, (1, CHUNK // planes)),
+        jnp.tile(slope_x, (1, width // planes)),
+        jnp.tile(slope_z, (1, width // planes)),
+        jnp.tile(shock_rate, (1, width // planes)),
+        jnp.tile(shock_rate / height, (1, CHUNK // planes)),
+        spacing_lane,
+        eta_lane,
         planes,
+        COURANT / total_rows,
     )
     shock_new = shock_height + COURANT / total_rows * shock_rate
     return (state_new, shock_new)

time: 121 us -> 65.3 us (0.54)
  the two profiles are of different devices: /device:TPU:25 before, /device:TPU:232 now
where the time goes in v2:
time: 65.3 us; the launch traced here: 64.8 us
  starting transfers between devices  23.5 us (36%)
  local copies, waits for them, and re-layouts  13.8 us (21%)
  Pallas kernels  12.8 us (20%)
  waiting for transfers between devices  10.3 us (16%)
  other arithmetic  3.28 us (5%)
  between operations  1.11 us (2%)
    pallas_call x1, Pallas kernels, update(): pl.pallas_call(kern, out_shape=jax.ShapeDtypeStruct((6, columns, length),...  12.8 us
    ppermute x3, starting transfers between devices, padded(): lax.ppermute(lax.slice_in_dim(block, 0, width, axis=dim), axis, backward)  12.5 us
    ppermute x4, waiting for transfers between devices, broadcast(): received = lax.ppermute(array, axis, pairs)  10.3 us
    ppermute x3, starting transfers between devices, padded(): lax.ppermute(lax.slice_in_dim(block, block.shape[dim] - width, None, axis...  7.71 us
    ppermute x4, starting transfers between devices, broadcast(): received = lax.ppermute(array, axis, pairs)  3.28 us
    slice x2, local copies, waits for them, and re-layouts, padded(): lax.slice_in_dim(block, block.shape[dim] - width, None, axis=dim)  2.15 us
    concatenate x1, other arithmetic, shards(): conserved_x = jnp.concatenate([conserved_x, conserved_x[:, -2:]], axis=1)  1.42 us
    slice x1, local copies, waits for them, and re-layouts, edge_fill(): trailing = lax.slice_in_dim(values, cells + 2, cells + 3, axis=axis_at)  1.35 us
  transfers between devices with their start and end apart: 10, of which 1 were waited for; matrix products, arithmetic and copies ran while one was open for 22% of the time, Pallas kernels for 0%

profile of v2, /device:TPU:232, one launch (start us, length us, event | category | flops | bytes accessed | tf_op | source)
XLA Modules:
  0.0 64.8 jit_solution(7741849138569044427)
XLA Ops:
  0.7 0.8 %fusion.20 = (f32[3,32]{1,0:T(4,128)S(1)}, f32[3,32]{1,0:T(4,128)S(1)}) fusion(f32[16,32]{1,0:T(8,128)} %param.6), kind=kLoop, calls=%fused_computation.64 | loop fusion | bytes 1536 | tf_op jit(solution)/shard_map/slice | solution.py:171
  1.5 3.4 %collective-permute-start.4 = (f32[3,32]{1,0:T(4,128)S(1)}, f32[3,32]{1,0:T(4,128)S(1)}, u32[]{:S(2)}, u32[]{:S(2)}) collective-permute-start(f32[3,32]{1,0:T(4,128)S(1)} %get-tuple-element.28), channel_id=1, source_target_pairs={{0,16},{16,32},{32,48},{48,64},{64,80},{80,96},{96,112},{112,128},... | collective-permute-start | bytes 1160 | tf_op jit(solution)/shard_map/ppermute | solution.py:170
  4.9 4.6 %collective-permute-start.5 = (f32[3,32]{1,0:T(4,128)S(1)}, f32[3,32]{1,0:T(4,128)S(1)}, u32[]{:S(2)}, u32[]{:S(2)}) collective-permute-start(f32[3,32]{1,0:T(4,128)S(1)} %get-tuple-element.29), channel_id=1, source_target_pairs={{16,0},{32,16},{48,32},{64,48},{80,64},{96,80},{112,96},{128,112},... | collective-permute-start | bytes 1160 | tf_op jit(solution)/shard_map/ppermute | solution.py:173
  9.4 0.9 %slice.190 = f32[6,16,32]{2,1,0:T(8,128)S(1)} slice(f32[6,16,3072]{2,1,0:T(8,128)} %param.5), slice={[0:6], [0:16], [3040:3072]} | slice | bytes 24576 | tf_op jit(solution)/shard_map/slice | solution.py:502
  10.3 0.7 %collective-permute-start.6 = (f32[6,16,32]{2,1,0:T(8,128)S(1)}, f32[6,16,32]{2,1,0:T(8,128)S(1)}, u32[]{:S(2)}, u32[]{:S(2)}) collective-permute-start(f32[6,16,32]{2,1,0:T(8,128)S(1)} %slice.190), channel_id=1, source_target_pairs={{15,0},{31,16},{47,32},{63,48},{79,64},{95,80},{111,96},{127,112},... | collective-permute-start | bytes 36872 | tf_op jit(solution)/shard_map/ppermute | solution.py:185
  11.0 0.9 %fusion.13 = (f32[6,16,96]{2,1,0:T(8,128)S(1)}, f32[6,16,96]{2,1,0:T(8,128)S(1)}) fusion(f32[6,16,3072]{2,1,0:T(8,128)} %param.5), kind=kLoop, calls=%fused_computation.57 | loop fusion | bytes 147456 | tf_op jit(solution)/shard_map/slice | solution.py:497
  11.9 1.9 %collective-permute-start.3 = (f32[6,16,96]{2,1,0:T(8,128)S(1)}, f32[6,16,96]{2,1,0:T(8,128)S(1)}, u32[]{:S(2)}, u32[]{:S(2)}) collective-permute-start(f32[6,16,96]{2,1,0:T(8,128)S(1)} %get-tuple-element.10), channel_id=1, source_target_pairs={{1,0},{2,1},{3,2},{4,3},{5,4},{6,5},{7,6},{8,7},{9,8},{10,9},{11,1... | collective-permute-start | bytes 110600 | tf_op jit(solution)/shard_map/ppermute | solution.py:173
  13.8 2.4 %collective-permute-start.2 = (f32[6,16,96]{2,1,0:T(8,128)S(1)}, f32[6,16,96]{2,1,0:T(8,128)S(1)}, u32[]{:S(2)}, u32[]{:S(2)}) collective-permute-start(f32[6,16,96]{2,1,0:T(8,128)S(1)} %get-tuple-element.11), channel_id=1, source_target_pairs={{0,1},{1,2},{2,3},{3,4},{4,5},{5,6},{6,7},{7,8},{8,9},{9,10},{10,1... | collective-permute-start | bytes 110600 | tf_op jit(solution)/shard_map/ppermute | solution.py:170
  16.2 0.7 %slice_bitcast_fusion.7 = (f32[32]{0:T(128)S(1)}, f32[32]{0:T(128)S(1)}) fusion(f32[16,32]{1,0:T(8,128)} %param.6), kind=kLoop, calls=%fused_computation.55 | loop fusion | bytes 512 | tf_op jit(solution)/shard_map/jit(_where)/broadcast_in_dim | solution.py:466
  16.9 1.3 %fusion.14 = (f32[6,1,3072]{2,1,0:T(1,128)S(1)}, f32[6,1,3072]{2,1,0:T(1,128)S(1)}) fusion(f32[6,16,3072]{2,1,0:T(8,128)} %param.5), kind=kLoop, calls=%fused_computation.58 | loop fusion | bytes 294912 | tf_op jit(solution)/shard_map/slice | solution.py:464
  18.3 1.4 %fusion.15 = (f32[6,3,3072]{2,1,0:T(4,128)S(1)}, f32[6,3,3072]{2,1,0:T(4,128)S(1)}) fusion(f32[6,16,3072]{2,1,0:T(8,128)} %param.5), kind=kLoop, calls=%fused_computation.59 | loop fusion | bytes 884736 | tf_op jit(solution)/shard_map/slice | solution.py:171
  19.7 0.2 select_reduce_fusion.1
  20.3 0.7 %broadcast_in_dim_reshape.6.s_ref = f32[1,3072]{1,0:T(1,128)} reshape(f32[96,32]{1,0:T(8,128)S(1)} %broadcast_in_dim.127) | data formatting | bytes 24576 | tf_op jit(solution)/shard_map/broadcast_in_dim;reshape | solution.py:513
  21.1 0.7 %broadcast_in_dim_reshape.7.eta_ref = f32[1,3328]{1,0:T(1,128)} reshape(f32[104,32]{1,0:T(8,128)S(1)} %broadcast_in_dim.128) | data formatting | bytes 26624 | tf_op jit(solution)/shard_map/broadcast_in_dim;reshape | solution.py:515
  21.8 0.1 tile.32
  22.1 1.9 %collective-permute-start = (f32[6,3,3072]{2,1,0:T(4,128)S(1)}, f32[6,3,3072]{2,1,0:T(4,128)S(1)}, u32[]{:S(2)}, u32[]{:S(2)}) collective-permute-start(f32[6,3,3072]{2,1,0:T(4,128)S(1)} %get-tuple-element.14), channel_id=1, source_target_pairs={{0,16},{16,32},{32,48},{48,64},{64,80},{80,96},{96,112},{112,128},... | collective-permute-start | bytes 663560 | tf_op jit(solution)/shard_map/ppermute | solution.py:170
  24.0 6.0 %collective-permute-start.1 = (f32[6,3,3072]{2,1,0:T(4,128)S(1)}, f32[6,3,3072]{2,1,0:T(4,128)S(1)}, u32[]{:S(2)}, u32[]{:S(2)}) collective-permute-start(f32[6,3,3072]{2,1,0:T(4,128)S(1)} %get-tuple-element.15), channel_id=1, source_target_pairs={{16,0},{32,16},{48,32},{64,48},{80,64},{96,80},{112,96},{128,112},... | collective-permute-start | bytes 663560 | tf_op jit(solution)/shard_map/ppermute | solution.py:173
  30.5 0.7 %tile.34.hx_ref = f32[24,256]{1,0:T(8,128)} reshape(f32[24,8,32]{2,1,0:T(8,128)S(1)} %tile.33) | data formatting | bytes 49152 | tf_op jit(solution)/shard_map/tile | solution.py:516
  31.4 0.7 %collective-permute-start.7 = (f32[6,16,32]{2,1,0:T(8,128)S(1)}, f32[6,16,32]{2,1,0:T(8,128)S(1)}, u32[]{:S(2)}, u32[]{:S(2)}) collective-permute-start(f32[6,16,32]{2,1,0:T(8,128)S(1)} %get-tuple-element.6), channel_id=1, source_target_pairs={{15,1},{0,2},{31,17},{16,18},{47,33},{32,34},{63,49},{48,50},{79,6... | collective-permute-start | bytes 36872 | tf_op jit(solution)/shard_map/ppermute | solution.py:185
  32.1 0.7 %collective-permute-start.8 = (f32[6,16,32]{2,1,0:T(8,128)S(1)}, f32[6,16,32]{2,1,0:T(8,128)S(1)}, u32[]{:S(2)}, u32[]{:S(2)}) collective-permute-start(f32[6,16,32]{2,1,0:T(8,128)S(1)} %broadcast_select_fusion.1), channel_id=1, source_target_pairs={{15,3},{0,4},{1,5},{2,6},{31,19},{16,20},{17,21},{18,22},{47,35},{... | collective-permute-start | bytes 36872 | tf_op jit(solution)/shard_map/ppermute | solution.py:185
  32.8 1.3 %collective-permute-start.9 = (f32[6,16,32]{2,1,0:T(8,128)S(1)}, f32[6,16,32]{2,1,0:T(8,128)S(1)}, u32[]{:S(2)}, u32[]{:S(2)}) collective-permute-start(f32[6,16,32]{2,1,0:T(8,128)S(1)} %broadcast_select_fusion.2), channel_id=1, source_target_pairs={{15,7},{0,8},{1,9},{2,10},{3,11},{4,12},{5,13},{6,14},{31,23},{16,... | collective-permute-start | bytes 36872 | tf_op jit(solution)/shard_map/ppermute | solution.py:185
  34.3 1.2 %concatenate.61.qy_ref = f32[6,16,3328]{2,1,0:T(8,128)} concatenate(f32[6,16,32]{2,1,0:T(8,128)S(1)} %bitcast.45, f32[6,16,96]{2,1,0:T(8,128)S(1)} %broadcast_select_fusion.5, f32[6,16,3072]{2,1,0:T(8,128)S(1)} %copy-done, f32[6,16,96]{2,1,0:T(8,128)S(1)} %broadcast_select_fusion.4, f32[6,16,32]{2,1,0:T(8,128)S(1)} %slice.225), dimensions={2} | concatenate | bytes 2555904 | tf_op jit(solution)/shard_map/concatenate | solution.py:505
  35.5 10.3 %collective-permute-done.9 = f32[6,16,32]{2,1,0:T(8,128)S(1)} collective-permute-done((f32[6,16,32]{2,1,0:T(8,128)S(1)}, f32[6,16,32]{2,1,0:T(8,128)S(1)}, u32[]{:S(2)}, u32[]{:S(2)}) %collective-permute-start.9) | collective-permute-done | bytes 12320 | tf_op jit(solution)/shard_map/ppermute | solution.py:185
  45.8 0.7 %multiply_add_fusion = (f32[16,32]{1,0:T(8,128)}, f32[16,32]{1,0:T(8,128)S(1)}, f32[16,32]{1,0:T(8,128)S(1)}, f32[16,32]{1,0:T(8,128)S(1)}) fusion(f32[16,32]{1,0:T(8,128)S(1)} %copy-done.1, f32[6,16,32]{2,1,0:T(8,128)S(1)} %broadcast_select_fusion.3, f32[16,2]{1,0:T(8,128)S(1)} %get-tuple-element.19, f32[16,30]{1,0:T(8,128)S(1)} %get-tuple-element.21, ...), kind=kLoop, calls=%fused_computation.43 | loop fusion | flops 27136 | bytes 38912 | tf_op jit(solution)/shard_map/add | solution.py:531
  46.5 0.7 %tile.84.rh_ref = f32[16,256]{1,0:T(8,128)} reshape(f32[16,8,32]{2,1,0:T(8,128)S(1)} %tile.83) | data formatting | bytes 32768 | tf_op jit(solution)/shard_map/tile | solution.py:525
  47.2 0.7 %tile.36.hz_ref = f32[16,256]{1,0:T(8,128)} reshape(f32[16,8,32]{2,1,0:T(8,128)S(1)} %tile.35) | data formatting | bytes 32768 | tf_op jit(solution)/shard_map/tile | solution.py:521
  47.9 0.7 %tile.82.rt_ref = f32[16,512]{1,0:T(8,128)} reshape(f32[16,16,32]{2,1,0:T(8,128)S(1)} %tile.81) | data formatting | bytes 65536 | tf_op jit(solution)/shard_map/tile | solution.py:524
  48.6 0.7 %tile.80.sz_ref = f32[16,512]{1,0:T(8,128)} reshape(f32[16,16,32]{2,1,0:T(8,128)S(1)} %tile.39) | data formatting | bytes 65536 | tf_op jit(solution)/shard_map/tile | solution.py:523
  49.4 0.7 %tile.38.sx_ref = f32[16,512]{1,0:T(8,128)} reshape(f32[16,16,32]{2,1,0:T(8,128)S(1)} %tile.37) | data formatting | bytes 65536 | tf_op jit(solution)/shard_map/tile | solution.py:522
  50.1 0.4 fusion
  50.5 1.4 %pad_maximum_fusion.qx_ref = f32[6,24,3072]{2,1,0:T(8,128)} fusion(f32[6,2,3072]{2,1,0:T(2,128)S(1)} %slice.217, f32[6,22,3072]{2,1,0:T(8,128)S(1)} %fusion), kind=kLoop, calls=%fused_computation.2 | loop fusion | flops 442368 | bytes 3538944 | tf_op jit(solution)/shard_map/concatenate | solution.py:508
  52.0 12.8 %shard_map.68 = f32[6,16,3072]{2,1,0:T(8,128)} custom-call(f32[6,24,3072]{2,1,0:T(8,128)} %pad_maximum_fusion.qx_ref, f32[6,16,3328]{2,1,0:T(8,128)} %concatenate.61.qy_ref, f32[24,256]{1,0:T(8,128)} %tile.34.hx_ref, f32[16,256]{1,0:T(8,128)} %tile.36.hz_ref, f32[16,512]{1,0:T(8,128)} %tile.38.sx_ref, f32[16,512]{1,0:T(8,128)} %tile.80.sz_ref, ...), custom_call_target="tpu_custom_call" | custom-call | tf_op jit(solution)/shard_map/pallas_call | solution.py:156
  (59 shorter events, 1.4 us)
Async XLA Ops:
  0.6 29.4 %copy-start.1 = (f32[16,32]{1,0:T(8,128)S(1)}, f32[16,32]{1,0:T(8,128)}, u32[]{:S(2)}) copy-start(f32[16,32]{1,0:T(8,128)} %param.6) | copy-start | bytes 6148
  0.6 30.5 %copy-start = (f32[6,16,3072]{2,1,0:T(8,128)S(1)}, f32[6,16,3072]{2,1,0:T(8,128)}, u32[]{:S(2)}) copy-start(f32[6,16,3072]{2,1,0:T(8,128)} %param.5) | copy-start | bytes 3538948
  0.7 19.1 %copy-start.3 = (s32[16]{0:T(128)S(1)}, s32[16]{0:T(128)}, u32[]{:S(2)}) copy-start(s32[16]{0:T(128)} %param.8) | copy-start | bytes 196
  0.7 19.1 %copy-start.4 = (s32[16]{0:T(128)S(1)}, s32[16]{0:T(128)}, u32[]{:S(2)}) copy-start(s32[16]{0:T(128)} %param.7) | copy-start | bytes 196
  0.7 19.3 %copy-start.2 = (f32[16,32]{1,0:T(8,128)S(1)}, f32[16,32]{1,0:T(8,128)}, u32[]{:S(2)}) copy-start(f32[16,32]{1,0:T(8,128)} %param.9) | copy-start | bytes 6148
  1.5 20.6 %collective-permute-start.4 = (f32[3,32]{1,0:T(4,128)S(1)}, f32[3,32]{1,0:T(4,128)S(1)}, u32[]{:S(2)}, u32[]{:S(2)}) collective-permute-start(f32[3,32]{1,0:T(4,128)S(1)} %get-tuple-element.28), channel_id=1, source_target_pairs={{0,16},{16,32},{32,48},{48,64},{64,80},{80,96},{96,112},{112,128},... | collective-permute-start | bytes 1160 | tf_op jit(solution)/shard_map/ppermute | solution.py:170
  4.9 19.1 %collective-permute-start.5 = (f32[3,32]{1,0:T(4,128)S(1)}, f32[3,32]{1,0:T(4,128)S(1)}, u32[]{:S(2)}, u32[]{:S(2)}) collective-permute-start(f32[3,32]{1,0:T(4,128)S(1)} %get-tuple-element.29), channel_id=1, source_target_pairs={{16,0},{32,16},{48,32},{64,48},{80,64},{96,80},{112,96},{128,112},... | collective-permute-start | bytes 1160 | tf_op jit(solution)/shard_map/ppermute | solution.py:173
  10.3 20.8 %collective-permute-start.6 = (f32[6,16,32]{2,1,0:T(8,128)S(1)}, f32[6,16,32]{2,1,0:T(8,128)S(1)}, u32[]{:S(2)}, u32[]{:S(2)}) collective-permute-start(f32[6,16,32]{2,1,0:T(8,128)S(1)} %slice.190), channel_id=1, source_target_pairs={{15,0},{31,16},{47,32},{63,48},{79,64},{95,80},{111,96},{127,112},... | collective-permute-start | bytes 36872 | tf_op jit(solution)/shard_map/ppermute | solution.py:185
  11.9 22.3 %collective-permute-start.3 = (f32[6,16,96]{2,1,0:T(8,128)S(1)}, f32[6,16,96]{2,1,0:T(8,128)S(1)}, u32[]{:S(2)}, u32[]{:S(2)}) collective-permute-start(f32[6,16,96]{2,1,0:T(8,128)S(1)} %get-tuple-element.10), channel_id=1, source_target_pairs={{1,0},{2,1},{3,2},{4,3},{5,4},{6,5},{7,6},{8,7},{9,8},{10,9},{11,1... | collective-permute-start | bytes 110600 | tf_op jit(solution)/shard_map/ppermute | solution.py:173
  13.8 20.3 %collective-permute-start.2 = (f32[6,16,96]{2,1,0:T(8,128)S(1)}, f32[6,16,96]{2,1,0:T(8,128)S(1)}, u32[]{:S(2)}, u32[]{:S(2)}) collective-permute-start(f32[6,16,96]{2,1,0:T(8,128)S(1)} %get-tuple-element.11), channel_id=1, source_target_pairs={{0,1},{1,2},{2,3},{3,4},{4,5},{5,6},{6,7},{7,8},{8,9},{9,10},{10,1... | collective-permute-start | bytes 110600 | tf_op jit(solution)/shard_map/ppermute | solution.py:170
  22.1 28.0 %collective-permute-start = (f32[6,3,3072]{2,1,0:T(4,128)S(1)}, f32[6,3,3072]{2,1,0:T(4,128)S(1)}, u32[]{:S(2)}, u32[]{:S(2)}) collective-permute-start(f32[6,3,3072]{2,1,0:T(4,128)S(1)} %get-tuple-element.14), channel_id=1, source_target_pairs={{0,16},{16,32},{32,48},{48,64},{64,80},{80,96},{96,112},{112,128},... | collective-permute-start | bytes 663560 | tf_op jit(solution)/shard_map/ppermute | solution.py:170
  24.0 26.1 %collective-permute-start.1 = (f32[6,3,3072]{2,1,0:T(4,128)S(1)}, f32[6,3,3072]{2,1,0:T(4,128)S(1)}, u32[]{:S(2)}, u32[]{:S(2)}) collective-permute-start(f32[6,3,3072]{2,1,0:T(4,128)S(1)} %get-tuple-element.15), channel_id=1, source_target_pairs={{16,0},{32,16},{48,32},{64,48},{80,64},{96,80},{112,96},{128,112},... | collective-permute-start | bytes 663560 | tf_op jit(solution)/shard_map/ppermute | solution.py:173
  31.4 0.7 %collective-permute-start.7 = (f32[6,16,32]{2,1,0:T(8,128)S(1)}, f32[6,16,32]{2,1,0:T(8,128)S(1)}, u32[]{:S(2)}, u32[]{:S(2)}) collective-permute-start(f32[6,16,32]{2,1,0:T(8,128)S(1)} %get-tuple-element.6), channel_id=1, source_target_pairs={{15,1},{0,2},{31,17},{16,18},{47,33},{32,34},{63,49},{48,50},{79,6... | collective-permute-start | bytes 36872 | tf_op jit(solution)/shard_map/ppermute | solution.py:185
  32.1 0.7 %collective-permute-start.8 = (f32[6,16,32]{2,1,0:T(8,128)S(1)}, f32[6,16,32]{2,1,0:T(8,128)S(1)}, u32[]{:S(2)}, u32[]{:S(2)}) collective-permute-start(f32[6,16,32]{2,1,0:T(8,128)S(1)} %broadcast_select_fusion.1), channel_id=1, source_target_pairs={{15,3},{0,4},{1,5},{2,6},{31,19},{16,20},{17,21},{18,22},{47,35},{... | collective-permute-start | bytes 36872 | tf_op jit(solution)/shard_map/ppermute | solution.py:185
  32.8 13.0 %collective-permute-start.9 = (f32[6,16,32]{2,1,0:T(8,128)S(1)}, f32[6,16,32]{2,1,0:T(8,128)S(1)}, u32[]{:S(2)}, u32[]{:S(2)}) collective-permute-start(f32[6,16,32]{2,1,0:T(8,128)S(1)} %broadcast_select_fusion.2), channel_id=1, source_target_pairs={{15,7},{0,8},{1,9},{2,10},{3,11},{4,12},{5,13},{6,14},{31,23},{16,... | collective-permute-start | bytes 36872 | tf_op jit(solution)/shard_map/ppermute | solution.py:185

commit v3 on v2

v3 whole, which is shorter than its diff:
```python
import math

import jax
import jax.numpy as jnp
from jax import lax
from jax.experimental import pallas as pl
from jax.experimental.pallas import tpu as pltpu
from jax.sharding import PartitionSpec as P

HEAT_RATIO = 1.4
STREAM_STEP = 0.05
SPAN_STEP = 0.05
STRETCH_RATE = 2.0
CHARACTER_KELVIN = 3.0
WHITE_LAW_FACTOR = 1.0
LANDAU_TELLER = 0.002
FREE_PRESSURE = 0.1
FREE_MACH = 6.0
COURANT = 0.05

PLUS_WEIGHTS = (-2.0, 15.0, -60.0, 20.0, 30.0, -3.0, 0.0)
MINUS_WEIGHTS = (0.0, 3.0, -30.0, -20.0, 60.0, -15.0, 2.0)
CHUNK = 256
PAD = 128
HALO = 3
XPAD = 8
LANES = 128


def kernel_primitives(q):
    inverse = 1.0 / q[0]
    vel_x = q[1] * inverse
    vel_y = q[2] * inverse
    vel_z = q[3] * inverse
    stress = (HEAT_RATIO - 1.0) * (q[4] - 0.5 * (q[1] * vel_x + q[2] * vel_y + q[3] * vel_z) - q[5])
    sound = jnp.sqrt(HEAT_RATIO * stress * inverse)
    return inverse, vel_x, vel_y, vel_z, stress, sound


def combined(plus, minus, t):
    a = PLUS_WEIGHTS[t + 3]
    b = MINUS_WEIGHTS[t + 3]
    if a == 0.0:
        return b * minus
    if b == 0.0:
        return a * plus
    return a * plus + b * minus


def lane_tile(values, width):
    return jnp.concatenate([values] * (width // values.shape[-1]), axis=-1)


def stretch_factors(rows, total_rows):
    growth = jnp.exp(STRETCH_RATE * (rows + 0.5) / total_rows)
    denominator = math.exp(STRETCH_RATE) - 1.0
    return (growth - 1.0) / denominator, STRETCH_RATE * growth / (total_rows * denominator)


def make_kernel(columns, length, planes, total_rows, dt):
    width = CHUNK + 2 * PAD
    face_area = STREAM_STEP * SPAN_STEP
    xrows = columns + 2 * XPAD

    def kernel(flags_ref, state_ref, xlo_ref, xhi_ref, ylo_ref, yhi_ref, geo_ref,
               out_ref, qx_ref, qy_ref, px_ref, mx_ref):
        first_row = flags_ref[0]
        for c in range(6):
            qx_ref[c, 0:XPAD, :] = state_ref[c, 0:XPAD, :]
            qx_ref[c, XPAD:XPAD + columns, :] = state_ref[c]
            qx_ref[c, XPAD + columns:, :] = state_ref[c, columns - XPAD:, :]
            qx_ref[c, XPAD - HALO:XPAD, :] = xlo_ref[c]
            qx_ref[c, XPAD + columns:XPAD + columns + HALO, :] = xhi_ref[c]
            qy_ref[c, :, 0:PAD] = ylo_ref[c]
            qy_ref[c, :, PAD:PAD + length] = state_ref[c]
            qy_ref[c, :, PAD + length:] = yhi_ref[c]

        @pl.when(flags_ref[1] == 1)
        def _():
            for c in range(6):
                qx_ref[c, XPAD - HALO:XPAD, :] = jnp.broadcast_to(state_ref[c, 0:1, :], (HALO, length))

        @pl.when(flags_ref[2] == 1)
        def _():
            for c in range(6):
                qx_ref[c, XPAD + columns:XPAD + columns + HALO, :] = jnp.broadcast_to(
                    state_ref[c, columns - 1:columns, :], (HALO, length))

        height_x = lane_tile(geo_ref[0:xrows, :], CHUNK)
        slope_x = lane_tile(geo_ref[xrows:xrows + columns, :], width)
        slope_z = lane_tile(geo_ref[xrows + columns:xrows + 2 * columns, :], width)
        rate = lane_tile(geo_ref[xrows + 2 * columns:xrows + 3 * columns, :], width)
        ratio = lane_tile(geo_ref[xrows + 3 * columns:xrows + 4 * columns, :], CHUNK)
        height = lane_tile(geo_ref[xrows + 4 * columns:xrows + 5 * columns, :], CHUNK)
        lane = lax.broadcasted_iota(jnp.int32, (columns, CHUNK), 1) % planes
        lane_in = lax.broadcasted_iota(jnp.int32, (1, CHUNK), 1)
        lane_out = lax.broadcasted_iota(jnp.int32, (1, width), 1)

        def body(k, carry):
            o = pl.multiple_of(k * CHUNK, CHUNK)
            rows_in = (first_row + (o + lane_in) // planes).astype(jnp.float32)
            spacing = stretch_factors(rows_in, total_rows)[1]
            rows_out = (first_row - PAD // planes + (o + lane_out) // planes).astype(jnp.float32)
            eta = stretch_factors(rows_out, total_rows)[0]
            xa = [qx_ref[c, :, pl.ds(o, CHUNK)] for c in range(6)]
            inverse, vel_x, vel_y, vel_z, stress, sound = kernel_primitives(xa)
            metric = STREAM_STEP * height_x * spacing
            fluxes = [xa[1], xa[1] * vel_x + stress, xa[2] * vel_x, xa[3] * vel_x,
                      (xa[4] + stress) * vel_x, xa[5] * vel_x]
            speed = (jnp.abs(vel_x) + sound) * metric
            for c in range(6):
                f = fluxes[c] * metric
                px_ref[c] = 0.5 * (f + speed * xa[c])
                mx_ref[c] = 0.5 * (f - speed * xa[c])
            div = []
            for c in range(6):
                acc = None
                for t in range(-3, 4):
                    term = None
                    a = PLUS_WEIGHTS[t + 3]
                    b = MINUS_WEIGHTS[t + 3]
                    if a != 0.0:
                        term = a * px_ref[c, pl.ds(XPAD + t, columns), :]
                    if b != 0.0:
                        mterm = b * mx_ref[c, pl.ds(XPAD + t, columns), :]
                        term = mterm if term is None else term + mterm
                    acc = term if acc is None else acc + term
                div.append(acc)
            ya = [qy_ref[c, :, pl.ds(o, width)] for c in range(6)]
            inverse, vel_x, vel_y, vel_z, stress, sound = kernel_primitives(ya)
            scaled = -face_area * eta
            metric_x = scaled * slope_x
            metric_z = scaled * slope_z
            metric_t = scaled * rate
            contra = metric_t + metric_x * vel_x + face_area * vel_y + metric_z * vel_z
            fluxes = [ya[0] * contra, ya[1] * contra + metric_x * stress,
                      ya[2] * contra + face_area * stress, ya[3] * contra + metric_z * stress,
                      (ya[4] + stress) * contra - metric_t * stress, ya[5] * contra]
            speed = jnp.abs(contra) + sound * jnp.sqrt(
                metric_x * metric_x + face_area * face_area + metric_z * metric_z)
            for c in range(6):
                plus = 0.5 * (fluxes[c] + speed * ya[c])
                minus = 0.5 * (fluxes[c] - speed * ya[c])
                acc = None
                for t in range(-3, 4):
                    term = combined(plus, minus, t)
                    if t != 0:
                        term = pltpu.roll(term, (-planes * t) % width, 1)
                    acc = term if acc is None else acc + term
                div[c] = div[c] + acc[:, PAD:PAD + CHUNK]
            q = [v[:, PAD:PAD + CHUNK] for v in ya]
            inverse = inverse[:, PAD:PAD + CHUNK]
            vel_z = vel_z[:, PAD:PAD + CHUNK]
            stress = stress[:, PAD:PAD + CHUNK]
            sound = sound[:, PAD:PAD + CHUNK]
            metric = STREAM_STEP * height * spacing
            fluxes = [q[3], q[1] * vel_z, q[2] * vel_z, q[3] * vel_z + stress,
                      (q[4] + stress) * vel_z, q[5] * vel_z]
            speed = (jnp.abs(vel_z) + sound) * metric
            for c in range(6):
                f = fluxes[c] * metric
                plus = 0.5 * (f + speed * q[c])
                minus = 0.5 * (f - speed * q[c])
                acc = None
                for t in range(-3, 4):
                    term = combined(plus, minus, t)
                    if t > 0:
                        term = jnp.where(lane < planes - t, pltpu.roll(term, CHUNK - t, 1),
                                         pltpu.roll(term, planes - t, 1))
                    elif t < 0:
                        term = jnp.where(lane >= -t, pltpu.roll(term, -t, 1),
                                         pltpu.roll(term, (CHUNK - planes - t) % CHUNK, 1))
                    acc = term if acc is None else acc + term
                div[c] = div[c] + acc
            kelvin = stress * inverse
            balanced = CHARACTER_KELVIN / (jnp.exp(CHARACTER_KELVIN / kelvin) - 1.0)
            teller = stress / (LANDAU_TELLER * jnp.exp(
                WHITE_LAW_FACTOR * jnp.exp(-jnp.log(kelvin) / 3.0)))
            source = q[0] * (balanced - q[5] * inverse) * teller
            volume = face_area * height * spacing
            for c in range(6):
                change = -(div[c] * (1.0 / 60.0)) / volume - q[c] * ratio
                if c == 5:
                    change = change + source
                out_ref[c, :, pl.ds(o, CHUNK)] = q[c] + dt * change
            return carry

        lax.fori_loop(0, length // CHUNK, body, 0)

    return kernel


def update(flags, state, xlo, xhi, ylo, yhi, geo, planes, total_rows, dt):
    columns = state.shape[1]
    length = state.shape[2]
    kern = make_kernel(columns, length, planes, total_rows, dt)
    vmem = pl.BlockSpec(memory_space=pltpu.VMEM)
    return pl.pallas_call(
        kern,
        out_shape=jax.ShapeDtypeStruct((6, columns, length), jnp.float32),
        in_specs=[pl.BlockSpec(memory_space=pltpu.SMEM)] + [vmem] * 6,
        out_specs=vmem,
        scratch_shapes=[
            pltpu.VMEM((6, columns + 2 * XPAD, length), jnp.float32),
            pltpu.VMEM((6, columns, length + 2 * PAD), jnp.float32),
            pltpu.VMEM((6, columns + 2 * XPAD, CHUNK), jnp.float32),
            pltpu.VMEM((6, columns + 2 * XPAD, CHUNK), jnp.float32),
        ],
    )(flags, state, xlo, xhi, ylo, yhi, geo)


def shifted(block, axis, forward, cyclic=False):
    count = lax.axis_size(axis)
    pairs = [(i, i + 1) for i in range(count - 1)]
    if cyclic and count > 1:
        pairs.append((count - 1, 0))
    if not forward:
        pairs = [(target, source) for source, target in pairs]
    return lax.ppermute(block, axis, pairs)


def broadcast(array, axis, holders):
    count = lax.axis_size(axis)
    index = lax.axis_index(axis)
    while len(holders) < count:
        waiting = [i for i in range(count) if i not in holders]
        pairs = list(zip(holders, waiting))
        received = lax.ppermute(array, axis, pairs)
        targets = jnp.zeros((), jnp.bool_)
        for _, target in pairs:
            targets = targets | (index == target)
        array = jnp.where(targets, received, array)
        holders = holders + [target for _, target in pairs]
    return array


def zshift(values, offset, planes):
    length = values.shape[-1]
    plane_at = jnp.arange(length, dtype=jnp.int32) % planes
    if offset > 0:
        return jnp.where(
            plane_at >= offset,
            jnp.roll(values, offset, axis=-1),
            jnp.roll(values, offset - planes, axis=-1),
        )
    return jnp.where(
        plane_at < planes + offset,
        jnp.roll(values, offset, axis=-1),
        jnp.roll(values, offset + planes, axis=-1),
    )


def primitives(conserved):
    specific_volume_inverse = conserved[0]
    vel_x = conserved[1] / specific_volume_inverse
    vel_y = conserved[2] / specific_volume_inverse
    vel_z = conserved[3] / specific_volume_inverse
    thermodynamic_stress = (HEAT_RATIO - 1.0) * (
        conserved[4]
        - 0.5 * (conserved[1] * vel_x + conserved[2] * vel_y + conserved[3] * vel_z)
        - conserved[5]
    )
    sound_speed = jnp.sqrt(HEAT_RATIO * thermodynamic_stress / specific_volume_inverse)
    return (specific_volume_inverse, vel_x, vel_y, vel_z, thermodynamic_stress, sound_speed)


def slopes(height_ext, planes):
    columns = height_ext.shape[0] - 6
    slope_x = (
        height_ext[1 : columns + 1]
        - 8.0 * height_ext[2 : columns + 2]
        + 8.0 * height_ext[4 : columns + 4]
        - height_ext[5 : columns + 5]
    ) / (12.0 * STREAM_STEP)
    height = height_ext[3 : columns + 3]
    slope_z = (
        zshift(height, 2, planes)
        - 8.0 * zshift(height, 1, planes)
        + 8.0 * zshift(height, -1, planes)
        - zshift(height, -2, planes)
    ) / (12.0 * SPAN_STEP)
    return (slope_x, slope_z)


def shock_speed(top_row, slope_x, slope_z):
    specific_volume_inverse, vel_x, vel_y, vel_z, thermodynamic_stress, sound_speed = primitives(
        top_row
    )
    tilt_norm = jnp.sqrt(1.0 + slope_x * slope_x + slope_z * slope_z)
    normal = (vel_y - vel_x * slope_x - vel_z * slope_z) / tilt_norm
    sine_sq = slope_x * slope_x / (tilt_norm * tilt_norm)
    jump_pressure = FREE_PRESSURE * (
        1.0 + 2.0 * HEAT_RATIO / (HEAT_RATIO + 1.0) * (FREE_MACH * FREE_MACH * sine_sq - 1.0)
    )
    return tilt_norm * (
        normal + (jump_pressure - thermodynamic_stress) / (specific_volume_inverse * sound_speed)
    )


def wall_ghosts(first_rows, blowing, planes):
    mirror = jnp.concatenate(
        [
            first_rows[..., 2 * planes : 3 * planes],
            first_rows[..., planes : 2 * planes],
            first_rows[..., 0:planes],
        ],
        axis=-1,
    )
    blown_y = 2.0 * jnp.tile(blowing, (1, 3)) - mirror[2]
    stagnation_enthalpy_sum = (
        mirror[4] + 0.5 * (blown_y * blown_y - mirror[2] * mirror[2]) / mirror[0]
    )
    return jnp.stack([mirror[0], mirror[1], blown_y, mirror[3], stagnation_enthalpy_sum, mirror[5]])


def wall_flux(wall_segment, segment_level, blow_table):
    seg_hit = wall_segment[:, None] == jnp.arange(segment_level.shape[0], dtype=jnp.int32)[None, :]
    levels = jnp.sum(jnp.where(seg_hit, segment_level[None, :], 0), axis=1)
    level_hit = levels[:, None] == jnp.arange(blow_table.shape[0], dtype=jnp.int32)[None, :]
    return jnp.sum(jnp.where(level_hit[:, :, None], blow_table[None, :, :], 0.0), axis=1)


def replicate_lanes(small, planes):
    pick = (
        jnp.arange(LANES, dtype=jnp.int32)[None, :] % planes
        == jnp.arange(planes, dtype=jnp.int32)[:, None]
    ).astype(jnp.float32)
    return jnp.dot(small, pick, precision=lax.Precision.HIGHEST, preferred_element_type=jnp.float32)


def shards(state, shock_height, wall_segment, segment_level, blow_table):
    planes = blow_table.shape[1]
    columns = state.shape[1]
    length = state.shape[2]
    row_count = length // planes
    col_devs = lax.axis_size("gx")
    row_devs = lax.axis_size("gy")
    col_dev = lax.axis_index("gx")
    row_dev = lax.axis_index("gy")
    total_rows = row_count * row_devs
    band = HALO * planes

    def pack(cols, heights):
        extra = jnp.zeros((1, HALO, length), jnp.float32)
        extra = lax.dynamic_update_slice(extra, heights[None], (0, 0, 0))
        return jnp.concatenate([cols, extra], axis=0)

    from_low = shifted(pack(state[:, columns - HALO :], shock_height[columns - HALO :]), "gx", True)
    from_high = shifted(pack(state[:, :HALO], shock_height[:HALO]), "gx", False)
    below = shifted(state[..., length - band :], "gy", True, cyclic=True)
    above = shifted(state[..., :band], "gy", False)

    low_height = jnp.where(
        col_dev == 0, jnp.broadcast_to(shock_height[:1], (HALO, planes)), from_low[6, :, :planes]
    )
    high_height = jnp.where(
        col_dev == col_devs - 1,
        jnp.broadcast_to(shock_height[columns - 1 :], (HALO, planes)),
        from_high[6, :, :planes],
    )
    height_ext = jnp.concatenate([low_height, shock_height, high_height], axis=0)
    slope_x, slope_z = slopes(height_ext, planes)

    top_seed = jnp.where(
        row_dev == row_devs - 1, state[..., length - planes :], below[..., band - planes :]
    )
    top_row = broadcast(top_seed, "gy", [row_devs - 1, 0] if row_devs > 1 else [0])
    shock_rate = shock_speed(top_row, slope_x, slope_z)

    blowing = wall_flux(wall_segment, segment_level, blow_table)
    ghost_below = jnp.where(row_dev == 0, wall_ghosts(state[..., :band], blowing, planes), below)
    ghost_above = jnp.where(
        row_dev == row_devs - 1, jnp.tile(state[..., length - planes :], (1, 1, HALO)), above
    )
    ylo = jnp.concatenate([ghost_below[..., : PAD - band], ghost_below], axis=2)
    yhi = jnp.concatenate([ghost_above, ghost_above[..., band - (PAD - band) :]], axis=2)

    height = shock_height
    xrows = columns + 2 * XPAD
    height_x = jnp.concatenate(
        [
            jnp.broadcast_to(height_ext[:1], (XPAD - HALO, planes)),
            height_ext,
            jnp.broadcast_to(height_ext[-1:], (XPAD - HALO, planes)),
        ],
        axis=0,
    )
    small = jnp.concatenate(
        [height_x, slope_x, slope_z, shock_rate, shock_rate / height, height], axis=0
    )
    geo = replicate_lanes(small, planes)
    flags = jnp.stack(
        [
            (row_dev * row_count).astype(jnp.int32),
            (col_dev == 0).astype(jnp.int32),
            (col_dev == col_devs - 1).astype(jnp.int32),
            jnp.zeros((), jnp.int32),
        ]
    )
    state_new = update(
        flags,
        state,
        from_low,
        from_high,
        ylo,
        yhi,
        geo,
        planes,
        total_rows,
        COURANT / total_rows,
    )
    shock_new = shock_height + COURANT / total_rows * shock_rate
    return (state_new, shock_new)


def solution(mesh):
    in_specs = (P(None, "gx", "gy"), P("gx", None), P("gx"), P(), P())
    out_specs = (P(None, "gx", "gy"), P("gx", None))
    return jax.shard_map(shards, mesh=mesh, in_specs=in_specs, out_specs=out_specs, check_vma=False)
```

time: 65.3 us -> 46.6 us (0.71)
  the two profiles are of different devices: /device:TPU:232 before, /device:TPU:113 now
where the time goes in v3:
time: 46.6 us; the launch traced here: 45.7 us
  starting transfers between devices  15.3 us (33%)
  Pallas kernels  13.5 us (29%)
  waiting for transfers between devices  6.75 us (14%)
  other arithmetic  4.56 us (10%)
  local copies, waits for them, and re-layouts  3.72 us (8%)
  between operations  0.94 us (2%)
  matrix products  0.89 us (2%)
    pallas_call x1, Pallas kernels, update(): pl.pallas_call(kern, out_shape=jax.ShapeDtypeStruct((6, columns, length),...  13.5 us
    ppermute x4, starting transfers between devices, shifted(): return lax.ppermute(block, axis, pairs)  12.7 us
    ppermute x3, waiting for transfers between devices, broadcast(): received = lax.ppermute(array, axis, pairs)  6.74 us
    ppermute x3, starting transfers between devices, broadcast(): received = lax.ppermute(array, axis, pairs)  2.62 us
    slice x1, local copies, waits for them, and re-layouts, shards(): from_high = shifted(pack(state[:, :HALO], shock_height[:HALO]), 'gx', False)  1.35 us
    select_n x1, other arithmetic, shards(): jnp.where(row_dev == row_devs - 1, state[..., length - planes:], below[.....  1.07 us
  transfers between devices with their start and end apart: 7, of which 1 were waited for; matrix products, arithmetic and copies ran while one was open for 13% of the time, Pallas kernels for 0%

profile of v3, /device:TPU:113, one launch (start us, length us, event | category | flops | bytes accessed | tf_op | source)
XLA Modules:
  0.0 45.7 jit_solution(17547511709521929316)
XLA Ops:
  0.6 0.9 %fusion.20 = (f32[6,16,96]{2,1,0:T(8,128)S(1)}, f32[6,16,96]{2,1,0:T(8,128)S(1)}) fusion(f32[6,16,3072]{2,1,0:T(8,128)} %state_ref.1), kind=kLoop, calls=%fused_computation.70 | loop fusion | bytes 147456 | tf_op jit(solution)/shard_map/slice | solution.py:371
  1.5 2.6 %collective-permute-start.3 = (f32[6,16,96]{2,1,0:T(8,128)S(1)}, f32[6,16,96]{2,1,0:T(8,128)S(1)}, u32[]{:S(2)}, u32[]{:S(2)}) collective-permute-start(f32[6,16,96]{2,1,0:T(8,128)S(1)} %get-tuple-element.11), channel_id=1, source_target_pairs={{1,0},{2,1},{3,2},{4,3},{5,4},{6,5},{7,6},{8,7},{9,8},{10,9},{11,1... | collective-permute-start | bytes 110600 | tf_op jit(solution)/shard_map/ppermute | solution.py:219
  4.2 2.8 %collective-permute-start.2 = (f32[6,16,96]{2,1,0:T(8,128)S(1)}, f32[6,16,96]{2,1,0:T(8,128)S(1)}, u32[]{:S(2)}, u32[]{:S(2)}) collective-permute-start(f32[6,16,96]{2,1,0:T(8,128)S(1)} %get-tuple-element.12), channel_id=1, source_target_pairs={{0,1},{1,2},{2,3},{3,4},{4,5},{5,6},{6,7},{7,8},{8,9},{9,10},{10,1... | collective-permute-start | bytes 110600 | tf_op jit(solution)/shard_map/ppermute | solution.py:219
  6.9 1.3 %fusion.21 = (f32[6,3,3072]{2,1,0:T(4,128)S(1)}, f32[6,3,3072]{2,1,0:T(4,128)S(1)}) fusion(f32[6,16,3072]{2,1,0:T(8,128)} %state_ref.1), kind=kLoop, calls=%fused_computation.71 | loop fusion | bytes 884736 | tf_op jit(solution)/shard_map/slice | solution.py:349
  8.4 3.1 %collective-permute-start = (f32[7,3,3072]{2,1,0:T(4,128)S(1)}, f32[7,3,3072]{2,1,0:T(4,128)S(1)}, u32[]{:S(2)}, u32[]{:S(2)}) collective-permute-start(f32[7,3,3072]{2,1,0:T(4,128)S(1)} %select_maximum_fusion.1), channel_id=1, source_target_pairs={{0,16},{16,32},{32,48},{48,64},{64,80},{80,96},{96,112},{112,128},... | collective-permute-start | bytes 774152 | tf_op jit(solution)/shard_map/ppermute | solution.py:219
  11.6 4.3 %collective-permute-start.1 = (f32[7,3,3072]{2,1,0:T(4,128)S(1)}, f32[7,3,3072]{2,1,0:T(4,128)S(1)}, u32[]{:S(2)}, u32[]{:S(2)}) collective-permute-start(f32[7,3,3072]{2,1,0:T(4,128)S(1)} %select_maximum_fusion), channel_id=1, source_target_pairs={{16,0},{32,16},{48,32},{64,48},{80,64},{96,80},{112,96},{128,112},... | collective-permute-start | bytes 774152 | tf_op jit(solution)/shard_map/ppermute | solution.py:219
  16.2 0.2 select_reduce_fusion.1
  16.4 0.1 iota_compare_fusion.3
  16.4 0.1 select_reduce_fusion
  16.6 0.7 %pad_add_fusion.flags_ref = s32[4]{0:T(128)} fusion(s32[1]{0:T(128)} %constant.40.clone.1, s32[1]{0:T(128)} %bitcast.2, s32[1]{0:T(128)} %bitcast.1, s32[1]{0:T(128)} %bitcast), kind=kLoop, calls=%fused_computation.65 | loop fusion | flops 12 | bytes 32 | tf_op jit(solution)/shard_map/stack | solution.py:392
  17.2 0.1 copy.16
  17.3 0.1 mul.124
  17.4 1.1 %slice_select_fusion = (f32[6,16,32]{2,1,0:T(8,128)S(1)}, f32[6,16,32]{2,1,0:T(8,128)S(1)}, f32[6,16,32]{2,1,0:T(8,128)S(1)}, f32[6,16,32]{2,1,0:T(8,128)S(1)}, f32[6,16,32]{2,1,0:T(8,128)S(1)}) fusion(f32[6,16,96]{2,1,0:T(8,128)S(1)} %collective-permute-done.2, pred[]{:T(512)S(6)} %eq.116, f32[6,16,3072]{2,1,0:T(8,128)} %state_ref.1), kind=kLoop, calls=%fused_computation.4 | loop fusion | flops 3072 | bytes 122881 | tf_op jit(solution)/shard_map/jit(_where)/select_n | solution.py:364
  18.5 0.1 pad_maximum_fusion
  18.7 0.7 %collective-permute-start.4 = (f32[6,16,32]{2,1,0:T(8,128)S(1)}, f32[6,16,32]{2,1,0:T(8,128)S(1)}, u32[]{:S(2)}, u32[]{:S(2)}) collective-permute-start(f32[6,16,32]{2,1,0:T(8,128)S(1)} %get-tuple-element.6), channel_id=1, source_target_pairs={{15,1},{0,2},{31,17},{16,18},{47,33},{32,34},{63,49},{48,50},{79,6... | collective-permute-start | bytes 36872 | tf_op jit(solution)/shard_map/ppermute | solution.py:228
  19.4 0.1 tile.8
  19.6 0.7 %collective-permute-start.5 = (f32[6,16,32]{2,1,0:T(8,128)S(1)}, f32[6,16,32]{2,1,0:T(8,128)S(1)}, u32[]{:S(2)}, u32[]{:S(2)}) collective-permute-start(f32[6,16,32]{2,1,0:T(8,128)S(1)} %broadcast_select_fusion), channel_id=1, source_target_pairs={{15,3},{0,4},{1,5},{2,6},{31,19},{16,20},{17,21},{18,22},{47,35},{... | collective-permute-start | bytes 36872 | tf_op jit(solution)/shard_map/ppermute | solution.py:228
  20.2 0.7 %pad_maximum_fusion.1.ylo_ref = f32[6,16,128]{2,1,0:T(8,128)} fusion(f32[6,16,96]{2,1,0:T(8,128)S(1)} %broadcast_select_fusion.4, f32[6,16,32]{2,1,0:T(8,128)S(1)} %bitcast.61), kind=kLoop, calls=%fused_computation.6 | loop fusion | flops 12288 | bytes 98304 | tf_op jit(solution)/shard_map/concatenate | solution.py:375
  20.9 0.1 slice.219
  21.0 1.3 %collective-permute-start.6 = (f32[6,16,32]{2,1,0:T(8,128)S(1)}, f32[6,16,32]{2,1,0:T(8,128)S(1)}, u32[]{:S(2)}, u32[]{:S(2)}) collective-permute-start(f32[6,16,32]{2,1,0:T(8,128)S(1)} %broadcast_select_fusion.1), channel_id=1, source_target_pairs={{15,7},{0,8},{1,9},{2,10},{3,11},{4,12},{5,13},{6,14},{31,23},{16,... | collective-permute-start | bytes 36872 | tf_op jit(solution)/shard_map/ppermute | solution.py:228
  22.3 0.7 %pad_maximum_fusion.2.yhi_ref = f32[6,16,128]{2,1,0:T(8,128)} fusion(f32[6,16,32]{2,1,0:T(8,128)S(1)} %slice.219, f32[6,16,96]{2,1,0:T(8,128)S(1)} %broadcast_select_fusion.3), kind=kLoop, calls=%fused_computation.7 | loop fusion | flops 12288 | bytes 98304 | tf_op jit(solution)/shard_map/concatenate | solution.py:376
  23.0 6.7 %collective-permute-done.6 = f32[6,16,32]{2,1,0:T(8,128)S(1)} collective-permute-done((f32[6,16,32]{2,1,0:T(8,128)S(1)}, f32[6,16,32]{2,1,0:T(8,128)S(1)}, u32[]{:S(2)}, u32[]{:S(2)}) %collective-permute-start.6) | collective-permute-done | bytes 12320 | tf_op jit(solution)/shard_map/ppermute | solution.py:228
  29.8 0.1 copy.15
  29.9 0.7 %multiply_add_fusion = (f32[16,32]{1,0:T(8,128)}, f32[16,32]{1,0:T(8,128)S(1)}, f32[16,32]{1,0:T(8,128)S(1)}, f32[16,32]{1,0:T(8,128)S(1)}) fusion(f32[16,32]{1,0:T(8,128)S(1)} %copy-done, f32[6,16,32]{2,1,0:T(8,128)S(1)} %broadcast_select_fusion.2, f32[16,2]{1,0:T(8,128)S(1)} %get-tuple-element.16, f32[16,30]{1,0:T(8,128)S(1)} %get-tuple-element.18, ...), kind=kLoop, calls=%fused_computation.50 | loop fusion | flops 29184 | bytes 31488 | tf_op jit(solution)/shard_map/add | solution.py:412
  30.7 0.1 copy.20
  30.7 0.1 copy.17
  30.8 0.1 copy.21
  30.9 0.1 copy.19
  31.0 0.1 copy.18
  31.2 0.1 concatenate.63
  31.3 0.9 %fusion.geo_ref = f32[112,128]{1,0:T(8,128)} fusion(f32[112,32]{0,1:T(8,128)S(1)} %concatenate.63, s32[128]{0:T(128)S(1)} %and_select_fusion), kind=kOutput, calls=%fused_computation.15 | convolution fusion | flops 5509120 | bytes 72192 | tf_op jit(solution)/shard_map/dot_general | solution.py:328
  32.2 13.5 %shard_map.68 = f32[6,16,3072]{2,1,0:T(8,128)} custom-call(s32[4]{0:T(128)} %pad_add_fusion.flags_ref, f32[6,16,3072]{2,1,0:T(8,128)} %state_ref.1, f32[7,3,3072]{2,1,0:T(4,128)} %copy-done.1, f32[7,3,3072]{2,1,0:T(4,128)} %copy-done.2, f32[6,16,128]{2,1,0:T(8,128)} %pad_maximum_fusion.1.ylo_ref, f32[6,16,128]{2,1,0:T(8,128)} %pad_maximum_fusion.2.yhi_ref, ...), custom_call_target="tpu_custom_call" | custom-call | tf_op jit(solution)/shard_map/pallas_call | solution.py:198
  (47 shorter events, 0.8 us)
Async XLA Ops:
  0.6 7.6 %copy-start = (f32[16,32]{1,0:T(8,128)S(1)}, f32[16,32]{1,0:T(8,128)}, u32[]{:S(2)}) copy-start(f32[16,32]{1,0:T(8,128)} %param.6) | copy-start | bytes 6148
  1.5 18.0 %collective-permute-start.3 = (f32[6,16,96]{2,1,0:T(8,128)S(1)}, f32[6,16,96]{2,1,0:T(8,128)S(1)}, u32[]{:S(2)}, u32[]{:S(2)}) collective-permute-start(f32[6,16,96]{2,1,0:T(8,128)S(1)} %get-tuple-element.11), channel_id=1, source_target_pairs={{1,0},{2,1},{3,2},{4,3},{5,4},{6,5},{7,6},{8,7},{9,8},{10,9},{11,1... | collective-permute-start | bytes 110600 | tf_op jit(solution)/shard_map/ppermute | solution.py:219
  4.1 12.1 %copy-start.4 = (s32[16]{0:T(128)S(1)}, s32[16]{0:T(128)}, u32[]{:S(2)}) copy-start(s32[16]{0:T(128)} %param.8) | copy-start | bytes 196
  4.1 12.0 %copy-start.5 = (s32[16]{0:T(128)S(1)}, s32[16]{0:T(128)}, u32[]{:S(2)}) copy-start(s32[16]{0:T(128)} %param.7) | copy-start | bytes 196
  4.2 12.3 %copy-start.3 = (f32[16,32]{1,0:T(8,128)S(1)}, f32[16,32]{1,0:T(8,128)}, u32[]{:S(2)}) copy-start(f32[16,32]{1,0:T(8,128)} %param.9) | copy-start | bytes 6148
  4.2 13.2 %collective-permute-start.2 = (f32[6,16,96]{2,1,0:T(8,128)S(1)}, f32[6,16,96]{2,1,0:T(8,128)S(1)}, u32[]{:S(2)}, u32[]{:S(2)}) collective-permute-start(f32[6,16,96]{2,1,0:T(8,128)S(1)} %get-tuple-element.12), channel_id=1, source_target_pairs={{0,1},{1,2},{2,3},{3,4},{4,5},{5,6},{6,7},{7,8},{8,9},{9,10},{10,1... | collective-permute-start | bytes 110600 | tf_op jit(solution)/shard_map/ppermute | solution.py:219
  8.4 21.4 %collective-permute-start = (f32[7,3,3072]{2,1,0:T(4,128)S(1)}, f32[7,3,3072]{2,1,0:T(4,128)S(1)}, u32[]{:S(2)}, u32[]{:S(2)}) collective-permute-start(f32[7,3,3072]{2,1,0:T(4,128)S(1)} %select_maximum_fusion.1), channel_id=1, source_target_pairs={{0,16},{16,32},{32,48},{48,64},{64,80},{80,96},{96,112},{112,128},... | collective-permute-start | bytes 774152 | tf_op jit(solution)/shard_map/ppermute | solution.py:219
  11.6 18.3 %collective-permute-start.1 = (f32[7,3,3072]{2,1,0:T(4,128)S(1)}, f32[7,3,3072]{2,1,0:T(4,128)S(1)}, u32[]{:S(2)}, u32[]{:S(2)}) collective-permute-start(f32[7,3,3072]{2,1,0:T(4,128)S(1)} %select_maximum_fusion), channel_id=1, source_target_pairs={{16,0},{32,16},{48,32},{64,48},{80,64},{96,80},{112,96},{128,112},... | collective-permute-start | bytes 774152 | tf_op jit(solution)/shard_map/ppermute | solution.py:219
  18.7 0.9 %collective-permute-start.4 = (f32[6,16,32]{2,1,0:T(8,128)S(1)}, f32[6,16,32]{2,1,0:T(8,128)S(1)}, u32[]{:S(2)}, u32[]{:S(2)}) collective-permute-start(f32[6,16,32]{2,1,0:T(8,128)S(1)} %get-tuple-element.6), channel_id=1, source_target_pairs={{15,1},{0,2},{31,17},{16,18},{47,33},{32,34},{63,49},{48,50},{79,6... | collective-permute-start | bytes 36872 | tf_op jit(solution)/shard_map/ppermute | solution.py:228
  19.6 1.5 %collective-permute-start.5 = (f32[6,16,32]{2,1,0:T(8,128)S(1)}, f32[6,16,32]{2,1,0:T(8,128)S(1)}, u32[]{:S(2)}, u32[]{:S(2)}) collective-permute-start(f32[6,16,32]{2,1,0:T(8,128)S(1)} %broadcast_select_fusion), channel_id=1, source_target_pairs={{15,3},{0,4},{1,5},{2,6},{31,19},{16,20},{17,21},{18,22},{47,35},{... | collective-permute-start | bytes 36872 | tf_op jit(solution)/shard_map/ppermute | solution.py:228
  21.0 8.7 %collective-permute-start.6 = (f32[6,16,32]{2,1,0:T(8,128)S(1)}, f32[6,16,32]{2,1,0:T(8,128)S(1)}, u32[]{:S(2)}, u32[]{:S(2)}) collective-permute-start(f32[6,16,32]{2,1,0:T(8,128)S(1)} %broadcast_select_fusion.1), channel_id=1, source_target_pairs={{15,7},{0,8},{1,9},{2,10},{3,11},{4,12},{5,13},{6,14},{31,23},{16,... | collective-permute-start | bytes 36872 | tf_op jit(solution)/shard_map/ppermute | solution.py:228
  29.8 2.4 %copy-start.1 = (f32[7,3,3072]{2,1,0:T(4,128)}, f32[7,3,3072]{2,1,0:T(4,128)S(1)}, u32[]{:S(2)}) copy-start(f32[7,3,3072]{2,1,0:T(4,128)S(1)} %collective-permute-done.xlo_ref) | copy-start | bytes 774148
  29.9 2.3 %copy-start.2 = (f32[7,3,3072]{2,1,0:T(4,128)}, f32[7,3,3072]{2,1,0:T(4,128)S(1)}, u32[]{:S(2)}) copy-start(f32[7,3,3072]{2,1,0:T(4,128)S(1)} %collective-permute-done.1.xhi_ref) | copy-start | bytes 774148

commit v4 on v3

--- a/solution.py
+++ b/solution.py
@@ -361,10 +361,8 @@
     height_ext = jnp.concatenate([low_height, shock_height, high_height], axis=0)
     slope_x, slope_z = slopes(height_ext, planes)
 
-    top_seed = jnp.where(
-        row_dev == row_devs - 1, state[..., length - planes :], below[..., band - planes :]
-    )
-    top_row = broadcast(top_seed, "gy", [row_devs - 1, 0] if row_devs > 1 else [0])
+    top_copies = jnp.broadcast_to(state[None, ..., length - planes :], (row_devs, 6, columns, planes))
+    top_row = lax.all_to_all(top_copies, "gy", 0, 0)[row_devs - 1]
     shock_rate = shock_speed(top_row, slope_x, slope_z)
 
     blowing = wall_flux(wall_segment, segment_level, blow_table)

time: 46.6 us -> 53.2 us (1.14)
  the two profiles are of different devices: /device:TPU:113 before, /device:TPU:17 now
where the time goes in v4:
time: 53.2 us; the launch traced here: 52.8 us
  starting transfers between devices  19.6 us (37%)
  Pallas kernels  13.5 us (25%)
  waiting for transfers between devices  6.76 us (13%)
  local copies, waits for them, and re-layouts  6.61 us (12%)
  other arithmetic  4.51 us (8%)
  between operations  0.89 us (2%)
  matrix products  0.87 us (2%)
    pallas_call x1, Pallas kernels, update(): pl.pallas_call(kern, out_shape=jax.ShapeDtypeStruct((6, columns, length),...  13.5 us
    ppermute x4, starting transfers between devices, shifted(): return lax.ppermute(block, axis, pairs)  11.5 us
    all_to_all x1, starting transfers between devices, shards(): top_row = lax.all_to_all(top_copies, 'gy', 0, 0)[row_devs - 1]  8.13 us
    all_to_all x1, waiting for transfers between devices, shards(): top_row = lax.all_to_all(top_copies, 'gy', 0, 0)[row_devs - 1]  6.75 us
    unnamed x17, local copies, waits for them, and re-layouts  1.37 us
    slice x1, local copies, waits for them, and re-layouts, shards(): from_high = shifted(pack(state[:, :HALO], shock_height[:HALO]), 'gx', False)  1.35 us
    all_to_all x1, other arithmetic, shards(): top_row = lax.all_to_all(top_copies, 'gy', 0, 0)[row_devs - 1]  1.11 us
  transfers between devices with their start and end apart: 5, of which 1 were waited for; matrix products, arithmetic and copies ran while one was open for 13% of the time, Pallas kernels for 0%

profile of v4, /device:TPU:17, one launch (start us, length us, event | category | flops | bytes accessed | tf_op | source)
XLA Modules:
  0.0 52.8 jit_solution(8241200679802118425)
XLA Ops:
  0.6 0.9 %fusion.20 = (f32[6,16,96]{2,1,0:T(8,128)S(1)}, f32[6,16,96]{2,1,0:T(8,128)S(1)}) fusion(f32[6,16,3072]{2,1,0:T(8,128)} %state_ref.1), kind=kLoop, calls=%fused_computation.66 | loop fusion | bytes 147456 | tf_op jit(solution)/shard_map/slice | solution.py:369
  1.5 2.6 %collective-permute-start.3 = (f32[6,16,96]{2,1,0:T(8,128)S(1)}, f32[6,16,96]{2,1,0:T(8,128)S(1)}, u32[]{:S(2)}, u32[]{:S(2)}) collective-permute-start(f32[6,16,96]{2,1,0:T(8,128)S(1)} %get-tuple-element.8), channel_id=1, source_target_pairs={{1,0},{2,1},{3,2},{4,3},{5,4},{6,5},{7,6},{8,7},{9,8},{10,9},{11,1... | collective-permute-start | bytes 110600 | tf_op jit(solution)/shard_map/ppermute | solution.py:219
  4.1 1.5 %collective-permute-start.2 = (f32[6,16,96]{2,1,0:T(8,128)S(1)}, f32[6,16,96]{2,1,0:T(8,128)S(1)}, u32[]{:S(2)}, u32[]{:S(2)}) collective-permute-start(f32[6,16,96]{2,1,0:T(8,128)S(1)} %get-tuple-element.9), channel_id=1, source_target_pairs={{0,1},{1,2},{2,3},{3,4},{4,5},{5,6},{6,7},{7,8},{8,9},{9,10},{10,1... | collective-permute-start | bytes 110600 | tf_op jit(solution)/shard_map/ppermute | solution.py:219
  5.7 1.3 %fusion.22 = (f32[6,3,3072]{2,1,0:T(4,128)S(1)}, f32[6,3,3072]{2,1,0:T(4,128)S(1)}) fusion(f32[6,16,3072]{2,1,0:T(8,128)} %state_ref.1), kind=kLoop, calls=%fused_computation.68 | loop fusion | bytes 884736 | tf_op jit(solution)/shard_map/slice | solution.py:349
  7.1 3.1 %collective-permute-start = (f32[7,3,3072]{2,1,0:T(4,128)S(1)}, f32[7,3,3072]{2,1,0:T(4,128)S(1)}, u32[]{:S(2)}, u32[]{:S(2)}) collective-permute-start(f32[7,3,3072]{2,1,0:T(4,128)S(1)} %select_maximum_fusion.1), channel_id=1, source_target_pairs={{0,16},{16,32},{32,48},{48,64},{64,80},{80,96},{96,112},{112,128},... | collective-permute-start | bytes 774152 | tf_op jit(solution)/shard_map/ppermute | solution.py:219
  10.3 4.3 %collective-permute-start.1 = (f32[7,3,3072]{2,1,0:T(4,128)S(1)}, f32[7,3,3072]{2,1,0:T(4,128)S(1)}, u32[]{:S(2)}, u32[]{:S(2)}) collective-permute-start(f32[7,3,3072]{2,1,0:T(4,128)S(1)} %select_maximum_fusion), channel_id=1, source_target_pairs={{16,0},{32,16},{48,32},{64,48},{80,64},{96,80},{112,96},{128,112},... | collective-permute-start | bytes 774152 | tf_op jit(solution)/shard_map/ppermute | solution.py:219
  14.6 1.0 %fusion.21 = (f32[6,16,32]{2,1,0:T(8,128)S(1)}, f32[6,16,32]{2,1,0:T(8,128)S(1)}, f32[6,16,32]{2,1,0:T(8,128)S(1)}, f32[6,16,32]{2,1,0:T(8,128)S(1)}) fusion(f32[6,16,3072]{2,1,0:T(8,128)} %state_ref.1), kind=kLoop, calls=%fused_computation.67 | loop fusion | bytes 98304 | tf_op jit(solution)/shard_map/slice | solution.py:371
  15.8 1.0 %reshape.84 = f32[16,1,3072]{2,1,0:T(1,128)} reshape(f32[16,6,16,32]{3,2,1,0:T(8,128)S(1)} %broadcast_in_dim.101) | data formatting | bytes 393216
  16.8 8.1 %all-to-all-start = ((f32[16,1,3072]{2,1,0:T(1,128)}), f32[16,1,3072]{2,1,0:T(1,128)S(1)}, u32[]{:S(2)}, u32[]{:S(2)}) async-start(f32[16,1,3072]{2,1,0:T(1,128)} %reshape.84), calls=%async_computation | async-start | bytes 393216 | tf_op jit(solution)/shard_map/all_to_all | solution.py:365
  25.3 0.2 select_reduce_fusion.1
  25.4 0.1 iota_compare_fusion.3
  25.5 0.1 select_reduce_fusion
  25.7 0.1 mul.124
  25.8 0.1 pad_maximum_fusion
  25.9 0.6 %pad_add_fusion.flags_ref = s32[4]{0:T(128)} fusion(s32[1]{0:T(128)} %constant.64.clone.1, s32[1]{0:T(128)} %bitcast.2, s32[1]{0:T(128)} %bitcast.1, s32[1]{0:T(128)} %bitcast), kind=kLoop, calls=%fused_computation.61 | loop fusion | flops 12 | bytes 32 | tf_op jit(solution)/shard_map/stack | solution.py:390
  26.5 0.1 copy.36
  26.7 0.1 tile.8
  26.8 0.1 slice.228
  26.9 0.7 %pad_maximum_fusion.1.ylo_ref = f32[6,16,128]{2,1,0:T(8,128)} fusion(f32[6,16,96]{2,1,0:T(8,128)S(1)} %broadcast_select_fusion.1, f32[6,16,32]{2,1,0:T(8,128)S(1)} %bitcast.61), kind=kLoop, calls=%fused_computation.5 | loop fusion | flops 12288 | bytes 98304 | tf_op jit(solution)/shard_map/concatenate | solution.py:373
  27.6 0.7 %pad_maximum_fusion.2.yhi_ref = f32[6,16,128]{2,1,0:T(8,128)} fusion(f32[6,16,32]{2,1,0:T(8,128)S(1)} %slice.228, f32[6,16,96]{2,1,0:T(8,128)S(1)} %broadcast_select_fusion), kind=kLoop, calls=%fused_computation.6 | loop fusion | flops 12288 | bytes 98304 | tf_op jit(solution)/shard_map/concatenate | solution.py:374
  28.3 0.1 copy.35
  28.4 0.1 copy.37
  28.5 6.8 %all-to-all-done = f32[16,1,3072]{2,1,0:T(1,128)S(1)} async-done(((f32[16,1,3072]{2,1,0:T(1,128)}), f32[16,1,3072]{2,1,0:T(1,128)S(1)}, u32[]{:S(2)}, u32[]{:S(2)}) %all-to-all-start) | async-done | bytes 196640 | tf_op jit(solution)/shard_map/all_to_all | solution.py:365
  35.3 0.5 broadcast.114
  35.8 1.1 %reduce = f32[16,3072]{1,0:T(8,128)S(1)} reduce(f32[16,1,3072]{2,1,0:T(1,128)S(1)} %all-to-all-done, f32[]{:T(128)} %broadcast.114), dimensions={1}, to_apply=%all_to_all.3.reduce_sub_computation | reduce | bytes 393220 | tf_op jit(solution)/shard_map/all_to_all | solution.py:365
  36.9 0.2 reshape.85
  37.1 0.7 %multiply_add_fusion = (f32[16,32]{1,0:T(8,128)}, f32[16,32]{1,0:T(8,128)S(1)}, f32[16,32]{1,0:T(8,128)S(1)}, f32[16,32]{1,0:T(8,128)S(1)}) fusion(f32[16,32]{1,0:T(8,128)S(1)} %copy-done, f32[16,6,16,32]{3,2,1,0:T(8,128)S(1)} %reshape.85, f32[16,2]{1,0:T(8,128)S(1)} %get-tuple-element.17, f32[16,30]{1,0:T(8,128)S(1)} %get-tuple-element.19, ...), kind=kLoop, calls=%fused_computation.46 | loop fusion | flops 29184 | bytes 31488 | tf_op jit(solution)/shard_map/add | solution.py:410
  37.9 0.1 copy.40
  37.9 0.1 copy.41
  38.3 0.1 concatenate.63
  38.4 0.9 %fusion.geo_ref = f32[112,128]{1,0:T(8,128)} fusion(f32[112,32]{0,1:T(8,128)S(1)} %concatenate.63, s32[128]{0:T(128)S(1)} %and_select_fusion), kind=kOutput, calls=%fused_computation.11 | convolution fusion | flops 5509120 | bytes 72192 | tf_op jit(solution)/shard_map/dot_general | solution.py:328
  39.3 13.5 %shard_map.68 = f32[6,16,3072]{2,1,0:T(8,128)} custom-call(s32[4]{0:T(128)} %pad_add_fusion.flags_ref, f32[6,16,3072]{2,1,0:T(8,128)} %state_ref.1, f32[7,3,3072]{2,1,0:T(4,128)} %copy-done.1, f32[7,3,3072]{2,1,0:T(4,128)} %copy-done.2, f32[6,16,128]{2,1,0:T(8,128)} %pad_maximum_fusion.1.ylo_ref, f32[6,16,128]{2,1,0:T(8,128)} %pad_maximum_fusion.2.yhi_ref, ...), custom_call_target="tpu_custom_call" | custom-call | tf_op jit(solution)/shard_map/pallas_call | solution.py:198
  (45 shorter events, 0.9 us)
Async XLA Ops:
  0.6 6.4 %copy-start = (f32[16,32]{1,0:T(8,128)S(1)}, f32[16,32]{1,0:T(8,128)}, u32[]{:S(2)}) copy-start(f32[16,32]{1,0:T(8,128)} %param.6) | copy-start | bytes 6148
  1.5 25.3 %collective-permute-start.3 = (f32[6,16,96]{2,1,0:T(8,128)S(1)}, f32[6,16,96]{2,1,0:T(8,128)S(1)}, u32[]{:S(2)}, u32[]{:S(2)}) collective-permute-start(f32[6,16,96]{2,1,0:T(8,128)S(1)} %get-tuple-element.8), channel_id=1, source_target_pairs={{1,0},{2,1},{3,2},{4,3},{5,4},{6,5},{7,6},{8,7},{9,8},{10,9},{11,1... | collective-permute-start | bytes 110600 | tf_op jit(solution)/shard_map/ppermute | solution.py:219
  4.1 22.7 %collective-permute-start.2 = (f32[6,16,96]{2,1,0:T(8,128)S(1)}, f32[6,16,96]{2,1,0:T(8,128)S(1)}, u32[]{:S(2)}, u32[]{:S(2)}) collective-permute-start(f32[6,16,96]{2,1,0:T(8,128)S(1)} %get-tuple-element.9), channel_id=1, source_target_pairs={{0,1},{1,2},{2,3},{3,4},{4,5},{5,6},{6,7},{7,8},{8,9},{9,10},{10,1... | collective-permute-start | bytes 110600 | tf_op jit(solution)/shard_map/ppermute | solution.py:219
  7.1 21.2 %collective-permute-start = (f32[7,3,3072]{2,1,0:T(4,128)S(1)}, f32[7,3,3072]{2,1,0:T(4,128)S(1)}, u32[]{:S(2)}, u32[]{:S(2)}) collective-permute-start(f32[7,3,3072]{2,1,0:T(4,128)S(1)} %select_maximum_fusion.1), channel_id=1, source_target_pairs={{0,16},{16,32},{32,48},{48,64},{64,80},{80,96},{96,112},{112,128},... | collective-permute-start | bytes 774152 | tf_op jit(solution)/shard_map/ppermute | solution.py:219
  10.3 18.1 %collective-permute-start.1 = (f32[7,3,3072]{2,1,0:T(4,128)S(1)}, f32[7,3,3072]{2,1,0:T(4,128)S(1)}, u32[]{:S(2)}, u32[]{:S(2)}) collective-permute-start(f32[7,3,3072]{2,1,0:T(4,128)S(1)} %select_maximum_fusion), channel_id=1, source_target_pairs={{16,0},{32,16},{48,32},{64,48},{80,64},{96,80},{112,96},{128,112},... | collective-permute-start | bytes 774152 | tf_op jit(solution)/shard_map/ppermute | solution.py:219
  15.7 9.6 %copy-start.4 = (s32[16]{0:T(128)S(1)}, s32[16]{0:T(128)}, u32[]{:S(2)}) copy-start(s32[16]{0:T(128)} %param.8) | copy-start | bytes 196
  15.7 9.6 %copy-start.5 = (s32[16]{0:T(128)S(1)}, s32[16]{0:T(128)}, u32[]{:S(2)}) copy-start(s32[16]{0:T(128)} %param.7) | copy-start | bytes 196
  15.7 9.8 %copy-start.3 = (f32[16,32]{1,0:T(8,128)S(1)}, f32[16,32]{1,0:T(8,128)}, u32[]{:S(2)}) copy-start(f32[16,32]{1,0:T(8,128)} %param.9) | copy-start | bytes 6148
  16.8 18.5 %all-to-all-start = ((f32[16,1,3072]{2,1,0:T(1,128)}), f32[16,1,3072]{2,1,0:T(1,128)S(1)}, u32[]{:S(2)}, u32[]{:S(2)}) async-start(f32[16,1,3072]{2,1,0:T(1,128)} %reshape.84), calls=%async_computation | async-start | bytes 393216 | tf_op jit(solution)/shard_map/all_to_all | solution.py:365
  28.3 11.0 %copy-start.1 = (f32[7,3,3072]{2,1,0:T(4,128)}, f32[7,3,3072]{2,1,0:T(4,128)S(1)}, u32[]{:S(2)}) copy-start(f32[7,3,3072]{2,1,0:T(4,128)S(1)} %collective-permute-done.xlo_ref) | copy-start | bytes 774148
  28.4 10.9 %copy-start.2 = (f32[7,3,3072]{2,1,0:T(4,128)}, f32[7,3,3072]{2,1,0:T(4,128)S(1)}, u32[]{:S(2)}) copy-start(f32[7,3,3072]{2,1,0:T(4,128)S(1)} %collective-permute-done.1.xhi_ref) | copy-start | bytes 774148

commit v5 on v3

--- a/solution.py
+++ b/solution.py
@@ -62,25 +62,26 @@
     face_area = STREAM_STEP * SPAN_STEP
     xrows = columns + 2 * XPAD
 
-    def kernel(flags_ref, state_ref, xlo_ref, xhi_ref, ylo_ref, yhi_ref, geo_ref,
+    def kernel(state_ref, xlo_ref, xhi_ref, yhalo_ref, geo_ref,
                out_ref, qx_ref, qy_ref, px_ref, mx_ref):
-        first_row = flags_ref[0]
+        col_dev = lax.axis_index("gx")
+        first_row = lax.axis_index("gy") * (length // planes)
         for c in range(6):
             qx_ref[c, 0:XPAD, :] = state_ref[c, 0:XPAD, :]
             qx_ref[c, XPAD:XPAD + columns, :] = state_ref[c]
             qx_ref[c, XPAD + columns:, :] = state_ref[c, columns - XPAD:, :]
             qx_ref[c, XPAD - HALO:XPAD, :] = xlo_ref[c]
             qx_ref[c, XPAD + columns:XPAD + columns + HALO, :] = xhi_ref[c]
-            qy_ref[c, :, 0:PAD] = ylo_ref[c]
+            qy_ref[c, :, 0:PAD] = yhalo_ref[0, c]
             qy_ref[c, :, PAD:PAD + length] = state_ref[c]
-            qy_ref[c, :, PAD + length:] = yhi_ref[c]
-
-        @pl.when(flags_ref[1] == 1)
+            qy_ref[c, :, PAD + length:] = yhalo_ref[1, c, :, 0:PAD]
+
+        @pl.when(col_dev == 0)
         def _():
             for c in range(6):
                 qx_ref[c, XPAD - HALO:XPAD, :] = jnp.broadcast_to(state_ref[c, 0:1, :], (HALO, length))
 
-        @pl.when(flags_ref[2] == 1)
+        @pl.when(col_dev == lax.axis_size("gx") - 1)
         def _():
             for c in range(6):
                 qx_ref[c, XPAD + columns:XPAD + columns + HALO, :] = jnp.broadcast_to(
@@ -190,7 +191,7 @@
     return kernel
 
 
-def update(flags, state, xlo, xhi, ylo, yhi, geo, planes, total_rows, dt):
+def update(state, xlo, xhi, yhalo, geo, planes, total_rows, dt):
     columns = state.shape[1]
     length = state.shape[2]
     kern = make_kernel(columns, length, planes, total_rows, dt)
@@ -198,7 +199,7 @@
     return pl.pallas_call(
         kern,
         out_shape=jax.ShapeDtypeStruct((6, columns, length), jnp.float32),
-        in_specs=[pl.BlockSpec(memory_space=pltpu.SMEM)] + [vmem] * 6,
+        in_specs=[vmem] * 5,
         out_specs=vmem,
         scratch_shapes=[
             pltpu.VMEM((6, columns + 2 * XPAD, length), jnp.float32),
@@ -206,7 +207,7 @@
             pltpu.VMEM((6, columns + 2 * XPAD, CHUNK), jnp.float32),
             pltpu.VMEM((6, columns + 2 * XPAD, CHUNK), jnp.float32),
         ],
-    )(flags, state, xlo, xhi, ylo, yhi, geo)
+    )(state, xlo, xhi, yhalo, geo)
 
 
 def shifted(block, axis, forward, cyclic=False):
@@ -219,18 +220,29 @@
     return lax.ppermute(block, axis, pairs)
 
 
-def broadcast(array, axis, holders):
+def broadcast(array, axis, holders, fanouts):
     count = lax.axis_size(axis)
     index = lax.axis_index(axis)
-    while len(holders) < count:
+    for fanout in fanouts:
+        if len(holders) >= count:
+            break
         waiting = [i for i in range(count) if i not in holders]
-        pairs = list(zip(holders, waiting))
-        received = lax.ppermute(array, axis, pairs)
         targets = jnp.zeros((), jnp.bool_)
-        for _, target in pairs:
-            targets = targets | (index == target)
-        array = jnp.where(targets, received, array)
-        holders = holders + [target for _, target in pairs]
+        arrived = array
+        reached = []
+        for _ in range(fanout):
+            pairs = list(zip(holders, waiting))
+            waiting = waiting[len(pairs) :]
+            if not pairs:
+                break
+            received = lax.ppermute(array, axis, pairs)
+            hit = jnp.zeros((), jnp.bool_)
+            for _, target in pairs:
+                hit = hit | (index == target)
+            arrived = jnp.where(hit, received, arrived)
+            reached = reached + [target for _, target in pairs]
+        array = arrived
+        holders = holders + reached
     return array
 
 
@@ -348,7 +360,9 @@
     from_low = shifted(pack(state[:, columns - HALO :], shock_height[columns - HALO :]), "gx", True)
     from_high = shifted(pack(state[:, :HALO], shock_height[:HALO]), "gx", False)
     below = shifted(state[..., length - band :], "gy", True, cyclic=True)
-    above = shifted(state[..., :band], "gy", False)
+    above = shifted(
+        jnp.concatenate([state[..., :band], state[..., length - planes :]], axis=2), "gy", False
+    )
 
     low_height = jnp.where(
         col_dev == 0, jnp.broadcast_to(shock_height[:1], (HALO, planes)), from_low[6, :, :planes]
@@ -362,18 +376,20 @@
     slope_x, slope_z = slopes(height_ext, planes)
 
     top_seed = jnp.where(
-        row_dev == row_devs - 1, state[..., length - planes :], below[..., band - planes :]
-    )
-    top_row = broadcast(top_seed, "gy", [row_devs - 1, 0] if row_devs > 1 else [0])
+        row_dev == row_devs - 1,
+        state[..., length - planes :],
+        jnp.where(row_dev == 0, below[..., band - planes :], above[..., band:]),
+    )
+    seeded = sorted({row_devs - 1, 0, max(row_devs - 2, 0)}, reverse=True)
+    top_row = broadcast(top_seed, "gy", seeded, (2, 1, 1, 1, 1))
     shock_rate = shock_speed(top_row, slope_x, slope_z)
 
     blowing = wall_flux(wall_segment, segment_level, blow_table)
     ghost_below = jnp.where(row_dev == 0, wall_ghosts(state[..., :band], blowing, planes), below)
     ghost_above = jnp.where(
-        row_dev == row_devs - 1, jnp.tile(state[..., length - planes :], (1, 1, HALO)), above
-    )
-    ylo = jnp.concatenate([ghost_below[..., : PAD - band], ghost_below], axis=2)
-    yhi = jnp.concatenate([ghost_above, ghost_above[..., band - (PAD - band) :]], axis=2)
+        row_dev == row_devs - 1, jnp.tile(state[..., length - planes :], (1, 1, HALO + 1)), above
+    )
+    yhalo = jnp.stack([jnp.concatenate([ghost_below[..., : PAD - band], ghost_below], axis=2), ghost_above])
 
     height = shock_height
     xrows = columns + 2 * XPAD
@@ -389,21 +405,11 @@
         [height_x, slope_x, slope_z, shock_rate, shock_rate / height, height], axis=0
     )
     geo = replicate_lanes(small, planes)
-    flags = jnp.stack(
-        [
-            (row_dev * row_count).astype(jnp.int32),
-            (col_dev == 0).astype(jnp.int32),
-            (col_dev == col_devs - 1).astype(jnp.int32),
-            jnp.zeros((), jnp.int32),
-        ]
-    )
     state_new = update(
-        flags,
         state,
         from_low,
         from_high,
-        ylo,
-        yhi,
+        yhalo,
         geo,
         planes,
         total_rows,

time: 46.6 us -> 47.4 us (1.017)
  waiting for transfers between devices: 6.75 us -> 8.33 us
  other arithmetic: 4.56 us -> 3.31 us
  local copies, waits for them, and re-layouts: 3.72 us -> 4.53 us
    ppermute x3, waiting for transfers between devices: 6.74 us -> 8.32 us  [broadcast(): received = lax.ppermute(array, axis, pairs)]
    concatenate x2 -> x1, other arithmetic: 1.41 us -> 0.08 us  [shards(): jnp.concatenate([state[..., :band], state[..., length - planes:]], axis=2)]
    slice x2, local copies, waits for them, and re-layouts: 0.98 us -> 1.79 us  [the longest x1 0.91 us: shards(): below = shifted(state[..., length - band:], 'gy', True, cyclic=True)]
    select_n x5 -> x3, other arithmetic: 1.11 us -> 1.11 us  [the longest x1 1.09 us: shards(): jnp.where(row_dev == row_devs - 1, state[..., length - planes:], jnp.wher...]
  transfers between devices with their start and end apart: 7 -> 7, of which waited for: 1 -> 1; matrix products, arithmetic and copies ran while one was open for 13% -> 10% of each run, Pallas kernels for 0% -> 0%
where the time goes in v5:
time: 47.4 us; the launch traced here: 46.9 us
  starting transfers between devices  15.4 us (32%)
  Pallas kernels  13.5 us (28%)
  waiting for transfers between devices  8.33 us (18%)
  local copies, waits for them, and re-layouts  4.53 us (10%)
  other arithmetic  3.31 us (7%)
  between operations  1.01 us (2%)
  matrix products  0.88 us (2%)
    pallas_call x1, Pallas kernels, update(): pl.pallas_call(kern, out_shape=jax.ShapeDtypeStruct((6, columns, length),...  13.5 us
    ppermute x4, starting transfers between devices, shifted(): return lax.ppermute(block, axis, pairs)  12.7 us
    ppermute x3, waiting for transfers between devices, broadcast(): received = lax.ppermute(array, axis, pairs)  8.32 us
    ppermute x3, starting transfers between devices, broadcast(): received = lax.ppermute(array, axis, pairs)  2.62 us
    slice x1, local copies, waits for them, and re-layouts, shards(): from_high = shifted(pack(state[:, :HALO], shock_height[:HALO]), 'gx', False)  1.35 us
    select_n x1, other arithmetic, shards(): jnp.where(row_dev == row_devs - 1, state[..., length - planes:], jnp.wher...  1.09 us
  transfers between devices with their start and end apart: 7, of which 1 were waited for; matrix products, arithmetic and copies ran while one was open for 10% of the time, Pallas kernels for 0%

profile of v5, /device:TPU:113, one launch (start us, length us, event | category | flops | bytes accessed | tf_op | source)
XLA Modules:
  0.0 46.9 jit_solution(9642020944137342462)
XLA Ops:
  0.6 0.9 %slice.185 = f32[6,16,32]{2,1,0:T(8,128)S(1)} slice(f32[6,16,3072]{2,1,0:T(8,128)} %state_ref.1), slice={[0:6], [0:16], [3040:3072]} | slice | bytes 24576 | tf_op jit(solution)/shard_map/slice | solution.py:390
  1.5 0.9 %fusion.21 = (f32[6,16,96]{2,1,0:T(8,128)S(1)}, f32[6,16,96]{2,1,0:T(8,128)S(1)}) fusion(f32[6,16,3072]{2,1,0:T(8,128)} %state_ref.1), kind=kLoop, calls=%fused_computation.70 | loop fusion | bytes 147456 | tf_op jit(solution)/shard_map/slice | solution.py:362
  2.4 0.1 pad_maximum_fusion.2
  2.5 2.6 %collective-permute-start.3 = (f32[6,16,128]{2,1,0:T(8,128)S(1)}, f32[6,16,128]{2,1,0:T(8,128)S(1)}, u32[]{:S(2)}, u32[]{:S(2)}) collective-permute-start(f32[6,16,128]{2,1,0:T(8,128)S(1)} %pad_maximum_fusion.2), channel_id=1, source_target_pairs={{1,0},{2,1},{3,2},{4,3},{5,4},{6,5},{7,6},{8,7},{9,8},{10,9},{11,1... | collective-permute-start | bytes 147464 | tf_op jit(solution)/shard_map/ppermute | solution.py:220
  5.1 2.8 %collective-permute-start.2 = (f32[6,16,96]{2,1,0:T(8,128)S(1)}, f32[6,16,96]{2,1,0:T(8,128)S(1)}, u32[]{:S(2)}, u32[]{:S(2)}) collective-permute-start(f32[6,16,96]{2,1,0:T(8,128)S(1)} %get-tuple-element.10), channel_id=1, source_target_pairs={{0,1},{1,2},{2,3},{3,4},{4,5},{5,6},{6,7},{7,8},{8,9},{9,10},{10,1... | collective-permute-start | bytes 110600 | tf_op jit(solution)/shard_map/ppermute | solution.py:220
  7.9 1.3 %fusion.22 = (f32[6,3,3072]{2,1,0:T(4,128)S(1)}, f32[6,3,3072]{2,1,0:T(4,128)S(1)}) fusion(f32[6,16,3072]{2,1,0:T(8,128)} %state_ref.1), kind=kLoop, calls=%fused_computation.71 | loop fusion | bytes 884736 | tf_op jit(solution)/shard_map/slice | solution.py:361
  9.3 3.1 %collective-permute-start = (f32[7,3,3072]{2,1,0:T(4,128)S(1)}, f32[7,3,3072]{2,1,0:T(4,128)S(1)}, u32[]{:S(2)}, u32[]{:S(2)}) collective-permute-start(f32[7,3,3072]{2,1,0:T(4,128)S(1)} %select_maximum_fusion.1), channel_id=1, source_target_pairs={{0,16},{16,32},{32,48},{48,64},{64,80},{80,96},{96,112},{112,128},... | collective-permute-start | bytes 774152 | tf_op jit(solution)/shard_map/ppermute | solution.py:220
  12.6 4.3 %collective-permute-start.1 = (f32[7,3,3072]{2,1,0:T(4,128)S(1)}, f32[7,3,3072]{2,1,0:T(4,128)S(1)}, u32[]{:S(2)}, u32[]{:S(2)}) collective-permute-start(f32[7,3,3072]{2,1,0:T(4,128)S(1)} %select_maximum_fusion), channel_id=1, source_target_pairs={{16,0},{32,16},{48,32},{64,48},{80,64},{96,80},{112,96},{128,112},... | collective-permute-start | bytes 774152 | tf_op jit(solution)/shard_map/ppermute | solution.py:220
  17.1 0.2 select_reduce_fusion.1
  17.3 0.1 iota_compare_fusion.3
  17.4 0.1 select_reduce_fusion
  17.6 0.1 copy.16
  17.7 0.1 mul.120
  17.8 0.1 tile.8
  18.0 1.1 %fusion = (f32[6,16,32]{2,1,0:T(8,128)S(1)}, f32[6,16,32]{2,1,0:T(8,128)S(1)}, f32[6,16,32]{2,1,0:T(8,128)S(1)}, f32[6,16,32]{2,1,0:T(8,128)S(1)}) fusion(f32[6,16,128]{2,1,0:T(8,128)S(1)} %collective-permute-done.3, f32[6,16,96]{2,1,0:T(8,128)S(1)} %collective-permute-done.2, pred[]{:T(512)S(6)} %eq.103, pred[]{:T(512)S(6)} %eq.110, f32[6,16,3072]{2,1,0:T(8,128)} %state_ref.1), kind=kLoop, calls=%fused_computation.6 | loop fusion | flops 6144 | bytes 122882 | tf_op jit(solution)/shard_map/jit(_where)/select_n | solution.py:378
  19.1 0.7 %collective-permute-start.5 = (f32[6,16,32]{2,1,0:T(8,128)S(1)}, f32[6,16,32]{2,1,0:T(8,128)S(1)}, u32[]{:S(2)}, u32[]{:S(2)}) collective-permute-start(f32[6,16,32]{2,1,0:T(8,128)S(1)} %get-tuple-element.6), channel_id=1, source_target_pairs={{15,1},{14,2},{0,3},{31,17},{30,18},{16,19},{47,33},{46,34},{32,35... | collective-permute-start | bytes 36872 | tf_op jit(solution)/shard_map/ppermute | solution.py:238
  19.7 0.7 %collective-permute-start.4 = (f32[6,16,32]{2,1,0:T(8,128)S(1)}, f32[6,16,32]{2,1,0:T(8,128)S(1)}, u32[]{:S(2)}, u32[]{:S(2)}) collective-permute-start(f32[6,16,32]{2,1,0:T(8,128)S(1)} %get-tuple-element.6), channel_id=1, source_target_pairs={{15,4},{14,5},{0,6},{31,20},{30,21},{16,22},{47,36},{46,37},{32,38... | collective-permute-start | bytes 36872 | tf_op jit(solution)/shard_map/ppermute | solution.py:238
  20.4 0.1 pad_maximum_fusion.1
  20.6 0.1 maximum_bitcast_fusion
  20.7 1.3 %collective-permute-start.6 = (f32[6,16,32]{2,1,0:T(8,128)S(1)}, f32[6,16,32]{2,1,0:T(8,128)S(1)}, u32[]{:S(2)}, u32[]{:S(2)}) collective-permute-start(f32[6,16,32]{2,1,0:T(8,128)S(1)} %select_select_fusion), channel_id=1, source_target_pairs={{15,7},{14,8},{0,9},{1,10},{2,11},{3,12},{4,13},{31,23},{30,24},{1... | collective-permute-start | bytes 36872 | tf_op jit(solution)/shard_map/ppermute | solution.py:238
  22.0 0.6 %pad_maximum_fusion.yhalo_ref = f32[2,6,16,128]{3,2,1,0:T(8,128)} fusion(f32[1,6,16,128]{3,2,1,0:T(8,128)S(1)} %select_bitcast_fusion, f32[1,6,16,128]{3,2,1,0:T(8,128)S(1)} %maximum_bitcast_fusion), kind=kLoop, calls=%fused_computation.4 | loop fusion | flops 24576 | bytes 196608 | tf_op jit(solution)/shard_map/stack | solution.py:392
  22.7 8.3 %collective-permute-done.6 = f32[6,16,32]{2,1,0:T(8,128)S(1)} collective-permute-done((f32[6,16,32]{2,1,0:T(8,128)S(1)}, f32[6,16,32]{2,1,0:T(8,128)S(1)}, u32[]{:S(2)}, u32[]{:S(2)}) %collective-permute-start.6) | collective-permute-done | bytes 12320 | tf_op jit(solution)/shard_map/ppermute | solution.py:238
  31.0 0.1 copy.15
  31.2 0.7 %multiply_add_fusion = (f32[16,32]{1,0:T(8,128)}, f32[16,32]{1,0:T(8,128)S(1)}, f32[16,32]{1,0:T(8,128)S(1)}, f32[16,32]{1,0:T(8,128)S(1)}) fusion(f32[16,32]{1,0:T(8,128)S(1)} %copy-done, f32[6,16,32]{2,1,0:T(8,128)S(1)} %broadcast_select_fusion, f32[16,2]{1,0:T(8,128)S(1)} %get-tuple-element.15, f32[16,30]{1,0:T(8,128)S(1)} %get-tuple-element.17, ...), kind=kLoop, calls=%fused_computation.51 | loop fusion | flops 29184 | bytes 31488 | tf_op jit(solution)/shard_map/add | solution.py:418
  31.9 0.1 copy.20
  32.0 0.1 copy.17
  32.0 0.1 copy.21
  32.1 0.1 copy.19
  32.2 0.1 copy.18
  32.4 0.1 concatenate.63
  32.5 0.9 %fusion.1.geo_ref = f32[112,128]{1,0:T(8,128)} fusion(f32[112,32]{0,1:T(8,128)S(1)} %concatenate.63, s32[128]{0:T(128)S(1)} %and_select_fusion), kind=kOutput, calls=%fused_computation.16 | convolution fusion | flops 5509120 | bytes 72192 | tf_op jit(solution)/shard_map/dot_general | solution.py:340
  33.4 13.5 %shard_map.68 = f32[6,16,3072]{2,1,0:T(8,128)} custom-call(f32[6,16,3072]{2,1,0:T(8,128)} %state_ref.1, f32[7,3,3072]{2,1,0:T(4,128)} %copy-done.1, f32[7,3,3072]{2,1,0:T(4,128)} %copy-done.2, f32[2,6,16,128]{3,2,1,0:T(8,128)} %pad_maximum_fusion.yhalo_ref, f32[112,128]{1,0:T(8,128)} %fusion.1.geo_ref), custom_call_target="tpu_custom_call" | custom-call | tf_op jit(solution)/shard_map/pallas_call | solution.py:199
  (46 shorter events, 0.8 us)
Async XLA Ops:
  0.6 8.6 %copy-start = (f32[16,32]{1,0:T(8,128)S(1)}, f32[16,32]{1,0:T(8,128)}, u32[]{:S(2)}) copy-start(f32[16,32]{1,0:T(8,128)} %param.6) | copy-start | bytes 6148
  2.5 15.5 %collective-permute-start.3 = (f32[6,16,128]{2,1,0:T(8,128)S(1)}, f32[6,16,128]{2,1,0:T(8,128)S(1)}, u32[]{:S(2)}, u32[]{:S(2)}) collective-permute-start(f32[6,16,128]{2,1,0:T(8,128)S(1)} %pad_maximum_fusion.2), channel_id=1, source_target_pairs={{1,0},{2,1},{3,2},{4,3},{5,4},{6,5},{7,6},{8,7},{9,8},{10,9},{11,1... | collective-permute-start | bytes 147464 | tf_op jit(solution)/shard_map/ppermute | solution.py:220
  5.1 12.0 %copy-start.4 = (s32[16]{0:T(128)S(1)}, s32[16]{0:T(128)}, u32[]{:S(2)}) copy-start(s32[16]{0:T(128)} %param.8) | copy-start | bytes 196
  5.1 12.0 %copy-start.5 = (s32[16]{0:T(128)S(1)}, s32[16]{0:T(128)}, u32[]{:S(2)}) copy-start(s32[16]{0:T(128)} %param.7) | copy-start | bytes 196
  5.1 12.3 %copy-start.3 = (f32[16,32]{1,0:T(8,128)S(1)}, f32[16,32]{1,0:T(8,128)}, u32[]{:S(2)}) copy-start(f32[16,32]{1,0:T(8,128)} %param.9) | copy-start | bytes 6148
  5.1 12.8 %collective-permute-start.2 = (f32[6,16,96]{2,1,0:T(8,128)S(1)}, f32[6,16,96]{2,1,0:T(8,128)S(1)}, u32[]{:S(2)}, u32[]{:S(2)}) collective-permute-start(f32[6,16,96]{2,1,0:T(8,128)S(1)} %get-tuple-element.10), channel_id=1, source_target_pairs={{0,1},{1,2},{2,3},{3,4},{4,5},{5,6},{6,7},{7,8},{8,9},{9,10},{10,1... | collective-permute-start | bytes 110600 | tf_op jit(solution)/shard_map/ppermute | solution.py:220
  9.3 21.7 %collective-permute-start = (f32[7,3,3072]{2,1,0:T(4,128)S(1)}, f32[7,3,3072]{2,1,0:T(4,128)S(1)}, u32[]{:S(2)}, u32[]{:S(2)}) collective-permute-start(f32[7,3,3072]{2,1,0:T(4,128)S(1)} %select_maximum_fusion.1), channel_id=1, source_target_pairs={{0,16},{16,32},{32,48},{48,64},{64,80},{80,96},{96,112},{112,128},... | collective-permute-start | bytes 774152 | tf_op jit(solution)/shard_map/ppermute | solution.py:220
  12.6 18.6 %collective-permute-start.1 = (f32[7,3,3072]{2,1,0:T(4,128)S(1)}, f32[7,3,3072]{2,1,0:T(4,128)S(1)}, u32[]{:S(2)}, u32[]{:S(2)}) collective-permute-start(f32[7,3,3072]{2,1,0:T(4,128)S(1)} %select_maximum_fusion), channel_id=1, source_target_pairs={{16,0},{32,16},{48,32},{64,48},{80,64},{96,80},{112,96},{128,112},... | collective-permute-start | bytes 774152 | tf_op jit(solution)/shard_map/ppermute | solution.py:220
  19.1 1.6 %collective-permute-start.5 = (f32[6,16,32]{2,1,0:T(8,128)S(1)}, f32[6,16,32]{2,1,0:T(8,128)S(1)}, u32[]{:S(2)}, u32[]{:S(2)}) collective-permute-start(f32[6,16,32]{2,1,0:T(8,128)S(1)} %get-tuple-element.6), channel_id=1, source_target_pairs={{15,1},{14,2},{0,3},{31,17},{30,18},{16,19},{47,33},{46,34},{32,35... | collective-permute-start | bytes 36872 | tf_op jit(solution)/shard_map/ppermute | solution.py:238
  19.7 1.0 %collective-permute-start.4 = (f32[6,16,32]{2,1,0:T(8,128)S(1)}, f32[6,16,32]{2,1,0:T(8,128)S(1)}, u32[]{:S(2)}, u32[]{:S(2)}) collective-permute-start(f32[6,16,32]{2,1,0:T(8,128)S(1)} %get-tuple-element.6), channel_id=1, source_target_pairs={{15,4},{14,5},{0,6},{31,20},{30,21},{16,22},{47,36},{46,37},{32,38... | collective-permute-start | bytes 36872 | tf_op jit(solution)/shard_map/ppermute | solution.py:238
  20.7 10.3 %collective-permute-start.6 = (f32[6,16,32]{2,1,0:T(8,128)S(1)}, f32[6,16,32]{2,1,0:T(8,128)S(1)}, u32[]{:S(2)}, u32[]{:S(2)}) collective-permute-start(f32[6,16,32]{2,1,0:T(8,128)S(1)} %select_select_fusion), channel_id=1, source_target_pairs={{15,7},{14,8},{0,9},{1,10},{2,11},{3,12},{4,13},{31,23},{30,24},{1... | collective-permute-start | bytes 36872 | tf_op jit(solution)/shard_map/ppermute | solution.py:238
  31.0 2.4 %copy-start.1 = (f32[7,3,3072]{2,1,0:T(4,128)}, f32[7,3,3072]{2,1,0:T(4,128)S(1)}, u32[]{:S(2)}) copy-start(f32[7,3,3072]{2,1,0:T(4,128)S(1)} %collective-permute-done.xlo_ref) | copy-start | bytes 774148
  31.1 2.3 %copy-start.2 = (f32[7,3,3072]{2,1,0:T(4,128)}, f32[7,3,3072]{2,1,0:T(4,128)S(1)}, u32[]{:S(2)}) copy-start(f32[7,3,3072]{2,1,0:T(4,128)S(1)} %collective-permute-done.1.xhi_ref) | copy-start | bytes 774148

commit v6 on v5

--- a/solution.py
+++ b/solution.py
@@ -20,10 +20,10 @@
 
 PLUS_WEIGHTS = (-2.0, 15.0, -60.0, 20.0, 30.0, -3.0, 0.0)
 MINUS_WEIGHTS = (0.0, 3.0, -30.0, -20.0, 60.0, -15.0, 2.0)
-CHUNK = 256
+CHUNK = 512
 PAD = 128
 HALO = 3
-XPAD = 8
+XPAD = 3
 LANES = 128
 
 
@@ -60,17 +60,16 @@
 def make_kernel(columns, length, planes, total_rows, dt):
     width = CHUNK + 2 * PAD
     face_area = STREAM_STEP * SPAN_STEP
-    xrows = columns + 2 * XPAD
+    xrows = columns + 2 * XPAD + 2
 
     def kernel(state_ref, xlo_ref, xhi_ref, yhalo_ref, geo_ref,
                out_ref, qx_ref, qy_ref, px_ref, mx_ref):
         col_dev = lax.axis_index("gx")
         first_row = lax.axis_index("gy") * (length // planes)
         for c in range(6):
-            qx_ref[c, 0:XPAD, :] = state_ref[c, 0:XPAD, :]
             qx_ref[c, XPAD:XPAD + columns, :] = state_ref[c]
-            qx_ref[c, XPAD + columns:, :] = state_ref[c, columns - XPAD:, :]
-            qx_ref[c, XPAD - HALO:XPAD, :] = xlo_ref[c]
+            qx_ref[c, XPAD + columns + HALO:, :] = state_ref[c, 2 * columns + 2 * XPAD - xrows:columns, :]
+            qx_ref[c, 0:HALO, :] = xlo_ref[c]
             qx_ref[c, XPAD + columns:XPAD + columns + HALO, :] = xhi_ref[c]
             qy_ref[c, :, 0:PAD] = yhalo_ref[0, c]
             qy_ref[c, :, PAD:PAD + length] = state_ref[c]
@@ -202,10 +201,10 @@
         in_specs=[vmem] * 5,
         out_specs=vmem,
         scratch_shapes=[
-            pltpu.VMEM((6, columns + 2 * XPAD, length), jnp.float32),
+            pltpu.VMEM((6, columns + 2 * XPAD + 2, length), jnp.float32),
             pltpu.VMEM((6, columns, length + 2 * PAD), jnp.float32),
-            pltpu.VMEM((6, columns + 2 * XPAD, CHUNK), jnp.float32),
-            pltpu.VMEM((6, columns + 2 * XPAD, CHUNK), jnp.float32),
+            pltpu.VMEM((6, columns + 2 * XPAD + 2, CHUNK), jnp.float32),
+            pltpu.VMEM((6, columns + 2 * XPAD + 2, CHUNK), jnp.float32),
         ],
     )(state, xlo, xhi, yhalo, geo)
 
@@ -392,15 +391,7 @@
     yhalo = jnp.stack([jnp.concatenate([ghost_below[..., : PAD - band], ghost_below], axis=2), ghost_above])
 
     height = shock_height
-    xrows = columns + 2 * XPAD
-    height_x = jnp.concatenate(
-        [
-            jnp.broadcast_to(height_ext[:1], (XPAD - HALO, planes)),
-            height_ext,
-            jnp.broadcast_to(height_ext[-1:], (XPAD - HALO, planes)),
-        ],
-        axis=0,
-    )
+    height_x = jnp.concatenate([height_ext, jnp.broadcast_to(height_ext[-1:], (2, planes))], axis=0)
     small = jnp.concatenate(
         [height_x, slope_x, slope_z, shock_rate, shock_rate / height, height], axis=0
     )

time: 47.4 us -> 46.6 us (0.983)
  Pallas kernels: 13.5 us -> 12.8 us
    pallas_call x1, Pallas kernels: 13.5 us -> 12.8 us  [update(): pl.pallas_call(kern, out_shape=jax.ShapeDtypeStruct((6, columns, length),...]
where the time goes in v6:
time: 46.6 us; the launch traced here: 46.2 us
  starting transfers between devices  15.4 us (33%)
  Pallas kernels  12.8 us (27%)
  waiting for transfers between devices  8.33 us (18%)
  local copies, waits for them, and re-layouts  4.46 us (10%)
  other arithmetic  3.31 us (7%)
  between operations  1 us (2%)
  matrix products  0.89 us (2%)
    pallas_call x1, Pallas kernels, update(): pl.pallas_call(kern, out_shape=jax.ShapeDtypeStruct((6, columns, length),...  12.8 us
    ppermute x4, starting transfers between devices, shifted(): return lax.ppermute(block, axis, pairs)  12.7 us
    ppermute x3, waiting for transfers between devices, broadcast(): received = lax.ppermute(array, axis, pairs)  8.32 us
    ppermute x3, starting transfers between devices, broadcast(): received = lax.ppermute(array, axis, pairs)  2.62 us
    slice x1, local copies, waits for them, and re-layouts, shards(): from_high = shifted(pack(state[:, :HALO], shock_height[:HALO]), 'gx', False)  1.35 us
    select_n x1, other arithmetic, shards(): jnp.where(row_dev == row_devs - 1, state[..., length - planes:], jnp.wher...  1.09 us
  transfers between devices with their start and end apart: 7, of which 1 were waited for; matrix products, arithmetic and copies ran while one was open for 10% of the time, Pallas kernels for 0%

profile of v6, /device:TPU:113, one launch (start us, length us, event | category | flops | bytes accessed | tf_op | source)
XLA Modules:
  0.0 46.2 jit_solution(9355338387322833845)
XLA Ops:
  0.6 0.9 %slice.182 = f32[6,16,32]{2,1,0:T(8,128)S(1)} slice(f32[6,16,3072]{2,1,0:T(8,128)} %state_ref.1), slice={[0:6], [0:16], [3040:3072]} | slice | bytes 24576 | tf_op jit(solution)/shard_map/slice | solution.py:389
  1.5 0.9 %fusion.21 = (f32[6,16,96]{2,1,0:T(8,128)S(1)}, f32[6,16,96]{2,1,0:T(8,128)S(1)}) fusion(f32[6,16,3072]{2,1,0:T(8,128)} %state_ref.1), kind=kLoop, calls=%fused_computation.69 | loop fusion | bytes 147456 | tf_op jit(solution)/shard_map/slice | solution.py:361
  2.4 0.1 pad_maximum_fusion.2
  2.5 2.6 %collective-permute-start.3 = (f32[6,16,128]{2,1,0:T(8,128)S(1)}, f32[6,16,128]{2,1,0:T(8,128)S(1)}, u32[]{:S(2)}, u32[]{:S(2)}) collective-permute-start(f32[6,16,128]{2,1,0:T(8,128)S(1)} %pad_maximum_fusion.2), channel_id=1, source_target_pairs={{1,0},{2,1},{3,2},{4,3},{5,4},{6,5},{7,6},{8,7},{9,8},{10,9},{11,1... | collective-permute-start | bytes 147464 | tf_op jit(solution)/shard_map/ppermute | solution.py:219
  5.1 2.8 %collective-permute-start.2 = (f32[6,16,96]{2,1,0:T(8,128)S(1)}, f32[6,16,96]{2,1,0:T(8,128)S(1)}, u32[]{:S(2)}, u32[]{:S(2)}) collective-permute-start(f32[6,16,96]{2,1,0:T(8,128)S(1)} %get-tuple-element.10), channel_id=1, source_target_pairs={{0,1},{1,2},{2,3},{3,4},{4,5},{5,6},{6,7},{7,8},{8,9},{9,10},{10,1... | collective-permute-start | bytes 110600 | tf_op jit(solution)/shard_map/ppermute | solution.py:219
  7.9 1.3 %fusion.22 = (f32[6,3,3072]{2,1,0:T(4,128)S(1)}, f32[6,3,3072]{2,1,0:T(4,128)S(1)}) fusion(f32[6,16,3072]{2,1,0:T(8,128)} %state_ref.1), kind=kLoop, calls=%fused_computation.70 | loop fusion | bytes 884736 | tf_op jit(solution)/shard_map/slice | solution.py:360
  9.3 3.1 %collective-permute-start = (f32[7,3,3072]{2,1,0:T(4,128)S(1)}, f32[7,3,3072]{2,1,0:T(4,128)S(1)}, u32[]{:S(2)}, u32[]{:S(2)}) collective-permute-start(f32[7,3,3072]{2,1,0:T(4,128)S(1)} %select_maximum_fusion.1), channel_id=1, source_target_pairs={{0,16},{16,32},{32,48},{48,64},{64,80},{80,96},{96,112},{112,128},... | collective-permute-start | bytes 774152 | tf_op jit(solution)/shard_map/ppermute | solution.py:219
  12.6 4.3 %collective-permute-start.1 = (f32[7,3,3072]{2,1,0:T(4,128)S(1)}, f32[7,3,3072]{2,1,0:T(4,128)S(1)}, u32[]{:S(2)}, u32[]{:S(2)}) collective-permute-start(f32[7,3,3072]{2,1,0:T(4,128)S(1)} %select_maximum_fusion), channel_id=1, source_target_pairs={{16,0},{32,16},{48,32},{64,48},{80,64},{96,80},{112,96},{128,112},... | collective-permute-start | bytes 774152 | tf_op jit(solution)/shard_map/ppermute | solution.py:219
  17.1 0.2 select_reduce_fusion.1
  17.3 0.1 iota_compare_fusion.3
  17.4 0.1 select_reduce_fusion
  17.6 0.1 copy.16
  17.7 0.1 mul.120
  17.8 0.1 tile.8
  18.0 1.1 %fusion = (f32[6,16,32]{2,1,0:T(8,128)S(1)}, f32[6,16,32]{2,1,0:T(8,128)S(1)}, f32[6,16,32]{2,1,0:T(8,128)S(1)}, f32[6,16,32]{2,1,0:T(8,128)S(1)}) fusion(f32[6,16,128]{2,1,0:T(8,128)S(1)} %collective-permute-done.3, f32[6,16,96]{2,1,0:T(8,128)S(1)} %collective-permute-done.2, pred[]{:T(512)S(6)} %eq.103, pred[]{:T(512)S(6)} %eq.110, f32[6,16,3072]{2,1,0:T(8,128)} %state_ref.1), kind=kLoop, calls=%fused_computation.6 | loop fusion | flops 6144 | bytes 122882 | tf_op jit(solution)/shard_map/jit(_where)/select_n | solution.py:377
  19.1 0.7 %collective-permute-start.5 = (f32[6,16,32]{2,1,0:T(8,128)S(1)}, f32[6,16,32]{2,1,0:T(8,128)S(1)}, u32[]{:S(2)}, u32[]{:S(2)}) collective-permute-start(f32[6,16,32]{2,1,0:T(8,128)S(1)} %get-tuple-element.6), channel_id=1, source_target_pairs={{15,1},{14,2},{0,3},{31,17},{30,18},{16,19},{47,33},{46,34},{32,35... | collective-permute-start | bytes 36872 | tf_op jit(solution)/shard_map/ppermute | solution.py:237
  19.7 0.7 %collective-permute-start.4 = (f32[6,16,32]{2,1,0:T(8,128)S(1)}, f32[6,16,32]{2,1,0:T(8,128)S(1)}, u32[]{:S(2)}, u32[]{:S(2)}) collective-permute-start(f32[6,16,32]{2,1,0:T(8,128)S(1)} %get-tuple-element.6), channel_id=1, source_target_pairs={{15,4},{14,5},{0,6},{31,20},{30,21},{16,22},{47,36},{46,37},{32,38... | collective-permute-start | bytes 36872 | tf_op jit(solution)/shard_map/ppermute | solution.py:237
  20.4 0.1 pad_maximum_fusion.1
  20.6 0.1 maximum_bitcast_fusion
  20.7 1.3 %collective-permute-start.6 = (f32[6,16,32]{2,1,0:T(8,128)S(1)}, f32[6,16,32]{2,1,0:T(8,128)S(1)}, u32[]{:S(2)}, u32[]{:S(2)}) collective-permute-start(f32[6,16,32]{2,1,0:T(8,128)S(1)} %select_select_fusion), channel_id=1, source_target_pairs={{15,7},{14,8},{0,9},{1,10},{2,11},{3,12},{4,13},{31,23},{30,24},{1... | collective-permute-start | bytes 36872 | tf_op jit(solution)/shard_map/ppermute | solution.py:237
  22.0 0.6 %pad_maximum_fusion.yhalo_ref = f32[2,6,16,128]{3,2,1,0:T(8,128)} fusion(f32[1,6,16,128]{3,2,1,0:T(8,128)S(1)} %select_bitcast_fusion, f32[1,6,16,128]{3,2,1,0:T(8,128)S(1)} %maximum_bitcast_fusion), kind=kLoop, calls=%fused_computation.4 | loop fusion | flops 24576 | bytes 196608 | tf_op jit(solution)/shard_map/stack | solution.py:391
  22.7 8.3 %collective-permute-done.6 = f32[6,16,32]{2,1,0:T(8,128)S(1)} collective-permute-done((f32[6,16,32]{2,1,0:T(8,128)S(1)}, f32[6,16,32]{2,1,0:T(8,128)S(1)}, u32[]{:S(2)}, u32[]{:S(2)}) %collective-permute-start.6) | collective-permute-done | bytes 12320 | tf_op jit(solution)/shard_map/ppermute | solution.py:237
  31.0 0.1 copy.15
  31.1 0.7 %multiply_add_fusion = (f32[16,32]{1,0:T(8,128)}, f32[16,32]{1,0:T(8,128)S(1)}, f32[16,32]{1,0:T(8,128)S(1)}, f32[16,32]{1,0:T(8,128)S(1)}) fusion(f32[16,32]{1,0:T(8,128)S(1)} %copy-done, f32[6,16,32]{2,1,0:T(8,128)S(1)} %broadcast_select_fusion, f32[16,2]{1,0:T(8,128)S(1)} %get-tuple-element.15, f32[16,30]{1,0:T(8,128)S(1)} %get-tuple-element.17, ...), kind=kLoop, calls=%fused_computation.51 | loop fusion | flops 29184 | bytes 31488 | tf_op jit(solution)/shard_map/add | solution.py:409
  31.9 0.1 copy.20
  32.0 0.1 copy.17
  32.0 0.1 copy.21
  32.1 0.1 copy.19
  32.2 0.1 copy.18
  32.3 0.1 concatenate.63
  32.4 0.9 %fusion.1.geo_ref = f32[104,128]{1,0:T(8,128)} fusion(f32[104,32]{0,1:T(8,128)S(1)} %concatenate.63, s32[128]{0:T(128)S(1)} %and_select_fusion), kind=kOutput, calls=%fused_computation.16 | convolution fusion | flops 5115904 | bytes 67072 | tf_op jit(solution)/shard_map/dot_general | solution.py:339
  33.3 12.8 %shard_map.68 = f32[6,16,3072]{2,1,0:T(8,128)} custom-call(f32[6,16,3072]{2,1,0:T(8,128)} %state_ref.1, f32[7,3,3072]{2,1,0:T(4,128)} %copy-done.1, f32[7,3,3072]{2,1,0:T(4,128)} %copy-done.2, f32[2,6,16,128]{3,2,1,0:T(8,128)} %pad_maximum_fusion.yhalo_ref, f32[104,128]{1,0:T(8,128)} %fusion.1.geo_ref), custom_call_target="tpu_custom_call" | custom-call | tf_op jit(solution)/shard_map/pallas_call | solution.py:198
  (44 shorter events, 0.7 us)
Async XLA Ops:
  0.6 8.6 %copy-start = (f32[16,32]{1,0:T(8,128)S(1)}, f32[16,32]{1,0:T(8,128)}, u32[]{:S(2)}) copy-start(f32[16,32]{1,0:T(8,128)} %param.6) | copy-start | bytes 6148
  2.5 15.5 %collective-permute-start.3 = (f32[6,16,128]{2,1,0:T(8,128)S(1)}, f32[6,16,128]{2,1,0:T(8,128)S(1)}, u32[]{:S(2)}, u32[]{:S(2)}) collective-permute-start(f32[6,16,128]{2,1,0:T(8,128)S(1)} %pad_maximum_fusion.2), channel_id=1, source_target_pairs={{1,0},{2,1},{3,2},{4,3},{5,4},{6,5},{7,6},{8,7},{9,8},{10,9},{11,1... | collective-permute-start | bytes 147464 | tf_op jit(solution)/shard_map/ppermute | solution.py:219
  5.1 12.0 %copy-start.4 = (s32[16]{0:T(128)S(1)}, s32[16]{0:T(128)}, u32[]{:S(2)}) copy-start(s32[16]{0:T(128)} %param.8) | copy-start | bytes 196
  5.1 12.0 %copy-start.5 = (s32[16]{0:T(128)S(1)}, s32[16]{0:T(128)}, u32[]{:S(2)}) copy-start(s32[16]{0:T(128)} %param.7) | copy-start | bytes 196
  5.1 12.3 %copy-start.3 = (f32[16,32]{1,0:T(8,128)S(1)}, f32[16,32]{1,0:T(8,128)}, u32[]{:S(2)}) copy-start(f32[16,32]{1,0:T(8,128)} %param.9) | copy-start | bytes 6148
  5.1 12.8 %collective-permute-start.2 = (f32[6,16,96]{2,1,0:T(8,128)S(1)}, f32[6,16,96]{2,1,0:T(8,128)S(1)}, u32[]{:S(2)}, u32[]{:S(2)}) collective-permute-start(f32[6,16,96]{2,1,0:T(8,128)S(1)} %get-tuple-element.10), channel_id=1, source_target_pairs={{0,1},{1,2},{2,3},{3,4},{4,5},{5,6},{6,7},{7,8},{8,9},{9,10},{10,1... | collective-permute-start | bytes 110600 | tf_op jit(solution)/shard_map/ppermute | solution.py:219
  9.3 21.7 %collective-permute-start = (f32[7,3,3072]{2,1,0:T(4,128)S(1)}, f32[7,3,3072]{2,1,0:T(4,128)S(1)}, u32[]{:S(2)}, u32[]{:S(2)}) collective-permute-start(f32[7,3,3072]{2,1,0:T(4,128)S(1)} %select_maximum_fusion.1), channel_id=1, source_target_pairs={{0,16},{16,32},{32,48},{48,64},{64,80},{80,96},{96,112},{112,128},... | collective-permute-start | bytes 774152 | tf_op jit(solution)/shard_map/ppermute | solution.py:219
  12.6 18.6 %collective-permute-start.1 = (f32[7,3,3072]{2,1,0:T(4,128)S(1)}, f32[7,3,3072]{2,1,0:T(4,128)S(1)}, u32[]{:S(2)}, u32[]{:S(2)}) collective-permute-start(f32[7,3,3072]{2,1,0:T(4,128)S(1)} %select_maximum_fusion), channel_id=1, source_target_pairs={{16,0},{32,16},{48,32},{64,48},{80,64},{96,80},{112,96},{128,112},... | collective-permute-start | bytes 774152 | tf_op jit(solution)/shard_map/ppermute | solution.py:219
  19.1 1.6 %collective-permute-start.5 = (f32[6,16,32]{2,1,0:T(8,128)S(1)}, f32[6,16,32]{2,1,0:T(8,128)S(1)}, u32[]{:S(2)}, u32[]{:S(2)}) collective-permute-start(f32[6,16,32]{2,1,0:T(8,128)S(1)} %get-tuple-element.6), channel_id=1, source_target_pairs={{15,1},{14,2},{0,3},{31,17},{30,18},{16,19},{47,33},{46,34},{32,35... | collective-permute-start | bytes 36872 | tf_op jit(solution)/shard_map/ppermute | solution.py:237
  19.7 1.0 %collective-permute-start.4 = (f32[6,16,32]{2,1,0:T(8,128)S(1)}, f32[6,16,32]{2,1,0:T(8,128)S(1)}, u32[]{:S(2)}, u32[]{:S(2)}) collective-permute-start(f32[6,16,32]{2,1,0:T(8,128)S(1)} %get-tuple-element.6), channel_id=1, source_target_pairs={{15,4},{14,5},{0,6},{31,20},{30,21},{16,22},{47,36},{46,37},{32,38... | collective-permute-start | bytes 36872 | tf_op jit(solution)/shard_map/ppermute | solution.py:237
  20.7 10.3 %collective-permute-start.6 = (f32[6,16,32]{2,1,0:T(8,128)S(1)}, f32[6,16,32]{2,1,0:T(8,128)S(1)}, u32[]{:S(2)}, u32[]{:S(2)}) collective-permute-start(f32[6,16,32]{2,1,0:T(8,128)S(1)} %select_select_fusion), channel_id=1, source_target_pairs={{15,7},{14,8},{0,9},{1,10},{2,11},{3,12},{4,13},{31,23},{30,24},{1... | collective-permute-start | bytes 36872 | tf_op jit(solution)/shard_map/ppermute | solution.py:237
  31.0 2.3 %copy-start.1 = (f32[7,3,3072]{2,1,0:T(4,128)}, f32[7,3,3072]{2,1,0:T(4,128)S(1)}, u32[]{:S(2)}) copy-start(f32[7,3,3072]{2,1,0:T(4,128)S(1)} %collective-permute-done.xlo_ref) | copy-start | bytes 774148
  31.1 2.2 %copy-start.2 = (f32[7,3,3072]{2,1,0:T(4,128)}, f32[7,3,3072]{2,1,0:T(4,128)S(1)}, u32[]{:S(2)}) copy-start(f32[7,3,3072]{2,1,0:T(4,128)S(1)} %collective-permute-done.1.xhi_ref) | copy-start | bytes 774148

commit v7 on v6

--- a/solution.py
+++ b/solution.py
@@ -57,13 +57,11 @@
     return (growth - 1.0) / denominator, STRETCH_RATE * growth / (total_rows * denominator)
 
 
-def make_kernel(columns, length, planes, total_rows, dt):
-    width = CHUNK + 2 * PAD
+def stream_kernel(columns, length, planes, total_rows, dt):
     face_area = STREAM_STEP * SPAN_STEP
     xrows = columns + 2 * XPAD + 2
 
-    def kernel(state_ref, xlo_ref, xhi_ref, yhalo_ref, geo_ref,
-               out_ref, qx_ref, qy_ref, px_ref, mx_ref):
+    def kernel(state_ref, xlo_ref, xhi_ref, geo_ref, out_ref, qx_ref, px_ref, mx_ref):
         col_dev = lax.axis_index("gx")
         first_row = lax.axis_index("gy") * (length // planes)
         for c in range(6):
@@ -71,9 +69,6 @@
             qx_ref[c, XPAD + columns + HALO:, :] = state_ref[c, 2 * columns + 2 * XPAD - xrows:columns, :]
             qx_ref[c, 0:HALO, :] = xlo_ref[c]
             qx_ref[c, XPAD + columns:XPAD + columns + HALO, :] = xhi_ref[c]
-            qy_ref[c, :, 0:PAD] = yhalo_ref[0, c]
-            qy_ref[c, :, PAD:PAD + length] = state_ref[c]
-            qy_ref[c, :, PAD + length:] = yhalo_ref[1, c, :, 0:PAD]
 
         @pl.when(col_dev == 0)
         def _():
@@ -87,21 +82,14 @@
                     state_ref[c, columns - 1:columns, :], (HALO, length))
 
         height_x = lane_tile(geo_ref[0:xrows, :], CHUNK)
-        slope_x = lane_tile(geo_ref[xrows:xrows + columns, :], width)
-        slope_z = lane_tile(geo_ref[xrows + columns:xrows + 2 * columns, :], width)
-        rate = lane_tile(geo_ref[xrows + 2 * columns:xrows + 3 * columns, :], width)
-        ratio = lane_tile(geo_ref[xrows + 3 * columns:xrows + 4 * columns, :], CHUNK)
-        height = lane_tile(geo_ref[xrows + 4 * columns:xrows + 5 * columns, :], CHUNK)
+        height = lane_tile(geo_ref[xrows:xrows + columns, :], CHUNK)
         lane = lax.broadcasted_iota(jnp.int32, (columns, CHUNK), 1) % planes
         lane_in = lax.broadcasted_iota(jnp.int32, (1, CHUNK), 1)
-        lane_out = lax.broadcasted_iota(jnp.int32, (1, width), 1)
 
         def body(k, carry):
             o = pl.multiple_of(k * CHUNK, CHUNK)
             rows_in = (first_row + (o + lane_in) // planes).astype(jnp.float32)
             spacing = stretch_factors(rows_in, total_rows)[1]
-            rows_out = (first_row - PAD // planes + (o + lane_out) // planes).astype(jnp.float32)
-            eta = stretch_factors(rows_out, total_rows)[0]
             xa = [qx_ref[c, :, pl.ds(o, CHUNK)] for c in range(6)]
             inverse, vel_x, vel_y, vel_z, stress, sound = kernel_primitives(xa)
             metric = STREAM_STEP * height_x * spacing
@@ -126,33 +114,8 @@
                         term = mterm if term is None else term + mterm
                     acc = term if acc is None else acc + term
                 div.append(acc)
-            ya = [qy_ref[c, :, pl.ds(o, width)] for c in range(6)]
-            inverse, vel_x, vel_y, vel_z, stress, sound = kernel_primitives(ya)
-            scaled = -face_area * eta
-            metric_x = scaled * slope_x
-            metric_z = scaled * slope_z
-            metric_t = scaled * rate
-            contra = metric_t + metric_x * vel_x + face_area * vel_y + metric_z * vel_z
-            fluxes = [ya[0] * contra, ya[1] * contra + metric_x * stress,
-                      ya[2] * contra + face_area * stress, ya[3] * contra + metric_z * stress,
-                      (ya[4] + stress) * contra - metric_t * stress, ya[5] * contra]
-            speed = jnp.abs(contra) + sound * jnp.sqrt(
-                metric_x * metric_x + face_area * face_area + metric_z * metric_z)
-            for c in range(6):
-                plus = 0.5 * (fluxes[c] + speed * ya[c])
-                minus = 0.5 * (fluxes[c] - speed * ya[c])
-                acc = None
-                for t in range(-3, 4):
-                    term = combined(plus, minus, t)
-                    if t != 0:
-                        term = pltpu.roll(term, (-planes * t) % width, 1)
-                    acc = term if acc is None else acc + term
-                div[c] = div[c] + acc[:, PAD:PAD + CHUNK]
-            q = [v[:, PAD:PAD + CHUNK] for v in ya]
-            inverse = inverse[:, PAD:PAD + CHUNK]
-            vel_z = vel_z[:, PAD:PAD + CHUNK]
-            stress = stress[:, PAD:PAD + CHUNK]
-            sound = sound[:, PAD:PAD + CHUNK]
+            q = [state_ref[c, :, pl.ds(o, CHUNK)] for c in range(6)]
+            inverse, vel_x, vel_y, vel_z, stress, sound = kernel_primitives(q)
             metric = STREAM_STEP * height * spacing
             fluxes = [q[3], q[1] * vel_z, q[2] * vel_z, q[3] * vel_z + stress,
                       (q[4] + stress) * vel_z, q[5] * vel_z]
@@ -179,7 +142,7 @@
             source = q[0] * (balanced - q[5] * inverse) * teller
             volume = face_area * height * spacing
             for c in range(6):
-                change = -(div[c] * (1.0 / 60.0)) / volume - q[c] * ratio
+                change = -(div[c] * (1.0 / 60.0)) / volume
                 if c == 5:
                     change = change + source
                 out_ref[c, :, pl.ds(o, CHUNK)] = q[c] + dt * change
@@ -190,23 +153,97 @@
     return kernel
 
 
-def update(state, xlo, xhi, yhalo, geo, planes, total_rows, dt):
+def normal_kernel(columns, length, planes, total_rows, dt):
+    width = CHUNK + 2 * PAD
+    face_area = STREAM_STEP * SPAN_STEP
+
+    def kernel(state_ref, yhalo_ref, geo_ref, part_ref, out_ref, qy_ref):
+        first_row = lax.axis_index("gy") * (length // planes)
+        for c in range(6):
+            qy_ref[c, :, 0:PAD] = yhalo_ref[0, c]
+            qy_ref[c, :, PAD:PAD + length] = state_ref[c]
+            qy_ref[c, :, PAD + length:] = yhalo_ref[1, c]
+
+        slope_x = lane_tile(geo_ref[0:columns, :], width)
+        slope_z = lane_tile(geo_ref[columns:2 * columns, :], width)
+        rate = lane_tile(geo_ref[2 * columns:3 * columns, :], width)
+        ratio = lane_tile(geo_ref[3 * columns:4 * columns, :], CHUNK)
+        height = lane_tile(geo_ref[4 * columns:5 * columns, :], CHUNK)
+        lane_in = lax.broadcasted_iota(jnp.int32, (1, CHUNK), 1)
+        lane_out = lax.broadcasted_iota(jnp.int32, (1, width), 1)
+
+        def body(k, carry):
+            o = pl.multiple_of(k * CHUNK, CHUNK)
+            rows_in = (first_row + (o + lane_in) // planes).astype(jnp.float32)
+            spacing = stretch_factors(rows_in, total_rows)[1]
+            rows_out = (first_row - PAD // planes + (o + lane_out) // planes).astype(jnp.float32)
+            eta = stretch_factors(rows_out, total_rows)[0]
+            ya = [qy_ref[c, :, pl.ds(o, width)] for c in range(6)]
+            inverse, vel_x, vel_y, vel_z, stress, sound = kernel_primitives(ya)
+            scaled = -face_area * eta
+            metric_x = scaled * slope_x
+            metric_z = scaled * slope_z
+            metric_t = scaled * rate
+            contra = metric_t + metric_x * vel_x + face_area * vel_y + metric_z * vel_z
+            fluxes = [ya[0] * contra, ya[1] * contra + metric_x * stress,
+                      ya[2] * contra + face_area * stress, ya[3] * contra + metric_z * stress,
+                      (ya[4] + stress) * contra - metric_t * stress, ya[5] * contra]
+            speed = jnp.abs(contra) + sound * jnp.sqrt(
+                metric_x * metric_x + face_area * face_area + metric_z * metric_z)
+            volume = face_area * height * spacing
+            for c in range(6):
+                plus = 0.5 * (fluxes[c] + speed * ya[c])
+                minus = 0.5 * (fluxes[c] - speed * ya[c])
+                acc = None
+                for t in range(-3, 4):
+                    term = combined(plus, minus, t)
+                    if t != 0:
+                        term = pltpu.roll(term, (-planes * t) % width, 1)
+                    acc = term if acc is None else acc + term
+                div = acc[:, PAD:PAD + CHUNK]
+                q = ya[c][:, PAD:PAD + CHUNK]
+                change = -(div * (1.0 / 60.0)) / volume - q * ratio
+                out_ref[c, :, pl.ds(o, CHUNK)] = part_ref[c, :, pl.ds(o, CHUNK)] + dt * change
+            return carry
+
+        lax.fori_loop(0, length // CHUNK, body, 0)
+
+    return kernel
+
+
+def stream_update(state, xlo, xhi, geo, planes, total_rows, dt):
     columns = state.shape[1]
     length = state.shape[2]
-    kern = make_kernel(columns, length, planes, total_rows, dt)
     vmem = pl.BlockSpec(memory_space=pltpu.VMEM)
+    cells = 6 * columns * length
     return pl.pallas_call(
-        kern,
+        stream_kernel(columns, length, planes, total_rows, dt),
         out_shape=jax.ShapeDtypeStruct((6, columns, length), jnp.float32),
-        in_specs=[vmem] * 5,
+        in_specs=[vmem] * 4,
         out_specs=vmem,
         scratch_shapes=[
             pltpu.VMEM((6, columns + 2 * XPAD + 2, length), jnp.float32),
-            pltpu.VMEM((6, columns, length + 2 * PAD), jnp.float32),
             pltpu.VMEM((6, columns + 2 * XPAD + 2, CHUNK), jnp.float32),
             pltpu.VMEM((6, columns + 2 * XPAD + 2, CHUNK), jnp.float32),
         ],
-    )(state, xlo, xhi, yhalo, geo)
+        cost_estimate=pl.CostEstimate(flops=150 * cells, transcendentals=cells, bytes_accessed=12 * cells),
+    )(state, xlo, xhi, geo)
+
+
+def normal_update(state, yhalo, geo, part, planes, total_rows, dt):
+    columns = state.shape[1]
+    length = state.shape[2]
+    vmem = pl.BlockSpec(memory_space=pltpu.VMEM)
+    cells = 6 * columns * length
+    return pl.pallas_call(
+        normal_kernel(columns, length, planes, total_rows, dt),
+        out_shape=jax.ShapeDtypeStruct((6, columns, length), jnp.float32),
+        in_specs=[vmem] * 4,
+        out_specs=vmem,
+        input_output_aliases={3: 0},
+        scratch_shapes=[pltpu.VMEM((6, columns, length + 2 * PAD), jnp.float32)],
+        cost_estimate=pl.CostEstimate(flops=150 * cells, transcendentals=cells, bytes_accessed=12 * cells),
+    )(state, yhalo, geo, part)
 
 
 def shifted(block, axis, forward, cyclic=False):
@@ -380,6 +417,10 @@
         jnp.where(row_dev == 0, below[..., band - planes :], above[..., band:]),
     )
     seeded = sorted({row_devs - 1, 0, max(row_devs - 2, 0)}, reverse=True)
+    height_x = jnp.concatenate([height_ext, jnp.broadcast_to(height_ext[-1:], (2, planes))], axis=0)
+    geo_x = replicate_lanes(jnp.concatenate([height_x, shock_height], axis=0), planes)
+    part = stream_update(state, from_low, from_high, geo_x, planes, total_rows, COURANT / total_rows)
+    top_seed, part = lax.optimization_barrier((top_seed, part))
     top_row = broadcast(top_seed, "gy", seeded, (2, 1, 1, 1, 1))
     shock_rate = shock_speed(top_row, slope_x, slope_z)
 
@@ -391,21 +432,9 @@
     yhalo = jnp.stack([jnp.concatenate([ghost_below[..., : PAD - band], ghost_below], axis=2), ghost_above])
 
     height = shock_height
-    height_x = jnp.concatenate([height_ext, jnp.broadcast_to(height_ext[-1:], (2, planes))], axis=0)
-    small = jnp.concatenate(
-        [height_x, slope_x, slope_z, shock_rate, shock_rate / height, height], axis=0
-    )
+    small = jnp.concatenate([slope_x, slope_z, shock_rate, shock_rate / height, height], axis=0)
     geo = replicate_lanes(small, planes)
-    state_new = update(
-        state,
-        from_low,
-        from_high,
-        yhalo,
-        geo,
-        planes,
-        total_rows,
-        COURANT / total_rows,
-    )
+    state_new = normal_update(state, yhalo, geo, part, planes, total_rows, COURANT / total_rows)
     shock_new = shock_height + COURANT / total_rows * shock_rate
     return (state_new, shock_new)
 

time: 46.6 us -> 56.6 us (1.21)
  the two profiles are of different devices: /device:TPU:113 before, /device:TPU:199 now
where the time goes in v7:
time: 56.6 us; the launch traced here: 56.2 us
  waiting for transfers between devices  18.9 us (33%)
  Pallas kernels  15.5 us (27%)
  starting transfers between devices  11.6 us (20%)
  local copies, waits for them, and re-layouts  4.34 us (8%)
  other arithmetic  3.31 us (6%)
  matrix products  1.61 us (3%)
  between operations  1 us (2%)
    ppermute x3, waiting for transfers between devices, broadcast(): received = lax.ppermute(array, axis, pairs)  9.58 us
    ppermute x4, waiting for transfers between devices, shifted(): return lax.ppermute(block, axis, pairs)  9.31 us
    pallas_call x1, Pallas kernels, stream_update(): pl.pallas_call(stream_kernel(columns, length, planes, total_rows, dt), ou...  9.13 us
    ppermute x4, starting transfers between devices, shifted(): return lax.ppermute(block, axis, pairs)  8.95 us
    pallas_call x1, Pallas kernels, normal_update(): pl.pallas_call(normal_kernel(columns, length, planes, total_rows, dt), ou...  6.34 us
    ppermute x3, starting transfers between devices, broadcast(): received = lax.ppermute(array, axis, pairs)  2.61 us
    dot_general x2, matrix products, replicate_lanes(): jnp.dot(small, pick, precision=lax.Precision.HIGHEST, preferred_element_t...  1.61 us
    slice x1, local copies, waits for them, and re-layouts, shards(): from_high = shifted(pack(state[:, :HALO], shock_height[:HALO]), 'gx', False)  1.35 us
  transfers between devices with their start and end apart: 7, of which 2 were waited for; matrix products, arithmetic and copies ran while one was open for 8% of the time, Pallas kernels for 0%

profile of v7, /device:TPU:199, one launch (start us, length us, event | category | flops | bytes accessed | tf_op | source)
XLA Modules:
  0.0 56.2 jit_solution(15099625412112668195)
XLA Ops:
  0.6 0.9 %slice.178 = f32[6,16,32]{2,1,0:T(8,128)S(1)} slice(f32[6,16,3072]{2,1,0:T(8,128)} %state_ref.3), slice={[0:6], [0:16], [3040:3072]} | slice | bytes 24576 | tf_op jit(solution)/shard_map/slice | solution.py:430
  1.5 0.9 %fusion.24 = (f32[6,16,96]{2,1,0:T(8,128)S(1)}, f32[6,16,96]{2,1,0:T(8,128)S(1)}) fusion(f32[6,16,3072]{2,1,0:T(8,128)} %state_ref.3), kind=kLoop, calls=%fused_computation.72 | loop fusion | bytes 147456 | tf_op jit(solution)/shard_map/slice | solution.py:398
  2.4 0.1 pad_maximum_fusion.2
  2.5 2.6 %collective-permute-start.1 = (f32[6,16,128]{2,1,0:T(8,128)S(1)}, f32[6,16,128]{2,1,0:T(8,128)S(1)}, u32[]{:S(2)}, u32[]{:S(2)}) collective-permute-start(f32[6,16,128]{2,1,0:T(8,128)S(1)} %pad_maximum_fusion.2), channel_id=1, source_target_pairs={{1,0},{2,1},{3,2},{4,3},{5,4},{6,5},{7,6},{8,7},{9,8},{10,9},{11,1... | collective-permute-start | bytes 147464 | tf_op jit(solution)/shard_map/ppermute | solution.py:256
  5.1 1.1 %collective-permute-start = (f32[6,16,96]{2,1,0:T(8,128)S(1)}, f32[6,16,96]{2,1,0:T(8,128)S(1)}, u32[]{:S(2)}, u32[]{:S(2)}) collective-permute-start(f32[6,16,96]{2,1,0:T(8,128)S(1)} %get-tuple-element.16), channel_id=1, source_target_pairs={{0,1},{1,2},{2,3},{3,4},{4,5},{5,6},{6,7},{7,8},{8,9},{9,10},{10,1... | collective-permute-start | bytes 110600 | tf_op jit(solution)/shard_map/ppermute | solution.py:256
  6.2 1.3 %fusion.23 = (f32[6,3,3072]{2,1,0:T(4,128)S(1)}, f32[6,3,3072]{2,1,0:T(4,128)S(1)}) fusion(f32[6,16,3072]{2,1,0:T(8,128)} %state_ref.3), kind=kLoop, calls=%fused_computation.71 | loop fusion | bytes 884736 | tf_op jit(solution)/shard_map/slice | solution.py:397
  7.7 3.1 %collective-permute-start.2 = (f32[7,3,3072]{2,1,0:T(4,128)S(1)}, f32[7,3,3072]{2,1,0:T(4,128)S(1)}, u32[]{:S(2)}, u32[]{:S(2)}) collective-permute-start(f32[7,3,3072]{2,1,0:T(4,128)S(1)} %select_maximum_fusion.1), channel_id=1, source_target_pairs={{0,16},{16,32},{32,48},{48,64},{64,80},{80,96},{96,112},{112,128},... | collective-permute-start | bytes 774152 | tf_op jit(solution)/shard_map/ppermute | solution.py:256
  10.9 2.2 %collective-permute-start.3 = (f32[7,3,3072]{2,1,0:T(4,128)S(1)}, f32[7,3,3072]{2,1,0:T(4,128)S(1)}, u32[]{:S(2)}, u32[]{:S(2)}) collective-permute-start(f32[7,3,3072]{2,1,0:T(4,128)S(1)} %select_maximum_fusion), channel_id=1, source_target_pairs={{16,0},{32,16},{48,32},{64,48},{80,64},{96,80},{112,96},{128,112},... | collective-permute-start | bytes 774152 | tf_op jit(solution)/shard_map/ppermute | solution.py:256
  13.4 0.2 select_reduce_fusion.1
  13.5 0.1 iota_compare_fusion.4
  13.6 0.1 select_reduce_fusion
  13.8 0.1 copy.17
  13.9 0.1 mul.120
  14.0 0.1 tile.8
  14.2 1.1 %fusion = (f32[6,16,32]{2,1,0:T(8,128)S(1)}, f32[6,16,32]{2,1,0:T(8,128)S(1)}, f32[6,16,32]{2,1,0:T(8,128)S(1)}, f32[6,16,32]{2,1,0:T(8,128)S(1)}) fusion(f32[6,16,128]{2,1,0:T(8,128)S(1)} %collective-permute-done.1, f32[6,16,96]{2,1,0:T(8,128)S(1)} %collective-permute-done, pred[]{:T(512)S(6)} %eq.117, pred[]{:T(512)S(6)} %eq.124, f32[6,16,3072]{2,1,0:T(8,128)} %state_ref.3), kind=kLoop, calls=%fused_computation.6 | loop fusion | flops 6144 | bytes 122882 | tf_op jit(solution)/shard_map/jit(_where)/select_n | solution.py:414
  15.3 0.1 pad_maximum_fusion.1
  15.5 9.3 %collective-permute-done.3.xhi_ref = f32[7,3,3072]{2,1,0:T(4,128)S(1)} collective-permute-done((f32[7,3,3072]{2,1,0:T(4,128)S(1)}, f32[7,3,3072]{2,1,0:T(4,128)S(1)}, u32[]{:S(2)}, u32[]{:S(2)}) %collective-permute-start.3) | collective-permute-done | bytes 258080 | tf_op jit(solution)/shard_map/ppermute | solution.py:256
  24.8 0.1 concatenate.66
  25.0 0.8 %fusion.2.geo_ref = f32[40,128]{1,0:T(8,128)} fusion(f32[40,32]{1,0:T(8,128)S(1)} %concatenate.66, s32[128]{0:T(128)S(1)} %and_select_fusion), kind=kOutput, calls=%fused_computation.17 | convolution fusion | flops 1970176 | bytes 26112 | tf_op jit(solution)/shard_map/dot_general | solution.py:376
  25.7 9.1 %shard_map.68.part_ref = f32[6,16,3072]{2,1,0:T(8,128)} custom-call(f32[6,16,3072]{2,1,0:T(8,128)} %state_ref.3, f32[7,3,3072]{2,1,0:T(4,128)} %copy-done.1, f32[7,3,3072]{2,1,0:T(4,128)} %copy-done.2, f32[40,128]{1,0:T(8,128)} %fusion.2.geo_ref), custom_call_target="tpu_custom_call" | custom-call | flops 44236800 | bytes 3538944 | tf_op jit(solution)/shard_map/pallas_call | solution.py:219
  34.9 0.7 %collective-permute-start.5 = (f32[6,16,32]{2,1,0:T(8,128)S(1)}, f32[6,16,32]{2,1,0:T(8,128)S(1)}, u32[]{:S(2)}, u32[]{:S(2)}) collective-permute-start(f32[6,16,32]{2,1,0:T(8,128)S(1)} %get-tuple-element.4), channel_id=1, source_target_pairs={{15,1},{14,2},{0,3},{31,17},{30,18},{16,19},{47,33},{46,34},{32,35... | collective-permute-start | bytes 36872 | tf_op jit(solution)/shard_map/ppermute | solution.py:274
  35.5 0.7 %collective-permute-start.4 = (f32[6,16,32]{2,1,0:T(8,128)S(1)}, f32[6,16,32]{2,1,0:T(8,128)S(1)}, u32[]{:S(2)}, u32[]{:S(2)}) collective-permute-start(f32[6,16,32]{2,1,0:T(8,128)S(1)} %get-tuple-element.4), channel_id=1, source_target_pairs={{15,4},{14,5},{0,6},{31,20},{30,21},{16,22},{47,36},{46,37},{32,38... | collective-permute-start | bytes 36872 | tf_op jit(solution)/shard_map/ppermute | solution.py:274
  36.2 0.1 maximum_bitcast_fusion
  36.3 1.3 %collective-permute-start.6 = (f32[6,16,32]{2,1,0:T(8,128)S(1)}, f32[6,16,32]{2,1,0:T(8,128)S(1)}, u32[]{:S(2)}, u32[]{:S(2)}) collective-permute-start(f32[6,16,32]{2,1,0:T(8,128)S(1)} %select_select_fusion), channel_id=1, source_target_pairs={{15,7},{14,8},{0,9},{1,10},{2,11},{3,12},{4,13},{31,23},{30,24},{1... | collective-permute-start | bytes 36872 | tf_op jit(solution)/shard_map/ppermute | solution.py:274
  37.6 0.7 %pad_maximum_fusion.yhalo_ref = f32[2,6,16,128]{3,2,1,0:T(8,128)} fusion(f32[1,6,16,128]{3,2,1,0:T(8,128)S(1)} %select_bitcast_fusion, f32[1,6,16,128]{3,2,1,0:T(8,128)S(1)} %maximum_bitcast_fusion), kind=kLoop, calls=%fused_computation.4 | loop fusion | flops 24576 | bytes 196608 | tf_op jit(solution)/shard_map/stack | solution.py:432
  38.3 9.6 %collective-permute-done.6 = f32[6,16,32]{2,1,0:T(8,128)S(1)} collective-permute-done((f32[6,16,32]{2,1,0:T(8,128)S(1)}, f32[6,16,32]{2,1,0:T(8,128)S(1)}, u32[]{:S(2)}, u32[]{:S(2)}) %collective-permute-start.6) | collective-permute-done | bytes 12320 | tf_op jit(solution)/shard_map/ppermute | solution.py:274
  47.9 0.7 %multiply_add_fusion = (f32[16,32]{1,0:T(8,128)}, f32[16,32]{1,0:T(8,128)S(1)}, f32[16,32]{1,0:T(8,128)S(1)}, f32[16,32]{1,0:T(8,128)S(1)}) fusion(f32[16,32]{1,0:T(8,128)S(1)} %copy-done, f32[6,16,32]{2,1,0:T(8,128)S(1)} %broadcast_select_fusion, f32[16,2]{1,0:T(8,128)S(1)} %get-tuple-element.19, f32[16,30]{1,0:T(8,128)S(1)} %get-tuple-element.21, ...), kind=kLoop, calls=%fused_computation.52 | loop fusion | flops 29184 | bytes 31488 | tf_op jit(solution)/shard_map/add | solution.py:438
  48.6 0.1 copy.15
  48.8 0.1 copy.13
  48.9 0.1 concatenate.67
  49.0 0.9 %fusion.1.geo_ref = f32[80,128]{1,0:T(8,128)} fusion(f32[80,32]{0,1:T(8,128)S(1)} %concatenate.67, s32[128]{0:T(128)S(1)} %and_select_fusion), kind=kOutput, calls=%fused_computation.16 | convolution fusion | flops 3936256 | bytes 51712 | tf_op jit(solution)/shard_map/dot_general | solution.py:376
  49.8 6.3 %shard_map.69 = f32[6,16,3072]{2,1,0:T(8,128)} custom-call(f32[6,16,3072]{2,1,0:T(8,128)} %state_ref.3, f32[2,6,16,128]{3,2,1,0:T(8,128)} %pad_maximum_fusion.yhalo_ref, f32[80,128]{1,0:T(8,128)} %fusion.1.geo_ref, f32[6,16,3072]{2,1,0:T(8,128)} %shard_map.68.part_ref), custom_call_target="tpu_custom_call", output_to_operand_aliasing={{}: (3, {})} | custom-call | flops 44236800 | bytes 3538944 | tf_op jit(solution)/shard_map/pallas_call | solution.py:238
  (45 shorter events, 0.8 us)
Async XLA Ops:
  0.6 6.9 %copy-start = (f32[16,32]{1,0:T(8,128)S(1)}, f32[16,32]{1,0:T(8,128)}, u32[]{:S(2)}) copy-start(f32[16,32]{1,0:T(8,128)} %param.6) | copy-start | bytes 6148
  2.5 11.7 %collective-permute-start.1 = (f32[6,16,128]{2,1,0:T(8,128)S(1)}, f32[6,16,128]{2,1,0:T(8,128)S(1)}, u32[]{:S(2)}, u32[]{:S(2)}) collective-permute-start(f32[6,16,128]{2,1,0:T(8,128)S(1)} %pad_maximum_fusion.2), channel_id=1, source_target_pairs={{1,0},{2,1},{3,2},{4,3},{5,4},{6,5},{7,6},{8,7},{9,8},{10,9},{11,1... | collective-permute-start | bytes 147464 | tf_op jit(solution)/shard_map/ppermute | solution.py:256
  5.1 8.3 %copy-start.4 = (s32[16]{0:T(128)S(1)}, s32[16]{0:T(128)}, u32[]{:S(2)}) copy-start(s32[16]{0:T(128)} %param.8) | copy-start | bytes 196
  5.1 8.2 %copy-start.5 = (s32[16]{0:T(128)S(1)}, s32[16]{0:T(128)}, u32[]{:S(2)}) copy-start(s32[16]{0:T(128)} %param.7) | copy-start | bytes 196
  5.1 8.5 %copy-start.3 = (f32[16,32]{1,0:T(8,128)S(1)}, f32[16,32]{1,0:T(8,128)}, u32[]{:S(2)}) copy-start(f32[16,32]{1,0:T(8,128)} %param.9) | copy-start | bytes 6148
  5.1 9.0 %collective-permute-start = (f32[6,16,96]{2,1,0:T(8,128)S(1)}, f32[6,16,96]{2,1,0:T(8,128)S(1)}, u32[]{:S(2)}, u32[]{:S(2)}) collective-permute-start(f32[6,16,96]{2,1,0:T(8,128)S(1)} %get-tuple-element.16), channel_id=1, source_target_pairs={{0,1},{1,2},{2,3},{3,4},{4,5},{5,6},{6,7},{7,8},{8,9},{9,10},{10,1... | collective-permute-start | bytes 110600 | tf_op jit(solution)/shard_map/ppermute | solution.py:256
  7.7 17.1 %collective-permute-start.2 = (f32[7,3,3072]{2,1,0:T(4,128)S(1)}, f32[7,3,3072]{2,1,0:T(4,128)S(1)}, u32[]{:S(2)}, u32[]{:S(2)}) collective-permute-start(f32[7,3,3072]{2,1,0:T(4,128)S(1)} %select_maximum_fusion.1), channel_id=1, source_target_pairs={{0,16},{16,32},{32,48},{48,64},{64,80},{80,96},{96,112},{112,128},... | collective-permute-start | bytes 774152 | tf_op jit(solution)/shard_map/ppermute | solution.py:256
  10.9 13.9 %collective-permute-start.3 = (f32[7,3,3072]{2,1,0:T(4,128)S(1)}, f32[7,3,3072]{2,1,0:T(4,128)S(1)}, u32[]{:S(2)}, u32[]{:S(2)}) collective-permute-start(f32[7,3,3072]{2,1,0:T(4,128)S(1)} %select_maximum_fusion), channel_id=1, source_target_pairs={{16,0},{32,16},{48,32},{64,48},{80,64},{96,80},{112,96},{128,112},... | collective-permute-start | bytes 774152 | tf_op jit(solution)/shard_map/ppermute | solution.py:256
  24.8 1.0 %copy-start.2 = (f32[7,3,3072]{2,1,0:T(4,128)}, f32[7,3,3072]{2,1,0:T(4,128)S(1)}, u32[]{:S(2)}) copy-start(f32[7,3,3072]{2,1,0:T(4,128)S(1)} %collective-permute-done.3.xhi_ref) | copy-start | bytes 774148
  24.8 0.9 %copy-start.1 = (f32[7,3,3072]{2,1,0:T(4,128)}, f32[7,3,3072]{2,1,0:T(4,128)S(1)}, u32[]{:S(2)}) copy-start(f32[7,3,3072]{2,1,0:T(4,128)S(1)} %collective-permute-done.2.xlo_ref) | copy-start | bytes 774148
  34.9 1.4 %collective-permute-start.5 = (f32[6,16,32]{2,1,0:T(8,128)S(1)}, f32[6,16,32]{2,1,0:T(8,128)S(1)}, u32[]{:S(2)}, u32[]{:S(2)}) collective-permute-start(f32[6,16,32]{2,1,0:T(8,128)S(1)} %get-tuple-element.4), channel_id=1, source_target_pairs={{15,1},{14,2},{0,3},{31,17},{30,18},{16,19},{47,33},{46,34},{32,35... | collective-permute-start | bytes 36872 | tf_op jit(solution)/shard_map/ppermute | solution.py:274
  35.5 0.8 %collective-permute-start.4 = (f32[6,16,32]{2,1,0:T(8,128)S(1)}, f32[6,16,32]{2,1,0:T(8,128)S(1)}, u32[]{:S(2)}, u32[]{:S(2)}) collective-permute-start(f32[6,16,32]{2,1,0:T(8,128)S(1)} %get-tuple-element.4), channel_id=1, source_target_pairs={{15,4},{14,5},{0,6},{31,20},{30,21},{16,22},{47,36},{46,37},{32,38... | collective-permute-start | bytes 36872 | tf_op jit(solution)/shard_map/ppermute | solution.py:274
  36.3 11.5 %collective-permute-start.6 = (f32[6,16,32]{2,1,0:T(8,128)S(1)}, f32[6,16,32]{2,1,0:T(8,128)S(1)}, u32[]{:S(2)}, u32[]{:S(2)}) collective-permute-start(f32[6,16,32]{2,1,0:T(8,128)S(1)} %select_select_fusion), channel_id=1, source_target_pairs={{15,7},{14,8},{0,9},{1,10},{2,11},{3,12},{4,13},{31,23},{30,24},{1... | collective-permute-start | bytes 36872 | tf_op jit(solution)/shard_map/ppermute | solution.py:274

commit v8 on v6

--- a/solution.py
+++ b/solution.py
@@ -356,12 +356,14 @@
         extra = lax.dynamic_update_slice(extra, heights[None], (0, 0, 0))
         return jnp.concatenate([cols, extra], axis=0)
 
-    from_low = shifted(pack(state[:, columns - HALO :], shock_height[columns - HALO :]), "gx", True)
-    from_high = shifted(pack(state[:, :HALO], shock_height[:HALO]), "gx", False)
-    below = shifted(state[..., length - band :], "gy", True, cyclic=True)
-    above = shifted(
-        jnp.concatenate([state[..., :band], state[..., length - planes :]], axis=2), "gy", False
-    )
+    top_row = broadcast(state[..., length - planes :], "gy", [row_devs - 1], (1, 2, 2, 2, 2))
+    low_cols, high_cols, low_rows, high_rows, top_row = lax.optimization_barrier(
+        (state[:, columns - HALO :], state[:, :HALO], state[..., length - band :], state[..., :band], top_row)
+    )
+    from_low = shifted(pack(low_cols, shock_height[columns - HALO :]), "gx", True)
+    from_high = shifted(pack(high_cols, shock_height[:HALO]), "gx", False)
+    below = shifted(low_rows, "gy", True)
+    above = shifted(high_rows, "gy", False)
 
     low_height = jnp.where(
         col_dev == 0, jnp.broadcast_to(shock_height[:1], (HALO, planes)), from_low[6, :, :planes]
@@ -374,21 +376,19 @@
     height_ext = jnp.concatenate([low_height, shock_height, high_height], axis=0)
     slope_x, slope_z = slopes(height_ext, planes)
 
-    top_seed = jnp.where(
-        row_dev == row_devs - 1,
-        state[..., length - planes :],
-        jnp.where(row_dev == 0, below[..., band - planes :], above[..., band:]),
-    )
-    seeded = sorted({row_devs - 1, 0, max(row_devs - 2, 0)}, reverse=True)
-    top_row = broadcast(top_seed, "gy", seeded, (2, 1, 1, 1, 1))
     shock_rate = shock_speed(top_row, slope_x, slope_z)
 
     blowing = wall_flux(wall_segment, segment_level, blow_table)
     ghost_below = jnp.where(row_dev == 0, wall_ghosts(state[..., :band], blowing, planes), below)
     ghost_above = jnp.where(
-        row_dev == row_devs - 1, jnp.tile(state[..., length - planes :], (1, 1, HALO + 1)), above
-    )
-    yhalo = jnp.stack([jnp.concatenate([ghost_below[..., : PAD - band], ghost_below], axis=2), ghost_above])
+        row_dev == row_devs - 1, jnp.tile(state[..., length - planes :], (1, 1, HALO)), above
+    )
+    yhalo = jnp.stack(
+        [
+            jnp.concatenate([ghost_below[..., : PAD - band], ghost_below], axis=2),
+            jnp.concatenate([ghost_above, ghost_above[..., band - (PAD - band) :]], axis=2),
+        ]
+    )
 
     height = shock_height
     height_x = jnp.concatenate([height_ext, jnp.broadcast_to(height_ext[-1:], (2, planes))], axis=0)

time: 46.6 us -> 61.5 us (1.32)
  waiting for transfers between devices: 8.33 us -> 18.3 us
  starting transfers between devices: 15.4 us -> 18.9 us
  local copies, waits for them, and re-layouts: 4.46 us -> 6.97 us
  other arithmetic: 3.31 us -> 1.67 us
    ppermute x4, waiting for transfers between devices: 0.01 us -> 8.58 us  [shifted(): return lax.ppermute(block, axis, pairs)]
    ppermute x4, starting transfers between devices: 12.7 us -> 14.9 us  [shifted(): return lax.ppermute(block, axis, pairs)]
    unnamed x15, local copies, waits for them, and re-layouts: 0.11 us -> 1.55 us
    ppermute x3 -> x5, waiting for transfers between devices: 8.32 us -> 9.7 us  [broadcast(): received = lax.ppermute(array, axis, pairs)]
    ppermute x3 -> x5, starting transfers between devices: 2.62 us -> 3.96 us  [broadcast(): received = lax.ppermute(array, axis, pairs)]
    select_n x1, other arithmetic: 1.09 us -> 0.01 us  [shards(): jnp.where(row_dev == row_devs - 1, jnp.tile(state[..., length - planes:],...]
    broadcast_in_dim x1, local copies, waits for them, and re-layouts: 0.01 us -> 0.71 us  [pack(): extra = lax.dynamic_update_slice(extra, heights[None], (0, 0, 0))]
    broadcast_in_dim x1, local copies, waits for them, and re-layouts: 0.01 us -> 0.71 us  [shards(): jnp.broadcast_to(shock_height[columns - 1:], (HALO, planes))]
  transfers between devices with their start and end apart: 7 -> 9, of which waited for: 1 -> 3; matrix products, arithmetic and copies ran while one was open for 10% -> 11% of each run, Pallas kernels for 0% -> 0%
where the time goes in v8:
time: 61.5 us; the launch traced here: 60.5 us
  starting transfers between devices  18.9 us (31%)
  waiting for transfers between devices  18.3 us (30%)
  Pallas kernels  12.8 us (21%)
  local copies, waits for them, and re-layouts  6.97 us (11%)
  other arithmetic  1.67 us (3%)
  between operations  1.05 us (2%)
  matrix products  0.88 us (1%)
    ppermute x4, starting transfers between devices, shifted(): return lax.ppermute(block, axis, pairs)  14.9 us
    pallas_call x1, Pallas kernels, update(): pl.pallas_call(kern, out_shape=jax.ShapeDtypeStruct((6, columns, length),...  12.8 us
    ppermute x5, waiting for transfers between devices, broadcast(): received = lax.ppermute(array, axis, pairs)  9.7 us
    ppermute x4, waiting for transfers between devices, shifted(): return lax.ppermute(block, axis, pairs)  8.58 us
    ppermute x5, starting transfers between devices, broadcast(): received = lax.ppermute(array, axis, pairs)  3.96 us
    unnamed x15, local copies, waits for them, and re-layouts  1.55 us
    slice x1, local copies, waits for them, and re-layouts, shards(): state[:, :HALO]  1.35 us
  transfers between devices with their start and end apart: 9, of which 3 were waited for; matrix products, arithmetic and copies ran while one was open for 11% of the time, Pallas kernels for 0%

profile of v8, /device:TPU:113, one launch (start us, length us, event | category | flops | bytes accessed | tf_op | source)
XLA Modules:
  0.0 60.5 jit_solution(14195817384467760830)
XLA Ops:
  0.7 1.0 %fusion.23 = (f32[6,16,32]{2,1,0:T(8,128)S(1)}, f32[6,16,32]{2,1,0:T(8,128)S(1)}, f32[6,16,32]{2,1,0:T(8,128)S(1)}, f32[6,16,32]{2,1,0:T(8,128)S(1)}) fusion(f32[6,16,3072]{2,1,0:T(8,128)} %state_ref.1), kind=kLoop, calls=%fused_computation.70 | loop fusion | bytes 98304 | tf_op jit(solution)/shard_map/slice | solution.py:314
  1.7 0.1 copy.49
  1.8 0.7 %collective-permute-start = (f32[6,16,32]{1,2,0:T(8,128)S(1)}, f32[6,16,32]{1,2,0:T(8,128)S(1)}, u32[]{:S(2)}, u32[]{:S(2)}) collective-permute-start(f32[6,16,32]{1,2,0:T(8,128)S(1)} %copy.49), channel_id=1, source_target_pairs={{15,0},{31,16},{47,32},{63,48},{79,64},{95,80},{111,96},{127,112},... | collective-permute-start | bytes 36872 | tf_op jit(solution)/shard_map/ppermute | solution.py:237
  2.5 0.7 %slice_bitcast_fusion.2 = (f32[1,3,32]{2,1,0:T(4,128)S(1)}, f32[1,3,32]{2,1,0:T(4,128)S(1)}) fusion(f32[16,32]{1,0:T(8,128)} %param.6), kind=kLoop, calls=%fused_computation.64 | loop fusion | bytes 1536 | tf_op jit(solution)/shard_map/broadcast_in_dim | solution.py:356
  3.2 0.8 %copy.44 = f32[16,32]{0,1:T(8,128)S(1)} copy(f32[16,32]{1,0:T(8,128)} %param.6) | data formatting | bytes 4096 | tf_op args[1]
  4.0 0.9 %fusion.24 = (f32[6,16,96]{2,1,0:T(8,128)S(1)}, f32[6,16,96]{2,1,0:T(8,128)S(1)}) fusion(f32[6,16,3072]{2,1,0:T(8,128)} %state_ref.1), kind=kLoop, calls=%fused_computation.71 | loop fusion | bytes 147456 | tf_op jit(solution)/shard_map/slice | solution.py:361
  4.9 1.4 %fusion.25 = (f32[6,3,3072]{2,1,0:T(4,128)S(1)}, f32[6,3,3072]{2,1,0:T(4,128)S(1)}) fusion(f32[6,16,3072]{2,1,0:T(8,128)} %state_ref.1), kind=kLoop, calls=%fused_computation.72 | loop fusion | bytes 884736 | tf_op jit(solution)/shard_map/slice | solution.py:361
  6.3 0.2 select_reduce_fusion.1
  6.5 0.1 select_reduce_fusion
  6.8 0.1 pad_maximum_fusion.1
  6.9 0.7 %slice_bitcast_fusion.5 = (f32[32]{0:T(128)S(1)}, f32[32]{0:T(128)S(1)}) fusion(f32[16,32]{1,0:T(8,128)} %param.6), kind=kLoop, calls=%fused_computation.68 | loop fusion | bytes 512 | tf_op jit(solution)/shard_map/broadcast_in_dim | solution.py:373
  7.7 0.7 %collective-permute-start.2 = (f32[6,16,32]{1,2,0:T(8,128)S(1)}, f32[6,16,32]{1,2,0:T(8,128)S(1)}, u32[]{:S(2)}, u32[]{:S(2)}) collective-permute-start(f32[6,16,32]{1,2,0:T(8,128)S(1)} %broadcast_select_fusion), channel_id=1, source_target_pairs={{15,1},{0,2},{31,17},{16,18},{47,33},{32,34},{63,49},{48,50},{79,6... | collective-permute-start | bytes 36872 | tf_op jit(solution)/shard_map/ppermute | solution.py:237
  8.3 0.7 %collective-permute-start.1 = (f32[6,16,32]{1,2,0:T(8,128)S(1)}, f32[6,16,32]{1,2,0:T(8,128)S(1)}, u32[]{:S(2)}, u32[]{:S(2)}) collective-permute-start(f32[6,16,32]{1,2,0:T(8,128)S(1)} %broadcast_select_fusion), channel_id=1, source_target_pairs={{15,3},{0,4},{31,19},{16,20},{47,35},{32,36},{63,51},{48,52},{79,6... | collective-permute-start | bytes 36872 | tf_op jit(solution)/shard_map/ppermute | solution.py:237
  9.1 1.3 %collective-permute-start.4 = (f32[6,16,32]{1,2,0:T(8,128)S(1)}, f32[6,16,32]{1,2,0:T(8,128)S(1)}, u32[]{:S(2)}, u32[]{:S(2)}) collective-permute-start(f32[6,16,32]{1,2,0:T(8,128)S(1)} %select_select_fusion.1), channel_id=1, source_target_pairs={{15,5},{0,6},{1,7},{2,8},{3,9},{4,10},{31,21},{16,22},{17,23},{18,... | collective-permute-start | bytes 36872 | tf_op jit(solution)/shard_map/ppermute | solution.py:237
  10.4 0.7 %collective-permute-start.3 = (f32[6,16,32]{1,2,0:T(8,128)S(1)}, f32[6,16,32]{1,2,0:T(8,128)S(1)}, u32[]{:S(2)}, u32[]{:S(2)}) collective-permute-start(f32[6,16,32]{1,2,0:T(8,128)S(1)} %select_select_fusion.1), channel_id=1, source_target_pairs={{15,11},{0,12},{1,13},{2,14},{31,27},{16,28},{17,29},{18,30},{47,4... | collective-permute-start | bytes 36872 | tf_op jit(solution)/shard_map/ppermute | solution.py:237
  11.1 0.1 tile.8
  11.3 9.7 %collective-permute-done.4 = f32[6,16,32]{1,2,0:T(8,128)S(1)} collective-permute-done((f32[6,16,32]{1,2,0:T(8,128)S(1)}, f32[6,16,32]{1,2,0:T(8,128)S(1)}, u32[]{:S(2)}, u32[]{:S(2)}) %collective-permute-start.4) | collective-permute-done | bytes 12320 | tf_op jit(solution)/shard_map/ppermute | solution.py:237
  21.0 6.8 %collective-permute-start.7 = (f32[6,16,96]{2,1,0:T(8,128)S(1)}, f32[6,16,96]{2,1,0:T(8,128)S(1)}, u32[]{:S(2)}, u32[]{:S(2)}) collective-permute-start(f32[6,16,96]{2,1,0:T(8,128)S(1)} %get-tuple-element.9), channel_id=1, source_target_pairs={{0,1},{1,2},{2,3},{3,4},{4,5},{5,6},{6,7},{7,8},{8,9},{9,10},{10,1... | collective-permute-start | bytes 110600 | tf_op jit(solution)/shard_map/ppermute | solution.py:219
  27.8 1.9 %collective-permute-start.8 = (f32[6,16,96]{2,1,0:T(8,128)S(1)}, f32[6,16,96]{2,1,0:T(8,128)S(1)}, u32[]{:S(2)}, u32[]{:S(2)}) collective-permute-start(f32[6,16,96]{2,1,0:T(8,128)S(1)} %get-tuple-element.10), channel_id=1, source_target_pairs={{1,0},{2,1},{3,2},{4,3},{5,4},{6,5},{7,6},{8,7},{9,8},{10,9},{11,1... | collective-permute-start | bytes 110600 | tf_op jit(solution)/shard_map/ppermute | solution.py:219
  29.8 4.3 %collective-permute-start.6 = (f32[7,3,3072]{2,1,0:T(4,128)S(1)}, f32[7,3,3072]{2,1,0:T(4,128)S(1)}, u32[]{:S(2)}, u32[]{:S(2)}) collective-permute-start(f32[7,3,3072]{2,1,0:T(4,128)S(1)} %select_maximum_fusion), channel_id=1, source_target_pairs={{16,0},{32,16},{48,32},{64,48},{80,64},{96,80},{112,96},{128,112},... | collective-permute-start | bytes 774152 | tf_op jit(solution)/shard_map/ppermute | solution.py:219
  34.2 1.9 %collective-permute-start.5 = (f32[7,3,3072]{2,1,0:T(4,128)S(1)}, f32[7,3,3072]{2,1,0:T(4,128)S(1)}, u32[]{:S(2)}, u32[]{:S(2)}) collective-permute-start(f32[7,3,3072]{2,1,0:T(4,128)S(1)} %select_maximum_fusion.1), channel_id=1, source_target_pairs={{0,16},{16,32},{32,48},{48,64},{64,80},{80,96},{96,112},{112,128},... | collective-permute-start | bytes 774152 | tf_op jit(solution)/shard_map/ppermute | solution.py:219
  36.3 0.1 maximum_bitcast_fusion.1
  36.4 0.6 %pad_maximum_fusion.yhalo_ref = f32[2,6,16,128]{3,2,1,0:T(8,128)} fusion(f32[1,6,16,128]{3,2,1,0:T(8,128)S(1)} %maximum_bitcast_fusion.1, f32[1,6,16,128]{3,2,1,0:T(8,128)S(1)} %maximum_bitcast_fusion), kind=kLoop, calls=%fused_computation.4 | loop fusion | flops 24576 | bytes 196608 | tf_op jit(solution)/shard_map/stack | solution.py:386
  37.1 2.4 %collective-permute-done.6.xhi_ref = f32[7,3,3072]{2,1,0:T(4,128)S(1)} collective-permute-done((f32[7,3,3072]{2,1,0:T(4,128)S(1)}, f32[7,3,3072]{2,1,0:T(4,128)S(1)}, u32[]{:S(2)}, u32[]{:S(2)}) %collective-permute-start.6) | collective-permute-done | bytes 258080 | tf_op jit(solution)/shard_map/ppermute | solution.py:219
  39.4 0.1 copy.45
  39.5 6.2 %collective-permute-done.5.xlo_ref = f32[7,3,3072]{2,1,0:T(4,128)S(1)} collective-permute-done((f32[7,3,3072]{2,1,0:T(4,128)S(1)}, f32[7,3,3072]{2,1,0:T(4,128)S(1)}, u32[]{:S(2)}, u32[]{:S(2)}) %collective-permute-start.5) | collective-permute-done | bytes 258080 | tf_op jit(solution)/shard_map/ppermute | solution.py:219
  45.7 0.1 copy.43
  45.8 0.1 multiply_add_fusion
  46.0 0.7 %copy.48 = f32[16,32]{1,0:T(8,128)} copy(f32[16,32]{0,1:T(8,128)S(1)} %get-tuple-element.16) | data formatting | bytes 4096
  46.7 0.1 concatenate.63
  46.8 0.9 %fusion.15.geo_ref = f32[104,128]{1,0:T(8,128)} fusion(f32[104,32]{0,1:T(8,128)S(1)} %concatenate.63, s32[128]{0:T(128)S(1)} %and_select_fusion), kind=kOutput, calls=%fused_computation.47 | convolution fusion | flops 5115904 | bytes 67072 | tf_op jit(solution)/shard_map/dot_general | solution.py:339
  47.7 12.8 %shard_map.68 = f32[6,16,3072]{2,1,0:T(8,128)} custom-call(f32[6,16,3072]{2,1,0:T(8,128)} %state_ref.1, f32[7,3,3072]{2,1,0:T(4,128)} %copy-done.1, f32[7,3,3072]{2,1,0:T(4,128)} %copy-done, f32[2,6,16,128]{3,2,1,0:T(8,128)} %pad_maximum_fusion.yhalo_ref, f32[104,128]{1,0:T(8,128)} %fusion.15.geo_ref), custom_call_target="tpu_custom_call" | custom-call | tf_op jit(solution)/shard_map/pallas_call | solution.py:198
  (45 shorter events, 0.7 us)
Async XLA Ops:
  0.6 5.6 %copy-start.3 = (s32[16]{0:T(128)S(1)}, s32[16]{0:T(128)}, u32[]{:S(2)}) copy-start(s32[16]{0:T(128)} %param.8) | copy-start | bytes 196
  0.6 5.6 %copy-start.4 = (s32[16]{0:T(128)S(1)}, s32[16]{0:T(128)}, u32[]{:S(2)}) copy-start(s32[16]{0:T(128)} %param.7) | copy-start | bytes 196
  0.7 5.9 %copy-start.2 = (f32[16,32]{1,0:T(8,128)S(1)}, f32[16,32]{1,0:T(8,128)}, u32[]{:S(2)}) copy-start(f32[16,32]{1,0:T(8,128)} %param.9) | copy-start | bytes 6148
  1.8 5.8 %collective-permute-start = (f32[6,16,32]{1,2,0:T(8,128)S(1)}, f32[6,16,32]{1,2,0:T(8,128)S(1)}, u32[]{:S(2)}, u32[]{:S(2)}) collective-permute-start(f32[6,16,32]{1,2,0:T(8,128)S(1)} %copy.49), channel_id=1, source_target_pairs={{15,0},{31,16},{47,32},{63,48},{79,64},{95,80},{111,96},{127,112},... | collective-permute-start | bytes 36872 | tf_op jit(solution)/shard_map/ppermute | solution.py:237
  7.7 1.4 %collective-permute-start.2 = (f32[6,16,32]{1,2,0:T(8,128)S(1)}, f32[6,16,32]{1,2,0:T(8,128)S(1)}, u32[]{:S(2)}, u32[]{:S(2)}) collective-permute-start(f32[6,16,32]{1,2,0:T(8,128)S(1)} %broadcast_select_fusion), channel_id=1, source_target_pairs={{15,1},{0,2},{31,17},{16,18},{47,33},{32,34},{63,49},{48,50},{79,6... | collective-permute-start | bytes 36872 | tf_op jit(solution)/shard_map/ppermute | solution.py:237
  8.3 0.7 %collective-permute-start.1 = (f32[6,16,32]{1,2,0:T(8,128)S(1)}, f32[6,16,32]{1,2,0:T(8,128)S(1)}, u32[]{:S(2)}, u32[]{:S(2)}) collective-permute-start(f32[6,16,32]{1,2,0:T(8,128)S(1)} %broadcast_select_fusion), channel_id=1, source_target_pairs={{15,3},{0,4},{31,19},{16,20},{47,35},{32,36},{63,51},{48,52},{79,6... | collective-permute-start | bytes 36872 | tf_op jit(solution)/shard_map/ppermute | solution.py:237
  9.1 11.9 %collective-permute-start.4 = (f32[6,16,32]{1,2,0:T(8,128)S(1)}, f32[6,16,32]{1,2,0:T(8,128)S(1)}, u32[]{:S(2)}, u32[]{:S(2)}) collective-permute-start(f32[6,16,32]{1,2,0:T(8,128)S(1)} %select_select_fusion.1), channel_id=1, source_target_pairs={{15,5},{0,6},{1,7},{2,8},{3,9},{4,10},{31,21},{16,22},{17,23},{18,... | collective-permute-start | bytes 36872 | tf_op jit(solution)/shard_map/ppermute | solution.py:237
  10.4 10.6 %collective-permute-start.3 = (f32[6,16,32]{1,2,0:T(8,128)S(1)}, f32[6,16,32]{1,2,0:T(8,128)S(1)}, u32[]{:S(2)}, u32[]{:S(2)}) collective-permute-start(f32[6,16,32]{1,2,0:T(8,128)S(1)} %select_select_fusion.1), channel_id=1, source_target_pairs={{15,11},{0,12},{1,13},{2,14},{31,27},{16,28},{17,29},{18,30},{47,4... | collective-permute-start | bytes 36872 | tf_op jit(solution)/shard_map/ppermute | solution.py:237
  21.0 15.1 %collective-permute-start.7 = (f32[6,16,96]{2,1,0:T(8,128)S(1)}, f32[6,16,96]{2,1,0:T(8,128)S(1)}, u32[]{:S(2)}, u32[]{:S(2)}) collective-permute-start(f32[6,16,96]{2,1,0:T(8,128)S(1)} %get-tuple-element.9), channel_id=1, source_target_pairs={{0,1},{1,2},{2,3},{3,4},{4,5},{5,6},{6,7},{7,8},{8,9},{9,10},{10,1... | collective-permute-start | bytes 110600 | tf_op jit(solution)/shard_map/ppermute | solution.py:219
  27.8 8.3 %collective-permute-start.8 = (f32[6,16,96]{2,1,0:T(8,128)S(1)}, f32[6,16,96]{2,1,0:T(8,128)S(1)}, u32[]{:S(2)}, u32[]{:S(2)}) collective-permute-start(f32[6,16,96]{2,1,0:T(8,128)S(1)} %get-tuple-element.10), channel_id=1, source_target_pairs={{1,0},{2,1},{3,2},{4,3},{5,4},{6,5},{7,6},{8,7},{9,8},{10,9},{11,1... | collective-permute-start | bytes 110600 | tf_op jit(solution)/shard_map/ppermute | solution.py:219
  29.8 9.6 %collective-permute-start.6 = (f32[7,3,3072]{2,1,0:T(4,128)S(1)}, f32[7,3,3072]{2,1,0:T(4,128)S(1)}, u32[]{:S(2)}, u32[]{:S(2)}) collective-permute-start(f32[7,3,3072]{2,1,0:T(4,128)S(1)} %select_maximum_fusion), channel_id=1, source_target_pairs={{16,0},{32,16},{48,32},{64,48},{80,64},{96,80},{112,96},{128,112},... | collective-permute-start | bytes 774152 | tf_op jit(solution)/shard_map/ppermute | solution.py:219
  34.2 11.6 %collective-permute-start.5 = (f32[7,3,3072]{2,1,0:T(4,128)S(1)}, f32[7,3,3072]{2,1,0:T(4,128)S(1)}, u32[]{:S(2)}, u32[]{:S(2)}) collective-permute-start(f32[7,3,3072]{2,1,0:T(4,128)S(1)} %select_maximum_fusion.1), channel_id=1, source_target_pairs={{0,16},{16,32},{32,48},{48,64},{64,80},{80,96},{96,112},{112,128},... | collective-permute-start | bytes 774152 | tf_op jit(solution)/shard_map/ppermute | solution.py:219
  39.4 8.3 %copy-start = (f32[7,3,3072]{2,1,0:T(4,128)}, f32[7,3,3072]{2,1,0:T(4,128)S(1)}, u32[]{:S(2)}) copy-start(f32[7,3,3072]{2,1,0:T(4,128)S(1)} %collective-permute-done.6.xhi_ref) | copy-start | bytes 774148
  45.7 2.0 %copy-start.1 = (f32[7,3,3072]{2,1,0:T(4,128)}, f32[7,3,3072]{2,1,0:T(4,128)S(1)}, u32[]{:S(2)}) copy-start(f32[7,3,3072]{2,1,0:T(4,128)S(1)} %collective-permute-done.5.xlo_ref) | copy-start | bytes 774148

commit v9 on v5

--- a/solution.py
+++ b/solution.py
@@ -18,9 +18,9 @@
 FREE_MACH = 6.0
 COURANT = 0.05
 
-PLUS_WEIGHTS = (-2.0, 15.0, -60.0, 20.0, 30.0, -3.0, 0.0)
-MINUS_WEIGHTS = (0.0, 3.0, -30.0, -20.0, 60.0, -15.0, 2.0)
-CHUNK = 256
+FLUX_WEIGHTS = (45.0, -9.0, 1.0)
+SPEED_WEIGHTS = (20.0, -15.0, 6.0, -1.0)
+CHUNK = 512
 PAD = 128
 HALO = 3
 XPAD = 8
@@ -37,14 +37,14 @@
     return inverse, vel_x, vel_y, vel_z, stress, sound
 
 
-def combined(plus, minus, t):
-    a = PLUS_WEIGHTS[t + 3]
-    b = MINUS_WEIGHTS[t + 3]
-    if a == 0.0:
-        return b * minus
-    if b == 0.0:
-        return a * plus
-    return a * plus + b * minus
+def pair_terms(flux, damped, t):
+    odd = FLUX_WEIGHTS[t - 1]
+    even = SPEED_WEIGHTS[t]
+    odd_part = flux if odd == 1.0 else odd * flux
+    if even == -1.0:
+        return odd_part - damped, -(odd_part + damped)
+    even_part = even * damped
+    return even_part + odd_part, even_part - odd_part
 
 
 def lane_tile(values, width):
@@ -63,7 +63,7 @@
     xrows = columns + 2 * XPAD
 
     def kernel(state_ref, xlo_ref, xhi_ref, yhalo_ref, geo_ref,
-               out_ref, qx_ref, qy_ref, px_ref, mx_ref):
+               out_ref, qx_ref, qy_ref, pair_ref):
         col_dev = lax.axis_index("gx")
         first_row = lax.axis_index("gy") * (length // planes)
         for c in range(6):
@@ -109,23 +109,18 @@
             fluxes = [xa[1], xa[1] * vel_x + stress, xa[2] * vel_x, xa[3] * vel_x,
                       (xa[4] + stress) * vel_x, xa[5] * vel_x]
             speed = (jnp.abs(vel_x) + sound) * metric
-            for c in range(6):
-                f = fluxes[c] * metric
-                px_ref[c] = 0.5 * (f + speed * xa[c])
-                mx_ref[c] = 0.5 * (f - speed * xa[c])
             div = []
             for c in range(6):
-                acc = None
-                for t in range(-3, 4):
-                    term = None
-                    a = PLUS_WEIGHTS[t + 3]
-                    b = MINUS_WEIGHTS[t + 3]
-                    if a != 0.0:
-                        term = a * px_ref[c, pl.ds(XPAD + t, columns), :]
-                    if b != 0.0:
-                        mterm = b * mx_ref[c, pl.ds(XPAD + t, columns), :]
-                        term = mterm if term is None else term + mterm
-                    acc = term if acc is None else acc + term
+                flux = fluxes[c] * metric
+                damped = speed * xa[c]
+                for t in range(1, 4):
+                    up, down = pair_terms(flux, damped, t)
+                    pair_ref[c, 2 * t - 2] = up
+                    pair_ref[c, 2 * t - 1] = down
+                acc = SPEED_WEIGHTS[0] * damped[XPAD:XPAD + columns]
+                for t in range(1, 4):
+                    acc = acc + pair_ref[c, 2 * t - 2, pl.ds(XPAD + t, columns), :]
+                    acc = acc + pair_ref[c, 2 * t - 1, pl.ds(XPAD - t, columns), :]
                 div.append(acc)
             ya = [qy_ref[c, :, pl.ds(o, width)] for c in range(6)]
             inverse, vel_x, vel_y, vel_z, stress, sound = kernel_primitives(ya)
@@ -140,14 +135,11 @@
             speed = jnp.abs(contra) + sound * jnp.sqrt(
                 metric_x * metric_x + face_area * face_area + metric_z * metric_z)
             for c in range(6):
-                plus = 0.5 * (fluxes[c] + speed * ya[c])
-                minus = 0.5 * (fluxes[c] - speed * ya[c])
-                acc = None
-                for t in range(-3, 4):
-                    term = combined(plus, minus, t)
-                    if t != 0:
-                        term = pltpu.roll(term, (-planes * t) % width, 1)
-                    acc = term if acc is None else acc + term
+                damped = speed * ya[c]
+                acc = SPEED_WEIGHTS[0] * damped
+                for t in range(1, 4):
+                    up, down = pair_terms(fluxes[c], damped, t)
+                    acc = acc + pltpu.roll(up, (-planes * t) % width, 1) + pltpu.roll(down, planes * t, 1)
                 div[c] = div[c] + acc[:, PAD:PAD + CHUNK]
             q = [v[:, PAD:PAD + CHUNK] for v in ya]
             inverse = inverse[:, PAD:PAD + CHUNK]
@@ -159,28 +151,24 @@
                       (q[4] + stress) * vel_z, q[5] * vel_z]
             speed = (jnp.abs(vel_z) + sound) * metric
             for c in range(6):
-                f = fluxes[c] * metric
-                plus = 0.5 * (f + speed * q[c])
-                minus = 0.5 * (f - speed * q[c])
-                acc = None
-                for t in range(-3, 4):
-                    term = combined(plus, minus, t)
-                    if t > 0:
-                        term = jnp.where(lane < planes - t, pltpu.roll(term, CHUNK - t, 1),
-                                         pltpu.roll(term, planes - t, 1))
-                    elif t < 0:
-                        term = jnp.where(lane >= -t, pltpu.roll(term, -t, 1),
-                                         pltpu.roll(term, (CHUNK - planes - t) % CHUNK, 1))
-                    acc = term if acc is None else acc + term
+                damped = speed * q[c]
+                acc = SPEED_WEIGHTS[0] * damped
+                for t in range(1, 4):
+                    up, down = pair_terms(fluxes[c] * metric, damped, t)
+                    up = jnp.where(lane < planes - t, pltpu.roll(up, CHUNK - t, 1),
+                                   pltpu.roll(up, planes - t, 1))
+                    down = jnp.where(lane >= t, pltpu.roll(down, t, 1),
+                                     pltpu.roll(down, CHUNK - planes + t, 1))
+                    acc = acc + up + down
                 div[c] = div[c] + acc
             kelvin = stress * inverse
             balanced = CHARACTER_KELVIN / (jnp.exp(CHARACTER_KELVIN / kelvin) - 1.0)
             teller = stress / (LANDAU_TELLER * jnp.exp(
                 WHITE_LAW_FACTOR * jnp.exp(-jnp.log(kelvin) / 3.0)))
             source = q[0] * (balanced - q[5] * inverse) * teller
-            volume = face_area * height * spacing
-            for c in range(6):
-                change = -(div[c] * (1.0 / 60.0)) / volume - q[c] * ratio
+            scale = 1.0 / (60.0 * (face_area * height * spacing))
+            for c in range(6):
+                change = -(div[c] * scale) - q[c] * ratio
                 if c == 5:
                     change = change + source
                 out_ref[c, :, pl.ds(o, CHUNK)] = q[c] + dt * change
@@ -204,8 +192,7 @@
         scratch_shapes=[
             pltpu.VMEM((6, columns + 2 * XPAD, length), jnp.float32),
             pltpu.VMEM((6, columns, length + 2 * PAD), jnp.float32),
-            pltpu.VMEM((6, columns + 2 * XPAD, CHUNK), jnp.float32),
-            pltpu.VMEM((6, columns + 2 * XPAD, CHUNK), jnp.float32),
+            pltpu.VMEM((6, 6, columns + 2 * XPAD, CHUNK), jnp.float32),
         ],
     )(state, xlo, xhi, yhalo, geo)
 
@@ -392,7 +379,6 @@
     yhalo = jnp.stack([jnp.concatenate([ghost_below[..., : PAD - band], ghost_below], axis=2), ghost_above])
 
     height = shock_height
-    xrows = columns + 2 * XPAD
     height_x = jnp.concatenate(
         [
             jnp.broadcast_to(height_ext[:1], (XPAD - HALO, planes)),

time: 47.4 us -> 46 us (0.970)
  Pallas kernels: 13.5 us -> 12.1 us
    pallas_call x1, Pallas kernels: 13.5 us -> 12.1 us  [update(): pl.pallas_call(kern, out_shape=jax.ShapeDtypeStruct((6, columns, length),...]
where the time goes in v9:
time: 46 us; the launch traced here: 45.5 us
  starting transfers between devices  15.4 us (33%)
  Pallas kernels  12.1 us (26%)
  waiting for transfers between devices  8.33 us (18%)
  local copies, waits for them, and re-layouts  4.53 us (10%)
  other arithmetic  3.31 us (7%)
  between operations  1.01 us (2%)
  matrix products  0.88 us (2%)
    ppermute x4, starting transfers between devices, shifted(): return lax.ppermute(block, axis, pairs)  12.7 us
    pallas_call x1, Pallas kernels, update(): pl.pallas_call(kern, out_shape=jax.ShapeDtypeStruct((6, columns, length),...  12.1 us
    ppermute x3, waiting for transfers between devices, broadcast(): received = lax.ppermute(array, axis, pairs)  8.32 us
    ppermute x3, starting transfers between devices, broadcast(): received = lax.ppermute(array, axis, pairs)  2.62 us
    slice x1, local copies, waits for them, and re-layouts, shards(): from_high = shifted(pack(state[:, :HALO], shock_height[:HALO]), 'gx', False)  1.35 us
    select_n x1, other arithmetic, shards(): jnp.where(row_dev == row_devs - 1, state[..., length - planes:], jnp.wher...  1.09 us
  transfers between devices with their start and end apart: 7, of which 1 were waited for; matrix products, arithmetic and copies ran while one was open for 10% of the time, Pallas kernels for 0%

profile of v9, /device:TPU:113, one launch (start us, length us, event | category | flops | bytes accessed | tf_op | source)
XLA Modules:
  0.0 45.5 jit_solution(2228607655220124565)
XLA Ops:
  0.6 0.9 %slice.185 = f32[6,16,32]{2,1,0:T(8,128)S(1)} slice(f32[6,16,3072]{2,1,0:T(8,128)} %state_ref.1), slice={[0:6], [0:16], [3040:3072]} | slice | bytes 24576 | tf_op jit(solution)/shard_map/slice | solution.py:377
  1.5 0.9 %fusion.21 = (f32[6,16,96]{2,1,0:T(8,128)S(1)}, f32[6,16,96]{2,1,0:T(8,128)S(1)}) fusion(f32[6,16,3072]{2,1,0:T(8,128)} %state_ref.1), kind=kLoop, calls=%fused_computation.70 | loop fusion | bytes 147456 | tf_op jit(solution)/shard_map/slice | solution.py:349
  2.4 0.1 pad_maximum_fusion.2
  2.5 2.6 %collective-permute-start.3 = (f32[6,16,128]{2,1,0:T(8,128)S(1)}, f32[6,16,128]{2,1,0:T(8,128)S(1)}, u32[]{:S(2)}, u32[]{:S(2)}) collective-permute-start(f32[6,16,128]{2,1,0:T(8,128)S(1)} %pad_maximum_fusion.2), channel_id=1, source_target_pairs={{1,0},{2,1},{3,2},{4,3},{5,4},{6,5},{7,6},{8,7},{9,8},{10,9},{11,1... | collective-permute-start | bytes 147464 | tf_op jit(solution)/shard_map/ppermute | solution.py:207
  5.1 2.8 %collective-permute-start.2 = (f32[6,16,96]{2,1,0:T(8,128)S(1)}, f32[6,16,96]{2,1,0:T(8,128)S(1)}, u32[]{:S(2)}, u32[]{:S(2)}) collective-permute-start(f32[6,16,96]{2,1,0:T(8,128)S(1)} %get-tuple-element.10), channel_id=1, source_target_pairs={{0,1},{1,2},{2,3},{3,4},{4,5},{5,6},{6,7},{7,8},{8,9},{9,10},{10,1... | collective-permute-start | bytes 110600 | tf_op jit(solution)/shard_map/ppermute | solution.py:207
  7.9 1.3 %fusion.22 = (f32[6,3,3072]{2,1,0:T(4,128)S(1)}, f32[6,3,3072]{2,1,0:T(4,128)S(1)}) fusion(f32[6,16,3072]{2,1,0:T(8,128)} %state_ref.1), kind=kLoop, calls=%fused_computation.71 | loop fusion | bytes 884736 | tf_op jit(solution)/shard_map/slice | solution.py:348
  9.3 3.1 %collective-permute-start = (f32[7,3,3072]{2,1,0:T(4,128)S(1)}, f32[7,3,3072]{2,1,0:T(4,128)S(1)}, u32[]{:S(2)}, u32[]{:S(2)}) collective-permute-start(f32[7,3,3072]{2,1,0:T(4,128)S(1)} %select_maximum_fusion.1), channel_id=1, source_target_pairs={{0,16},{16,32},{32,48},{48,64},{64,80},{80,96},{96,112},{112,128},... | collective-permute-start | bytes 774152 | tf_op jit(solution)/shard_map/ppermute | solution.py:207
  12.6 4.3 %collective-permute-start.1 = (f32[7,3,3072]{2,1,0:T(4,128)S(1)}, f32[7,3,3072]{2,1,0:T(4,128)S(1)}, u32[]{:S(2)}, u32[]{:S(2)}) collective-permute-start(f32[7,3,3072]{2,1,0:T(4,128)S(1)} %select_maximum_fusion), channel_id=1, source_target_pairs={{16,0},{32,16},{48,32},{64,48},{80,64},{96,80},{112,96},{128,112},... | collective-permute-start | bytes 774152 | tf_op jit(solution)/shard_map/ppermute | solution.py:207
  17.1 0.2 select_reduce_fusion.1
  17.3 0.1 iota_compare_fusion.3
  17.4 0.1 select_reduce_fusion
  17.6 0.1 copy.16
  17.7 0.1 mul.120
  17.8 0.1 tile.8
  18.0 1.1 %fusion = (f32[6,16,32]{2,1,0:T(8,128)S(1)}, f32[6,16,32]{2,1,0:T(8,128)S(1)}, f32[6,16,32]{2,1,0:T(8,128)S(1)}, f32[6,16,32]{2,1,0:T(8,128)S(1)}) fusion(f32[6,16,128]{2,1,0:T(8,128)S(1)} %collective-permute-done.3, f32[6,16,96]{2,1,0:T(8,128)S(1)} %collective-permute-done.2, pred[]{:T(512)S(6)} %eq.103, pred[]{:T(512)S(6)} %eq.110, f32[6,16,3072]{2,1,0:T(8,128)} %state_ref.1), kind=kLoop, calls=%fused_computation.6 | loop fusion | flops 6144 | bytes 122882 | tf_op jit(solution)/shard_map/jit(_where)/select_n | solution.py:365
  19.1 0.7 %collective-permute-start.5 = (f32[6,16,32]{2,1,0:T(8,128)S(1)}, f32[6,16,32]{2,1,0:T(8,128)S(1)}, u32[]{:S(2)}, u32[]{:S(2)}) collective-permute-start(f32[6,16,32]{2,1,0:T(8,128)S(1)} %get-tuple-element.6), channel_id=1, source_target_pairs={{15,1},{14,2},{0,3},{31,17},{30,18},{16,19},{47,33},{46,34},{32,35... | collective-permute-start | bytes 36872 | tf_op jit(solution)/shard_map/ppermute | solution.py:225
  19.7 0.7 %collective-permute-start.4 = (f32[6,16,32]{2,1,0:T(8,128)S(1)}, f32[6,16,32]{2,1,0:T(8,128)S(1)}, u32[]{:S(2)}, u32[]{:S(2)}) collective-permute-start(f32[6,16,32]{2,1,0:T(8,128)S(1)} %get-tuple-element.6), channel_id=1, source_target_pairs={{15,4},{14,5},{0,6},{31,20},{30,21},{16,22},{47,36},{46,37},{32,38... | collective-permute-start | bytes 36872 | tf_op jit(solution)/shard_map/ppermute | solution.py:225
  20.4 0.1 pad_maximum_fusion.1
  20.6 0.1 maximum_bitcast_fusion
  20.7 1.3 %collective-permute-start.6 = (f32[6,16,32]{2,1,0:T(8,128)S(1)}, f32[6,16,32]{2,1,0:T(8,128)S(1)}, u32[]{:S(2)}, u32[]{:S(2)}) collective-permute-start(f32[6,16,32]{2,1,0:T(8,128)S(1)} %select_select_fusion), channel_id=1, source_target_pairs={{15,7},{14,8},{0,9},{1,10},{2,11},{3,12},{4,13},{31,23},{30,24},{1... | collective-permute-start | bytes 36872 | tf_op jit(solution)/shard_map/ppermute | solution.py:225
  22.0 0.6 %pad_maximum_fusion.yhalo_ref = f32[2,6,16,128]{3,2,1,0:T(8,128)} fusion(f32[1,6,16,128]{3,2,1,0:T(8,128)S(1)} %select_bitcast_fusion, f32[1,6,16,128]{3,2,1,0:T(8,128)S(1)} %maximum_bitcast_fusion), kind=kLoop, calls=%fused_computation.4 | loop fusion | flops 24576 | bytes 196608 | tf_op jit(solution)/shard_map/stack | solution.py:379
  22.7 8.3 %collective-permute-done.6 = f32[6,16,32]{2,1,0:T(8,128)S(1)} collective-permute-done((f32[6,16,32]{2,1,0:T(8,128)S(1)}, f32[6,16,32]{2,1,0:T(8,128)S(1)}, u32[]{:S(2)}, u32[]{:S(2)}) %collective-permute-start.6) | collective-permute-done | bytes 12320 | tf_op jit(solution)/shard_map/ppermute | solution.py:225
  31.0 0.1 copy.15
  31.2 0.7 %multiply_add_fusion = (f32[16,32]{1,0:T(8,128)}, f32[16,32]{1,0:T(8,128)S(1)}, f32[16,32]{1,0:T(8,128)S(1)}, f32[16,32]{1,0:T(8,128)S(1)}) fusion(f32[16,32]{1,0:T(8,128)S(1)} %copy-done, f32[6,16,32]{2,1,0:T(8,128)S(1)} %broadcast_select_fusion, f32[16,2]{1,0:T(8,128)S(1)} %get-tuple-element.15, f32[16,30]{1,0:T(8,128)S(1)} %get-tuple-element.17, ...), kind=kLoop, calls=%fused_computation.51 | loop fusion | flops 29184 | bytes 31488 | tf_op jit(solution)/shard_map/add | solution.py:404
  31.9 0.1 copy.20
  32.0 0.1 copy.17
  32.0 0.1 copy.21
  32.1 0.1 copy.19
  32.2 0.1 copy.18
  32.4 0.1 concatenate.63
  32.5 0.9 %fusion.1.geo_ref = f32[112,128]{1,0:T(8,128)} fusion(f32[112,32]{0,1:T(8,128)S(1)} %concatenate.63, s32[128]{0:T(128)S(1)} %and_select_fusion), kind=kOutput, calls=%fused_computation.16 | convolution fusion | flops 5509120 | bytes 72192 | tf_op jit(solution)/shard_map/dot_general | solution.py:327
  33.4 12.1 %shard_map.68 = f32[6,16,3072]{2,1,0:T(8,128)} custom-call(f32[6,16,3072]{2,1,0:T(8,128)} %state_ref.1, f32[7,3,3072]{2,1,0:T(4,128)} %copy-done.1, f32[7,3,3072]{2,1,0:T(4,128)} %copy-done.2, f32[2,6,16,128]{3,2,1,0:T(8,128)} %pad_maximum_fusion.yhalo_ref, f32[112,128]{1,0:T(8,128)} %fusion.1.geo_ref), custom_call_target="tpu_custom_call" | custom-call | tf_op jit(solution)/shard_map/pallas_call | solution.py:187
  (46 shorter events, 0.8 us)
Async XLA Ops:
  0.6 8.6 %copy-start = (f32[16,32]{1,0:T(8,128)S(1)}, f32[16,32]{1,0:T(8,128)}, u32[]{:S(2)}) copy-start(f32[16,32]{1,0:T(8,128)} %param.6) | copy-start | bytes 6148
  2.5 15.5 %collective-permute-start.3 = (f32[6,16,128]{2,1,0:T(8,128)S(1)}, f32[6,16,128]{2,1,0:T(8,128)S(1)}, u32[]{:S(2)}, u32[]{:S(2)}) collective-permute-start(f32[6,16,128]{2,1,0:T(8,128)S(1)} %pad_maximum_fusion.2), channel_id=1, source_target_pairs={{1,0},{2,1},{3,2},{4,3},{5,4},{6,5},{7,6},{8,7},{9,8},{10,9},{11,1... | collective-permute-start | bytes 147464 | tf_op jit(solution)/shard_map/ppermute | solution.py:207
  5.1 12.0 %copy-start.4 = (s32[16]{0:T(128)S(1)}, s32[16]{0:T(128)}, u32[]{:S(2)}) copy-start(s32[16]{0:T(128)} %param.8) | copy-start | bytes 196
  5.1 12.0 %copy-start.5 = (s32[16]{0:T(128)S(1)}, s32[16]{0:T(128)}, u32[]{:S(2)}) copy-start(s32[16]{0:T(128)} %param.7) | copy-start | bytes 196
  5.1 12.3 %copy-start.3 = (f32[16,32]{1,0:T(8,128)S(1)}, f32[16,32]{1,0:T(8,128)}, u32[]{:S(2)}) copy-start(f32[16,32]{1,0:T(8,128)} %param.9) | copy-start | bytes 6148
  5.1 12.8 %collective-permute-start.2 = (f32[6,16,96]{2,1,0:T(8,128)S(1)}, f32[6,16,96]{2,1,0:T(8,128)S(1)}, u32[]{:S(2)}, u32[]{:S(2)}) collective-permute-start(f32[6,16,96]{2,1,0:T(8,128)S(1)} %get-tuple-element.10), channel_id=1, source_target_pairs={{0,1},{1,2},{2,3},{3,4},{4,5},{5,6},{6,7},{7,8},{8,9},{9,10},{10,1... | collective-permute-start | bytes 110600 | tf_op jit(solution)/shard_map/ppermute | solution.py:207
  9.3 21.7 %collective-permute-start = (f32[7,3,3072]{2,1,0:T(4,128)S(1)}, f32[7,3,3072]{2,1,0:T(4,128)S(1)}, u32[]{:S(2)}, u32[]{:S(2)}) collective-permute-start(f32[7,3,3072]{2,1,0:T(4,128)S(1)} %select_maximum_fusion.1), channel_id=1, source_target_pairs={{0,16},{16,32},{32,48},{48,64},{64,80},{80,96},{96,112},{112,128},... | collective-permute-start | bytes 774152 | tf_op jit(solution)/shard_map/ppermute | solution.py:207
  12.6 18.6 %collective-permute-start.1 = (f32[7,3,3072]{2,1,0:T(4,128)S(1)}, f32[7,3,3072]{2,1,0:T(4,128)S(1)}, u32[]{:S(2)}, u32[]{:S(2)}) collective-permute-start(f32[7,3,3072]{2,1,0:T(4,128)S(1)} %select_maximum_fusion), channel_id=1, source_target_pairs={{16,0},{32,16},{48,32},{64,48},{80,64},{96,80},{112,96},{128,112},... | collective-permute-start | bytes 774152 | tf_op jit(solution)/shard_map/ppermute | solution.py:207
  19.1 1.6 %collective-permute-start.5 = (f32[6,16,32]{2,1,0:T(8,128)S(1)}, f32[6,16,32]{2,1,0:T(8,128)S(1)}, u32[]{:S(2)}, u32[]{:S(2)}) collective-permute-start(f32[6,16,32]{2,1,0:T(8,128)S(1)} %get-tuple-element.6), channel_id=1, source_target_pairs={{15,1},{14,2},{0,3},{31,17},{30,18},{16,19},{47,33},{46,34},{32,35... | collective-permute-start | bytes 36872 | tf_op jit(solution)/shard_map/ppermute | solution.py:225
  19.7 1.0 %collective-permute-start.4 = (f32[6,16,32]{2,1,0:T(8,128)S(1)}, f32[6,16,32]{2,1,0:T(8,128)S(1)}, u32[]{:S(2)}, u32[]{:S(2)}) collective-permute-start(f32[6,16,32]{2,1,0:T(8,128)S(1)} %get-tuple-element.6), channel_id=1, source_target_pairs={{15,4},{14,5},{0,6},{31,20},{30,21},{16,22},{47,36},{46,37},{32,38... | collective-permute-start | bytes 36872 | tf_op jit(solution)/shard_map/ppermute | solution.py:225
  20.7 10.3 %collective-permute-start.6 = (f32[6,16,32]{2,1,0:T(8,128)S(1)}, f32[6,16,32]{2,1,0:T(8,128)S(1)}, u32[]{:S(2)}, u32[]{:S(2)}) collective-permute-start(f32[6,16,32]{2,1,0:T(8,128)S(1)} %select_select_fusion), channel_id=1, source_target_pairs={{15,7},{14,8},{0,9},{1,10},{2,11},{3,12},{4,13},{31,23},{30,24},{1... | collective-permute-start | bytes 36872 | tf_op jit(solution)/shard_map/ppermute | solution.py:225
  31.0 2.4 %copy-start.1 = (f32[7,3,3072]{2,1,0:T(4,128)}, f32[7,3,3072]{2,1,0:T(4,128)S(1)}, u32[]{:S(2)}) copy-start(f32[7,3,3072]{2,1,0:T(4,128)S(1)} %collective-permute-done.xlo_ref) | copy-start | bytes 774148
  31.1 2.3 %copy-start.2 = (f32[7,3,3072]{2,1,0:T(4,128)}, f32[7,3,3072]{2,1,0:T(4,128)S(1)}, u32[]{:S(2)}) copy-start(f32[7,3,3072]{2,1,0:T(4,128)S(1)} %collective-permute-done.1.xhi_ref) | copy-start | bytes 774148

commit v10 on v9

--- a/solution.py
+++ b/solution.py
@@ -207,10 +207,12 @@
     return lax.ppermute(block, axis, pairs)
 
 
-def broadcast(array, axis, holders, fanouts):
+def broadcast(array, axis, holders, fanouts, tied=None):
     count = lax.axis_size(axis)
     index = lax.axis_index(axis)
-    for fanout in fanouts:
+    for step, fanout in enumerate(fanouts):
+        if step == 1 and tied is not None:
+            array, tied = lax.optimization_barrier((array, tied))
         if len(holders) >= count:
             break
         waiting = [i for i in range(count) if i not in holders]
@@ -230,7 +232,7 @@
             reached = reached + [target for _, target in pairs]
         array = arrived
         holders = holders + reached
-    return array
+    return array, tied
 
 
 def zshift(values, offset, planes):
@@ -344,13 +346,24 @@
         extra = lax.dynamic_update_slice(extra, heights[None], (0, 0, 0))
         return jnp.concatenate([cols, extra], axis=0)
 
-    from_low = shifted(pack(state[:, columns - HALO :], shock_height[columns - HALO :]), "gx", True)
-    from_high = shifted(pack(state[:, :HALO], shock_height[:HALO]), "gx", False)
     below = shifted(state[..., length - band :], "gy", True, cyclic=True)
     above = shifted(
         jnp.concatenate([state[..., :band], state[..., length - planes :]], axis=2), "gy", False
     )
 
+    top_seed = jnp.where(
+        row_dev == row_devs - 1,
+        state[..., length - planes :],
+        jnp.where(row_dev == 0, below[..., band - planes :], above[..., band:]),
+    )
+    seeded = sorted({row_devs - 1, 0, max(row_devs - 2, 0)}, reverse=True)
+    sends = (
+        pack(state[:, columns - HALO :], shock_height[columns - HALO :]),
+        pack(state[:, :HALO], shock_height[:HALO]),
+    )
+    top_row, sends = broadcast(top_seed, "gy", seeded, (2, 1, 1, 1, 1), sends)
+    from_low = shifted(sends[0], "gx", True)
+    from_high = shifted(sends[1], "gx", False)
     low_height = jnp.where(
         col_dev == 0, jnp.broadcast_to(shock_height[:1], (HALO, planes)), from_low[6, :, :planes]
     )
@@ -362,13 +375,6 @@
     height_ext = jnp.concatenate([low_height, shock_height, high_height], axis=0)
     slope_x, slope_z = slopes(height_ext, planes)
 
-    top_seed = jnp.where(
-        row_dev == row_devs - 1,
-        state[..., length - planes :],
-        jnp.where(row_dev == 0, below[..., band - planes :], above[..., band:]),
-    )
-    seeded = sorted({row_devs - 1, 0, max(row_devs - 2, 0)}, reverse=True)
-    top_row = broadcast(top_seed, "gy", seeded, (2, 1, 1, 1, 1))
     shock_rate = shock_speed(top_row, slope_x, slope_z)
 
     blowing = wall_flux(wall_segment, segment_level, blow_table)

time: 46 us -> 57.6 us (1.25)
  the two profiles are of different devices: /device:TPU:113 before, /device:TPU:70 now
where the time goes in v10:
time: 57.6 us; the launch traced here: 56.7 us
  waiting for transfers between devices  18.9 us (33%)
  Pallas kernels  12.1 us (21%)
  starting transfers between devices  11.5 us (20%)
  local copies, waits for them, and re-layouts  9.05 us (16%)
  other arithmetic  3.28 us (6%)
  between operations  0.97 us (2%)
  matrix products  0.87 us (2%)
    pallas_call x1, Pallas kernels, update(): pl.pallas_call(kern, out_shape=jax.ShapeDtypeStruct((6, columns, length),...  12.1 us
    ppermute x4, waiting for transfers between devices, shifted(): return lax.ppermute(block, axis, pairs)  11.9 us
    ppermute x4, starting transfers between devices, shifted(): return lax.ppermute(block, axis, pairs)  8.26 us
    ppermute x3, waiting for transfers between devices, broadcast(): received = lax.ppermute(array, axis, pairs)  6.94 us
    slice x4, local copies, waits for them, and re-layouts, zshift(): jnp.roll(values, offset, axis=-1)  3.38 us
    ppermute x3, starting transfers between devices, broadcast(): received = lax.ppermute(array, axis, pairs)  3.25 us
    slice x1, local copies, waits for them, and re-layouts, shards(): state[:, :HALO]  1.36 us
  transfers between devices with their start and end apart: 7, of which 3 were waited for; matrix products, arithmetic and copies ran while one was open for 14% of the time, Pallas kernels for 0%

profile of v10, /device:TPU:70, one launch (start us, length us, event | category | flops | bytes accessed | tf_op | source)
XLA Modules:
  0.0 56.7 jit_solution(8361149830242903047)
XLA Ops:
  0.7 0.9 %slice.170 = f32[6,16,32]{2,1,0:T(8,128)S(1)} slice(f32[6,16,3072]{2,1,0:T(8,128)} %state_ref.1), slice={[0:6], [0:16], [3040:3072]} | slice | bytes 24576 | tf_op jit(solution)/shard_map/slice | solution.py:356
  1.6 0.9 %fusion.23 = (f32[6,16,96]{2,1,0:T(8,128)S(1)}, f32[6,16,96]{2,1,0:T(8,128)S(1)}) fusion(f32[6,16,3072]{2,1,0:T(8,128)} %state_ref.1), kind=kLoop, calls=%fused_computation.72 | loop fusion | bytes 147456 | tf_op jit(solution)/shard_map/slice | solution.py:349
  2.5 1.9 %collective-permute-start.1 = (f32[6,16,128]{2,1,0:T(8,128)S(1)}, f32[6,16,128]{2,1,0:T(8,128)S(1)}, u32[]{:S(2)}, u32[]{:S(2)}) collective-permute-start(f32[6,16,128]{2,1,0:T(8,128)S(1)} %pad_maximum_fusion.1), channel_id=1, source_target_pairs={{1,0},{2,1},{3,2},{4,3},{5,4},{6,5},{7,6},{8,7},{9,8},{10,9},{11,1... | collective-permute-start | bytes 147464 | tf_op jit(solution)/shard_map/ppermute | solution.py:207
  4.5 0.5 collective-permute-start
  5.0 0.7 %slice_bitcast_fusion.11 = (f32[32]{0:T(128)S(1)}, f32[32]{0:T(128)S(1)}) fusion(f32[16,32]{1,0:T(8,128)} %param.6), kind=kLoop, calls=%fused_computation.67 | loop fusion | bytes 512 | tf_op jit(solution)/shard_map/broadcast_in_dim | solution.py:372
  5.7 0.7 %slice_bitcast_fusion.8 = (f32[1,3,32]{2,1,0:T(4,128)S(1)}, f32[1,3,32]{2,1,0:T(4,128)S(1)}) fusion(f32[16,32]{1,0:T(8,128)} %param.6), kind=kLoop, calls=%fused_computation.63 | loop fusion | bytes 1536 | tf_op jit(solution)/shard_map/broadcast_in_dim | solution.py:346
  6.4 0.8 %fusion.24 = (f32[16,2]{1,0:T(8,128)S(1)}, f32[16,2]{1,0:T(8,128)S(1)}) fusion(f32[16,32]{1,0:T(8,128)} %param.6), kind=kLoop, calls=%fused_computation.73 | loop fusion | bytes 512 | tf_op jit(solution)/shard_map/jit(_roll_static)/slice | solution.py:244
  7.2 0.8 %fusion.25 = (f32[16,30]{1,0:T(8,128)S(1)}, f32[16,30]{1,0:T(8,128)S(1)}) fusion(f32[16,32]{1,0:T(8,128)} %param.6), kind=kLoop, calls=%fused_computation.74 | loop fusion | bytes 7680 | tf_op jit(solution)/shard_map/jit(_roll_static)/slice | solution.py:244
  8.1 0.8 %fusion.27 = (f32[16,31]{1,0:T(8,128)S(1)}, f32[16,31]{1,0:T(8,128)S(1)}) fusion(f32[16,32]{1,0:T(8,128)} %param.6), kind=kLoop, calls=%fused_computation.76 | loop fusion | bytes 7936 | tf_op jit(solution)/shard_map/jit(_roll_static)/slice | solution.py:244
  8.9 0.8 %fusion.26 = (f32[16,1]{1,0:T(8,128)S(1)}, f32[16,1]{1,0:T(8,128)S(1)}) fusion(f32[16,32]{1,0:T(8,128)} %param.6), kind=kLoop, calls=%fused_computation.75 | loop fusion | bytes 256 | tf_op jit(solution)/shard_map/jit(_roll_static)/slice | solution.py:244
  9.8 1.4 %fusion.22 = (f32[6,3,3072]{2,1,0:T(4,128)S(1)}, f32[6,3,3072]{2,1,0:T(4,128)S(1)}) fusion(f32[6,16,3072]{2,1,0:T(8,128)} %state_ref.1), kind=kLoop, calls=%fused_computation.71 | loop fusion | bytes 884736 | tf_op jit(solution)/shard_map/slice | solution.py:362
  11.2 0.2 select_reduce_fusion.1
  11.4 0.1 select_reduce_fusion
  11.6 0.2 select_maximum_fusion
  12.0 0.1 tile.8
  12.2 1.0 %fusion.21 = (f32[6,16,32]{2,1,0:T(8,128)S(1)}, f32[6,16,32]{2,1,0:T(8,128)S(1)}, f32[6,16,32]{2,1,0:T(8,128)S(1)}, f32[6,16,32]{2,1,0:T(8,128)S(1)}) fusion(f32[6,16,3072]{2,1,0:T(8,128)} %state_ref.1, f32[6,16,128]{2,1,0:T(8,128)S(1)} %collective-permute-done.1, f32[6,16,96]{2,1,0:T(8,128)S(1)} %collective-permute-done, pred[]{:T(512)S(6)} %eq.107, ...), kind=kLoop, calls=%fused_computation.70 | loop fusion | flops 6144 | bytes 122882 | tf_op jit(solution)/shard_map/slice | solution.py:304
  13.2 0.7 %collective-permute-start.3 = (f32[6,16,32]{2,1,0:T(8,128)S(1)}, f32[6,16,32]{2,1,0:T(8,128)S(1)}, u32[]{:S(2)}, u32[]{:S(2)}) collective-permute-start(f32[6,16,32]{2,1,0:T(8,128)S(1)} %get-tuple-element.13), channel_id=1, source_target_pairs={{15,1},{14,2},{0,3},{31,17},{30,18},{16,19},{47,33},{46,34},{32,35... | collective-permute-start | bytes 36872 | tf_op jit(solution)/shard_map/ppermute | solution.py:227
  13.9 1.3 %collective-permute-start.2 = (f32[6,16,32]{2,1,0:T(8,128)S(1)}, f32[6,16,32]{2,1,0:T(8,128)S(1)}, u32[]{:S(2)}, u32[]{:S(2)}) collective-permute-start(f32[6,16,32]{2,1,0:T(8,128)S(1)} %get-tuple-element.13), channel_id=1, source_target_pairs={{15,4},{14,5},{0,6},{31,20},{30,21},{16,22},{47,36},{46,37},{32,38... | collective-permute-start | bytes 36872 | tf_op jit(solution)/shard_map/ppermute | solution.py:227
  15.2 0.1 pad_maximum_fusion.2
  15.5 6.9 %collective-permute-done.2 = f32[6,16,32]{2,1,0:T(8,128)S(1)} collective-permute-done((f32[6,16,32]{2,1,0:T(8,128)S(1)}, f32[6,16,32]{2,1,0:T(8,128)S(1)}, u32[]{:S(2)}, u32[]{:S(2)}) %collective-permute-start.2) | collective-permute-done | bytes 12320 | tf_op jit(solution)/shard_map/ppermute | solution.py:227
  22.4 1.3 %collective-permute-start.6 = (f32[6,16,32]{2,1,0:T(8,128)S(1)}, f32[6,16,32]{2,1,0:T(8,128)S(1)}, u32[]{:S(2)}, u32[]{:S(2)}) collective-permute-start(f32[6,16,32]{2,1,0:T(8,128)S(1)} %select_select_fusion), channel_id=1, source_target_pairs={{15,7},{14,8},{0,9},{1,10},{2,11},{3,12},{4,13},{31,23},{30,24},{1... | collective-permute-start | bytes 36872 | tf_op jit(solution)/shard_map/ppermute | solution.py:227
  23.7 3.4 %collective-permute-start.4 = (f32[7,3,3072]{2,1,0:T(4,128)S(1)}, f32[7,3,3072]{2,1,0:T(4,128)S(1)}, u32[]{:S(2)}, u32[]{:S(2)}) collective-permute-start(f32[7,3,3072]{2,1,0:T(4,128)S(1)} %get-tuple-element.5), channel_id=1, source_target_pairs={{0,16},{16,32},{32,48},{48,64},{64,80},{80,96},{96,112},{112,128},... | collective-permute-start | bytes 774152 | tf_op jit(solution)/shard_map/ppermute | solution.py:207
  27.1 0.6 %pad_maximum_fusion.yhalo_ref = f32[2,6,16,128]{3,2,1,0:T(8,128)} fusion(f32[1,6,16,128]{3,2,1,0:T(8,128)S(1)} %select_bitcast_fusion, f32[1,6,16,128]{3,2,1,0:T(8,128)S(1)} %maximum_bitcast_fusion), kind=kLoop, calls=%fused_computation.4 | loop fusion | flops 24576 | bytes 196608 | tf_op jit(solution)/shard_map/stack | solution.py:385
  27.8 2.4 %collective-permute-start.5 = (f32[7,3,3072]{2,1,0:T(4,128)S(1)}, f32[7,3,3072]{2,1,0:T(4,128)S(1)}, u32[]{:S(2)}, u32[]{:S(2)}) collective-permute-start(f32[7,3,3072]{2,1,0:T(4,128)S(1)} %get-tuple-element.6), channel_id=1, source_target_pairs={{16,0},{32,16},{48,32},{64,48},{80,64},{96,80},{112,96},{128,112},... | collective-permute-start | bytes 774152 | tf_op jit(solution)/shard_map/ppermute | solution.py:207
  30.2 6.1 %collective-permute-done.4.xlo_ref = f32[7,3,3072]{2,1,0:T(4,128)S(1)} collective-permute-done((f32[7,3,3072]{2,1,0:T(4,128)S(1)}, f32[7,3,3072]{2,1,0:T(4,128)S(1)}, u32[]{:S(2)}, u32[]{:S(2)}) %collective-permute-start.4) | collective-permute-done | bytes 258080 | tf_op jit(solution)/shard_map/ppermute | solution.py:207
  36.4 0.1 copy.15
  36.5 5.8 %collective-permute-done.5.xhi_ref = f32[7,3,3072]{2,1,0:T(4,128)S(1)} collective-permute-done((f32[7,3,3072]{2,1,0:T(4,128)S(1)}, f32[7,3,3072]{2,1,0:T(4,128)S(1)}, u32[]{:S(2)}, u32[]{:S(2)}) %collective-permute-start.5) | collective-permute-done | bytes 258080 | tf_op jit(solution)/shard_map/ppermute | solution.py:207
  42.3 0.7 %multiply_add_fusion = (f32[16,32]{1,0:T(8,128)}, f32[16,32]{1,0:T(8,128)S(1)}, f32[16,32]{1,0:T(8,128)S(1)}, f32[16,32]{1,0:T(8,128)S(1)}) fusion(f32[16,32]{1,0:T(8,128)S(1)} %copy-done, f32[6,16,32]{2,1,0:T(8,128)S(1)} %broadcast_select_fusion, f32[16,2]{1,0:T(8,128)S(1)} %get-tuple-element.21, f32[16,30]{1,0:T(8,128)S(1)} %get-tuple-element.23, ...), kind=kLoop, calls=%fused_computation.51 | loop fusion | flops 29184 | bytes 31488 | tf_op jit(solution)/shard_map/add | solution.py:410
  43.1 0.1 copy.17
  43.5 0.1 concatenate.63
  43.7 0.9 %fusion.1.geo_ref = f32[112,128]{1,0:T(8,128)} fusion(f32[112,32]{0,1:T(8,128)S(1)} %concatenate.63, s32[128]{0:T(128)S(1)} %and_select_fusion), kind=kOutput, calls=%fused_computation.16 | convolution fusion | flops 5509120 | bytes 72192 | tf_op jit(solution)/shard_map/dot_general | solution.py:329
  44.5 12.1 %shard_map.68 = f32[6,16,3072]{2,1,0:T(8,128)} custom-call(f32[6,16,3072]{2,1,0:T(8,128)} %state_ref.1, f32[7,3,3072]{2,1,0:T(4,128)} %copy-done.1, f32[7,3,3072]{2,1,0:T(4,128)} %copy-done.2, f32[2,6,16,128]{3,2,1,0:T(8,128)} %pad_maximum_fusion.yhalo_ref, f32[112,128]{1,0:T(8,128)} %fusion.1.geo_ref), custom_call_target="tpu_custom_call" | custom-call | tf_op jit(solution)/shard_map/pallas_call | solution.py:187
  (45 shorter events, 1.0 us)
Async XLA Ops:
  0.6 10.5 %copy-start.4 = (s32[16]{0:T(128)S(1)}, s32[16]{0:T(128)}, u32[]{:S(2)}) copy-start(s32[16]{0:T(128)} %param.8) | copy-start | bytes 196
  0.6 10.5 %copy-start.5 = (s32[16]{0:T(128)S(1)}, s32[16]{0:T(128)}, u32[]{:S(2)}) copy-start(s32[16]{0:T(128)} %param.7) | copy-start | bytes 196
  0.7 10.8 %copy-start.3 = (f32[16,32]{1,0:T(8,128)S(1)}, f32[16,32]{1,0:T(8,128)}, u32[]{:S(2)}) copy-start(f32[16,32]{1,0:T(8,128)} %param.9) | copy-start | bytes 6148
  2.5 9.6 %collective-permute-start.1 = (f32[6,16,128]{2,1,0:T(8,128)S(1)}, f32[6,16,128]{2,1,0:T(8,128)S(1)}, u32[]{:S(2)}, u32[]{:S(2)}) collective-permute-start(f32[6,16,128]{2,1,0:T(8,128)S(1)} %pad_maximum_fusion.1), channel_id=1, source_target_pairs={{1,0},{2,1},{3,2},{4,3},{5,4},{6,5},{7,6},{8,7},{9,8},{10,9},{11,1... | collective-permute-start | bytes 147464 | tf_op jit(solution)/shard_map/ppermute | solution.py:207
  4.5 7.7 %collective-permute-start = (f32[6,16,96]{2,1,0:T(8,128)S(1)}, f32[6,16,96]{2,1,0:T(8,128)S(1)}, u32[]{:S(2)}, u32[]{:S(2)}) collective-permute-start(f32[6,16,96]{2,1,0:T(8,128)S(1)} %get-tuple-element.18), channel_id=1, source_target_pairs={{0,1},{1,2},{2,3},{3,4},{4,5},{5,6},{6,7},{7,8},{8,9},{9,10},{10,1... | collective-permute-start | bytes 110600 | tf_op jit(solution)/shard_map/ppermute | solution.py:207
  9.8 2.0 %copy-start = (f32[16,32]{1,0:T(8,128)S(1)}, f32[16,32]{1,0:T(8,128)}, u32[]{:S(2)}) copy-start(f32[16,32]{1,0:T(8,128)} %param.6) | copy-start | bytes 6148
  13.2 2.2 %collective-permute-start.3 = (f32[6,16,32]{2,1,0:T(8,128)S(1)}, f32[6,16,32]{2,1,0:T(8,128)S(1)}, u32[]{:S(2)}, u32[]{:S(2)}) collective-permute-start(f32[6,16,32]{2,1,0:T(8,128)S(1)} %get-tuple-element.13), channel_id=1, source_target_pairs={{15,1},{14,2},{0,3},{31,17},{30,18},{16,19},{47,33},{46,34},{32,35... | collective-permute-start | bytes 36872 | tf_op jit(solution)/shard_map/ppermute | solution.py:227
  13.9 8.5 %collective-permute-start.2 = (f32[6,16,32]{2,1,0:T(8,128)S(1)}, f32[6,16,32]{2,1,0:T(8,128)S(1)}, u32[]{:S(2)}, u32[]{:S(2)}) collective-permute-start(f32[6,16,32]{2,1,0:T(8,128)S(1)} %get-tuple-element.13), channel_id=1, source_target_pairs={{15,4},{14,5},{0,6},{31,20},{30,21},{16,22},{47,36},{46,37},{32,38... | collective-permute-start | bytes 36872 | tf_op jit(solution)/shard_map/ppermute | solution.py:227
  22.4 7.8 %collective-permute-start.6 = (f32[6,16,32]{2,1,0:T(8,128)S(1)}, f32[6,16,32]{2,1,0:T(8,128)S(1)}, u32[]{:S(2)}, u32[]{:S(2)}) collective-permute-start(f32[6,16,32]{2,1,0:T(8,128)S(1)} %select_select_fusion), channel_id=1, source_target_pairs={{15,7},{14,8},{0,9},{1,10},{2,11},{3,12},{4,13},{31,23},{30,24},{1... | collective-permute-start | bytes 36872 | tf_op jit(solution)/shard_map/ppermute | solution.py:227
  23.7 12.7 %collective-permute-start.4 = (f32[7,3,3072]{2,1,0:T(4,128)S(1)}, f32[7,3,3072]{2,1,0:T(4,128)S(1)}, u32[]{:S(2)}, u32[]{:S(2)}) collective-permute-start(f32[7,3,3072]{2,1,0:T(4,128)S(1)} %get-tuple-element.5), channel_id=1, source_target_pairs={{0,16},{16,32},{32,48},{48,64},{64,80},{80,96},{96,112},{112,128},... | collective-permute-start | bytes 774152 | tf_op jit(solution)/shard_map/ppermute | solution.py:207
  27.8 14.5 %collective-permute-start.5 = (f32[7,3,3072]{2,1,0:T(4,128)S(1)}, f32[7,3,3072]{2,1,0:T(4,128)S(1)}, u32[]{:S(2)}, u32[]{:S(2)}) collective-permute-start(f32[7,3,3072]{2,1,0:T(4,128)S(1)} %get-tuple-element.6), channel_id=1, source_target_pairs={{16,0},{32,16},{48,32},{64,48},{80,64},{96,80},{112,96},{128,112},... | collective-permute-start | bytes 774152 | tf_op jit(solution)/shard_map/ppermute | solution.py:207
  36.4 8.1 %copy-start.1 = (f32[7,3,3072]{2,1,0:T(4,128)}, f32[7,3,3072]{2,1,0:T(4,128)S(1)}, u32[]{:S(2)}) copy-start(f32[7,3,3072]{2,1,0:T(4,128)S(1)} %collective-permute-done.4.xlo_ref) | copy-start | bytes 774148
  42.3 2.3 %copy-start.2 = (f32[7,3,3072]{2,1,0:T(4,128)}, f32[7,3,3072]{2,1,0:T(4,128)S(1)}, u32[]{:S(2)}) copy-start(f32[7,3,3072]{2,1,0:T(4,128)S(1)} %collective-permute-done.5.xhi_ref) | copy-start | bytes 774148

commit v11 on v9

--- a/solution.py
+++ b/solution.py
@@ -62,8 +62,8 @@
     face_area = STREAM_STEP * SPAN_STEP
     xrows = columns + 2 * XPAD
 
-    def kernel(state_ref, xlo_ref, xhi_ref, yhalo_ref, geo_ref,
-               out_ref, qx_ref, qy_ref, pair_ref):
+    def kernel(state_ref, xlo_ref, xhi_ref, yhalo_ref, geo_ref, top_ref, height_ref,
+               out_ref, shock_ref, qx_ref, qy_ref, pair_ref):
         col_dev = lax.axis_index("gx")
         first_row = lax.axis_index("gy") * (length // planes)
         for c in range(6):
@@ -88,11 +88,24 @@
                     state_ref[c, columns - 1:columns, :], (HALO, length))
 
         height_x = lane_tile(geo_ref[0:xrows, :], CHUNK)
-        slope_x = lane_tile(geo_ref[xrows:xrows + columns, :], width)
-        slope_z = lane_tile(geo_ref[xrows + columns:xrows + 2 * columns, :], width)
-        rate = lane_tile(geo_ref[xrows + 2 * columns:xrows + 3 * columns, :], width)
-        ratio = lane_tile(geo_ref[xrows + 3 * columns:xrows + 4 * columns, :], CHUNK)
-        height = lane_tile(geo_ref[xrows + 4 * columns:xrows + 5 * columns, :], CHUNK)
+        slope_x_row = geo_ref[xrows:xrows + columns, :]
+        slope_z_row = geo_ref[xrows + columns:xrows + 2 * columns, :]
+        height_row = geo_ref[xrows + 2 * columns:xrows + 3 * columns, :]
+        group = lax.broadcasted_iota(jnp.int32, (columns, LANES), 1) // planes
+        top = []
+        for c in range(6):
+            held = top_ref[c]
+            spread = jnp.where(group == 0, pltpu.roll(held, planes, 1),
+                               jnp.where(group == 1, pltpu.roll(held, 2 * planes, 1),
+                                         jnp.where(group == 2, pltpu.roll(held, 3 * planes, 1), held)))
+            top.append(spread)
+        rate_row = shock_speed(top, slope_x_row, slope_z_row)
+        shock_ref[...] = height_ref[...] + dt * rate_row[:, 0:planes]
+        slope_x = lane_tile(slope_x_row, width)
+        slope_z = lane_tile(slope_z_row, width)
+        rate = lane_tile(rate_row, width)
+        ratio = lane_tile(rate_row / height_row, CHUNK)
+        height = lane_tile(height_row, CHUNK)
         lane = lax.broadcasted_iota(jnp.int32, (columns, CHUNK), 1) % planes
         lane_in = lax.broadcasted_iota(jnp.int32, (1, CHUNK), 1)
         lane_out = lax.broadcasted_iota(jnp.int32, (1, width), 1)
@@ -179,22 +192,25 @@
     return kernel
 
 
-def update(state, xlo, xhi, yhalo, geo, planes, total_rows, dt):
+def update(state, xlo, xhi, yhalo, geo, top, height, planes, total_rows, dt):
     columns = state.shape[1]
     length = state.shape[2]
     kern = make_kernel(columns, length, planes, total_rows, dt)
     vmem = pl.BlockSpec(memory_space=pltpu.VMEM)
     return pl.pallas_call(
         kern,
-        out_shape=jax.ShapeDtypeStruct((6, columns, length), jnp.float32),
-        in_specs=[vmem] * 5,
-        out_specs=vmem,
+        out_shape=(
+            jax.ShapeDtypeStruct((6, columns, length), jnp.float32),
+            jax.ShapeDtypeStruct((columns, planes), jnp.float32),
+        ),
+        in_specs=[vmem] * 7,
+        out_specs=(vmem, vmem),
         scratch_shapes=[
             pltpu.VMEM((6, columns + 2 * XPAD, length), jnp.float32),
             pltpu.VMEM((6, columns, length + 2 * PAD), jnp.float32),
             pltpu.VMEM((6, 6, columns + 2 * XPAD, CHUNK), jnp.float32),
         ],
-    )(state, xlo, xhi, yhalo, geo)
+    )(state, xlo, xhi, yhalo, geo, top, height)
 
 
 def shifted(block, axis, forward, cyclic=False):
@@ -346,11 +362,10 @@
 
     from_low = shifted(pack(state[:, columns - HALO :], shock_height[columns - HALO :]), "gx", True)
     from_high = shifted(pack(state[:, :HALO], shock_height[:HALO]), "gx", False)
-    below = shifted(state[..., length - band :], "gy", True, cyclic=True)
-    above = shifted(
-        jnp.concatenate([state[..., :band], state[..., length - planes :]], axis=2), "gy", False
-    )
-
+    plane_lane = jnp.arange(PAD, dtype=jnp.int32)[None, None, :]
+    top_block = state[..., length - PAD :]
+    below = shifted(top_block, "gy", True, cyclic=True)
+    above = shifted(jnp.where(plane_lane < band, state[..., :PAD], top_block), "gy", False)
     low_height = jnp.where(
         col_dev == 0, jnp.broadcast_to(shock_height[:1], (HALO, planes)), from_low[6, :, :planes]
     )
@@ -362,21 +377,19 @@
     height_ext = jnp.concatenate([low_height, shock_height, high_height], axis=0)
     slope_x, slope_z = slopes(height_ext, planes)
 
-    top_seed = jnp.where(
-        row_dev == row_devs - 1,
-        state[..., length - planes :],
-        jnp.where(row_dev == 0, below[..., band - planes :], above[..., band:]),
-    )
+    top_seed = jnp.where(row_dev == row_devs - 1, top_block, jnp.where(row_dev == 0, below, above))
     seeded = sorted({row_devs - 1, 0, max(row_devs - 2, 0)}, reverse=True)
-    top_row = broadcast(top_seed, "gy", seeded, (2, 1, 1, 1, 1))
-    shock_rate = shock_speed(top_row, slope_x, slope_z)
+    top_held = broadcast(top_seed, "gy", seeded, (2, 1, 1, 1, 1))
 
     blowing = wall_flux(wall_segment, segment_level, blow_table)
-    ghost_below = jnp.where(row_dev == 0, wall_ghosts(state[..., :band], blowing, planes), below)
+    wall_block = wall_ghosts(state[..., :band], blowing, planes)
+    ghost_below = jnp.where(
+        row_dev == 0, jnp.concatenate([wall_block[..., : PAD - band], wall_block], axis=2), below
+    )
     ghost_above = jnp.where(
-        row_dev == row_devs - 1, jnp.tile(state[..., length - planes :], (1, 1, HALO + 1)), above
-    )
-    yhalo = jnp.stack([jnp.concatenate([ghost_below[..., : PAD - band], ghost_below], axis=2), ghost_above])
+        row_dev == row_devs - 1, jnp.tile(state[..., length - planes :], (1, 1, PAD // planes)), above
+    )
+    yhalo = jnp.stack([ghost_below, ghost_above])
 
     height = shock_height
     height_x = jnp.concatenate(
@@ -387,21 +400,20 @@
         ],
         axis=0,
     )
-    small = jnp.concatenate(
-        [height_x, slope_x, slope_z, shock_rate, shock_rate / height, height], axis=0
-    )
+    small = jnp.concatenate([height_x, slope_x, slope_z, height], axis=0)
     geo = replicate_lanes(small, planes)
-    state_new = update(
+    state_new, shock_new = update(
         state,
         from_low,
         from_high,
         yhalo,
         geo,
+        top_held,
+        shock_height,
         planes,
         total_rows,
         COURANT / total_rows,
     )
-    shock_new = shock_height + COURANT / total_rows * shock_rate
     return (state_new, shock_new)
 
 

time: 46 us -> 45.8 us (level)
  the two profiles are of different devices: /device:TPU:113 before, /device:TPU:209 now
where the time goes in v11:
time: 45.8 us; the launch traced here: 45.3 us
  starting transfers between devices  13.2 us (29%)
  Pallas kernels  12.3 us (27%)
  waiting for transfers between devices  11 us (24%)
  other arithmetic  3.79 us (8%)
  local copies, waits for them, and re-layouts  3.18 us (7%)
  between operations  1.03 us (2%)
  matrix products  0.84 us (2%)
    pallas_call x1, Pallas kernels, update(): pl.pallas_call(kern, out_shape=(jax.ShapeDtypeStruct((6, columns, length)...  12.3 us
    ppermute x3, waiting for transfers between devices, broadcast(): received = lax.ppermute(array, axis, pairs)  11 us
    ppermute x4, starting transfers between devices, shifted(): return lax.ppermute(block, axis, pairs)  10.6 us
    ppermute x3, starting transfers between devices, broadcast(): received = lax.ppermute(array, axis, pairs)  2.62 us
    slice x1, local copies, waits for them, and re-layouts, shards(): from_high = shifted(pack(state[:, :HALO], shock_height[:HALO]), 'gx', False)  1.35 us
    slice x1, local copies, waits for them, and re-layouts, wall_ghosts(): first_rows[..., 2 * planes:3 * planes]  1.01 us
  transfers between devices with their start and end apart: 7, of which 1 were waited for; matrix products, arithmetic and copies ran while one was open for 13% of the time, Pallas kernels for 0%

profile of v11, /device:TPU:209, one launch (start us, length us, event | category | flops | bytes accessed | tf_op | source)
XLA Modules:
  0.0 45.3 jit_solution(2970972050465725064)
XLA Ops:
  0.7 0.8 %fusion.15 = (f32[6,16,128]{2,1,0:T(8,128)S(1)}, f32[6,16,128]{2,1,0:T(8,128)S(1)}) fusion(f32[6,16,3072]{2,1,0:T(8,128)} %state_ref.1, pred[128]{0:T(512)(128)(4,1)S(1)} %iota_compare_fusion.5), kind=kLoop, calls=%fused_computation.55 | loop fusion | flops 12288 | bytes 196736 | tf_op jit(solution)/shard_map/slice | solution.py:366
  1.5 1.3 %collective-permute-start.2 = (f32[6,16,128]{2,1,0:T(8,128)S(1)}, f32[6,16,128]{2,1,0:T(8,128)S(1)}, u32[]{:S(2)}, u32[]{:S(2)}) collective-permute-start(f32[6,16,128]{2,1,0:T(8,128)S(1)} %get-tuple-element.6), channel_id=1, source_target_pairs={{0,1},{1,2},{2,3},{3,4},{4,5},{5,6},{6,7},{7,8},{8,9},{9,10},{10,1... | collective-permute-start | bytes 147464 | tf_op jit(solution)/shard_map/ppermute | solution.py:223
  2.8 1.9 %collective-permute-start.3 = (f32[6,16,128]{2,1,0:T(8,128)S(1)}, f32[6,16,128]{2,1,0:T(8,128)S(1)}, u32[]{:S(2)}, u32[]{:S(2)}) collective-permute-start(f32[6,16,128]{2,1,0:T(8,128)S(1)} %get-tuple-element.7), channel_id=1, source_target_pairs={{1,0},{2,1},{3,2},{4,3},{5,4},{6,5},{7,6},{8,7},{9,8},{10,9},{11,1... | collective-permute-start | bytes 147464 | tf_op jit(solution)/shard_map/ppermute | solution.py:223
  4.7 1.3 %fusion.16 = (f32[6,3,3072]{2,1,0:T(4,128)S(1)}, f32[6,3,3072]{2,1,0:T(4,128)S(1)}) fusion(f32[6,16,3072]{2,1,0:T(8,128)} %state_ref.1), kind=kLoop, calls=%fused_computation.56 | loop fusion | bytes 884736 | tf_op jit(solution)/shard_map/slice | solution.py:364
  6.1 0.0 copy-start.4
  6.1 0.1 select_maximum_fusion.1
  6.2 3.1 %collective-permute-start = (f32[7,3,3072]{2,1,0:T(4,128)S(1)}, f32[7,3,3072]{2,1,0:T(4,128)S(1)}, u32[]{:S(2)}, u32[]{:S(2)}) collective-permute-start(f32[7,3,3072]{2,1,0:T(4,128)S(1)} %select_maximum_fusion.1), channel_id=1, source_target_pairs={{0,16},{16,32},{32,48},{48,64},{64,80},{80,96},{96,112},{112,128},... | collective-permute-start | bytes 774152 | tf_op jit(solution)/shard_map/ppermute | solution.py:223
  9.3 0.1 select_maximum_fusion
  9.4 4.3 %collective-permute-start.1 = (f32[7,3,3072]{2,1,0:T(4,128)S(1)}, f32[7,3,3072]{2,1,0:T(4,128)S(1)}, u32[]{:S(2)}, u32[]{:S(2)}) collective-permute-start(f32[7,3,3072]{2,1,0:T(4,128)S(1)} %select_maximum_fusion), channel_id=1, source_target_pairs={{16,0},{32,16},{48,32},{64,48},{80,64},{96,80},{112,96},{128,112},... | collective-permute-start | bytes 774152 | tf_op jit(solution)/shard_map/ppermute | solution.py:223
  13.7 0.1 copy.36
  13.8 1.0 %fusion.14 = (f32[6,16,32]{2,1,0:T(8,128)S(1)}, f32[6,16,32]{2,1,0:T(8,128)S(1)}, f32[6,16,32]{2,1,0:T(8,128)S(1)}, f32[6,16,32]{2,1,0:T(8,128)S(1)}) fusion(f32[6,16,3072]{2,1,0:T(8,128)} %state_ref.1), kind=kLoop, calls=%fused_computation.54 | loop fusion | bytes 98304 | tf_op jit(solution)/shard_map/slice | solution.py:318
  14.9 0.2 select_reduce_fusion.1
  15.0 0.1 iota_compare_fusion.3
  15.1 0.1 select_reduce_fusion
  15.3 0.1 mul.47
  15.3 0.1 pad_maximum_fusion.1
  15.6 0.1 tile.8
  15.7 0.9 %select_select_fusion.1 = (f32[6,16,128]{2,1,0:T(8,128)S(1)}, f32[1,6,16,128]{3,2,1,0:T(8,128)S(1)}, f32[1,6,16,128]{3,2,1,0:T(8,128)S(1)}) fusion(f32[6,16,128]{2,1,0:T(8,128)S(1)} %collective-permute-done.2, f32[6,16,128]{2,1,0:T(8,128)S(1)} %collective-permute-done.3, pred[]{:T(512)S(6)} %eq.110, pred[]{:T(512)S(6)} %eq.103, f32[6,16,3072]{2,1,0:T(8,128)} %state_ref.1, ...), kind=kLoop, calls=%fused_computation.9 | loop fusion | flops 61440 | bytes 393218 | tf_op jit(solution)/shard_map/jit(_where)/select_n | solution.py:380
  16.6 0.7 %collective-permute-start.5 = (f32[6,16,128]{2,1,0:T(8,128)S(1)}, f32[6,16,128]{2,1,0:T(8,128)S(1)}, u32[]{:S(2)}, u32[]{:S(2)}) collective-permute-start(f32[6,16,128]{2,1,0:T(8,128)S(1)} %get-tuple-element.10), channel_id=1, source_target_pairs={{15,1},{14,2},{0,3},{31,17},{30,18},{16,19},{47,33},{46,34},{32,35... | collective-permute-start | bytes 147464 | tf_op jit(solution)/shard_map/ppermute | solution.py:241
  17.3 0.7 %collective-permute-start.4 = (f32[6,16,128]{2,1,0:T(8,128)S(1)}, f32[6,16,128]{2,1,0:T(8,128)S(1)}, u32[]{:S(2)}, u32[]{:S(2)}) collective-permute-start(f32[6,16,128]{2,1,0:T(8,128)S(1)} %get-tuple-element.10), channel_id=1, source_target_pairs={{15,4},{14,5},{0,6},{31,20},{30,21},{16,22},{47,36},{46,37},{32,38... | collective-permute-start | bytes 147464 | tf_op jit(solution)/shard_map/ppermute | solution.py:241
  18.1 1.3 %collective-permute-start.6 = (f32[6,16,128]{2,1,0:T(8,128)S(1)}, f32[6,16,128]{2,1,0:T(8,128)S(1)}, u32[]{:S(2)}, u32[]{:S(2)}) collective-permute-start(f32[6,16,128]{2,1,0:T(8,128)S(1)} %select_select_fusion), channel_id=1, source_target_pairs={{15,7},{14,8},{0,9},{1,10},{2,11},{3,12},{4,13},{31,23},{30,24},{1... | collective-permute-start | bytes 147464 | tf_op jit(solution)/shard_map/ppermute | solution.py:241
  19.4 0.6 %pad_maximum_fusion.yhalo_ref = f32[2,6,16,128]{3,2,1,0:T(8,128)} fusion(f32[1,6,16,128]{3,2,1,0:T(8,128)S(1)} %get-tuple-element.11, f32[1,6,16,128]{3,2,1,0:T(8,128)S(1)} %get-tuple-element.12), kind=kLoop, calls=%fused_computation.4 | loop fusion | flops 24576 | bytes 196608 | tf_op jit(solution)/shard_map/stack | solution.py:392
  20.0 11.0 %collective-permute-done.6 = f32[6,16,128]{2,1,0:T(8,128)S(1)} collective-permute-done((f32[6,16,128]{2,1,0:T(8,128)S(1)}, f32[6,16,128]{2,1,0:T(8,128)S(1)}, u32[]{:S(2)}, u32[]{:S(2)}) %collective-permute-start.6) | collective-permute-done | bytes 49184 | tf_op jit(solution)/shard_map/ppermute | solution.py:241
  31.0 0.6 %broadcast_select_fusion.top_ref = f32[6,16,128]{2,1,0:T(8,128)} fusion(f32[6,16,128]{2,1,0:T(8,128)S(1)} %collective-permute-done.6, f32[6,16,128]{2,1,0:T(8,128)S(1)} %select_select_fusion, pred[]{:T(512)S(6)} %or.35), kind=kLoop, calls=%fused_computation.12 | loop fusion | flops 12288 | bytes 147457 | tf_op jit(solution)/shard_map/jit(_where)/select_n | solution.py:245
  31.7 0.1 copy.35
  31.8 0.1 copy.37
  31.9 0.1 fusion.2
  32.0 0.1 broadcast_in_dim.100
  32.1 0.1 broadcast_in_dim.104
  32.1 0.1 concatenate.59
  32.2 0.8 %fusion.9.geo_ref = f32[80,128]{1,0:T(8,128)} fusion(f32[80,32]{0,1:T(8,128)S(1)} %concatenate.59, s32[128]{0:T(128)S(1)} %and_select_fusion), kind=kOutput, calls=%fused_computation.29 | convolution fusion | flops 3936256 | bytes 51712 | tf_op jit(solution)/shard_map/dot_general | solution.py:343
  33.1 12.3 %shard_map.68 = (f32[6,16,3072]{2,1,0:T(8,128)}, f32[16,32]{1,0:T(8,128)}) custom-call(f32[6,16,3072]{2,1,0:T(8,128)} %state_ref.1, f32[7,3,3072]{2,1,0:T(4,128)} %copy-done, f32[7,3,3072]{2,1,0:T(4,128)} %copy-done.1, f32[2,6,16,128]{3,2,1,0:T(8,128)} %pad_maximum_fusion.yhalo_ref, f32[80,128]{1,0:T(8,128)} %fusion.9.geo_ref, ...), custom_call_target="tpu_custom_call" | custom-call | tf_op jit(solution)/shard_map/pallas_call | solution.py:200
  (39 shorter events, 0.2 us)
Async XLA Ops:
  0.6 5.4 %copy-start.2 = (f32[16,32]{1,0:T(8,128)S(1)}, f32[16,32]{1,0:T(8,128)}, u32[]{:S(2)}) copy-start(f32[16,32]{1,0:T(8,128)} %height_ref.1) | copy-start | bytes 6148
  1.5 14.2 %collective-permute-start.2 = (f32[6,16,128]{2,1,0:T(8,128)S(1)}, f32[6,16,128]{2,1,0:T(8,128)S(1)}, u32[]{:S(2)}, u32[]{:S(2)}) collective-permute-start(f32[6,16,128]{2,1,0:T(8,128)S(1)} %get-tuple-element.6), channel_id=1, source_target_pairs={{0,1},{1,2},{2,3},{3,4},{4,5},{5,6},{6,7},{7,8},{8,9},{9,10},{10,1... | collective-permute-start | bytes 147464 | tf_op jit(solution)/shard_map/ppermute | solution.py:223
  2.8 12.9 %collective-permute-start.3 = (f32[6,16,128]{2,1,0:T(8,128)S(1)}, f32[6,16,128]{2,1,0:T(8,128)S(1)}, u32[]{:S(2)}, u32[]{:S(2)}) collective-permute-start(f32[6,16,128]{2,1,0:T(8,128)S(1)} %get-tuple-element.7), channel_id=1, source_target_pairs={{1,0},{2,1},{3,2},{4,3},{5,4},{6,5},{7,6},{8,7},{9,8},{10,9},{11,1... | collective-permute-start | bytes 147464 | tf_op jit(solution)/shard_map/ppermute | solution.py:223
  6.1 8.8 %copy-start.4 = (s32[16]{0:T(128)S(1)}, s32[16]{0:T(128)}, u32[]{:S(2)}) copy-start(s32[16]{0:T(128)} %param.8) | copy-start | bytes 196
  6.1 8.8 %copy-start.5 = (s32[16]{0:T(128)S(1)}, s32[16]{0:T(128)}, u32[]{:S(2)}) copy-start(s32[16]{0:T(128)} %param.7) | copy-start | bytes 196
  6.1 9.0 %copy-start.3 = (f32[16,32]{1,0:T(8,128)S(1)}, f32[16,32]{1,0:T(8,128)}, u32[]{:S(2)}) copy-start(f32[16,32]{1,0:T(8,128)} %param.9) | copy-start | bytes 6148
  6.2 25.5 %collective-permute-start = (f32[7,3,3072]{2,1,0:T(4,128)S(1)}, f32[7,3,3072]{2,1,0:T(4,128)S(1)}, u32[]{:S(2)}, u32[]{:S(2)}) collective-permute-start(f32[7,3,3072]{2,1,0:T(4,128)S(1)} %select_maximum_fusion.1), channel_id=1, source_target_pairs={{0,16},{16,32},{32,48},{48,64},{64,80},{80,96},{96,112},{112,128},... | collective-permute-start | bytes 774152 | tf_op jit(solution)/shard_map/ppermute | solution.py:223
  9.4 22.4 %collective-permute-start.1 = (f32[7,3,3072]{2,1,0:T(4,128)S(1)}, f32[7,3,3072]{2,1,0:T(4,128)S(1)}, u32[]{:S(2)}, u32[]{:S(2)}) collective-permute-start(f32[7,3,3072]{2,1,0:T(4,128)S(1)} %select_maximum_fusion), channel_id=1, source_target_pairs={{16,0},{32,16},{48,32},{64,48},{80,64},{96,80},{112,96},{128,112},... | collective-permute-start | bytes 774152 | tf_op jit(solution)/shard_map/ppermute | solution.py:223
  16.6 1.4 %collective-permute-start.5 = (f32[6,16,128]{2,1,0:T(8,128)S(1)}, f32[6,16,128]{2,1,0:T(8,128)S(1)}, u32[]{:S(2)}, u32[]{:S(2)}) collective-permute-start(f32[6,16,128]{2,1,0:T(8,128)S(1)} %get-tuple-element.10), channel_id=1, source_target_pairs={{15,1},{14,2},{0,3},{31,17},{30,18},{16,19},{47,33},{46,34},{32,35... | collective-permute-start | bytes 147464 | tf_op jit(solution)/shard_map/ppermute | solution.py:241
  17.3 0.7 %collective-permute-start.4 = (f32[6,16,128]{2,1,0:T(8,128)S(1)}, f32[6,16,128]{2,1,0:T(8,128)S(1)}, u32[]{:S(2)}, u32[]{:S(2)}) collective-permute-start(f32[6,16,128]{2,1,0:T(8,128)S(1)} %get-tuple-element.10), channel_id=1, source_target_pairs={{15,4},{14,5},{0,6},{31,20},{30,21},{16,22},{47,36},{46,37},{32,38... | collective-permute-start | bytes 147464 | tf_op jit(solution)/shard_map/ppermute | solution.py:241
  18.1 12.9 %collective-permute-start.6 = (f32[6,16,128]{2,1,0:T(8,128)S(1)}, f32[6,16,128]{2,1,0:T(8,128)S(1)}, u32[]{:S(2)}, u32[]{:S(2)}) collective-permute-start(f32[6,16,128]{2,1,0:T(8,128)S(1)} %select_select_fusion), channel_id=1, source_target_pairs={{15,7},{14,8},{0,9},{1,10},{2,11},{3,12},{4,13},{31,23},{30,24},{1... | collective-permute-start | bytes 147464 | tf_op jit(solution)/shard_map/ppermute | solution.py:241
  31.7 1.4 %copy-start = (f32[7,3,3072]{2,1,0:T(4,128)}, f32[7,3,3072]{2,1,0:T(4,128)S(1)}, u32[]{:S(2)}) copy-start(f32[7,3,3072]{2,1,0:T(4,128)S(1)} %collective-permute-done.xlo_ref) | copy-start | bytes 774148
  31.8 1.3 %copy-start.1 = (f32[7,3,3072]{2,1,0:T(4,128)}, f32[7,3,3072]{2,1,0:T(4,128)S(1)}, u32[]{:S(2)}) copy-start(f32[7,3,3072]{2,1,0:T(4,128)S(1)} %collective-permute-done.1.xhi_ref) | copy-start | bytes 774148

commit v12 on v11

--- a/solution.py
+++ b/solution.py
@@ -57,12 +57,12 @@
     return (growth - 1.0) / denominator, STRETCH_RATE * growth / (total_rows * denominator)
 
 
-def make_kernel(columns, length, planes, total_rows, dt):
+def make_kernel(columns, length, planes, total_rows, dt, targets):
     width = CHUNK + 2 * PAD
     face_area = STREAM_STEP * SPAN_STEP
     xrows = columns + 2 * XPAD
 
-    def kernel(state_ref, xlo_ref, xhi_ref, yhalo_ref, geo_ref, top_ref, height_ref,
+    def kernel(state_ref, xlo_ref, xhi_ref, yhalo_ref, geo_ref, before_ref, last_ref, height_ref,
                out_ref, shock_ref, qx_ref, qy_ref, pair_ref):
         col_dev = lax.axis_index("gx")
         first_row = lax.axis_index("gy") * (length // planes)
@@ -93,8 +93,12 @@
         height_row = geo_ref[xrows + 2 * columns:xrows + 3 * columns, :]
         group = lax.broadcasted_iota(jnp.int32, (columns, LANES), 1) // planes
         top = []
+        row_dev = lax.axis_index("gy")
+        hit = jnp.zeros((columns, LANES), jnp.bool_)
+        for target in targets:
+            hit = hit | (row_dev == target)
         for c in range(6):
-            held = top_ref[c]
+            held = jnp.where(hit, last_ref[c], before_ref[c])
             spread = jnp.where(group == 0, pltpu.roll(held, planes, 1),
                                jnp.where(group == 1, pltpu.roll(held, 2 * planes, 1),
                                          jnp.where(group == 2, pltpu.roll(held, 3 * planes, 1), held)))
@@ -192,10 +196,10 @@
     return kernel
 
 
-def update(state, xlo, xhi, yhalo, geo, top, height, planes, total_rows, dt):
+def update(state, xlo, xhi, yhalo, geo, top_before, top_last, height, targets, planes, total_rows, dt):
     columns = state.shape[1]
     length = state.shape[2]
-    kern = make_kernel(columns, length, planes, total_rows, dt)
+    kern = make_kernel(columns, length, planes, total_rows, dt, targets)
     vmem = pl.BlockSpec(memory_space=pltpu.VMEM)
     return pl.pallas_call(
         kern,
@@ -203,14 +207,14 @@
             jax.ShapeDtypeStruct((6, columns, length), jnp.float32),
             jax.ShapeDtypeStruct((columns, planes), jnp.float32),
         ),
-        in_specs=[vmem] * 7,
+        in_specs=[vmem] * 8,
         out_specs=(vmem, vmem),
         scratch_shapes=[
             pltpu.VMEM((6, columns + 2 * XPAD, length), jnp.float32),
             pltpu.VMEM((6, columns, length + 2 * PAD), jnp.float32),
             pltpu.VMEM((6, 6, columns + 2 * XPAD, CHUNK), jnp.float32),
         ],
-    )(state, xlo, xhi, yhalo, geo, top, height)
+    )(state, xlo, xhi, yhalo, geo, top_before, top_last, height)
 
 
 def shifted(block, axis, forward, cyclic=False):
@@ -226,6 +230,7 @@
 def broadcast(array, axis, holders, fanouts):
     count = lax.axis_size(axis)
     index = lax.axis_index(axis)
+    last = (array, array, [])
     for fanout in fanouts:
         if len(holders) >= count:
             break
@@ -239,6 +244,7 @@
             if not pairs:
                 break
             received = lax.ppermute(array, axis, pairs)
+            last = (arrived, received, [target for _, target in pairs])
             hit = jnp.zeros((), jnp.bool_)
             for _, target in pairs:
                 hit = hit | (index == target)
@@ -246,7 +252,7 @@
             reached = reached + [target for _, target in pairs]
         array = arrived
         holders = holders + reached
-    return array
+    return last
 
 
 def zshift(values, offset, planes):
@@ -379,7 +385,7 @@
 
     top_seed = jnp.where(row_dev == row_devs - 1, top_block, jnp.where(row_dev == 0, below, above))
     seeded = sorted({row_devs - 1, 0, max(row_devs - 2, 0)}, reverse=True)
-    top_held = broadcast(top_seed, "gy", seeded, (2, 1, 1, 1, 1))
+    top_before, top_last, last_targets = broadcast(top_seed, "gy", seeded, (2, 1, 1, 1, 1))
 
     blowing = wall_flux(wall_segment, segment_level, blow_table)
     wall_block = wall_ghosts(state[..., :band], blowing, planes)
@@ -408,8 +414,10 @@
         from_high,
         yhalo,
         geo,
-        top_held,
+        top_before,
+        top_last,
         shock_height,
+        tuple(last_targets),
         planes,
         total_rows,
         COURANT / total_rows,

time: 45.8 us -> 44.5 us (0.972)
  waiting for transfers between devices: 11 us -> 9.64 us
  other arithmetic: 3.79 us -> 3.15 us
  local copies, waits for them, and re-layouts: 3.18 us -> 3.8 us
    ppermute x3, waiting for transfers between devices: 11 us -> 9.63 us  [broadcast(): received = lax.ppermute(array, axis, pairs)]
    select_n x2 -> x1, other arithmetic: 0.65 us -> 0.01 us  [broadcast(): arrived = jnp.where(hit, received, arrived)]
    unnamed x15 -> x19, local copies, waits for them, and re-layouts: 0.11 us -> 0.73 us
  transfers between devices with their start and end apart: 7 -> 7, of which waited for: 1 -> 1; matrix products, arithmetic and copies ran while one was open for 13% -> 14% of each run, Pallas kernels for 0% -> 0%
where the time goes in v12:
time: 44.5 us; the launch traced here: 44 us
  starting transfers between devices  13.2 us (30%)
  Pallas kernels  12.3 us (28%)
  waiting for transfers between devices  9.64 us (22%)
  local copies, waits for them, and re-layouts  3.8 us (9%)
  other arithmetic  3.15 us (7%)
  between operations  1.03 us (2%)
  matrix products  0.86 us (2%)
    pallas_call x1, Pallas kernels, update(): pl.pallas_call(kern, out_shape=(jax.ShapeDtypeStruct((6, columns, length)...  12.3 us
    ppermute x4, starting transfers between devices, shifted(): return lax.ppermute(block, axis, pairs)  10.6 us
    ppermute x3, waiting for transfers between devices, broadcast(): received = lax.ppermute(array, axis, pairs)  9.63 us
    ppermute x3, starting transfers between devices, broadcast(): received = lax.ppermute(array, axis, pairs)  2.62 us
    slice x1, local copies, waits for them, and re-layouts, shards(): from_high = shifted(pack(state[:, :HALO], shock_height[:HALO]), 'gx', False)  1.35 us
    slice x1, local copies, waits for them, and re-layouts, wall_ghosts(): first_rows[..., 2 * planes:3 * planes]  1.01 us
    select_n x1, other arithmetic, shards(): jnp.where(row_dev == row_devs - 1, top_block, jnp.where(row_dev == 0, bel...  0.89 us
  transfers between devices with their start and end apart: 7, of which 1 were waited for; matrix products, arithmetic and copies ran while one was open for 14% of the time, Pallas kernels for 0%

profile of v12, /device:TPU:209, one launch (start us, length us, event | category | flops | bytes accessed | tf_op | source)
XLA Modules:
  0.0 44.0 jit_solution(1049111121934872072)
XLA Ops:
  0.7 0.8 %fusion.15 = (f32[6,16,128]{2,1,0:T(8,128)S(1)}, f32[6,16,128]{2,1,0:T(8,128)S(1)}) fusion(f32[6,16,3072]{2,1,0:T(8,128)} %state_ref.1, pred[128]{0:T(512)(128)(4,1)S(1)} %iota_compare_fusion.5), kind=kLoop, calls=%fused_computation.54 | loop fusion | flops 12288 | bytes 196736 | tf_op jit(solution)/shard_map/slice | solution.py:372
  1.5 1.3 %collective-permute-start.2 = (f32[6,16,128]{2,1,0:T(8,128)S(1)}, f32[6,16,128]{2,1,0:T(8,128)S(1)}, u32[]{:S(2)}, u32[]{:S(2)}) collective-permute-start(f32[6,16,128]{2,1,0:T(8,128)S(1)} %get-tuple-element.6), channel_id=1, source_target_pairs={{0,1},{1,2},{2,3},{3,4},{4,5},{5,6},{6,7},{7,8},{8,9},{9,10},{10,1... | collective-permute-start | bytes 147464 | tf_op jit(solution)/shard_map/ppermute | solution.py:227
  2.8 1.9 %collective-permute-start.3 = (f32[6,16,128]{2,1,0:T(8,128)S(1)}, f32[6,16,128]{2,1,0:T(8,128)S(1)}, u32[]{:S(2)}, u32[]{:S(2)}) collective-permute-start(f32[6,16,128]{2,1,0:T(8,128)S(1)} %get-tuple-element.7), channel_id=1, source_target_pairs={{1,0},{2,1},{3,2},{4,3},{5,4},{6,5},{7,6},{8,7},{9,8},{10,9},{11,1... | collective-permute-start | bytes 147464 | tf_op jit(solution)/shard_map/ppermute | solution.py:227
  4.7 1.3 %fusion.16 = (f32[6,3,3072]{2,1,0:T(4,128)S(1)}, f32[6,3,3072]{2,1,0:T(4,128)S(1)}) fusion(f32[6,16,3072]{2,1,0:T(8,128)} %state_ref.1), kind=kLoop, calls=%fused_computation.55 | loop fusion | bytes 884736 | tf_op jit(solution)/shard_map/slice | solution.py:370
  6.1 0.0 copy-start.6
  6.1 0.1 select_maximum_fusion.1
  6.2 3.1 %collective-permute-start = (f32[7,3,3072]{2,1,0:T(4,128)S(1)}, f32[7,3,3072]{2,1,0:T(4,128)S(1)}, u32[]{:S(2)}, u32[]{:S(2)}) collective-permute-start(f32[7,3,3072]{2,1,0:T(4,128)S(1)} %select_maximum_fusion.1), channel_id=1, source_target_pairs={{0,16},{16,32},{32,48},{48,64},{64,80},{80,96},{96,112},{112,128},... | collective-permute-start | bytes 774152 | tf_op jit(solution)/shard_map/ppermute | solution.py:227
  9.3 0.1 select_maximum_fusion
  9.4 4.3 %collective-permute-start.1 = (f32[7,3,3072]{2,1,0:T(4,128)S(1)}, f32[7,3,3072]{2,1,0:T(4,128)S(1)}, u32[]{:S(2)}, u32[]{:S(2)}) collective-permute-start(f32[7,3,3072]{2,1,0:T(4,128)S(1)} %select_maximum_fusion), channel_id=1, source_target_pairs={{16,0},{32,16},{48,32},{64,48},{80,64},{96,80},{112,96},{128,112},... | collective-permute-start | bytes 774152 | tf_op jit(solution)/shard_map/ppermute | solution.py:227
  13.7 0.1 copy.36
  13.8 1.0 %fusion.14 = (f32[6,16,32]{2,1,0:T(8,128)S(1)}, f32[6,16,32]{2,1,0:T(8,128)S(1)}, f32[6,16,32]{2,1,0:T(8,128)S(1)}, f32[6,16,32]{2,1,0:T(8,128)S(1)}) fusion(f32[6,16,3072]{2,1,0:T(8,128)} %state_ref.1), kind=kLoop, calls=%fused_computation.53 | loop fusion | bytes 98304 | tf_op jit(solution)/shard_map/slice | solution.py:324
  14.9 0.2 select_reduce_fusion.1
  15.0 0.1 iota_compare_fusion.3
  15.1 0.1 select_reduce_fusion
  15.3 0.1 mul.47
  15.3 0.1 pad_maximum_fusion.1
  15.6 0.1 tile.8
  15.8 0.9 %select_select_fusion.1 = (f32[6,16,128]{2,1,0:T(8,128)S(1)}, f32[1,6,16,128]{3,2,1,0:T(8,128)S(1)}, f32[1,6,16,128]{3,2,1,0:T(8,128)S(1)}) fusion(f32[6,16,128]{2,1,0:T(8,128)S(1)} %collective-permute-done.2, f32[6,16,128]{2,1,0:T(8,128)S(1)} %collective-permute-done.3, pred[]{:T(512)S(6)} %eq.89, pred[]{:T(512)S(6)} %eq.82, f32[6,16,3072]{2,1,0:T(8,128)} %state_ref.1, ...), kind=kLoop, calls=%fused_computation.9 | loop fusion | flops 61440 | bytes 393218 | tf_op jit(solution)/shard_map/jit(_where)/select_n | solution.py:386
  16.7 0.7 %collective-permute-start.5 = (f32[6,16,128]{2,1,0:T(8,128)S(1)}, f32[6,16,128]{2,1,0:T(8,128)S(1)}, u32[]{:S(2)}, u32[]{:S(2)}) collective-permute-start(f32[6,16,128]{2,1,0:T(8,128)S(1)} %get-tuple-element.10), channel_id=1, source_target_pairs={{15,1},{14,2},{0,3},{31,17},{30,18},{16,19},{47,33},{46,34},{32,35... | collective-permute-start | bytes 147464 | tf_op jit(solution)/shard_map/ppermute | solution.py:246
  17.4 0.7 %collective-permute-start.4 = (f32[6,16,128]{2,1,0:T(8,128)S(1)}, f32[6,16,128]{2,1,0:T(8,128)S(1)}, u32[]{:S(2)}, u32[]{:S(2)}) collective-permute-start(f32[6,16,128]{2,1,0:T(8,128)S(1)} %get-tuple-element.10), channel_id=1, source_target_pairs={{15,4},{14,5},{0,6},{31,20},{30,21},{16,22},{47,36},{46,37},{32,38... | collective-permute-start | bytes 147464 | tf_op jit(solution)/shard_map/ppermute | solution.py:246
  18.0 0.6 %pad_maximum_fusion.yhalo_ref = f32[2,6,16,128]{3,2,1,0:T(8,128)} fusion(f32[1,6,16,128]{3,2,1,0:T(8,128)S(1)} %get-tuple-element.11, f32[1,6,16,128]{3,2,1,0:T(8,128)S(1)} %get-tuple-element.12), kind=kLoop, calls=%fused_computation.4 | loop fusion | flops 24576 | bytes 196608 | tf_op jit(solution)/shard_map/stack | solution.py:398
  18.7 1.3 %collective-permute-start.6 = (f32[6,16,128]{2,1,0:T(8,128)S(1)}, f32[6,16,128]{2,1,0:T(8,128)S(1)}, u32[]{:S(2)}, u32[]{:S(2)}) collective-permute-start(f32[6,16,128]{2,1,0:T(8,128)S(1)} %select_select_fusion.before_ref), channel_id=1, source_target_pairs={{15,7},{14,8},{0,9},{1,10},{2,11},{3,12},{4,13},{31,23},{30,24},{1... | collective-permute-start | bytes 147464 | tf_op jit(solution)/shard_map/ppermute | solution.py:246
  20.0 0.1 copy.35
  20.2 0.1 copy.37
  20.2 0.1 fusion.2
  20.4 0.1 broadcast_in_dim.100
  20.4 0.1 broadcast_in_dim.104
  20.5 0.1 concatenate.59
  20.6 0.9 %fusion.9.geo_ref = f32[80,128]{1,0:T(8,128)} fusion(f32[80,32]{0,1:T(8,128)S(1)} %concatenate.59, s32[128]{0:T(128)S(1)} %and_select_fusion), kind=kOutput, calls=%fused_computation.28 | convolution fusion | flops 3936256 | bytes 51712 | tf_op jit(solution)/shard_map/dot_general | solution.py:349
  21.5 9.6 %collective-permute-done.6.last_ref = f32[6,16,128]{2,1,0:T(8,128)S(1)} collective-permute-done((f32[6,16,128]{2,1,0:T(8,128)S(1)}, f32[6,16,128]{2,1,0:T(8,128)S(1)}, u32[]{:S(2)}, u32[]{:S(2)}) %collective-permute-start.6) | collective-permute-done | bytes 49184 | tf_op jit(solution)/shard_map/ppermute | solution.py:246
  31.1 0.6 %copy-done.4 = f32[6,16,128]{2,1,0:T(8,128)} copy-done((f32[6,16,128]{2,1,0:T(8,128)}, f32[6,16,128]{2,1,0:T(8,128)S(1)}, u32[]{:S(2)}) %copy-start.4) | copy-done | bytes 49176
  31.7 12.3 %shard_map.68 = (f32[6,16,3072]{2,1,0:T(8,128)}, f32[16,32]{1,0:T(8,128)}) custom-call(f32[6,16,3072]{2,1,0:T(8,128)} %state_ref.1, f32[7,3,3072]{2,1,0:T(4,128)} %copy-done, f32[7,3,3072]{2,1,0:T(4,128)} %copy-done.1, f32[2,6,16,128]{3,2,1,0:T(8,128)} %pad_maximum_fusion.yhalo_ref, f32[80,128]{1,0:T(8,128)} %fusion.9.geo_ref, f32[6,16,128]{2,1,0:T(8,128)} %copy-done.2, ...), custom_call_target="tpu_custom_call" | custom-call | tf_op jit(solution)/shard_map/pallas_call | solution.py:204
  (42 shorter events, 0.2 us)
Async XLA Ops:
  0.6 5.4 %copy-start.3 = (f32[16,32]{1,0:T(8,128)S(1)}, f32[16,32]{1,0:T(8,128)}, u32[]{:S(2)}) copy-start(f32[16,32]{1,0:T(8,128)} %height_ref.1) | copy-start | bytes 6148
  1.5 14.3 %collective-permute-start.2 = (f32[6,16,128]{2,1,0:T(8,128)S(1)}, f32[6,16,128]{2,1,0:T(8,128)S(1)}, u32[]{:S(2)}, u32[]{:S(2)}) collective-permute-start(f32[6,16,128]{2,1,0:T(8,128)S(1)} %get-tuple-element.6), channel_id=1, source_target_pairs={{0,1},{1,2},{2,3},{3,4},{4,5},{5,6},{6,7},{7,8},{8,9},{9,10},{10,1... | collective-permute-start | bytes 147464 | tf_op jit(solution)/shard_map/ppermute | solution.py:227
  2.8 13.0 %collective-permute-start.3 = (f32[6,16,128]{2,1,0:T(8,128)S(1)}, f32[6,16,128]{2,1,0:T(8,128)S(1)}, u32[]{:S(2)}, u32[]{:S(2)}) collective-permute-start(f32[6,16,128]{2,1,0:T(8,128)S(1)} %get-tuple-element.7), channel_id=1, source_target_pairs={{1,0},{2,1},{3,2},{4,3},{5,4},{6,5},{7,6},{8,7},{9,8},{10,9},{11,1... | collective-permute-start | bytes 147464 | tf_op jit(solution)/shard_map/ppermute | solution.py:227
  6.1 8.8 %copy-start.6 = (s32[16]{0:T(128)S(1)}, s32[16]{0:T(128)}, u32[]{:S(2)}) copy-start(s32[16]{0:T(128)} %param.8) | copy-start | bytes 196
  6.1 8.8 %copy-start.7 = (s32[16]{0:T(128)S(1)}, s32[16]{0:T(128)}, u32[]{:S(2)}) copy-start(s32[16]{0:T(128)} %param.7) | copy-start | bytes 196
  6.1 9.0 %copy-start.5 = (f32[16,32]{1,0:T(8,128)S(1)}, f32[16,32]{1,0:T(8,128)}, u32[]{:S(2)}) copy-start(f32[16,32]{1,0:T(8,128)} %param.9) | copy-start | bytes 6148
  6.2 13.8 %collective-permute-start = (f32[7,3,3072]{2,1,0:T(4,128)S(1)}, f32[7,3,3072]{2,1,0:T(4,128)S(1)}, u32[]{:S(2)}, u32[]{:S(2)}) collective-permute-start(f32[7,3,3072]{2,1,0:T(4,128)S(1)} %select_maximum_fusion.1), channel_id=1, source_target_pairs={{0,16},{16,32},{32,48},{48,64},{64,80},{80,96},{96,112},{112,128},... | collective-permute-start | bytes 774152 | tf_op jit(solution)/shard_map/ppermute | solution.py:227
  9.4 10.7 %collective-permute-start.1 = (f32[7,3,3072]{2,1,0:T(4,128)S(1)}, f32[7,3,3072]{2,1,0:T(4,128)S(1)}, u32[]{:S(2)}, u32[]{:S(2)}) collective-permute-start(f32[7,3,3072]{2,1,0:T(4,128)S(1)} %select_maximum_fusion), channel_id=1, source_target_pairs={{16,0},{32,16},{48,32},{64,48},{80,64},{96,80},{112,96},{128,112},... | collective-permute-start | bytes 774152 | tf_op jit(solution)/shard_map/ppermute | solution.py:227
  16.7 2.0 %collective-permute-start.5 = (f32[6,16,128]{2,1,0:T(8,128)S(1)}, f32[6,16,128]{2,1,0:T(8,128)S(1)}, u32[]{:S(2)}, u32[]{:S(2)}) collective-permute-start(f32[6,16,128]{2,1,0:T(8,128)S(1)} %get-tuple-element.10), channel_id=1, source_target_pairs={{15,1},{14,2},{0,3},{31,17},{30,18},{16,19},{47,33},{46,34},{32,35... | collective-permute-start | bytes 147464 | tf_op jit(solution)/shard_map/ppermute | solution.py:246
  17.4 1.3 %collective-permute-start.4 = (f32[6,16,128]{2,1,0:T(8,128)S(1)}, f32[6,16,128]{2,1,0:T(8,128)S(1)}, u32[]{:S(2)}, u32[]{:S(2)}) collective-permute-start(f32[6,16,128]{2,1,0:T(8,128)S(1)} %get-tuple-element.10), channel_id=1, source_target_pairs={{15,4},{14,5},{0,6},{31,20},{30,21},{16,22},{47,36},{46,37},{32,38... | collective-permute-start | bytes 147464 | tf_op jit(solution)/shard_map/ppermute | solution.py:246
  18.7 12.4 %copy-start.2 = (f32[6,16,128]{2,1,0:T(8,128)}, f32[6,16,128]{2,1,0:T(8,128)S(1)}, u32[]{:S(2)}) copy-start(f32[6,16,128]{2,1,0:T(8,128)S(1)} %select_select_fusion.before_ref) | copy-start | bytes 147460
  18.7 12.4 %collective-permute-start.6 = (f32[6,16,128]{2,1,0:T(8,128)S(1)}, f32[6,16,128]{2,1,0:T(8,128)S(1)}, u32[]{:S(2)}, u32[]{:S(2)}) collective-permute-start(f32[6,16,128]{2,1,0:T(8,128)S(1)} %select_select_fusion.before_ref), channel_id=1, source_target_pairs={{15,7},{14,8},{0,9},{1,10},{2,11},{3,12},{4,13},{31,23},{30,24},{1... | collective-permute-start | bytes 147464 | tf_op jit(solution)/shard_map/ppermute | solution.py:246
  20.0 11.1 %copy-start = (f32[7,3,3072]{2,1,0:T(4,128)}, f32[7,3,3072]{2,1,0:T(4,128)S(1)}, u32[]{:S(2)}) copy-start(f32[7,3,3072]{2,1,0:T(4,128)S(1)} %collective-permute-done.xlo_ref) | copy-start | bytes 774148
  20.1 11.0 %copy-start.1 = (f32[7,3,3072]{2,1,0:T(4,128)}, f32[7,3,3072]{2,1,0:T(4,128)S(1)}, u32[]{:S(2)}) copy-start(f32[7,3,3072]{2,1,0:T(4,128)S(1)} %collective-permute-done.1.xhi_ref) | copy-start | bytes 774148
  31.1 0.6 %copy-start.4 = (f32[6,16,128]{2,1,0:T(8,128)}, f32[6,16,128]{2,1,0:T(8,128)S(1)}, u32[]{:S(2)}) copy-start(f32[6,16,128]{2,1,0:T(8,128)S(1)} %collective-permute-done.6.last_ref) | copy-start | bytes 147460

commit v13 on v12

--- a/solution.py
+++ b/solution.py
@@ -384,6 +384,7 @@
     slope_x, slope_z = slopes(height_ext, planes)
 
     top_seed = jnp.where(row_dev == row_devs - 1, top_block, jnp.where(row_dev == 0, below, above))
+    top_seed, below, above = lax.optimization_barrier((top_seed, below, above))
     seeded = sorted({row_devs - 1, 0, max(row_devs - 2, 0)}, reverse=True)
     top_before, top_last, last_targets = broadcast(top_seed, "gy", seeded, (2, 1, 1, 1, 1))
 

time: 44.5 us -> 44.2 us (level)
  the two profiles are of different devices: /device:TPU:209 before, /device:TPU:113 now
where the time goes in v13:
time: 44.2 us; the launch traced here: 43.7 us
  starting transfers between devices  15.3 us (35%)
  Pallas kernels  12.3 us (28%)
  waiting for transfers between devices  7.22 us (16%)
  local copies, waits for them, and re-layouts  3.79 us (9%)
  other arithmetic  3.16 us (7%)
  between operations  1.04 us (2%)
  matrix products  0.86 us (2%)
    ppermute x4, starting transfers between devices, shifted(): return lax.ppermute(block, axis, pairs)  12.7 us
    pallas_call x1, Pallas kernels, update(): pl.pallas_call(kern, out_shape=(jax.ShapeDtypeStruct((6, columns, length)...  12.3 us
    ppermute x3, waiting for transfers between devices, broadcast(): received = lax.ppermute(array, axis, pairs)  7.21 us
    ppermute x3, starting transfers between devices, broadcast(): received = lax.ppermute(array, axis, pairs)  2.62 us
    slice x1, local copies, waits for them, and re-layouts, shards(): from_high = shifted(pack(state[:, :HALO], shock_height[:HALO]), 'gx', False)  1.35 us
    slice x1, local copies, waits for them, and re-layouts, wall_ghosts(): first_rows[..., 2 * planes:3 * planes]  1.01 us
  transfers between devices with their start and end apart: 7, of which 1 were waited for; matrix products, arithmetic and copies ran while one was open for 14% of the time, Pallas kernels for 0%

profile of v13, /device:TPU:113, one launch (start us, length us, event | category | flops | bytes accessed | tf_op | source)
XLA Modules:
  0.0 43.7 jit_solution(1404352562768588381)
XLA Ops:
  0.7 0.8 %slice_select_fusion = (f32[6,16,128]{2,1,0:T(8,128)S(1)}, f32[6,16,128]{2,1,0:T(8,128)S(1)}) fusion(f32[6,16,3072]{2,1,0:T(8,128)} %state_ref.1, pred[128]{0:T(512)(128)(4,1)S(1)} %iota_compare_fusion.5), kind=kLoop, calls=%fused_computation.11 | loop fusion | flops 12288 | bytes 196736 | tf_op jit(solution)/shard_map/jit(_where)/select_n | solution.py:374
  1.5 2.6 %collective-permute-start.3 = (f32[6,16,128]{2,1,0:T(8,128)S(1)}, f32[6,16,128]{2,1,0:T(8,128)S(1)}, u32[]{:S(2)}, u32[]{:S(2)}) collective-permute-start(f32[6,16,128]{2,1,0:T(8,128)S(1)} %get-tuple-element.12), channel_id=1, source_target_pairs={{1,0},{2,1},{3,2},{4,3},{5,4},{6,5},{7,6},{8,7},{9,8},{10,9},{11,1... | collective-permute-start | bytes 147464 | tf_op jit(solution)/shard_map/ppermute | solution.py:227
  4.1 2.8 %collective-permute-start.2 = (f32[6,16,128]{2,1,0:T(8,128)S(1)}, f32[6,16,128]{2,1,0:T(8,128)S(1)}, u32[]{:S(2)}, u32[]{:S(2)}) collective-permute-start(f32[6,16,128]{2,1,0:T(8,128)S(1)} %get-tuple-element.13), channel_id=1, source_target_pairs={{0,1},{1,2},{2,3},{3,4},{4,5},{5,6},{6,7},{7,8},{8,9},{9,10},{10,1... | collective-permute-start | bytes 147464 | tf_op jit(solution)/shard_map/ppermute | solution.py:227
  6.8 1.3 %fusion.15 = (f32[6,3,3072]{2,1,0:T(4,128)S(1)}, f32[6,3,3072]{2,1,0:T(4,128)S(1)}) fusion(f32[6,16,3072]{2,1,0:T(8,128)} %state_ref.1), kind=kLoop, calls=%fused_computation.54 | loop fusion | bytes 884736 | tf_op jit(solution)/shard_map/slice | solution.py:370
  8.2 0.1 select_maximum_fusion.1
  8.3 3.1 %collective-permute-start = (f32[7,3,3072]{2,1,0:T(4,128)S(1)}, f32[7,3,3072]{2,1,0:T(4,128)S(1)}, u32[]{:S(2)}, u32[]{:S(2)}) collective-permute-start(f32[7,3,3072]{2,1,0:T(4,128)S(1)} %select_maximum_fusion.1), channel_id=1, source_target_pairs={{0,16},{16,32},{32,48},{48,64},{64,80},{80,96},{96,112},{112,128},... | collective-permute-start | bytes 774152 | tf_op jit(solution)/shard_map/ppermute | solution.py:227
  11.4 0.1 select_maximum_fusion
  11.5 4.3 %collective-permute-start.1 = (f32[7,3,3072]{2,1,0:T(4,128)S(1)}, f32[7,3,3072]{2,1,0:T(4,128)S(1)}, u32[]{:S(2)}, u32[]{:S(2)}) collective-permute-start(f32[7,3,3072]{2,1,0:T(4,128)S(1)} %select_maximum_fusion), channel_id=1, source_target_pairs={{16,0},{32,16},{48,32},{64,48},{80,64},{96,80},{112,96},{128,112},... | collective-permute-start | bytes 774152 | tf_op jit(solution)/shard_map/ppermute | solution.py:227
  15.8 0.1 copy.36
  15.9 1.0 %fusion.14 = (f32[6,16,32]{2,1,0:T(8,128)S(1)}, f32[6,16,32]{2,1,0:T(8,128)S(1)}, f32[6,16,32]{2,1,0:T(8,128)S(1)}, f32[6,16,32]{2,1,0:T(8,128)S(1)}) fusion(f32[6,16,3072]{2,1,0:T(8,128)} %state_ref.1), kind=kLoop, calls=%fused_computation.53 | loop fusion | bytes 98304 | tf_op jit(solution)/shard_map/slice | solution.py:324
  17.0 0.2 select_reduce_fusion.1
  17.2 0.1 iota_compare_fusion.3
  17.2 0.1 select_reduce_fusion
  17.4 0.1 mul.47
  17.5 0.1 pad_maximum_fusion.1
  17.7 0.1 tile.8
  17.9 0.8 %select_select_fusion.1 = f32[6,16,128]{2,1,0:T(8,128)S(1)} fusion(f32[6,16,128]{2,1,0:T(8,128)S(1)} %collective-permute-done.2, f32[6,16,128]{2,1,0:T(8,128)S(1)} %collective-permute-done.3, pred[]{:T(512)S(6)} %eq.89, pred[]{:T(512)S(6)} %eq.82, f32[6,16,3072]{2,1,0:T(8,128)} %state_ref.1), kind=kLoop, calls=%fused_computation.10 | loop fusion | flops 24576 | bytes 196610 | tf_op jit(solution)/shard_map/jit(_where)/select_n | solution.py:386
  18.7 0.7 %collective-permute-start.5 = (f32[6,16,128]{2,1,0:T(8,128)S(1)}, f32[6,16,128]{2,1,0:T(8,128)S(1)}, u32[]{:S(2)}, u32[]{:S(2)}) collective-permute-start(f32[6,16,128]{2,1,0:T(8,128)S(1)} %select_select_fusion.1), channel_id=1, source_target_pairs={{15,1},{14,2},{0,3},{31,17},{30,18},{16,19},{47,33},{46,34},{32,35... | collective-permute-start | bytes 147464 | tf_op jit(solution)/shard_map/ppermute | solution.py:246
  19.4 0.7 %collective-permute-start.4 = (f32[6,16,128]{2,1,0:T(8,128)S(1)}, f32[6,16,128]{2,1,0:T(8,128)S(1)}, u32[]{:S(2)}, u32[]{:S(2)}) collective-permute-start(f32[6,16,128]{2,1,0:T(8,128)S(1)} %select_select_fusion.1), channel_id=1, source_target_pairs={{15,4},{14,5},{0,6},{31,20},{30,21},{16,22},{47,36},{46,37},{32,38... | collective-permute-start | bytes 147464 | tf_op jit(solution)/shard_map/ppermute | solution.py:246
  20.1 0.1 fusion
  20.2 0.6 %pad_maximum_fusion.yhalo_ref = f32[2,6,16,128]{3,2,1,0:T(8,128)} fusion(f32[1,6,16,128]{3,2,1,0:T(8,128)S(1)} %get-tuple-element.29, f32[1,6,16,128]{3,2,1,0:T(8,128)S(1)} %get-tuple-element.28), kind=kLoop, calls=%fused_computation.4 | loop fusion | flops 24576 | bytes 196608 | tf_op jit(solution)/shard_map/stack | solution.py:399
  20.8 1.3 %collective-permute-start.6 = (f32[6,16,128]{2,1,0:T(8,128)S(1)}, f32[6,16,128]{2,1,0:T(8,128)S(1)}, u32[]{:S(2)}, u32[]{:S(2)}) collective-permute-start(f32[6,16,128]{2,1,0:T(8,128)S(1)} %select_select_fusion.before_ref), channel_id=1, source_target_pairs={{15,7},{14,8},{0,9},{1,10},{2,11},{3,12},{4,13},{31,23},{30,24},{1... | collective-permute-start | bytes 147464 | tf_op jit(solution)/shard_map/ppermute | solution.py:246
  22.2 0.1 copy.35
  22.3 0.1 copy.37
  22.4 0.1 fusion.2
  22.5 0.1 broadcast_in_dim.100
  22.6 0.1 broadcast_in_dim.104
  22.6 0.1 concatenate.59
  22.7 0.9 %fusion.9.geo_ref = f32[80,128]{1,0:T(8,128)} fusion(f32[80,32]{0,1:T(8,128)S(1)} %concatenate.59, s32[128]{0:T(128)S(1)} %and_select_fusion), kind=kOutput, calls=%fused_computation.28 | convolution fusion | flops 3936256 | bytes 51712 | tf_op jit(solution)/shard_map/dot_general | solution.py:349
  23.6 7.2 %collective-permute-done.6.last_ref = f32[6,16,128]{2,1,0:T(8,128)S(1)} collective-permute-done((f32[6,16,128]{2,1,0:T(8,128)S(1)}, f32[6,16,128]{2,1,0:T(8,128)S(1)}, u32[]{:S(2)}, u32[]{:S(2)}) %collective-permute-start.6) | collective-permute-done | bytes 49184 | tf_op jit(solution)/shard_map/ppermute | solution.py:246
  30.8 0.6 %copy-done.4 = f32[6,16,128]{2,1,0:T(8,128)} copy-done((f32[6,16,128]{2,1,0:T(8,128)}, f32[6,16,128]{2,1,0:T(8,128)S(1)}, u32[]{:S(2)}) %copy-start.4) | copy-done | bytes 49176
  31.4 12.3 %shard_map.68 = (f32[6,16,3072]{2,1,0:T(8,128)}, f32[16,32]{1,0:T(8,128)}) custom-call(f32[6,16,3072]{2,1,0:T(8,128)} %state_ref.1, f32[7,3,3072]{2,1,0:T(4,128)} %copy-done, f32[7,3,3072]{2,1,0:T(4,128)} %copy-done.1, f32[2,6,16,128]{3,2,1,0:T(8,128)} %pad_maximum_fusion.yhalo_ref, f32[80,128]{1,0:T(8,128)} %fusion.9.geo_ref, f32[6,16,128]{2,1,0:T(8,128)} %copy-done.2, ...), custom_call_target="tpu_custom_call" | custom-call | tf_op jit(solution)/shard_map/pallas_call | solution.py:204
  (43 shorter events, 0.2 us)
Async XLA Ops:
  0.6 7.6 %copy-start.3 = (f32[16,32]{1,0:T(8,128)S(1)}, f32[16,32]{1,0:T(8,128)}, u32[]{:S(2)}) copy-start(f32[16,32]{1,0:T(8,128)} %height_ref.1) | copy-start | bytes 6148
  1.5 16.4 %collective-permute-start.3 = (f32[6,16,128]{2,1,0:T(8,128)S(1)}, f32[6,16,128]{2,1,0:T(8,128)S(1)}, u32[]{:S(2)}, u32[]{:S(2)}) collective-permute-start(f32[6,16,128]{2,1,0:T(8,128)S(1)} %get-tuple-element.12), channel_id=1, source_target_pairs={{1,0},{2,1},{3,2},{4,3},{5,4},{6,5},{7,6},{8,7},{9,8},{10,9},{11,1... | collective-permute-start | bytes 147464 | tf_op jit(solution)/shard_map/ppermute | solution.py:227
  4.1 13.8 %collective-permute-start.2 = (f32[6,16,128]{2,1,0:T(8,128)S(1)}, f32[6,16,128]{2,1,0:T(8,128)S(1)}, u32[]{:S(2)}, u32[]{:S(2)}) collective-permute-start(f32[6,16,128]{2,1,0:T(8,128)S(1)} %get-tuple-element.13), channel_id=1, source_target_pairs={{0,1},{1,2},{2,3},{3,4},{4,5},{5,6},{6,7},{7,8},{8,9},{9,10},{10,1... | collective-permute-start | bytes 147464 | tf_op jit(solution)/shard_map/ppermute | solution.py:227
  8.2 8.8 %copy-start.6 = (s32[16]{0:T(128)S(1)}, s32[16]{0:T(128)}, u32[]{:S(2)}) copy-start(s32[16]{0:T(128)} %param.8) | copy-start | bytes 196
  8.2 8.8 %copy-start.7 = (s32[16]{0:T(128)S(1)}, s32[16]{0:T(128)}, u32[]{:S(2)}) copy-start(s32[16]{0:T(128)} %param.7) | copy-start | bytes 196
  8.2 9.0 %copy-start.5 = (f32[16,32]{1,0:T(8,128)S(1)}, f32[16,32]{1,0:T(8,128)}, u32[]{:S(2)}) copy-start(f32[16,32]{1,0:T(8,128)} %param.9) | copy-start | bytes 6148
  8.3 13.8 %collective-permute-start = (f32[7,3,3072]{2,1,0:T(4,128)S(1)}, f32[7,3,3072]{2,1,0:T(4,128)S(1)}, u32[]{:S(2)}, u32[]{:S(2)}) collective-permute-start(f32[7,3,3072]{2,1,0:T(4,128)S(1)} %select_maximum_fusion.1), channel_id=1, source_target_pairs={{0,16},{16,32},{32,48},{48,64},{64,80},{80,96},{96,112},{112,128},... | collective-permute-start | bytes 774152 | tf_op jit(solution)/shard_map/ppermute | solution.py:227
  11.5 10.7 %collective-permute-start.1 = (f32[7,3,3072]{2,1,0:T(4,128)S(1)}, f32[7,3,3072]{2,1,0:T(4,128)S(1)}, u32[]{:S(2)}, u32[]{:S(2)}) collective-permute-start(f32[7,3,3072]{2,1,0:T(4,128)S(1)} %select_maximum_fusion), channel_id=1, source_target_pairs={{16,0},{32,16},{48,32},{64,48},{80,64},{96,80},{112,96},{128,112},... | collective-permute-start | bytes 774152 | tf_op jit(solution)/shard_map/ppermute | solution.py:227
  18.7 2.1 %collective-permute-start.5 = (f32[6,16,128]{2,1,0:T(8,128)S(1)}, f32[6,16,128]{2,1,0:T(8,128)S(1)}, u32[]{:S(2)}, u32[]{:S(2)}) collective-permute-start(f32[6,16,128]{2,1,0:T(8,128)S(1)} %select_select_fusion.1), channel_id=1, source_target_pairs={{15,1},{14,2},{0,3},{31,17},{30,18},{16,19},{47,33},{46,34},{32,35... | collective-permute-start | bytes 147464 | tf_op jit(solution)/shard_map/ppermute | solution.py:246
  19.4 1.4 %collective-permute-start.4 = (f32[6,16,128]{2,1,0:T(8,128)S(1)}, f32[6,16,128]{2,1,0:T(8,128)S(1)}, u32[]{:S(2)}, u32[]{:S(2)}) collective-permute-start(f32[6,16,128]{2,1,0:T(8,128)S(1)} %select_select_fusion.1), channel_id=1, source_target_pairs={{15,4},{14,5},{0,6},{31,20},{30,21},{16,22},{47,36},{46,37},{32,38... | collective-permute-start | bytes 147464 | tf_op jit(solution)/shard_map/ppermute | solution.py:246
  20.8 10.0 %copy-start.2 = (f32[6,16,128]{2,1,0:T(8,128)}, f32[6,16,128]{2,1,0:T(8,128)S(1)}, u32[]{:S(2)}) copy-start(f32[6,16,128]{2,1,0:T(8,128)S(1)} %select_select_fusion.before_ref) | copy-start | bytes 147460
  20.8 10.0 %collective-permute-start.6 = (f32[6,16,128]{2,1,0:T(8,128)S(1)}, f32[6,16,128]{2,1,0:T(8,128)S(1)}, u32[]{:S(2)}, u32[]{:S(2)}) collective-permute-start(f32[6,16,128]{2,1,0:T(8,128)S(1)} %select_select_fusion.before_ref), channel_id=1, source_target_pairs={{15,7},{14,8},{0,9},{1,10},{2,11},{3,12},{4,13},{31,23},{30,24},{1... | collective-permute-start | bytes 147464 | tf_op jit(solution)/shard_map/ppermute | solution.py:246
  22.1 8.7 %copy-start = (f32[7,3,3072]{2,1,0:T(4,128)}, f32[7,3,3072]{2,1,0:T(4,128)S(1)}, u32[]{:S(2)}) copy-start(f32[7,3,3072]{2,1,0:T(4,128)S(1)} %collective-permute-done.xlo_ref) | copy-start | bytes 774148
  22.3 8.5 %copy-start.1 = (f32[7,3,3072]{2,1,0:T(4,128)}, f32[7,3,3072]{2,1,0:T(4,128)S(1)}, u32[]{:S(2)}) copy-start(f32[7,3,3072]{2,1,0:T(4,128)S(1)} %collective-permute-done.1.xhi_ref) | copy-start | bytes 774148
  30.8 0.6 %copy-start.4 = (f32[6,16,128]{2,1,0:T(8,128)}, f32[6,16,128]{2,1,0:T(8,128)S(1)}, u32[]{:S(2)}) copy-start(f32[6,16,128]{2,1,0:T(8,128)S(1)} %collective-permute-done.6.last_ref) | copy-start | bytes 147460

commit v14 on v13

--- a/solution.py
+++ b/solution.py
@@ -63,29 +63,15 @@
     xrows = columns + 2 * XPAD
 
     def kernel(state_ref, xlo_ref, xhi_ref, yhalo_ref, geo_ref, before_ref, last_ref, height_ref,
-               out_ref, shock_ref, qx_ref, qy_ref, pair_ref):
+               out_ref, shock_ref, qy_ref, pair_ref):
         col_dev = lax.axis_index("gx")
         first_row = lax.axis_index("gy") * (length // planes)
         for c in range(6):
-            qx_ref[c, 0:XPAD, :] = state_ref[c, 0:XPAD, :]
-            qx_ref[c, XPAD:XPAD + columns, :] = state_ref[c]
-            qx_ref[c, XPAD + columns:, :] = state_ref[c, columns - XPAD:, :]
-            qx_ref[c, XPAD - HALO:XPAD, :] = xlo_ref[c]
-            qx_ref[c, XPAD + columns:XPAD + columns + HALO, :] = xhi_ref[c]
             qy_ref[c, :, 0:PAD] = yhalo_ref[0, c]
             qy_ref[c, :, PAD:PAD + length] = state_ref[c]
-            qy_ref[c, :, PAD + length:] = yhalo_ref[1, c, :, 0:PAD]
-
-        @pl.when(col_dev == 0)
-        def _():
-            for c in range(6):
-                qx_ref[c, XPAD - HALO:XPAD, :] = jnp.broadcast_to(state_ref[c, 0:1, :], (HALO, length))
-
-        @pl.when(col_dev == lax.axis_size("gx") - 1)
-        def _():
-            for c in range(6):
-                qx_ref[c, XPAD + columns:XPAD + columns + HALO, :] = jnp.broadcast_to(
-                    state_ref[c, columns - 1:columns, :], (HALO, length))
+            qy_ref[c, :, PAD + length:] = yhalo_ref[1, c]
+        first_col = col_dev == 0
+        last_col = col_dev == lax.axis_size("gx") - 1
 
         height_x = lane_tile(geo_ref[0:xrows, :], CHUNK)
         slope_x_row = geo_ref[xrows:xrows + columns, :]
@@ -120,7 +106,14 @@
             spacing = stretch_factors(rows_in, total_rows)[1]
             rows_out = (first_row - PAD // planes + (o + lane_out) // planes).astype(jnp.float32)
             eta = stretch_factors(rows_out, total_rows)[0]
-            xa = [qx_ref[c, :, pl.ds(o, CHUNK)] for c in range(6)]
+            xa = []
+            for c in range(6):
+                mid = state_ref[c, :, pl.ds(o, CHUNK)]
+                low = jnp.where(first_col, jnp.broadcast_to(mid[0:1], (XPAD, CHUNK)),
+                                xlo_ref[c, :, pl.ds(o, CHUNK)])
+                high = jnp.where(last_col, jnp.broadcast_to(mid[columns - 1:columns], (XPAD, CHUNK)),
+                                 xhi_ref[c, :, pl.ds(o, CHUNK)])
+                xa.append(jnp.concatenate([low, mid, high], axis=0))
             inverse, vel_x, vel_y, vel_z, stress, sound = kernel_primitives(xa)
             metric = STREAM_STEP * height_x * spacing
             fluxes = [xa[1], xa[1] * vel_x + stress, xa[2] * vel_x, xa[3] * vel_x,
@@ -210,7 +203,6 @@
         in_specs=[vmem] * 8,
         out_specs=(vmem, vmem),
         scratch_shapes=[
-            pltpu.VMEM((6, columns + 2 * XPAD, length), jnp.float32),
             pltpu.VMEM((6, columns, length + 2 * PAD), jnp.float32),
             pltpu.VMEM((6, 6, columns + 2 * XPAD, CHUNK), jnp.float32),
         ],
@@ -361,24 +353,27 @@
     total_rows = row_count * row_devs
     band = HALO * planes
 
-    def pack(cols, heights):
-        extra = jnp.zeros((1, HALO, length), jnp.float32)
-        extra = lax.dynamic_update_slice(extra, heights[None], (0, 0, 0))
-        return jnp.concatenate([cols, extra], axis=0)
-
-    from_low = shifted(pack(state[:, columns - HALO :], shock_height[columns - HALO :]), "gx", True)
-    from_high = shifted(pack(state[:, :HALO], shock_height[:HALO]), "gx", False)
+    from_low = shifted(
+        lax.dynamic_update_slice(state[:, columns - XPAD :], shock_height[columns - HALO :][None], (0, 0, 0)),
+        "gx",
+        True,
+    )
+    from_high = shifted(
+        lax.dynamic_update_slice(state[:, :XPAD], shock_height[:HALO][None], (0, XPAD - HALO, 0)),
+        "gx",
+        False,
+    )
     plane_lane = jnp.arange(PAD, dtype=jnp.int32)[None, None, :]
     top_block = state[..., length - PAD :]
     below = shifted(top_block, "gy", True, cyclic=True)
     above = shifted(jnp.where(plane_lane < band, state[..., :PAD], top_block), "gy", False)
     low_height = jnp.where(
-        col_dev == 0, jnp.broadcast_to(shock_height[:1], (HALO, planes)), from_low[6, :, :planes]
+        col_dev == 0, jnp.broadcast_to(shock_height[:1], (HALO, planes)), from_low[0, :HALO, :planes]
     )
     high_height = jnp.where(
         col_dev == col_devs - 1,
         jnp.broadcast_to(shock_height[columns - 1 :], (HALO, planes)),
-        from_high[6, :, :planes],
+        from_high[0, XPAD - HALO :, :planes],
     )
     height_ext = jnp.concatenate([low_height, shock_height, high_height], axis=0)
     slope_x, slope_z = slopes(height_ext, planes)

time: 44.2 us -> 44.7 us (1.011)
  local copies, waits for them, and re-layouts: 3.79 us -> 4.6 us
    ppermute x4, waiting for transfers between devices: 0.01 us -> 5.14 us  [shifted(): return lax.ppermute(block, axis, pairs)]
    ppermute x3, waiting for transfers between devices: 7.21 us -> 2.13 us  [broadcast(): received = lax.ppermute(array, axis, pairs)]
    dynamic_update_slice x0 -> x2, local copies, waits for them, and re-layouts: none -> 0.74 us  [the longest x1 0.37 us: shards(): lax.dynamic_update_slice(state[:, columns - XPAD:], shock_height[columns...]
  transfers between devices with their start and end apart: 7 -> 7, of which waited for: 1 -> 3; matrix products, arithmetic and copies ran while one was open for 14% -> 16% of each run, Pallas kernels for 0% -> 0%
where the time goes in v14:
time: 44.7 us; the launch traced here: 44.3 us
  starting transfers between devices  15.3 us (34%)
  Pallas kernels  12.2 us (27%)
  waiting for transfers between devices  7.27 us (16%)
  local copies, waits for them, and re-layouts  4.6 us (10%)
  other arithmetic  3 us (7%)
  between operations  1 us (2%)
  matrix products  0.85 us (2%)
    ppermute x4, starting transfers between devices, shifted(): return lax.ppermute(block, axis, pairs)  12.7 us
    pallas_call x1, Pallas kernels, update(): pl.pallas_call(kern, out_shape=(jax.ShapeDtypeStruct((6, columns, length)...  12.2 us
    ppermute x4, waiting for transfers between devices, shifted(): return lax.ppermute(block, axis, pairs)  5.14 us
    ppermute x3, starting transfers between devices, broadcast(): received = lax.ppermute(array, axis, pairs)  2.62 us
    ppermute x3, waiting for transfers between devices, broadcast(): received = lax.ppermute(array, axis, pairs)  2.13 us
    slice x1, local copies, waits for them, and re-layouts, shards(): state[:, :XPAD]  1.32 us
    slice x1, local copies, waits for them, and re-layouts, wall_ghosts(): first_rows[..., 2 * planes:3 * planes]  1.09 us
  transfers between devices with their start and end apart: 7, of which 3 were waited for; matrix products, arithmetic and copies ran while one was open for 16% of the time, Pallas kernels for 0%

profile of v14, /device:TPU:113, one launch (start us, length us, event | category | flops | bytes accessed | tf_op | source)
XLA Modules:
  0.0 44.3 jit_solution(7174916871839718869)
XLA Ops:
  0.6 0.8 %slice_select_fusion = (f32[6,16,128]{2,1,0:T(8,128)S(1)}, f32[6,16,128]{2,1,0:T(8,128)S(1)}) fusion(f32[6,16,3072]{2,1,0:T(8,128)} %state_ref.1, pred[128]{0:T(512)(128)(4,1)S(1)} %iota_compare_fusion.4), kind=kLoop, calls=%fused_computation.8 | loop fusion | flops 12288 | bytes 196736 | tf_op jit(solution)/shard_map/jit(_where)/select_n | solution.py:369
  1.5 2.6 %collective-permute-start.3 = (f32[6,16,128]{2,1,0:T(8,128)S(1)}, f32[6,16,128]{2,1,0:T(8,128)S(1)}, u32[]{:S(2)}, u32[]{:S(2)}) collective-permute-start(f32[6,16,128]{2,1,0:T(8,128)S(1)} %get-tuple-element.12), channel_id=1, source_target_pairs={{1,0},{2,1},{3,2},{4,3},{5,4},{6,5},{7,6},{8,7},{9,8},{10,9},{11,1... | collective-permute-start | bytes 147464 | tf_op jit(solution)/shard_map/ppermute | solution.py:219
  4.1 2.8 %collective-permute-start.2 = (f32[6,16,128]{2,1,0:T(8,128)S(1)}, f32[6,16,128]{2,1,0:T(8,128)S(1)}, u32[]{:S(2)}, u32[]{:S(2)}) collective-permute-start(f32[6,16,128]{2,1,0:T(8,128)S(1)} %get-tuple-element.13), channel_id=1, source_target_pairs={{0,1},{1,2},{2,3},{3,4},{4,5},{5,6},{6,7},{7,8},{8,9},{9,10},{10,1... | collective-permute-start | bytes 147464 | tf_op jit(solution)/shard_map/ppermute | solution.py:219
  6.9 1.3 %fusion.15 = (f32[6,8,3072]{2,1,0:T(8,128)S(1)}, f32[6,8,3072]{2,1,0:T(8,128)S(1)}) fusion(f32[6,16,3072]{2,1,0:T(8,128)} %state_ref.1), kind=kLoop, calls=%fused_computation.51 | loop fusion | bytes 2359296 | tf_op jit(solution)/shard_map/slice | solution.py:362
  8.2 0.4 dynamic_update_slice.6
  8.6 3.1 %collective-permute-start = (f32[6,8,3072]{2,1,0:T(8,128)S(1)}, f32[6,8,3072]{2,1,0:T(8,128)S(1)}, u32[]{:S(2)}, u32[]{:S(2)}) collective-permute-start(f32[6,8,3072]{2,1,0:T(8,128)S(1)} %dynamic_update_slice.6), channel_id=1, source_target_pairs={{0,16},{16,32},{32,48},{48,64},{64,80},{80,96},{96,112},{112,128},... | collective-permute-start | bytes 1769480 | tf_op jit(solution)/shard_map/ppermute | solution.py:219
  11.7 0.4 dynamic_update_slice.7
  12.1 4.3 %collective-permute-start.1 = (f32[6,8,3072]{2,1,0:T(8,128)S(1)}, f32[6,8,3072]{2,1,0:T(8,128)S(1)}, u32[]{:S(2)}, u32[]{:S(2)}) collective-permute-start(f32[6,8,3072]{2,1,0:T(8,128)S(1)} %dynamic_update_slice.7), channel_id=1, source_target_pairs={{16,0},{32,16},{48,32},{64,48},{80,64},{96,80},{112,96},{128,112},... | collective-permute-start | bytes 1769480 | tf_op jit(solution)/shard_map/ppermute | solution.py:219
  16.4 0.1 copy.36
  16.5 1.1 %fusion.14 = (f32[6,16,32]{2,1,0:T(8,128)S(1)}, f32[6,16,32]{2,1,0:T(8,128)S(1)}, f32[6,16,32]{2,1,0:T(8,128)S(1)}, f32[6,16,32]{2,1,0:T(8,128)S(1)}) fusion(f32[6,16,3072]{2,1,0:T(8,128)} %state_ref.1), kind=kLoop, calls=%fused_computation.50 | loop fusion | bytes 98304 | tf_op jit(solution)/shard_map/slice | solution.py:316
  17.6 0.2 select_reduce_fusion.1
  17.8 0.1 iota_compare_fusion.2
  17.9 0.1 select_reduce_fusion
  18.0 0.1 mul.47
  18.1 0.1 pad_maximum_fusion.1
  18.4 0.1 tile.8
  18.6 0.8 %select_select_fusion.1 = f32[6,16,128]{2,1,0:T(8,128)S(1)} fusion(f32[6,16,128]{2,1,0:T(8,128)S(1)} %collective-permute-done.2, f32[6,16,128]{2,1,0:T(8,128)S(1)} %collective-permute-done.3, pred[]{:T(512)S(6)} %eq.89, pred[]{:T(512)S(6)} %eq.82, f32[6,16,3072]{2,1,0:T(8,128)} %state_ref.1), kind=kLoop, calls=%fused_computation.7 | loop fusion | flops 24576 | bytes 196610 | tf_op jit(solution)/shard_map/jit(_where)/select_n | solution.py:381
  19.4 0.7 %collective-permute-start.5 = (f32[6,16,128]{2,1,0:T(8,128)S(1)}, f32[6,16,128]{2,1,0:T(8,128)S(1)}, u32[]{:S(2)}, u32[]{:S(2)}) collective-permute-start(f32[6,16,128]{2,1,0:T(8,128)S(1)} %select_select_fusion.1), channel_id=1, source_target_pairs={{15,1},{14,2},{0,3},{31,17},{30,18},{16,19},{47,33},{46,34},{32,35... | collective-permute-start | bytes 147464 | tf_op jit(solution)/shard_map/ppermute | solution.py:238
  20.1 0.7 %collective-permute-start.4 = (f32[6,16,128]{2,1,0:T(8,128)S(1)}, f32[6,16,128]{2,1,0:T(8,128)S(1)}, u32[]{:S(2)}, u32[]{:S(2)}) collective-permute-start(f32[6,16,128]{2,1,0:T(8,128)S(1)} %select_select_fusion.1), channel_id=1, source_target_pairs={{15,4},{14,5},{0,6},{31,20},{30,21},{16,22},{47,36},{46,37},{32,38... | collective-permute-start | bytes 147464 | tf_op jit(solution)/shard_map/ppermute | solution.py:238
  20.7 0.1 fusion
  20.8 0.6 %pad_maximum_fusion.yhalo_ref = f32[2,6,16,128]{3,2,1,0:T(8,128)} fusion(f32[1,6,16,128]{3,2,1,0:T(8,128)S(1)} %get-tuple-element.29, f32[1,6,16,128]{3,2,1,0:T(8,128)S(1)} %get-tuple-element.28), kind=kLoop, calls=%fused_computation.1 | loop fusion | flops 24576 | bytes 196608 | tf_op jit(solution)/shard_map/stack | solution.py:394
  21.5 1.3 %collective-permute-start.6 = (f32[6,16,128]{2,1,0:T(8,128)S(1)}, f32[6,16,128]{2,1,0:T(8,128)S(1)}, u32[]{:S(2)}, u32[]{:S(2)}) collective-permute-start(f32[6,16,128]{2,1,0:T(8,128)S(1)} %select_select_fusion.before_ref), channel_id=1, source_target_pairs={{15,7},{14,8},{0,9},{1,10},{2,11},{3,12},{4,13},{31,23},{30,24},{1... | collective-permute-start | bytes 147464 | tf_op jit(solution)/shard_map/ppermute | solution.py:238
  22.8 3.2 %collective-permute-done.xlo_ref = f32[6,8,3072]{2,1,0:T(8,128)S(1)} collective-permute-done((f32[6,8,3072]{2,1,0:T(8,128)S(1)}, f32[6,8,3072]{2,1,0:T(8,128)S(1)}, u32[]{:S(2)}, u32[]{:S(2)}) %collective-permute-start) | collective-permute-done | bytes 589856 | tf_op jit(solution)/shard_map/ppermute | solution.py:219
  26.0 0.1 copy.35
  26.1 1.9 %collective-permute-done.1.xhi_ref = f32[6,8,3072]{2,1,0:T(8,128)S(1)} collective-permute-done((f32[6,8,3072]{2,1,0:T(8,128)S(1)}, f32[6,8,3072]{2,1,0:T(8,128)S(1)}, u32[]{:S(2)}, u32[]{:S(2)}) %collective-permute-start.1) | collective-permute-done | bytes 589856 | tf_op jit(solution)/shard_map/ppermute | solution.py:219
  28.0 0.1 copy.37
  28.1 0.1 fusion.2
  28.4 0.1 concatenate.51
  28.5 0.9 %fusion.9.geo_ref = f32[80,128]{1,0:T(8,128)} fusion(f32[80,32]{0,1:T(8,128)S(1)} %concatenate.51, s32[128]{0:T(128)S(1)} %and_select_fusion), kind=kOutput, calls=%fused_computation.25 | convolution fusion | flops 3936256 | bytes 51712 | tf_op jit(solution)/shard_map/dot_general | solution.py:341
  29.3 2.1 %collective-permute-done.6.last_ref = f32[6,16,128]{2,1,0:T(8,128)S(1)} collective-permute-done((f32[6,16,128]{2,1,0:T(8,128)S(1)}, f32[6,16,128]{2,1,0:T(8,128)S(1)}, u32[]{:S(2)}, u32[]{:S(2)}) %collective-permute-start.6) | collective-permute-done | bytes 49184 | tf_op jit(solution)/shard_map/ppermute | solution.py:238
  31.5 0.6 %copy-done.4 = f32[6,16,128]{2,1,0:T(8,128)} copy-done((f32[6,16,128]{2,1,0:T(8,128)}, f32[6,16,128]{2,1,0:T(8,128)S(1)}, u32[]{:S(2)}) %copy-start.4) | copy-done | bytes 49176
  32.1 12.2 %shard_map.68 = (f32[6,16,3072]{2,1,0:T(8,128)}, f32[16,32]{1,0:T(8,128)}) custom-call(f32[6,16,3072]{2,1,0:T(8,128)} %state_ref.1, f32[6,8,3072]{2,1,0:T(8,128)} %copy-done, f32[6,8,3072]{2,1,0:T(8,128)} %copy-done.1, f32[2,6,16,128]{3,2,1,0:T(8,128)} %pad_maximum_fusion.yhalo_ref, f32[80,128]{1,0:T(8,128)} %fusion.9.geo_ref, f32[6,16,128]{2,1,0:T(8,128)} %copy-done.2, ...), custom_call_target="tpu_custom_call" | custom-call | tf_op jit(solution)/shard_map/pallas_call | solution.py:197
  (43 shorter events, 0.3 us)
Async XLA Ops:
  1.5 17.1 %collective-permute-start.3 = (f32[6,16,128]{2,1,0:T(8,128)S(1)}, f32[6,16,128]{2,1,0:T(8,128)S(1)}, u32[]{:S(2)}, u32[]{:S(2)}) collective-permute-start(f32[6,16,128]{2,1,0:T(8,128)S(1)} %get-tuple-element.12), channel_id=1, source_target_pairs={{1,0},{2,1},{3,2},{4,3},{5,4},{6,5},{7,6},{8,7},{9,8},{10,9},{11,1... | collective-permute-start | bytes 147464 | tf_op jit(solution)/shard_map/ppermute | solution.py:219
  4.1 4.1 %copy-start.3 = (f32[16,32]{1,0:T(8,128)S(1)}, f32[16,32]{1,0:T(8,128)}, u32[]{:S(2)}) copy-start(f32[16,32]{1,0:T(8,128)} %height_ref.1) | copy-start | bytes 6148
  4.1 13.5 %copy-start.6 = (s32[16]{0:T(128)S(1)}, s32[16]{0:T(128)}, u32[]{:S(2)}) copy-start(s32[16]{0:T(128)} %param.8) | copy-start | bytes 196
  4.1 13.5 %copy-start.7 = (s32[16]{0:T(128)S(1)}, s32[16]{0:T(128)}, u32[]{:S(2)}) copy-start(s32[16]{0:T(128)} %param.7) | copy-start | bytes 196
  4.1 13.8 %copy-start.5 = (f32[16,32]{1,0:T(8,128)S(1)}, f32[16,32]{1,0:T(8,128)}, u32[]{:S(2)}) copy-start(f32[16,32]{1,0:T(8,128)} %param.9) | copy-start | bytes 6148
  4.1 14.4 %collective-permute-start.2 = (f32[6,16,128]{2,1,0:T(8,128)S(1)}, f32[6,16,128]{2,1,0:T(8,128)S(1)}, u32[]{:S(2)}, u32[]{:S(2)}) collective-permute-start(f32[6,16,128]{2,1,0:T(8,128)S(1)} %get-tuple-element.13), channel_id=1, source_target_pairs={{0,1},{1,2},{2,3},{3,4},{4,5},{5,6},{6,7},{7,8},{8,9},{9,10},{10,1... | collective-permute-start | bytes 147464 | tf_op jit(solution)/shard_map/ppermute | solution.py:219
  8.6 17.4 %collective-permute-start = (f32[6,8,3072]{2,1,0:T(8,128)S(1)}, f32[6,8,3072]{2,1,0:T(8,128)S(1)}, u32[]{:S(2)}, u32[]{:S(2)}) collective-permute-start(f32[6,8,3072]{2,1,0:T(8,128)S(1)} %dynamic_update_slice.6), channel_id=1, source_target_pairs={{0,16},{16,32},{32,48},{48,64},{64,80},{80,96},{96,112},{112,128},... | collective-permute-start | bytes 1769480 | tf_op jit(solution)/shard_map/ppermute | solution.py:219
  12.1 15.9 %collective-permute-start.1 = (f32[6,8,3072]{2,1,0:T(8,128)S(1)}, f32[6,8,3072]{2,1,0:T(8,128)S(1)}, u32[]{:S(2)}, u32[]{:S(2)}) collective-permute-start(f32[6,8,3072]{2,1,0:T(8,128)S(1)} %dynamic_update_slice.7), channel_id=1, source_target_pairs={{16,0},{32,16},{48,32},{64,48},{80,64},{96,80},{112,96},{128,112},... | collective-permute-start | bytes 1769480 | tf_op jit(solution)/shard_map/ppermute | solution.py:219
  19.4 2.1 %collective-permute-start.5 = (f32[6,16,128]{2,1,0:T(8,128)S(1)}, f32[6,16,128]{2,1,0:T(8,128)S(1)}, u32[]{:S(2)}, u32[]{:S(2)}) collective-permute-start(f32[6,16,128]{2,1,0:T(8,128)S(1)} %select_select_fusion.1), channel_id=1, source_target_pairs={{15,1},{14,2},{0,3},{31,17},{30,18},{16,19},{47,33},{46,34},{32,35... | collective-permute-start | bytes 147464 | tf_op jit(solution)/shard_map/ppermute | solution.py:238
  20.1 1.4 %collective-permute-start.4 = (f32[6,16,128]{2,1,0:T(8,128)S(1)}, f32[6,16,128]{2,1,0:T(8,128)S(1)}, u32[]{:S(2)}, u32[]{:S(2)}) collective-permute-start(f32[6,16,128]{2,1,0:T(8,128)S(1)} %select_select_fusion.1), channel_id=1, source_target_pairs={{15,4},{14,5},{0,6},{31,20},{30,21},{16,22},{47,36},{46,37},{32,38... | collective-permute-start | bytes 147464 | tf_op jit(solution)/shard_map/ppermute | solution.py:238
  21.5 10.0 %copy-start.2 = (f32[6,16,128]{2,1,0:T(8,128)}, f32[6,16,128]{2,1,0:T(8,128)S(1)}, u32[]{:S(2)}) copy-start(f32[6,16,128]{2,1,0:T(8,128)S(1)} %select_select_fusion.before_ref) | copy-start | bytes 147460
  21.5 10.0 %collective-permute-start.6 = (f32[6,16,128]{2,1,0:T(8,128)S(1)}, f32[6,16,128]{2,1,0:T(8,128)S(1)}, u32[]{:S(2)}, u32[]{:S(2)}) collective-permute-start(f32[6,16,128]{2,1,0:T(8,128)S(1)} %select_select_fusion.before_ref), channel_id=1, source_target_pairs={{15,7},{14,8},{0,9},{1,10},{2,11},{3,12},{4,13},{31,23},{30,24},{1... | collective-permute-start | bytes 147464 | tf_op jit(solution)/shard_map/ppermute | solution.py:238
  26.0 5.4 %copy-start = (f32[6,8,3072]{2,1,0:T(8,128)}, f32[6,8,3072]{2,1,0:T(8,128)S(1)}, u32[]{:S(2)}) copy-start(f32[6,8,3072]{2,1,0:T(8,128)S(1)} %collective-permute-done.xlo_ref) | copy-start | bytes 1769476
  28.0 3.4 %copy-start.1 = (f32[6,8,3072]{2,1,0:T(8,128)}, f32[6,8,3072]{2,1,0:T(8,128)S(1)}, u32[]{:S(2)}) copy-start(f32[6,8,3072]{2,1,0:T(8,128)S(1)} %collective-permute-done.1.xhi_ref) | copy-start | bytes 1769476
  31.5 0.6 %copy-start.4 = (f32[6,16,128]{2,1,0:T(8,128)}, f32[6,16,128]{2,1,0:T(8,128)S(1)}, u32[]{:S(2)}) copy-start(f32[6,16,128]{2,1,0:T(8,128)S(1)} %collective-permute-done.6.last_ref) | copy-start | bytes 147460

commit v15 on v13

--- a/solution.py
+++ b/solution.py
@@ -386,7 +386,7 @@
     top_seed = jnp.where(row_dev == row_devs - 1, top_block, jnp.where(row_dev == 0, below, above))
     top_seed, below, above = lax.optimization_barrier((top_seed, below, above))
     seeded = sorted({row_devs - 1, 0, max(row_devs - 2, 0)}, reverse=True)
-    top_before, top_last, last_targets = broadcast(top_seed, "gy", seeded, (2, 1, 1, 1, 1))
+    top_before, top_last, last_targets = broadcast(top_seed, "gy", seeded, (5, 5, 5, 5))
 
     blowing = wall_flux(wall_segment, segment_level, blow_table)
     wall_block = wall_ghosts(state[..., :band], blowing, planes)

time: 44.2 us -> 50.6 us (1.14)
  the two profiles are of different devices: /device:TPU:113 before, /device:TPU:6 now
where the time goes in v15:
time: 50.6 us; the launch traced here: 50.2 us
  starting transfers between devices  20.9 us (41%)
  Pallas kernels  12.3 us (24%)
  waiting for transfers between devices  7.56 us (15%)
  local copies, waits for them, and re-layouts  3.79 us (7%)
  other arithmetic  3.78 us (7%)
  between operations  1.05 us (2%)
  matrix products  0.85 us (2%)
    ppermute x5, starting transfers between devices, broadcast(): received = lax.ppermute(array, axis, pairs)  12.6 us
    pallas_call x1, Pallas kernels, update(): pl.pallas_call(kern, out_shape=(jax.ShapeDtypeStruct((6, columns, length)...  12.3 us
    ppermute x4, starting transfers between devices, shifted(): return lax.ppermute(block, axis, pairs)  8.26 us
    ppermute x4, waiting for transfers between devices, shifted(): return lax.ppermute(block, axis, pairs)  7.54 us
    slice x1, local copies, waits for them, and re-layouts, shards(): from_high = shifted(pack(state[:, :HALO], shock_height[:HALO]), 'gx', False)  1.35 us
  transfers between devices with their start and end apart: 9, of which 2 were waited for; matrix products, arithmetic and copies ran while one was open for 14% of the time, Pallas kernels for 0%

profile of v15, /device:TPU:6, one launch (start us, length us, event | category | flops | bytes accessed | tf_op | source)
XLA Modules:
  0.0 50.2 jit_solution(1254422132993530345)
XLA Ops:
  0.7 0.8 %slice_select_fusion = (f32[6,16,128]{2,1,0:T(8,128)S(1)}, f32[6,16,128]{2,1,0:T(8,128)S(1)}) fusion(f32[6,16,3072]{2,1,0:T(8,128)} %state_ref.1, pred[128]{0:T(512)(128)(4,1)S(1)} %iota_compare_fusion.5), kind=kLoop, calls=%fused_computation.11 | loop fusion | flops 12288 | bytes 196736 | tf_op jit(solution)/shard_map/jit(_where)/select_n | solution.py:374
  1.5 1.3 %collective-permute-start.3 = (f32[6,16,128]{2,1,0:T(8,128)S(1)}, f32[6,16,128]{2,1,0:T(8,128)S(1)}, u32[]{:S(2)}, u32[]{:S(2)}) collective-permute-start(f32[6,16,128]{2,1,0:T(8,128)S(1)} %get-tuple-element.12), channel_id=1, source_target_pairs={{1,0},{2,1},{3,2},{4,3},{5,4},{6,5},{7,6},{8,7},{9,8},{10,9},{11,1... | collective-permute-start | bytes 147464 | tf_op jit(solution)/shard_map/ppermute | solution.py:227
  2.8 1.1 %collective-permute-start.2 = (f32[6,16,128]{2,1,0:T(8,128)S(1)}, f32[6,16,128]{2,1,0:T(8,128)S(1)}, u32[]{:S(2)}, u32[]{:S(2)}) collective-permute-start(f32[6,16,128]{2,1,0:T(8,128)S(1)} %get-tuple-element.13), channel_id=1, source_target_pairs={{0,1},{1,2},{2,3},{3,4},{4,5},{5,6},{6,7},{7,8},{8,9},{9,10},{10,1... | collective-permute-start | bytes 147464 | tf_op jit(solution)/shard_map/ppermute | solution.py:227
  4.0 1.3 %fusion.15 = (f32[6,3,3072]{2,1,0:T(4,128)S(1)}, f32[6,3,3072]{2,1,0:T(4,128)S(1)}) fusion(f32[6,16,3072]{2,1,0:T(8,128)} %state_ref.1), kind=kLoop, calls=%fused_computation.54 | loop fusion | bytes 884736 | tf_op jit(solution)/shard_map/slice | solution.py:370
  5.4 3.4 %collective-permute-start = (f32[7,3,3072]{2,1,0:T(4,128)S(1)}, f32[7,3,3072]{2,1,0:T(4,128)S(1)}, u32[]{:S(2)}, u32[]{:S(2)}) collective-permute-start(f32[7,3,3072]{2,1,0:T(4,128)S(1)} %select_maximum_fusion.1), channel_id=1, source_target_pairs={{0,16},{16,32},{32,48},{48,64},{64,80},{80,96},{96,112},{112,128},... | collective-permute-start | bytes 774152 | tf_op jit(solution)/shard_map/ppermute | solution.py:227
  8.8 0.1 copy.36
  8.9 1.0 %fusion.14 = (f32[6,16,32]{2,1,0:T(8,128)S(1)}, f32[6,16,32]{2,1,0:T(8,128)S(1)}, f32[6,16,32]{2,1,0:T(8,128)S(1)}, f32[6,16,32]{2,1,0:T(8,128)S(1)}) fusion(f32[6,16,3072]{2,1,0:T(8,128)} %state_ref.1), kind=kLoop, calls=%fused_computation.53 | loop fusion | bytes 98304 | tf_op jit(solution)/shard_map/slice | solution.py:324
  10.0 0.2 select_reduce_fusion.1
  10.2 0.1 iota_compare_fusion.3
  10.2 0.1 select_reduce_fusion
  10.4 0.1 mul.47
  10.5 0.1 pad_maximum_fusion.1
  10.8 0.1 tile.8
  11.0 0.2 collective-permute-done.2
  11.2 0.8 %select_select_fusion.1 = f32[6,16,128]{2,1,0:T(8,128)S(1)} fusion(f32[6,16,128]{2,1,0:T(8,128)S(1)} %collective-permute-done.2, f32[6,16,128]{2,1,0:T(8,128)S(1)} %collective-permute-done.3, pred[]{:T(512)S(6)} %eq.107, pred[]{:T(512)S(6)} %eq.100, f32[6,16,3072]{2,1,0:T(8,128)} %state_ref.1), kind=kLoop, calls=%fused_computation.10 | loop fusion | flops 24576 | bytes 196610 | tf_op jit(solution)/shard_map/jit(_where)/select_n | solution.py:386
  12.0 4.5 %collective-permute-start.7 = (f32[6,16,128]{2,1,0:T(8,128)S(1)}, f32[6,16,128]{2,1,0:T(8,128)S(1)}, u32[]{:S(2)}, u32[]{:S(2)}) collective-permute-start(f32[6,16,128]{2,1,0:T(8,128)S(1)} %select_select_fusion.1), channel_id=1, source_target_pairs={{15,1},{14,2},{0,3},{31,17},{30,18},{16,19},{47,33},{46,34},{32,35... | collective-permute-start | bytes 147464 | tf_op jit(solution)/shard_map/ppermute | solution.py:246
  16.5 2.5 %collective-permute-start.6 = (f32[6,16,128]{2,1,0:T(8,128)S(1)}, f32[6,16,128]{2,1,0:T(8,128)S(1)}, u32[]{:S(2)}, u32[]{:S(2)}) collective-permute-start(f32[6,16,128]{2,1,0:T(8,128)S(1)} %select_select_fusion.1), channel_id=1, source_target_pairs={{15,4},{14,5},{0,6},{31,20},{30,21},{16,22},{47,36},{46,37},{32,38... | collective-permute-start | bytes 147464 | tf_op jit(solution)/shard_map/ppermute | solution.py:246
  19.1 3.6 %collective-permute-start.5 = (f32[6,16,128]{2,1,0:T(8,128)S(1)}, f32[6,16,128]{2,1,0:T(8,128)S(1)}, u32[]{:S(2)}, u32[]{:S(2)}) collective-permute-start(f32[6,16,128]{2,1,0:T(8,128)S(1)} %select_select_fusion.1), channel_id=1, source_target_pairs={{15,7},{14,8},{0,9},{31,23},{30,24},{16,25},{47,39},{46,40},{32,41... | collective-permute-start | bytes 147464 | tf_op jit(solution)/shard_map/ppermute | solution.py:246
  22.7 1.3 %collective-permute-start.4 = (f32[6,16,128]{2,1,0:T(8,128)S(1)}, f32[6,16,128]{2,1,0:T(8,128)S(1)}, u32[]{:S(2)}, u32[]{:S(2)}) collective-permute-start(f32[6,16,128]{2,1,0:T(8,128)S(1)} %select_select_fusion.1), channel_id=1, source_target_pairs={{15,10},{14,11},{0,12},{31,26},{30,27},{16,28},{47,42},{46,43},{32... | collective-permute-start | bytes 147464 | tf_op jit(solution)/shard_map/ppermute | solution.py:246
  24.0 0.1 fusion
  24.1 0.7 %pad_maximum_fusion.yhalo_ref = f32[2,6,16,128]{3,2,1,0:T(8,128)} fusion(f32[1,6,16,128]{3,2,1,0:T(8,128)S(1)} %get-tuple-element.29, f32[1,6,16,128]{3,2,1,0:T(8,128)S(1)} %get-tuple-element.28), kind=kLoop, calls=%fused_computation.4 | loop fusion | flops 24576 | bytes 196608 | tf_op jit(solution)/shard_map/stack | solution.py:399
  24.7 2.4 %collective-permute-start.1 = (f32[7,3,3072]{2,1,0:T(4,128)S(1)}, f32[7,3,3072]{2,1,0:T(4,128)S(1)}, u32[]{:S(2)}, u32[]{:S(2)}) collective-permute-start(f32[7,3,3072]{2,1,0:T(4,128)S(1)} %select_maximum_fusion), channel_id=1, source_target_pairs={{16,0},{32,16},{48,32},{64,48},{80,64},{96,80},{112,96},{128,112},... | collective-permute-start | bytes 774152 | tf_op jit(solution)/shard_map/ppermute | solution.py:227
  27.2 0.7 %collective-permute-start.8 = (f32[6,16,128]{2,1,0:T(8,128)S(1)}, f32[6,16,128]{2,1,0:T(8,128)S(1)}, u32[]{:S(2)}, u32[]{:S(2)}) collective-permute-start(f32[6,16,128]{2,1,0:T(8,128)S(1)} %select_select_fusion.1), channel_id=1, source_target_pairs={{15,13},{31,29},{47,45},{63,61},{79,77},{95,93},{111,109},{127,125... | collective-permute-start | bytes 147464 | tf_op jit(solution)/shard_map/ppermute | solution.py:246
  27.9 0.6 %select_select_fusion.before_ref = f32[6,16,128]{2,1,0:T(8,128)} fusion(f32[6,16,128]{2,1,0:T(8,128)S(1)} %collective-permute-done.4, f32[6,16,128]{2,1,0:T(8,128)S(1)} %collective-permute-done.5, f32[6,16,128]{2,1,0:T(8,128)S(1)} %collective-permute-done.6, f32[6,16,128]{2,1,0:T(8,128)S(1)} %collective-permute-done.7, ...), kind=kLoop, calls=%fused_computation.8 | loop fusion | flops 49152 | bytes 294916 | tf_op jit(solution)/shard_map/jit(_where)/select_n | solution.py:251
  28.5 0.1 copy.35
  28.6 7.4 %collective-permute-done.1.xhi_ref = f32[7,3,3072]{2,1,0:T(4,128)S(1)} collective-permute-done((f32[7,3,3072]{2,1,0:T(4,128)S(1)}, f32[7,3,3072]{2,1,0:T(4,128)S(1)}, u32[]{:S(2)}, u32[]{:S(2)}) %collective-permute-start.1) | collective-permute-done | bytes 258080 | tf_op jit(solution)/shard_map/ppermute | solution.py:227
  36.0 0.1 copy.37
  36.1 0.1 fusion.2
  36.3 0.1 concatenate.59
  36.4 0.9 %fusion.9.geo_ref = f32[80,128]{1,0:T(8,128)} fusion(f32[80,32]{0,1:T(8,128)S(1)} %concatenate.59, s32[128]{0:T(128)S(1)} %and_select_fusion), kind=kOutput, calls=%fused_computation.28 | convolution fusion | flops 3936256 | bytes 51712 | tf_op jit(solution)/shard_map/dot_general | solution.py:349
  37.3 0.6 %copy-done.3 = f32[6,16,128]{2,1,0:T(8,128)} copy-done((f32[6,16,128]{2,1,0:T(8,128)}, f32[6,16,128]{2,1,0:T(8,128)S(1)}, u32[]{:S(2)}) %copy-start.3) | copy-done | bytes 49176
  37.9 12.3 %shard_map.68 = (f32[6,16,3072]{2,1,0:T(8,128)}, f32[16,32]{1,0:T(8,128)}) custom-call(f32[6,16,3072]{2,1,0:T(8,128)} %state_ref.1, f32[7,3,3072]{2,1,0:T(4,128)} %copy-done, f32[7,3,3072]{2,1,0:T(4,128)} %copy-done.1, f32[2,6,16,128]{3,2,1,0:T(8,128)} %pad_maximum_fusion.yhalo_ref, f32[80,128]{1,0:T(8,128)} %fusion.9.geo_ref, ...), custom_call_target="tpu_custom_call" | custom-call | tf_op jit(solution)/shard_map/pallas_call | solution.py:204
  (45 shorter events, 0.5 us)
Async XLA Ops:
  0.6 4.7 %copy-start.2 = (f32[16,32]{1,0:T(8,128)S(1)}, f32[16,32]{1,0:T(8,128)}, u32[]{:S(2)}) copy-start(f32[16,32]{1,0:T(8,128)} %height_ref.1) | copy-start | bytes 6148
  1.5 9.5 %collective-permute-start.3 = (f32[6,16,128]{2,1,0:T(8,128)S(1)}, f32[6,16,128]{2,1,0:T(8,128)S(1)}, u32[]{:S(2)}, u32[]{:S(2)}) collective-permute-start(f32[6,16,128]{2,1,0:T(8,128)S(1)} %get-tuple-element.12), channel_id=1, source_target_pairs={{1,0},{2,1},{3,2},{4,3},{5,4},{6,5},{7,6},{8,7},{9,8},{10,9},{11,1... | collective-permute-start | bytes 147464 | tf_op jit(solution)/shard_map/ppermute | solution.py:227
  2.8 7.2 %copy-start.5 = (s32[16]{0:T(128)S(1)}, s32[16]{0:T(128)}, u32[]{:S(2)}) copy-start(s32[16]{0:T(128)} %param.8) | copy-start | bytes 196
  2.8 7.2 %copy-start.6 = (s32[16]{0:T(128)S(1)}, s32[16]{0:T(128)}, u32[]{:S(2)}) copy-start(s32[16]{0:T(128)} %param.7) | copy-start | bytes 196
  2.8 7.4 %copy-start.4 = (f32[16,32]{1,0:T(8,128)S(1)}, f32[16,32]{1,0:T(8,128)}, u32[]{:S(2)}) copy-start(f32[16,32]{1,0:T(8,128)} %param.9) | copy-start | bytes 6148
  2.8 8.4 %collective-permute-start.2 = (f32[6,16,128]{2,1,0:T(8,128)S(1)}, f32[6,16,128]{2,1,0:T(8,128)S(1)}, u32[]{:S(2)}, u32[]{:S(2)}) collective-permute-start(f32[6,16,128]{2,1,0:T(8,128)S(1)} %get-tuple-element.13), channel_id=1, source_target_pairs={{0,1},{1,2},{2,3},{3,4},{4,5},{5,6},{6,7},{7,8},{8,9},{9,10},{10,1... | collective-permute-start | bytes 147464 | tf_op jit(solution)/shard_map/ppermute | solution.py:227
  5.4 23.1 %collective-permute-start = (f32[7,3,3072]{2,1,0:T(4,128)S(1)}, f32[7,3,3072]{2,1,0:T(4,128)S(1)}, u32[]{:S(2)}, u32[]{:S(2)}) collective-permute-start(f32[7,3,3072]{2,1,0:T(4,128)S(1)} %select_maximum_fusion.1), channel_id=1, source_target_pairs={{0,16},{16,32},{32,48},{48,64},{64,80},{80,96},{96,112},{112,128},... | collective-permute-start | bytes 774152 | tf_op jit(solution)/shard_map/ppermute | solution.py:227
  12.0 12.7 %collective-permute-start.7 = (f32[6,16,128]{2,1,0:T(8,128)S(1)}, f32[6,16,128]{2,1,0:T(8,128)S(1)}, u32[]{:S(2)}, u32[]{:S(2)}) collective-permute-start(f32[6,16,128]{2,1,0:T(8,128)S(1)} %select_select_fusion.1), channel_id=1, source_target_pairs={{15,1},{14,2},{0,3},{31,17},{30,18},{16,19},{47,33},{46,34},{32,35... | collective-permute-start | bytes 147464 | tf_op jit(solution)/shard_map/ppermute | solution.py:246
  16.5 10.6 %collective-permute-start.6 = (f32[6,16,128]{2,1,0:T(8,128)S(1)}, f32[6,16,128]{2,1,0:T(8,128)S(1)}, u32[]{:S(2)}, u32[]{:S(2)}) collective-permute-start(f32[6,16,128]{2,1,0:T(8,128)S(1)} %select_select_fusion.1), channel_id=1, source_target_pairs={{15,4},{14,5},{0,6},{31,20},{30,21},{16,22},{47,36},{46,37},{32,38... | collective-permute-start | bytes 147464 | tf_op jit(solution)/shard_map/ppermute | solution.py:246
  19.1 8.8 %collective-permute-start.5 = (f32[6,16,128]{2,1,0:T(8,128)S(1)}, f32[6,16,128]{2,1,0:T(8,128)S(1)}, u32[]{:S(2)}, u32[]{:S(2)}) collective-permute-start(f32[6,16,128]{2,1,0:T(8,128)S(1)} %select_select_fusion.1), channel_id=1, source_target_pairs={{15,7},{14,8},{0,9},{31,23},{30,24},{16,25},{47,39},{46,40},{32,41... | collective-permute-start | bytes 147464 | tf_op jit(solution)/shard_map/ppermute | solution.py:246
  22.7 5.2 %collective-permute-start.4 = (f32[6,16,128]{2,1,0:T(8,128)S(1)}, f32[6,16,128]{2,1,0:T(8,128)S(1)}, u32[]{:S(2)}, u32[]{:S(2)}) collective-permute-start(f32[6,16,128]{2,1,0:T(8,128)S(1)} %select_select_fusion.1), channel_id=1, source_target_pairs={{15,10},{14,11},{0,12},{31,26},{30,27},{16,28},{47,42},{46,43},{32... | collective-permute-start | bytes 147464 | tf_op jit(solution)/shard_map/ppermute | solution.py:246
  24.7 11.2 %collective-permute-start.1 = (f32[7,3,3072]{2,1,0:T(4,128)S(1)}, f32[7,3,3072]{2,1,0:T(4,128)S(1)}, u32[]{:S(2)}, u32[]{:S(2)}) collective-permute-start(f32[7,3,3072]{2,1,0:T(4,128)S(1)} %select_maximum_fusion), channel_id=1, source_target_pairs={{16,0},{32,16},{48,32},{64,48},{80,64},{96,80},{112,96},{128,112},... | collective-permute-start | bytes 774152 | tf_op jit(solution)/shard_map/ppermute | solution.py:227
  27.2 10.1 %collective-permute-start.8 = (f32[6,16,128]{2,1,0:T(8,128)S(1)}, f32[6,16,128]{2,1,0:T(8,128)S(1)}, u32[]{:S(2)}, u32[]{:S(2)}) collective-permute-start(f32[6,16,128]{2,1,0:T(8,128)S(1)} %select_select_fusion.1), channel_id=1, source_target_pairs={{15,13},{31,29},{47,45},{63,61},{79,77},{95,93},{111,109},{127,125... | collective-permute-start | bytes 147464 | tf_op jit(solution)/shard_map/ppermute | solution.py:246
  28.5 8.8 %copy-start = (f32[7,3,3072]{2,1,0:T(4,128)}, f32[7,3,3072]{2,1,0:T(4,128)S(1)}, u32[]{:S(2)}) copy-start(f32[7,3,3072]{2,1,0:T(4,128)S(1)} %collective-permute-done.xlo_ref) | copy-start | bytes 774148
  36.0 1.3 %copy-start.1 = (f32[7,3,3072]{2,1,0:T(4,128)}, f32[7,3,3072]{2,1,0:T(4,128)S(1)}, u32[]{:S(2)}) copy-start(f32[7,3,3072]{2,1,0:T(4,128)S(1)} %collective-permute-done.1.xhi_ref) | copy-start | bytes 774148
  37.3 0.6 %copy-start.3 = (f32[6,16,128]{2,1,0:T(8,128)}, f32[6,16,128]{2,1,0:T(8,128)S(1)}, u32[]{:S(2)}) copy-start(f32[6,16,128]{2,1,0:T(8,128)S(1)} %collective-permute-done.8.last_ref) | copy-start | bytes 147460

commit v16 on v13

--- a/solution.py
+++ b/solution.py
@@ -62,8 +62,8 @@
     face_area = STREAM_STEP * SPAN_STEP
     xrows = columns + 2 * XPAD
 
-    def kernel(state_ref, xlo_ref, xhi_ref, yhalo_ref, geo_ref, before_ref, last_ref, height_ref,
-               out_ref, shock_ref, qx_ref, qy_ref, pair_ref):
+    def kernel(state_ref, xlo_ref, xhi_ref, below_ref, above_ref, geo_ref, before_ref, last_ref,
+               height_ref, out_ref, shock_ref, qx_ref, qy_ref, pair_ref):
         col_dev = lax.axis_index("gx")
         first_row = lax.axis_index("gy") * (length // planes)
         for c in range(6):
@@ -72,9 +72,9 @@
             qx_ref[c, XPAD + columns:, :] = state_ref[c, columns - XPAD:, :]
             qx_ref[c, XPAD - HALO:XPAD, :] = xlo_ref[c]
             qx_ref[c, XPAD + columns:XPAD + columns + HALO, :] = xhi_ref[c]
-            qy_ref[c, :, 0:PAD] = yhalo_ref[0, c]
+            qy_ref[c, :, 0:PAD] = below_ref[c]
             qy_ref[c, :, PAD:PAD + length] = state_ref[c]
-            qy_ref[c, :, PAD + length:] = yhalo_ref[1, c, :, 0:PAD]
+            qy_ref[c, :, PAD + length:] = above_ref[c]
 
         @pl.when(col_dev == 0)
         def _():
@@ -92,6 +92,28 @@
         slope_z_row = geo_ref[xrows + columns:xrows + 2 * columns, :]
         height_row = geo_ref[xrows + 2 * columns:xrows + 3 * columns, :]
         group = lax.broadcasted_iota(jnp.int32, (columns, LANES), 1) // planes
+
+        @pl.when(lax.axis_index("gy") == 0)
+        def _():
+            mirror = []
+            for c in range(6):
+                rows = state_ref[c, :, 0:LANES]
+                mirror.append(jnp.where(group == 2, pltpu.roll(rows, planes, 1),
+                                        pltpu.roll(rows, 3 * planes, 1)))
+            blown_y = 2.0 * geo_ref[xrows + 3 * columns:xrows + 4 * columns, :] - mirror[2]
+            energy = mirror[4] + 0.5 * (blown_y * blown_y - mirror[2] * mirror[2]) / mirror[0]
+            ghosts = [mirror[0], mirror[1], blown_y, mirror[3], energy, mirror[5]]
+            for c in range(6):
+                qy_ref[c, :, 0:PAD] = ghosts[c]
+
+        @pl.when(lax.axis_index("gy") == lax.axis_size("gy") - 1)
+        def _():
+            for c in range(6):
+                rows = state_ref[c, :, length - LANES:]
+                qy_ref[c, :, PAD + length:] = jnp.where(
+                    group == 0, pltpu.roll(rows, planes, 1),
+                    jnp.where(group == 1, pltpu.roll(rows, 2 * planes, 1),
+                              jnp.where(group == 2, pltpu.roll(rows, 3 * planes, 1), rows)))
         top = []
         row_dev = lax.axis_index("gy")
         hit = jnp.zeros((columns, LANES), jnp.bool_)
@@ -196,7 +218,8 @@
     return kernel
 
 
-def update(state, xlo, xhi, yhalo, geo, top_before, top_last, height, targets, planes, total_rows, dt):
+def update(state, xlo, xhi, below, above, geo, top_before, top_last, height, targets, planes, total_rows,
+           dt):
     columns = state.shape[1]
     length = state.shape[2]
     kern = make_kernel(columns, length, planes, total_rows, dt, targets)
@@ -207,14 +230,14 @@
             jax.ShapeDtypeStruct((6, columns, length), jnp.float32),
             jax.ShapeDtypeStruct((columns, planes), jnp.float32),
         ),
-        in_specs=[vmem] * 8,
+        in_specs=[vmem] * 9,
         out_specs=(vmem, vmem),
         scratch_shapes=[
             pltpu.VMEM((6, columns + 2 * XPAD, length), jnp.float32),
             pltpu.VMEM((6, columns, length + 2 * PAD), jnp.float32),
             pltpu.VMEM((6, 6, columns + 2 * XPAD, CHUNK), jnp.float32),
         ],
-    )(state, xlo, xhi, yhalo, geo, top_before, top_last, height)
+    )(state, xlo, xhi, below, above, geo, top_before, top_last, height)
 
 
 def shifted(block, axis, forward, cyclic=False):
@@ -389,14 +412,6 @@
     top_before, top_last, last_targets = broadcast(top_seed, "gy", seeded, (2, 1, 1, 1, 1))
 
     blowing = wall_flux(wall_segment, segment_level, blow_table)
-    wall_block = wall_ghosts(state[..., :band], blowing, planes)
-    ghost_below = jnp.where(
-        row_dev == 0, jnp.concatenate([wall_block[..., : PAD - band], wall_block], axis=2), below
-    )
-    ghost_above = jnp.where(
-        row_dev == row_devs - 1, jnp.tile(state[..., length - planes :], (1, 1, PAD // planes)), above
-    )
-    yhalo = jnp.stack([ghost_below, ghost_above])
 
     height = shock_height
     height_x = jnp.concatenate(
@@ -407,13 +422,14 @@
         ],
         axis=0,
     )
-    small = jnp.concatenate([height_x, slope_x, slope_z, height], axis=0)
+    small = jnp.concatenate([height_x, slope_x, slope_z, height, blowing], axis=0)
     geo = replicate_lanes(small, planes)
     state_new, shock_new = update(
         state,
         from_low,
         from_high,
-        yhalo,
+        below,
+        above,
         geo,
         top_before,
         top_last,

time: 44.2 us -> 42.1 us (0.952)
  local copies, waits for them, and re-layouts: 3.79 us -> 2.6 us
  other arithmetic: 3.16 us -> 2.33 us
    ppermute x4, waiting for transfers between devices: 0.01 us -> 2.04 us  [shifted(): return lax.ppermute(block, axis, pairs)]
    ppermute x3, waiting for transfers between devices: 7.21 us -> 5.33 us  [broadcast(): received = lax.ppermute(array, axis, pairs)]
    slice x1 -> x0, local copies, waits for them, and re-layouts: 1.01 us -> none  [wall_ghosts(): first_rows[..., 2 * planes:3 * planes]]
    another operation x2 -> x0, other arithmetic: 0.73 us -> none  [shards(): yhalo = jnp.stack([ghost_below, ghost_above])]
  transfers between devices with their start and end apart: 7 -> 7, of which waited for: 1 -> 3; matrix products, arithmetic and copies ran while one was open for 14% -> 10% of each run, Pallas kernels for 0% -> 0%
where the time goes in v16:
time: 42.1 us; the launch traced here: 41.7 us
  starting transfers between devices  15.3 us (36%)
  Pallas kernels  12.2 us (29%)
  waiting for transfers between devices  7.37 us (18%)
  local copies, waits for them, and re-layouts  2.6 us (6%)
  other arithmetic  2.33 us (6%)
  between operations  0.95 us (2%)
  matrix products  0.86 us (2%)
    ppermute x4, starting transfers between devices, shifted(): return lax.ppermute(block, axis, pairs)  12.7 us
    pallas_call x1, Pallas kernels, update(): pl.pallas_call(kern, out_shape=(jax.ShapeDtypeStruct((6, columns, length)...  12.2 us
    ppermute x3, waiting for transfers between devices, broadcast(): received = lax.ppermute(array, axis, pairs)  5.33 us
    ppermute x3, starting transfers between devices, broadcast(): received = lax.ppermute(array, axis, pairs)  2.62 us
    ppermute x4, waiting for transfers between devices, shifted(): return lax.ppermute(block, axis, pairs)  2.04 us
    slice x1, local copies, waits for them, and re-layouts, shards(): from_high = shifted(pack(state[:, :HALO], shock_height[:HALO]), 'gx', False)  1.35 us
    dot_general x1, matrix products, replicate_lanes(): jnp.dot(small, pick, precision=lax.Precision.HIGHEST, preferred_element_t...  0.86 us
  transfers between devices with their start and end apart: 7, of which 3 were waited for; matrix products, arithmetic and copies ran while one was open for 10% of the time, Pallas kernels for 0%

profile of v16, /device:TPU:113, one launch (start us, length us, event | category | flops | bytes accessed | tf_op | source)
XLA Modules:
  0.0 41.7 jit_solution(18107965846633784479)
XLA Ops:
  0.6 0.0 copy-start.5
  0.7 0.8 %slice_select_fusion = (f32[6,16,128]{2,1,0:T(8,128)S(1)}, f32[6,16,128]{2,1,0:T(8,128)S(1)}) fusion(f32[6,16,3072]{2,1,0:T(8,128)} %state_ref.1, pred[128]{0:T(512)(128)(4,1)S(1)} %iota_compare_fusion.5), kind=kLoop, calls=%fused_computation.6 | loop fusion | flops 12288 | bytes 196736 | tf_op jit(solution)/shard_map/jit(_where)/select_n | solution.py:397
  1.5 2.6 %collective-permute-start.3 = (f32[6,16,128]{2,1,0:T(8,128)S(1)}, f32[6,16,128]{2,1,0:T(8,128)S(1)}, u32[]{:S(2)}, u32[]{:S(2)}) collective-permute-start(f32[6,16,128]{2,1,0:T(8,128)S(1)} %get-tuple-element.8), channel_id=1, source_target_pairs={{1,0},{2,1},{3,2},{4,3},{5,4},{6,5},{7,6},{8,7},{9,8},{10,9},{11,1... | collective-permute-start | bytes 147464 | tf_op jit(solution)/shard_map/ppermute | solution.py:250
  4.1 0.0 copy-start.9
  4.1 0.0 copy-start.7
  4.1 2.8 %collective-permute-start.2 = (f32[6,16,128]{2,1,0:T(8,128)S(1)}, f32[6,16,128]{2,1,0:T(8,128)S(1)}, u32[]{:S(2)}, u32[]{:S(2)}) collective-permute-start(f32[6,16,128]{2,1,0:T(8,128)S(1)} %get-tuple-element.9), channel_id=1, source_target_pairs={{0,1},{1,2},{2,3},{3,4},{4,5},{5,6},{6,7},{7,8},{8,9},{9,10},{10,1... | collective-permute-start | bytes 147464 | tf_op jit(solution)/shard_map/ppermute | solution.py:250
  6.9 1.3 %fusion.12 = (f32[6,3,3072]{2,1,0:T(4,128)S(1)}, f32[6,3,3072]{2,1,0:T(4,128)S(1)}) fusion(f32[6,16,3072]{2,1,0:T(8,128)} %state_ref.1), kind=kLoop, calls=%fused_computation.39 | loop fusion | bytes 884736 | tf_op jit(solution)/shard_map/slice | solution.py:393
  8.2 0.1 select_maximum_fusion.1
  8.3 3.1 %collective-permute-start = (f32[7,3,3072]{2,1,0:T(4,128)S(1)}, f32[7,3,3072]{2,1,0:T(4,128)S(1)}, u32[]{:S(2)}, u32[]{:S(2)}) collective-permute-start(f32[7,3,3072]{2,1,0:T(4,128)S(1)} %select_maximum_fusion.1), channel_id=1, source_target_pairs={{0,16},{16,32},{32,48},{48,64},{64,80},{80,96},{96,112},{112,128},... | collective-permute-start | bytes 774152 | tf_op jit(solution)/shard_map/ppermute | solution.py:250
  11.4 0.1 select_maximum_fusion
  11.5 4.3 %collective-permute-start.1 = (f32[7,3,3072]{2,1,0:T(4,128)S(1)}, f32[7,3,3072]{2,1,0:T(4,128)S(1)}, u32[]{:S(2)}, u32[]{:S(2)}) collective-permute-start(f32[7,3,3072]{2,1,0:T(4,128)S(1)} %select_maximum_fusion), channel_id=1, source_target_pairs={{16,0},{32,16},{48,32},{64,48},{80,64},{96,80},{112,96},{128,112},... | collective-permute-start | bytes 774152 | tf_op jit(solution)/shard_map/ppermute | solution.py:250
  15.8 0.1 copy.36
  16.0 0.2 select_reduce_fusion.1
  16.1 0.1 iota_compare_fusion.3
  16.2 0.1 select_reduce_fusion
  16.4 0.8 %select_select_fusion.1 = f32[6,16,128]{2,1,0:T(8,128)S(1)} fusion(f32[6,16,128]{2,1,0:T(8,128)S(1)} %collective-permute-done.2.below_ref, f32[6,16,128]{2,1,0:T(8,128)S(1)} %collective-permute-done.3.above_ref, pred[]{:T(512)S(6)} %eq.81, pred[]{:T(512)S(6)} %eq.80, f32[6,16,3072]{2,1,0:T(8,128)} %state_ref.1), kind=kLoop, calls=%fused_computation.5 | loop fusion | flops 24576 | bytes 196610 | tf_op jit(solution)/shard_map/jit(_where)/select_n | solution.py:409
  17.2 0.7 %collective-permute-start.5 = (f32[6,16,128]{2,1,0:T(8,128)S(1)}, f32[6,16,128]{2,1,0:T(8,128)S(1)}, u32[]{:S(2)}, u32[]{:S(2)}) collective-permute-start(f32[6,16,128]{2,1,0:T(8,128)S(1)} %select_select_fusion.1), channel_id=1, source_target_pairs={{15,1},{14,2},{0,3},{31,17},{30,18},{16,19},{47,33},{46,34},{32,35... | collective-permute-start | bytes 147464 | tf_op jit(solution)/shard_map/ppermute | solution.py:269
  17.9 0.7 %collective-permute-start.4 = (f32[6,16,128]{2,1,0:T(8,128)S(1)}, f32[6,16,128]{2,1,0:T(8,128)S(1)}, u32[]{:S(2)}, u32[]{:S(2)}) collective-permute-start(f32[6,16,128]{2,1,0:T(8,128)S(1)} %select_select_fusion.1), channel_id=1, source_target_pairs={{15,4},{14,5},{0,6},{31,20},{30,21},{16,22},{47,36},{46,37},{32,38... | collective-permute-start | bytes 147464 | tf_op jit(solution)/shard_map/ppermute | solution.py:269
  18.6 0.1 copy.39
  18.7 1.3 %collective-permute-start.6 = (f32[6,16,128]{2,1,0:T(8,128)S(1)}, f32[6,16,128]{2,1,0:T(8,128)S(1)}, u32[]{:S(2)}, u32[]{:S(2)}) collective-permute-start(f32[6,16,128]{2,1,0:T(8,128)S(1)} %select_select_fusion.before_ref), channel_id=1, source_target_pairs={{15,7},{14,8},{0,9},{1,10},{2,11},{3,12},{4,13},{31,23},{30,24},{1... | collective-permute-start | bytes 147464 | tf_op jit(solution)/shard_map/ppermute | solution.py:269
  20.0 0.3 collective-permute-done.xlo_ref
  20.3 0.1 copy.35
  20.4 1.7 %collective-permute-done.1.xhi_ref = f32[7,3,3072]{2,1,0:T(4,128)S(1)} collective-permute-done((f32[7,3,3072]{2,1,0:T(4,128)S(1)}, f32[7,3,3072]{2,1,0:T(4,128)S(1)}, u32[]{:S(2)}, u32[]{:S(2)}) %collective-permute-start.1) | collective-permute-done | bytes 258080 | tf_op jit(solution)/shard_map/ppermute | solution.py:250
  22.2 0.1 copy.37
  22.3 0.1 fusion.1
  22.4 0.1 broadcast_in_dim.95
  22.5 0.1 broadcast_in_dim.99
  22.5 0.1 concatenate.51
  22.6 0.9 %fusion.8.geo_ref = f32[96,128]{1,0:T(8,128)} fusion(f32[96,32]{0,1:T(8,128)S(1)} %concatenate.51, s32[128]{0:T(128)S(1)} %and_select_fusion), kind=kOutput, calls=%fused_computation.22 | convolution fusion | flops 4722688 | bytes 61952 | tf_op jit(solution)/shard_map/dot_general | solution.py:372
  23.5 5.3 %collective-permute-done.6.last_ref = f32[6,16,128]{2,1,0:T(8,128)S(1)} collective-permute-done((f32[6,16,128]{2,1,0:T(8,128)S(1)}, f32[6,16,128]{2,1,0:T(8,128)S(1)}, u32[]{:S(2)}, u32[]{:S(2)}) %collective-permute-start.6) | collective-permute-done | bytes 49184 | tf_op jit(solution)/shard_map/ppermute | solution.py:269
  28.9 0.6 %copy-done.6 = f32[6,16,128]{2,1,0:T(8,128)} copy-done((f32[6,16,128]{2,1,0:T(8,128)}, f32[6,16,128]{2,1,0:T(8,128)S(1)}, u32[]{:S(2)}) %copy-start.6) | copy-done | bytes 49176
  29.5 12.2 %shard_map.68 = (f32[6,16,3072]{2,1,0:T(8,128)}, f32[16,32]{1,0:T(8,128)}) custom-call(f32[6,16,3072]{2,1,0:T(8,128)} %state_ref.1, f32[7,3,3072]{2,1,0:T(4,128)} %copy-done, f32[7,3,3072]{2,1,0:T(4,128)} %copy-done.1, f32[6,16,128]{2,1,0:T(8,128)} %copy-done.3, f32[6,16,128]{2,1,0:T(8,128)} %copy-done.2, f32[96,128]{1,0:T(8,128)} %fusion.8.geo_ref, ...), custom_call_target="tpu_custom_call" | custom-call | tf_op jit(solution)/shard_map/pallas_call | solution.py:227
  (34 shorter events, 0.1 us)
Async XLA Ops:
  0.6 7.6 %copy-start.5 = (f32[16,32]{1,0:T(8,128)S(1)}, f32[16,32]{1,0:T(8,128)}, u32[]{:S(2)}) copy-start(f32[16,32]{1,0:T(8,128)} %height_ref.1) | copy-start | bytes 6148
  1.5 14.9 %collective-permute-start.3 = (f32[6,16,128]{2,1,0:T(8,128)S(1)}, f32[6,16,128]{2,1,0:T(8,128)S(1)}, u32[]{:S(2)}, u32[]{:S(2)}) collective-permute-start(f32[6,16,128]{2,1,0:T(8,128)S(1)} %get-tuple-element.8), channel_id=1, source_target_pairs={{1,0},{2,1},{3,2},{4,3},{5,4},{6,5},{7,6},{8,7},{9,8},{10,9},{11,1... | collective-permute-start | bytes 147464 | tf_op jit(solution)/shard_map/ppermute | solution.py:250
  4.1 11.9 %copy-start.8 = (s32[16]{0:T(128)S(1)}, s32[16]{0:T(128)}, u32[]{:S(2)}) copy-start(s32[16]{0:T(128)} %param.8) | copy-start | bytes 196
  4.1 11.9 %copy-start.9 = (s32[16]{0:T(128)S(1)}, s32[16]{0:T(128)}, u32[]{:S(2)}) copy-start(s32[16]{0:T(128)} %param.7) | copy-start | bytes 196
  4.1 12.1 %copy-start.7 = (f32[16,32]{1,0:T(8,128)S(1)}, f32[16,32]{1,0:T(8,128)}, u32[]{:S(2)}) copy-start(f32[16,32]{1,0:T(8,128)} %param.9) | copy-start | bytes 6148
  4.1 12.3 %collective-permute-start.2 = (f32[6,16,128]{2,1,0:T(8,128)S(1)}, f32[6,16,128]{2,1,0:T(8,128)S(1)}, u32[]{:S(2)}, u32[]{:S(2)}) collective-permute-start(f32[6,16,128]{2,1,0:T(8,128)S(1)} %get-tuple-element.9), channel_id=1, source_target_pairs={{0,1},{1,2},{2,3},{3,4},{4,5},{5,6},{6,7},{7,8},{8,9},{9,10},{10,1... | collective-permute-start | bytes 147464 | tf_op jit(solution)/shard_map/ppermute | solution.py:250
  8.3 12.0 %collective-permute-start = (f32[7,3,3072]{2,1,0:T(4,128)S(1)}, f32[7,3,3072]{2,1,0:T(4,128)S(1)}, u32[]{:S(2)}, u32[]{:S(2)}) collective-permute-start(f32[7,3,3072]{2,1,0:T(4,128)S(1)} %select_maximum_fusion.1), channel_id=1, source_target_pairs={{0,16},{16,32},{32,48},{48,64},{64,80},{80,96},{96,112},{112,128},... | collective-permute-start | bytes 774152 | tf_op jit(solution)/shard_map/ppermute | solution.py:250
  11.5 10.6 %collective-permute-start.1 = (f32[7,3,3072]{2,1,0:T(4,128)S(1)}, f32[7,3,3072]{2,1,0:T(4,128)S(1)}, u32[]{:S(2)}, u32[]{:S(2)}) collective-permute-start(f32[7,3,3072]{2,1,0:T(4,128)S(1)} %select_maximum_fusion), channel_id=1, source_target_pairs={{16,0},{32,16},{48,32},{64,48},{80,64},{96,80},{112,96},{128,112},... | collective-permute-start | bytes 774152 | tf_op jit(solution)/shard_map/ppermute | solution.py:250
  16.4 12.4 %copy-start.2 = (f32[6,16,128]{2,1,0:T(8,128)}, f32[6,16,128]{2,1,0:T(8,128)S(1)}, u32[]{:S(2)}) copy-start(f32[6,16,128]{2,1,0:T(8,128)S(1)} %collective-permute-done.3.above_ref) | copy-start | bytes 147460
  16.4 12.4 %copy-start.3 = (f32[6,16,128]{2,1,0:T(8,128)}, f32[6,16,128]{2,1,0:T(8,128)S(1)}, u32[]{:S(2)}) copy-start(f32[6,16,128]{2,1,0:T(8,128)S(1)} %collective-permute-done.2.below_ref) | copy-start | bytes 147460
  17.2 1.5 %collective-permute-start.5 = (f32[6,16,128]{2,1,0:T(8,128)S(1)}, f32[6,16,128]{2,1,0:T(8,128)S(1)}, u32[]{:S(2)}, u32[]{:S(2)}) collective-permute-start(f32[6,16,128]{2,1,0:T(8,128)S(1)} %select_select_fusion.1), channel_id=1, source_target_pairs={{15,1},{14,2},{0,3},{31,17},{30,18},{16,19},{47,33},{46,34},{32,35... | collective-permute-start | bytes 147464 | tf_op jit(solution)/shard_map/ppermute | solution.py:269
  17.9 0.8 %collective-permute-start.4 = (f32[6,16,128]{2,1,0:T(8,128)S(1)}, f32[6,16,128]{2,1,0:T(8,128)S(1)}, u32[]{:S(2)}, u32[]{:S(2)}) collective-permute-start(f32[6,16,128]{2,1,0:T(8,128)S(1)} %select_select_fusion.1), channel_id=1, source_target_pairs={{15,4},{14,5},{0,6},{31,20},{30,21},{16,22},{47,36},{46,37},{32,38... | collective-permute-start | bytes 147464 | tf_op jit(solution)/shard_map/ppermute | solution.py:269
  18.7 10.1 %copy-start.4 = (f32[6,16,128]{2,1,0:T(8,128)}, f32[6,16,128]{2,1,0:T(8,128)S(1)}, u32[]{:S(2)}) copy-start(f32[6,16,128]{2,1,0:T(8,128)S(1)} %select_select_fusion.before_ref) | copy-start | bytes 147460
  18.7 10.1 %collective-permute-start.6 = (f32[6,16,128]{2,1,0:T(8,128)S(1)}, f32[6,16,128]{2,1,0:T(8,128)S(1)}, u32[]{:S(2)}, u32[]{:S(2)}) collective-permute-start(f32[6,16,128]{2,1,0:T(8,128)S(1)} %select_select_fusion.before_ref), channel_id=1, source_target_pairs={{15,7},{14,8},{0,9},{1,10},{2,11},{3,12},{4,13},{31,23},{30,24},{1... | collective-permute-start | bytes 147464 | tf_op jit(solution)/shard_map/ppermute | solution.py:269
  20.3 8.5 %copy-start = (f32[7,3,3072]{2,1,0:T(4,128)}, f32[7,3,3072]{2,1,0:T(4,128)S(1)}, u32[]{:S(2)}) copy-start(f32[7,3,3072]{2,1,0:T(4,128)S(1)} %collective-permute-done.xlo_ref) | copy-start | bytes 774148
  22.2 6.7 %copy-start.1 = (f32[7,3,3072]{2,1,0:T(4,128)}, f32[7,3,3072]{2,1,0:T(4,128)S(1)}, u32[]{:S(2)}) copy-start(f32[7,3,3072]{2,1,0:T(4,128)S(1)} %collective-permute-done.1.xhi_ref) | copy-start | bytes 774148
  28.8 0.6 %copy-start.6 = (f32[6,16,128]{2,1,0:T(8,128)}, f32[6,16,128]{2,1,0:T(8,128)S(1)}, u32[]{:S(2)}) copy-start(f32[6,16,128]{2,1,0:T(8,128)S(1)} %collective-permute-done.6.last_ref) | copy-start | bytes 147460

commit v17 on v16

--- a/solution.py
+++ b/solution.py
@@ -409,7 +409,7 @@
     top_seed = jnp.where(row_dev == row_devs - 1, top_block, jnp.where(row_dev == 0, below, above))
     top_seed, below, above = lax.optimization_barrier((top_seed, below, above))
     seeded = sorted({row_devs - 1, 0, max(row_devs - 2, 0)}, reverse=True)
-    top_before, top_last, last_targets = broadcast(top_seed, "gy", seeded, (2, 1, 1, 1, 1))
+    top_before, top_last, last_targets = broadcast(top_seed, "gy", seeded, (1, 2, 1, 1, 1))
 
     blowing = wall_flux(wall_segment, segment_level, blow_table)
 

time: 42.1 us -> 42 us (level)
  the two profiles are of different devices: /device:TPU:113 before, /device:TPU:40 now
where the time goes in v17:
time: 42 us; the launch traced here: 41.6 us
  starting transfers between devices  13.6 us (32%)
  Pallas kernels  12.2 us (29%)
  waiting for transfers between devices  8.38 us (20%)
  other arithmetic  2.95 us (7%)
  local copies, waits for them, and re-layouts  2.59 us (6%)
  between operations  0.96 us (2%)
  matrix products  0.87 us (2%)
    pallas_call x1, Pallas kernels, update(): pl.pallas_call(kern, out_shape=(jax.ShapeDtypeStruct((6, columns, length)...  12.2 us
    ppermute x4, starting transfers between devices, shifted(): return lax.ppermute(block, axis, pairs)  10.4 us
    ppermute x3, waiting for transfers between devices, broadcast(): received = lax.ppermute(array, axis, pairs)  8.37 us
    ppermute x3, starting transfers between devices, broadcast(): received = lax.ppermute(array, axis, pairs)  3.23 us
    slice x1, local copies, waits for them, and re-layouts, shards(): from_high = shifted(pack(state[:, :HALO], shock_height[:HALO]), 'gx', False)  1.35 us
    dot_general x1, matrix products, replicate_lanes(): jnp.dot(small, pick, precision=lax.Precision.HIGHEST, preferred_element_t...  0.87 us
  transfers between devices with their start and end apart: 7, of which 2 were waited for; matrix products, arithmetic and copies ran while one was open for 12% of the time, Pallas kernels for 0%

profile of v17, /device:TPU:40, one launch (start us, length us, event | category | flops | bytes accessed | tf_op | source)
XLA Modules:
  0.0 41.6 jit_solution(5925326311223035961)
XLA Ops:
  0.6 0.0 copy-start.4
  0.7 0.8 %slice_select_fusion = (f32[6,16,128]{2,1,0:T(8,128)S(1)}, f32[6,16,128]{2,1,0:T(8,128)S(1)}) fusion(f32[6,16,3072]{2,1,0:T(8,128)} %state_ref.1, pred[128]{0:T(512)(128)(4,1)S(1)} %iota_compare_fusion.5), kind=kLoop, calls=%fused_computation.5 | loop fusion | flops 12288 | bytes 196736 | tf_op jit(solution)/shard_map/jit(_where)/select_n | solution.py:397
  1.5 1.9 %collective-permute-start.3 = (f32[6,16,128]{2,1,0:T(8,128)S(1)}, f32[6,16,128]{2,1,0:T(8,128)S(1)}, u32[]{:S(2)}, u32[]{:S(2)}) collective-permute-start(f32[6,16,128]{2,1,0:T(8,128)S(1)} %get-tuple-element.8), channel_id=1, source_target_pairs={{1,0},{2,1},{3,2},{4,3},{5,4},{6,5},{7,6},{8,7},{9,8},{10,9},{11,1... | collective-permute-start | bytes 147464 | tf_op jit(solution)/shard_map/ppermute | solution.py:250
  3.4 0.0 copy-start.7
  3.4 0.0 copy-start.8
  3.4 0.5 %collective-permute-start.2 = (f32[6,16,128]{2,1,0:T(8,128)S(1)}, f32[6,16,128]{2,1,0:T(8,128)S(1)}, u32[]{:S(2)}, u32[]{:S(2)}) collective-permute-start(f32[6,16,128]{2,1,0:T(8,128)S(1)} %get-tuple-element.9), channel_id=1, source_target_pairs={{0,1},{1,2},{2,3},{3,4},{4,5},{5,6},{6,7},{7,8},{8,9},{9,10},{10,1... | collective-permute-start | bytes 147464 | tf_op jit(solution)/shard_map/ppermute | solution.py:250
  4.0 1.3 %fusion.12 = (f32[6,3,3072]{2,1,0:T(4,128)S(1)}, f32[6,3,3072]{2,1,0:T(4,128)S(1)}) fusion(f32[6,16,3072]{2,1,0:T(8,128)} %state_ref.1), kind=kLoop, calls=%fused_computation.40 | loop fusion | bytes 884736 | tf_op jit(solution)/shard_map/slice | solution.py:393
  5.3 0.1 select_maximum_fusion.1
  5.4 3.4 %collective-permute-start = (f32[7,3,3072]{2,1,0:T(4,128)S(1)}, f32[7,3,3072]{2,1,0:T(4,128)S(1)}, u32[]{:S(2)}, u32[]{:S(2)}) collective-permute-start(f32[7,3,3072]{2,1,0:T(4,128)S(1)} %select_maximum_fusion.1), channel_id=1, source_target_pairs={{0,16},{16,32},{32,48},{48,64},{64,80},{80,96},{96,112},{112,128},... | collective-permute-start | bytes 774152 | tf_op jit(solution)/shard_map/ppermute | solution.py:250
  8.8 0.1 select_maximum_fusion
  8.9 4.6 %collective-permute-start.1 = (f32[7,3,3072]{2,1,0:T(4,128)S(1)}, f32[7,3,3072]{2,1,0:T(4,128)S(1)}, u32[]{:S(2)}, u32[]{:S(2)}) collective-permute-start(f32[7,3,3072]{2,1,0:T(4,128)S(1)} %select_maximum_fusion), channel_id=1, source_target_pairs={{16,0},{32,16},{48,32},{64,48},{80,64},{96,80},{112,96},{128,112},... | collective-permute-start | bytes 774152 | tf_op jit(solution)/shard_map/ppermute | solution.py:250
  13.5 0.1 copy.36
  13.6 0.2 select_reduce_fusion.1
  13.8 0.1 iota_compare_fusion.3
  13.9 0.1 select_reduce_fusion
  14.0 0.8 %select_select_fusion = f32[6,16,128]{2,1,0:T(8,128)S(1)} fusion(f32[6,16,128]{2,1,0:T(8,128)S(1)} %collective-permute-done.2.below_ref, f32[6,16,128]{2,1,0:T(8,128)S(1)} %collective-permute-done.3.above_ref, pred[]{:T(512)S(6)} %eq.90, pred[]{:T(512)S(6)} %eq.89, f32[6,16,3072]{2,1,0:T(8,128)} %state_ref.1), kind=kLoop, calls=%fused_computation.4 | loop fusion | flops 24576 | bytes 196610 | tf_op jit(solution)/shard_map/jit(_where)/select_n | solution.py:409
  14.9 1.3 %collective-permute-start.4 = (f32[6,16,128]{2,1,0:T(8,128)S(1)}, f32[6,16,128]{2,1,0:T(8,128)S(1)}, u32[]{:S(2)}, u32[]{:S(2)}) collective-permute-start(f32[6,16,128]{2,1,0:T(8,128)S(1)} %select_select_fusion), channel_id=1, source_target_pairs={{15,1},{14,2},{0,3},{31,17},{30,18},{16,19},{47,33},{46,34},{32,35... | collective-permute-start | bytes 147464 | tf_op jit(solution)/shard_map/ppermute | solution.py:269
  16.2 7.4 %collective-permute-done.4 = f32[6,16,128]{2,1,0:T(8,128)S(1)} collective-permute-done((f32[6,16,128]{2,1,0:T(8,128)S(1)}, f32[6,16,128]{2,1,0:T(8,128)S(1)}, u32[]{:S(2)}, u32[]{:S(2)}) %collective-permute-start.4) | collective-permute-done | bytes 49184 | tf_op jit(solution)/shard_map/ppermute | solution.py:269
  23.6 1.3 %collective-permute-start.5 = (f32[6,16,128]{2,1,0:T(8,128)S(1)}, f32[6,16,128]{2,1,0:T(8,128)S(1)}, u32[]{:S(2)}, u32[]{:S(2)}) collective-permute-start(f32[6,16,128]{2,1,0:T(8,128)S(1)} %broadcast_select_fusion), channel_id=1, source_target_pairs={{15,4},{14,5},{0,6},{1,7},{2,8},{3,9},{31,20},{30,21},{16,22},{17,... | collective-permute-start | bytes 147464 | tf_op jit(solution)/shard_map/ppermute | solution.py:269
  24.9 0.1 copy.39
  25.0 0.7 %collective-permute-start.6 = (f32[6,16,128]{2,1,0:T(8,128)S(1)}, f32[6,16,128]{2,1,0:T(8,128)S(1)}, u32[]{:S(2)}, u32[]{:S(2)}) collective-permute-start(f32[6,16,128]{2,1,0:T(8,128)S(1)} %broadcast_select_fusion), channel_id=1, source_target_pairs={{15,10},{14,11},{0,12},{1,13},{31,26},{30,27},{16,28},{17,29},{47,... | collective-permute-start | bytes 147464 | tf_op jit(solution)/shard_map/ppermute | solution.py:269
  25.7 1.0 %collective-permute-done.5 = f32[6,16,128]{2,1,0:T(8,128)S(1)} collective-permute-done((f32[6,16,128]{2,1,0:T(8,128)S(1)}, f32[6,16,128]{2,1,0:T(8,128)S(1)}, u32[]{:S(2)}, u32[]{:S(2)}) %collective-permute-start.5) | collective-permute-done | bytes 49184 | tf_op jit(solution)/shard_map/ppermute | solution.py:269
  26.6 0.6 %broadcast_select_fusion.1.before_ref = f32[6,16,128]{2,1,0:T(8,128)} fusion(f32[6,16,128]{2,1,0:T(8,128)S(1)} %collective-permute-done.5, f32[6,16,128]{2,1,0:T(8,128)S(1)} %broadcast_select_fusion, pred[]{:T(512)S(6)} %or.25), kind=kLoop, calls=%fused_computation.7 | loop fusion | flops 12288 | bytes 147457 | tf_op jit(solution)/shard_map/jit(_where)/select_n | solution.py:274
  27.3 0.1 copy.35
  27.4 0.1 copy.37
  27.5 0.1 fusion.1
  27.6 0.1 broadcast_in_dim.95
  27.7 0.1 broadcast_in_dim.99
  27.7 0.1 concatenate.51
  27.8 0.9 %fusion.8.geo_ref = f32[96,128]{1,0:T(8,128)} fusion(f32[96,32]{0,1:T(8,128)S(1)} %concatenate.51, s32[128]{0:T(128)S(1)} %and_select_fusion), kind=kOutput, calls=%fused_computation.23 | convolution fusion | flops 4722688 | bytes 61952 | tf_op jit(solution)/shard_map/dot_general | solution.py:372
  28.8 0.6 %copy-done.5 = f32[6,16,128]{2,1,0:T(8,128)} copy-done((f32[6,16,128]{2,1,0:T(8,128)}, f32[6,16,128]{2,1,0:T(8,128)S(1)}, u32[]{:S(2)}) %copy-start.5) | copy-done | bytes 49176
  29.4 12.2 %shard_map.68 = (f32[6,16,3072]{2,1,0:T(8,128)}, f32[16,32]{1,0:T(8,128)}) custom-call(f32[6,16,3072]{2,1,0:T(8,128)} %state_ref.1, f32[7,3,3072]{2,1,0:T(4,128)} %copy-done, f32[7,3,3072]{2,1,0:T(4,128)} %copy-done.1, f32[6,16,128]{2,1,0:T(8,128)} %copy-done.3, f32[6,16,128]{2,1,0:T(8,128)} %copy-done.2, f32[96,128]{1,0:T(8,128)} %fusion.8.geo_ref, ...), custom_call_target="tpu_custom_call" | custom-call | tf_op jit(solution)/shard_map/pallas_call | solution.py:227
  (33 shorter events, 0.1 us)
Async XLA Ops:
  0.6 4.7 %copy-start.4 = (f32[16,32]{1,0:T(8,128)S(1)}, f32[16,32]{1,0:T(8,128)}, u32[]{:S(2)}) copy-start(f32[16,32]{1,0:T(8,128)} %height_ref.1) | copy-start | bytes 6148
  1.5 12.5 %collective-permute-start.3 = (f32[6,16,128]{2,1,0:T(8,128)S(1)}, f32[6,16,128]{2,1,0:T(8,128)S(1)}, u32[]{:S(2)}, u32[]{:S(2)}) collective-permute-start(f32[6,16,128]{2,1,0:T(8,128)S(1)} %get-tuple-element.8), channel_id=1, source_target_pairs={{1,0},{2,1},{3,2},{4,3},{5,4},{6,5},{7,6},{8,7},{9,8},{10,9},{11,1... | collective-permute-start | bytes 147464 | tf_op jit(solution)/shard_map/ppermute | solution.py:250
  3.4 10.2 %copy-start.7 = (s32[16]{0:T(128)S(1)}, s32[16]{0:T(128)}, u32[]{:S(2)}) copy-start(s32[16]{0:T(128)} %param.8) | copy-start | bytes 196
  3.4 10.2 %copy-start.8 = (s32[16]{0:T(128)S(1)}, s32[16]{0:T(128)}, u32[]{:S(2)}) copy-start(s32[16]{0:T(128)} %param.7) | copy-start | bytes 196
  3.4 10.4 %copy-start.6 = (f32[16,32]{1,0:T(8,128)S(1)}, f32[16,32]{1,0:T(8,128)}, u32[]{:S(2)}) copy-start(f32[16,32]{1,0:T(8,128)} %param.9) | copy-start | bytes 6148
  3.4 10.6 %collective-permute-start.2 = (f32[6,16,128]{2,1,0:T(8,128)S(1)}, f32[6,16,128]{2,1,0:T(8,128)S(1)}, u32[]{:S(2)}, u32[]{:S(2)}) collective-permute-start(f32[6,16,128]{2,1,0:T(8,128)S(1)} %get-tuple-element.9), channel_id=1, source_target_pairs={{0,1},{1,2},{2,3},{3,4},{4,5},{5,6},{6,7},{7,8},{8,9},{9,10},{10,1... | collective-permute-start | bytes 147464 | tf_op jit(solution)/shard_map/ppermute | solution.py:250
  5.4 21.9 %collective-permute-start = (f32[7,3,3072]{2,1,0:T(4,128)S(1)}, f32[7,3,3072]{2,1,0:T(4,128)S(1)}, u32[]{:S(2)}, u32[]{:S(2)}) collective-permute-start(f32[7,3,3072]{2,1,0:T(4,128)S(1)} %select_maximum_fusion.1), channel_id=1, source_target_pairs={{0,16},{16,32},{32,48},{48,64},{64,80},{80,96},{96,112},{112,128},... | collective-permute-start | bytes 774152 | tf_op jit(solution)/shard_map/ppermute | solution.py:250
  8.9 18.5 %collective-permute-start.1 = (f32[7,3,3072]{2,1,0:T(4,128)S(1)}, f32[7,3,3072]{2,1,0:T(4,128)S(1)}, u32[]{:S(2)}, u32[]{:S(2)}) collective-permute-start(f32[7,3,3072]{2,1,0:T(4,128)S(1)} %select_maximum_fusion), channel_id=1, source_target_pairs={{16,0},{32,16},{48,32},{64,48},{80,64},{96,80},{112,96},{128,112},... | collective-permute-start | bytes 774152 | tf_op jit(solution)/shard_map/ppermute | solution.py:250
  14.0 14.7 %copy-start.2 = (f32[6,16,128]{2,1,0:T(8,128)}, f32[6,16,128]{2,1,0:T(8,128)S(1)}, u32[]{:S(2)}) copy-start(f32[6,16,128]{2,1,0:T(8,128)S(1)} %collective-permute-done.3.above_ref) | copy-start | bytes 147460
  14.0 14.7 %copy-start.3 = (f32[6,16,128]{2,1,0:T(8,128)}, f32[6,16,128]{2,1,0:T(8,128)S(1)}, u32[]{:S(2)}) copy-start(f32[6,16,128]{2,1,0:T(8,128)S(1)} %collective-permute-done.2.below_ref) | copy-start | bytes 147460
  14.9 8.7 %collective-permute-start.4 = (f32[6,16,128]{2,1,0:T(8,128)S(1)}, f32[6,16,128]{2,1,0:T(8,128)S(1)}, u32[]{:S(2)}, u32[]{:S(2)}) collective-permute-start(f32[6,16,128]{2,1,0:T(8,128)S(1)} %select_select_fusion), channel_id=1, source_target_pairs={{15,1},{14,2},{0,3},{31,17},{30,18},{16,19},{47,33},{46,34},{32,35... | collective-permute-start | bytes 147464 | tf_op jit(solution)/shard_map/ppermute | solution.py:269
  23.6 3.0 %collective-permute-start.5 = (f32[6,16,128]{2,1,0:T(8,128)S(1)}, f32[6,16,128]{2,1,0:T(8,128)S(1)}, u32[]{:S(2)}, u32[]{:S(2)}) collective-permute-start(f32[6,16,128]{2,1,0:T(8,128)S(1)} %broadcast_select_fusion), channel_id=1, source_target_pairs={{15,4},{14,5},{0,6},{1,7},{2,8},{3,9},{31,20},{30,21},{16,22},{17,... | collective-permute-start | bytes 147464 | tf_op jit(solution)/shard_map/ppermute | solution.py:269
  25.0 3.7 %collective-permute-start.6 = (f32[6,16,128]{2,1,0:T(8,128)S(1)}, f32[6,16,128]{2,1,0:T(8,128)S(1)}, u32[]{:S(2)}, u32[]{:S(2)}) collective-permute-start(f32[6,16,128]{2,1,0:T(8,128)S(1)} %broadcast_select_fusion), channel_id=1, source_target_pairs={{15,10},{14,11},{0,12},{1,13},{31,26},{30,27},{16,28},{17,29},{47,... | collective-permute-start | bytes 147464 | tf_op jit(solution)/shard_map/ppermute | solution.py:269
  27.3 1.4 %copy-start = (f32[7,3,3072]{2,1,0:T(4,128)}, f32[7,3,3072]{2,1,0:T(4,128)S(1)}, u32[]{:S(2)}) copy-start(f32[7,3,3072]{2,1,0:T(4,128)S(1)} %collective-permute-done.xlo_ref) | copy-start | bytes 774148
  27.4 1.4 %copy-start.1 = (f32[7,3,3072]{2,1,0:T(4,128)}, f32[7,3,3072]{2,1,0:T(4,128)S(1)}, u32[]{:S(2)}) copy-start(f32[7,3,3072]{2,1,0:T(4,128)S(1)} %collective-permute-done.1.xhi_ref) | copy-start | bytes 774148
  28.7 0.6 %copy-start.5 = (f32[6,16,128]{2,1,0:T(8,128)}, f32[6,16,128]{2,1,0:T(8,128)S(1)}, u32[]{:S(2)}) copy-start(f32[6,16,128]{2,1,0:T(8,128)S(1)} %collective-permute-done.6.last_ref) | copy-start | bytes 147460

commit v18 on v17

--- a/solution.py
+++ b/solution.py
@@ -70,8 +70,8 @@
             qx_ref[c, 0:XPAD, :] = state_ref[c, 0:XPAD, :]
             qx_ref[c, XPAD:XPAD + columns, :] = state_ref[c]
             qx_ref[c, XPAD + columns:, :] = state_ref[c, columns - XPAD:, :]
-            qx_ref[c, XPAD - HALO:XPAD, :] = xlo_ref[c]
-            qx_ref[c, XPAD + columns:XPAD + columns + HALO, :] = xhi_ref[c]
+            qx_ref[c, XPAD - HALO:XPAD, :] = xlo_ref[c, :, 0:length]
+            qx_ref[c, XPAD + columns:XPAD + columns + HALO, :] = xhi_ref[c, :, 0:length]
             qy_ref[c, :, 0:PAD] = below_ref[c]
             qy_ref[c, :, PAD:PAD + length] = state_ref[c]
             qy_ref[c, :, PAD + length:] = above_ref[c]
@@ -385,9 +385,9 @@
     band = HALO * planes
 
     def pack(cols, heights):
-        extra = jnp.zeros((1, HALO, length), jnp.float32)
+        extra = jnp.zeros((6, HALO, LANES), jnp.float32)
         extra = lax.dynamic_update_slice(extra, heights[None], (0, 0, 0))
-        return jnp.concatenate([cols, extra], axis=0)
+        return jnp.concatenate([cols, extra], axis=2)
 
     from_low = shifted(pack(state[:, columns - HALO :], shock_height[columns - HALO :]), "gx", True)
     from_high = shifted(pack(state[:, :HALO], shock_height[:HALO]), "gx", False)
@@ -396,12 +396,12 @@
     below = shifted(top_block, "gy", True, cyclic=True)
     above = shifted(jnp.where(plane_lane < band, state[..., :PAD], top_block), "gy", False)
     low_height = jnp.where(
-        col_dev == 0, jnp.broadcast_to(shock_height[:1], (HALO, planes)), from_low[6, :, :planes]
+        col_dev == 0, jnp.broadcast_to(shock_height[:1], (HALO, planes)), from_low[0, :, length : length + planes]
     )
     high_height = jnp.where(
         col_dev == col_devs - 1,
         jnp.broadcast_to(shock_height[columns - 1 :], (HALO, planes)),
-        from_high[6, :, :planes],
+        from_high[0, :, length : length + planes],
     )
     height_ext = jnp.concatenate([low_height, shock_height, high_height], axis=0)
     slope_x, slope_z = slopes(height_ext, planes)

time: 42 us -> 42 us (level)
  no operation moved by 1% of the time
where the time goes in v18:
time: 42 us; the launch traced here: 41.6 us
  starting transfers between devices  13.6 us (32%)
  Pallas kernels  12.3 us (29%)
  waiting for transfers between devices  8.38 us (20%)
  other arithmetic  2.98 us (7%)
  local copies, waits for them, and re-layouts  2.58 us (6%)
  between operations  0.96 us (2%)
  matrix products  0.85 us (2%)
    pallas_call x1, Pallas kernels, update(): pl.pallas_call(kern, out_shape=(jax.ShapeDtypeStruct((6, columns, length)...  12.3 us
    ppermute x4, starting transfers between devices, shifted(): return lax.ppermute(block, axis, pairs)  10.4 us
    ppermute x3, waiting for transfers between devices, broadcast(): received = lax.ppermute(array, axis, pairs)  8.37 us
    ppermute x3, starting transfers between devices, broadcast(): received = lax.ppermute(array, axis, pairs)  3.23 us
    slice x1, local copies, waits for them, and re-layouts, shards(): from_high = shifted(pack(state[:, :HALO], shock_height[:HALO]), 'gx', False)  1.35 us
    dot_general x1, matrix products, replicate_lanes(): jnp.dot(small, pick, precision=lax.Precision.HIGHEST, preferred_element_t...  0.85 us
  transfers between devices with their start and end apart: 7, of which 2 were waited for; matrix products, arithmetic and copies ran while one was open for 12% of the time, Pallas kernels for 0%

profile of v18, /device:TPU:40, one launch (start us, length us, event | category | flops | bytes accessed | tf_op | source)
XLA Modules:
  0.0 41.6 jit_solution(9033492084621911240)
XLA Ops:
  0.6 0.0 copy-start.4
  0.7 0.8 %slice_select_fusion = (f32[6,16,128]{2,1,0:T(8,128)S(1)}, f32[6,16,128]{2,1,0:T(8,128)S(1)}) fusion(f32[6,16,3072]{2,1,0:T(8,128)} %state_ref.1, pred[128]{0:T(512)(128)(4,1)S(1)} %iota_compare_fusion.5), kind=kLoop, calls=%fused_computation.5 | loop fusion | flops 12288 | bytes 196736 | tf_op jit(solution)/shard_map/jit(_where)/select_n | solution.py:397
  1.5 1.9 %collective-permute-start.3 = (f32[6,16,128]{2,1,0:T(8,128)S(1)}, f32[6,16,128]{2,1,0:T(8,128)S(1)}, u32[]{:S(2)}, u32[]{:S(2)}) collective-permute-start(f32[6,16,128]{2,1,0:T(8,128)S(1)} %get-tuple-element.8), channel_id=1, source_target_pairs={{1,0},{2,1},{3,2},{4,3},{5,4},{6,5},{7,6},{8,7},{9,8},{10,9},{11,1... | collective-permute-start | bytes 147464 | tf_op jit(solution)/shard_map/ppermute | solution.py:250
  3.4 0.0 copy-start.7
  3.4 0.0 copy-start.8
  3.4 0.5 %collective-permute-start.2 = (f32[6,16,128]{2,1,0:T(8,128)S(1)}, f32[6,16,128]{2,1,0:T(8,128)S(1)}, u32[]{:S(2)}, u32[]{:S(2)}) collective-permute-start(f32[6,16,128]{2,1,0:T(8,128)S(1)} %get-tuple-element.9), channel_id=1, source_target_pairs={{0,1},{1,2},{2,3},{3,4},{4,5},{5,6},{6,7},{7,8},{8,9},{9,10},{10,1... | collective-permute-start | bytes 147464 | tf_op jit(solution)/shard_map/ppermute | solution.py:250
  4.0 1.3 %fusion.12 = (f32[6,3,3072]{2,1,0:T(4,128)S(1)}, f32[6,3,3072]{2,1,0:T(4,128)S(1)}) fusion(f32[6,16,3072]{2,1,0:T(8,128)} %state_ref.1), kind=kLoop, calls=%fused_computation.40 | loop fusion | bytes 884736 | tf_op jit(solution)/shard_map/slice | solution.py:393
  5.3 0.1 select_maximum_fusion.1
  5.4 3.4 %collective-permute-start = (f32[6,3,3200]{2,1,0:T(4,128)S(1)}, f32[6,3,3200]{2,1,0:T(4,128)S(1)}, u32[]{:S(2)}, u32[]{:S(2)}) collective-permute-start(f32[6,3,3200]{2,1,0:T(4,128)S(1)} %select_maximum_fusion.1), channel_id=1, source_target_pairs={{0,16},{16,32},{32,48},{48,64},{64,80},{80,96},{96,112},{112,128},... | collective-permute-start | bytes 691208 | tf_op jit(solution)/shard_map/ppermute | solution.py:250
  8.8 0.1 select_maximum_fusion
  8.9 4.6 %collective-permute-start.1 = (f32[6,3,3200]{2,1,0:T(4,128)S(1)}, f32[6,3,3200]{2,1,0:T(4,128)S(1)}, u32[]{:S(2)}, u32[]{:S(2)}) collective-permute-start(f32[6,3,3200]{2,1,0:T(4,128)S(1)} %select_maximum_fusion), channel_id=1, source_target_pairs={{16,0},{32,16},{48,32},{64,48},{80,64},{96,80},{112,96},{128,112},... | collective-permute-start | bytes 691208 | tf_op jit(solution)/shard_map/ppermute | solution.py:250
  13.5 0.1 copy.36
  13.6 0.2 select_reduce_fusion.1
  13.8 0.1 iota_compare_fusion.3
  13.9 0.1 select_reduce_fusion
  14.1 0.8 %select_select_fusion = f32[6,16,128]{2,1,0:T(8,128)S(1)} fusion(f32[6,16,128]{2,1,0:T(8,128)S(1)} %collective-permute-done.2.below_ref, f32[6,16,128]{2,1,0:T(8,128)S(1)} %collective-permute-done.3.above_ref, pred[]{:T(512)S(6)} %eq.90, pred[]{:T(512)S(6)} %eq.89, f32[6,16,3072]{2,1,0:T(8,128)} %state_ref.1), kind=kLoop, calls=%fused_computation.4 | loop fusion | flops 24576 | bytes 196610 | tf_op jit(solution)/shard_map/jit(_where)/select_n | solution.py:409
  14.9 1.3 %collective-permute-start.4 = (f32[6,16,128]{2,1,0:T(8,128)S(1)}, f32[6,16,128]{2,1,0:T(8,128)S(1)}, u32[]{:S(2)}, u32[]{:S(2)}) collective-permute-start(f32[6,16,128]{2,1,0:T(8,128)S(1)} %select_select_fusion), channel_id=1, source_target_pairs={{15,1},{14,2},{0,3},{31,17},{30,18},{16,19},{47,33},{46,34},{32,35... | collective-permute-start | bytes 147464 | tf_op jit(solution)/shard_map/ppermute | solution.py:269
  16.2 7.4 %collective-permute-done.4 = f32[6,16,128]{2,1,0:T(8,128)S(1)} collective-permute-done((f32[6,16,128]{2,1,0:T(8,128)S(1)}, f32[6,16,128]{2,1,0:T(8,128)S(1)}, u32[]{:S(2)}, u32[]{:S(2)}) %collective-permute-start.4) | collective-permute-done | bytes 49184 | tf_op jit(solution)/shard_map/ppermute | solution.py:269
  23.6 1.3 %collective-permute-start.5 = (f32[6,16,128]{2,1,0:T(8,128)S(1)}, f32[6,16,128]{2,1,0:T(8,128)S(1)}, u32[]{:S(2)}, u32[]{:S(2)}) collective-permute-start(f32[6,16,128]{2,1,0:T(8,128)S(1)} %broadcast_select_fusion), channel_id=1, source_target_pairs={{15,4},{14,5},{0,6},{1,7},{2,8},{3,9},{31,20},{30,21},{16,22},{17,... | collective-permute-start | bytes 147464 | tf_op jit(solution)/shard_map/ppermute | solution.py:269
  25.0 0.1 copy.39
  25.0 0.7 %collective-permute-start.6 = (f32[6,16,128]{2,1,0:T(8,128)S(1)}, f32[6,16,128]{2,1,0:T(8,128)S(1)}, u32[]{:S(2)}, u32[]{:S(2)}) collective-permute-start(f32[6,16,128]{2,1,0:T(8,128)S(1)} %broadcast_select_fusion), channel_id=1, source_target_pairs={{15,10},{14,11},{0,12},{1,13},{31,26},{30,27},{16,28},{17,29},{47,... | collective-permute-start | bytes 147464 | tf_op jit(solution)/shard_map/ppermute | solution.py:269
  25.7 1.0 %collective-permute-done.5 = f32[6,16,128]{2,1,0:T(8,128)S(1)} collective-permute-done((f32[6,16,128]{2,1,0:T(8,128)S(1)}, f32[6,16,128]{2,1,0:T(8,128)S(1)}, u32[]{:S(2)}, u32[]{:S(2)}) %collective-permute-start.5) | collective-permute-done | bytes 49184 | tf_op jit(solution)/shard_map/ppermute | solution.py:269
  26.7 0.6 %broadcast_select_fusion.1.before_ref = f32[6,16,128]{2,1,0:T(8,128)} fusion(f32[6,16,128]{2,1,0:T(8,128)S(1)} %collective-permute-done.5, f32[6,16,128]{2,1,0:T(8,128)S(1)} %broadcast_select_fusion, pred[]{:T(512)S(6)} %or.25), kind=kLoop, calls=%fused_computation.7 | loop fusion | flops 12288 | bytes 147457 | tf_op jit(solution)/shard_map/jit(_where)/select_n | solution.py:274
  27.3 0.1 copy.35
  27.4 0.1 copy.37
  27.5 0.1 fusion.1
  27.6 0.1 broadcast_in_dim.95
  27.7 0.1 broadcast_in_dim.99
  27.8 0.1 concatenate.51
  27.9 0.9 %fusion.8.geo_ref = f32[96,128]{1,0:T(8,128)} fusion(f32[96,32]{0,1:T(8,128)S(1)} %concatenate.51, s32[128]{0:T(128)S(1)} %and_select_fusion), kind=kOutput, calls=%fused_computation.23 | convolution fusion | flops 4722688 | bytes 61952 | tf_op jit(solution)/shard_map/dot_general | solution.py:372
  28.8 0.6 %copy-done.5 = f32[6,16,128]{2,1,0:T(8,128)} copy-done((f32[6,16,128]{2,1,0:T(8,128)}, f32[6,16,128]{2,1,0:T(8,128)S(1)}, u32[]{:S(2)}) %copy-start.5) | copy-done | bytes 49176
  29.4 12.3 %shard_map.68 = (f32[6,16,3072]{2,1,0:T(8,128)}, f32[16,32]{1,0:T(8,128)}) custom-call(f32[6,16,3072]{2,1,0:T(8,128)} %state_ref.1, f32[6,3,3200]{2,1,0:T(4,128)} %copy-done, f32[6,3,3200]{2,1,0:T(4,128)} %copy-done.1, f32[6,16,128]{2,1,0:T(8,128)} %copy-done.3, f32[6,16,128]{2,1,0:T(8,128)} %copy-done.2, f32[96,128]{1,0:T(8,128)} %fusion.8.geo_ref, ...), custom_call_target="tpu_custom_call" | custom-call | tf_op jit(solution)/shard_map/pallas_call | solution.py:227
  (33 shorter events, 0.1 us)
Async XLA Ops:
  0.6 4.7 %copy-start.4 = (f32[16,32]{1,0:T(8,128)S(1)}, f32[16,32]{1,0:T(8,128)}, u32[]{:S(2)}) copy-start(f32[16,32]{1,0:T(8,128)} %height_ref.1) | copy-start | bytes 6148
  1.5 12.5 %collective-permute-start.3 = (f32[6,16,128]{2,1,0:T(8,128)S(1)}, f32[6,16,128]{2,1,0:T(8,128)S(1)}, u32[]{:S(2)}, u32[]{:S(2)}) collective-permute-start(f32[6,16,128]{2,1,0:T(8,128)S(1)} %get-tuple-element.8), channel_id=1, source_target_pairs={{1,0},{2,1},{3,2},{4,3},{5,4},{6,5},{7,6},{8,7},{9,8},{10,9},{11,1... | collective-permute-start | bytes 147464 | tf_op jit(solution)/shard_map/ppermute | solution.py:250
  3.4 10.2 %copy-start.7 = (s32[16]{0:T(128)S(1)}, s32[16]{0:T(128)}, u32[]{:S(2)}) copy-start(s32[16]{0:T(128)} %param.8) | copy-start | bytes 196
  3.4 10.2 %copy-start.8 = (s32[16]{0:T(128)S(1)}, s32[16]{0:T(128)}, u32[]{:S(2)}) copy-start(s32[16]{0:T(128)} %param.7) | copy-start | bytes 196
  3.4 10.4 %copy-start.6 = (f32[16,32]{1,0:T(8,128)S(1)}, f32[16,32]{1,0:T(8,128)}, u32[]{:S(2)}) copy-start(f32[16,32]{1,0:T(8,128)} %param.9) | copy-start | bytes 6148
  3.4 10.6 %collective-permute-start.2 = (f32[6,16,128]{2,1,0:T(8,128)S(1)}, f32[6,16,128]{2,1,0:T(8,128)S(1)}, u32[]{:S(2)}, u32[]{:S(2)}) collective-permute-start(f32[6,16,128]{2,1,0:T(8,128)S(1)} %get-tuple-element.9), channel_id=1, source_target_pairs={{0,1},{1,2},{2,3},{3,4},{4,5},{5,6},{6,7},{7,8},{8,9},{9,10},{10,1... | collective-permute-start | bytes 147464 | tf_op jit(solution)/shard_map/ppermute | solution.py:250
  5.4 21.9 %collective-permute-start = (f32[6,3,3200]{2,1,0:T(4,128)S(1)}, f32[6,3,3200]{2,1,0:T(4,128)S(1)}, u32[]{:S(2)}, u32[]{:S(2)}) collective-permute-start(f32[6,3,3200]{2,1,0:T(4,128)S(1)} %select_maximum_fusion.1), channel_id=1, source_target_pairs={{0,16},{16,32},{32,48},{48,64},{64,80},{80,96},{96,112},{112,128},... | collective-permute-start | bytes 691208 | tf_op jit(solution)/shard_map/ppermute | solution.py:250
  8.9 18.5 %collective-permute-start.1 = (f32[6,3,3200]{2,1,0:T(4,128)S(1)}, f32[6,3,3200]{2,1,0:T(4,128)S(1)}, u32[]{:S(2)}, u32[]{:S(2)}) collective-permute-start(f32[6,3,3200]{2,1,0:T(4,128)S(1)} %select_maximum_fusion), channel_id=1, source_target_pairs={{16,0},{32,16},{48,32},{64,48},{80,64},{96,80},{112,96},{128,112},... | collective-permute-start | bytes 691208 | tf_op jit(solution)/shard_map/ppermute | solution.py:250
  14.0 14.7 %copy-start.2 = (f32[6,16,128]{2,1,0:T(8,128)}, f32[6,16,128]{2,1,0:T(8,128)S(1)}, u32[]{:S(2)}) copy-start(f32[6,16,128]{2,1,0:T(8,128)S(1)} %collective-permute-done.3.above_ref) | copy-start | bytes 147460
  14.0 14.7 %copy-start.3 = (f32[6,16,128]{2,1,0:T(8,128)}, f32[6,16,128]{2,1,0:T(8,128)S(1)}, u32[]{:S(2)}) copy-start(f32[6,16,128]{2,1,0:T(8,128)S(1)} %collective-permute-done.2.below_ref) | copy-start | bytes 147460
  14.9 8.7 %collective-permute-start.4 = (f32[6,16,128]{2,1,0:T(8,128)S(1)}, f32[6,16,128]{2,1,0:T(8,128)S(1)}, u32[]{:S(2)}, u32[]{:S(2)}) collective-permute-start(f32[6,16,128]{2,1,0:T(8,128)S(1)} %select_select_fusion), channel_id=1, source_target_pairs={{15,1},{14,2},{0,3},{31,17},{30,18},{16,19},{47,33},{46,34},{32,35... | collective-permute-start | bytes 147464 | tf_op jit(solution)/shard_map/ppermute | solution.py:269
  23.6 3.0 %collective-permute-start.5 = (f32[6,16,128]{2,1,0:T(8,128)S(1)}, f32[6,16,128]{2,1,0:T(8,128)S(1)}, u32[]{:S(2)}, u32[]{:S(2)}) collective-permute-start(f32[6,16,128]{2,1,0:T(8,128)S(1)} %broadcast_select_fusion), channel_id=1, source_target_pairs={{15,4},{14,5},{0,6},{1,7},{2,8},{3,9},{31,20},{30,21},{16,22},{17,... | collective-permute-start | bytes 147464 | tf_op jit(solution)/shard_map/ppermute | solution.py:269
  25.0 3.7 %collective-permute-start.6 = (f32[6,16,128]{2,1,0:T(8,128)S(1)}, f32[6,16,128]{2,1,0:T(8,128)S(1)}, u32[]{:S(2)}, u32[]{:S(2)}) collective-permute-start(f32[6,16,128]{2,1,0:T(8,128)S(1)} %broadcast_select_fusion), channel_id=1, source_target_pairs={{15,10},{14,11},{0,12},{1,13},{31,26},{30,27},{16,28},{17,29},{47,... | collective-permute-start | bytes 147464 | tf_op jit(solution)/shard_map/ppermute | solution.py:269
  27.3 1.4 %copy-start = (f32[6,3,3200]{2,1,0:T(4,128)}, f32[6,3,3200]{2,1,0:T(4,128)S(1)}, u32[]{:S(2)}) copy-start(f32[6,3,3200]{2,1,0:T(4,128)S(1)} %collective-permute-done.xlo_ref) | copy-start | bytes 691204
  27.4 1.3 %copy-start.1 = (f32[6,3,3200]{2,1,0:T(4,128)}, f32[6,3,3200]{2,1,0:T(4,128)S(1)}, u32[]{:S(2)}) copy-start(f32[6,3,3200]{2,1,0:T(4,128)S(1)} %collective-permute-done.1.xhi_ref) | copy-start | bytes 691204
  28.8 0.6 %copy-start.5 = (f32[6,16,128]{2,1,0:T(8,128)}, f32[6,16,128]{2,1,0:T(8,128)S(1)}, u32[]{:S(2)}) copy-start(f32[6,16,128]{2,1,0:T(8,128)S(1)} %collective-permute-done.6.last_ref) | copy-start | bytes 147460

commit v19 on v17

--- a/solution.py
+++ b/solution.py
@@ -213,7 +213,7 @@
                 out_ref[c, :, pl.ds(o, CHUNK)] = q[c] + dt * change
             return carry
 
-        lax.fori_loop(0, length // CHUNK, body, 0)
+        lax.fori_loop(0, length // CHUNK, body, 0, unroll=True)
 
     return kernel
 

time: 42 us -> 41.2 us (0.981)
  Pallas kernels: 12.2 us -> 11.5 us
    pallas_call x1, Pallas kernels: 12.2 us -> 11.5 us  [update(): pl.pallas_call(kern, out_shape=(jax.ShapeDtypeStruct((6, columns, length)...]
where the time goes in v19:
time: 41.2 us; the launch traced here: 40.8 us
  starting transfers between devices  13.6 us (33%)
  Pallas kernels  11.5 us (28%)
  waiting for transfers between devices  8.38 us (20%)
  other arithmetic  2.95 us (7%)
  local copies, waits for them, and re-layouts  2.59 us (6%)
  between operations  0.96 us (2%)
  matrix products  0.87 us (2%)
    pallas_call x1, Pallas kernels, update(): pl.pallas_call(kern, out_shape=(jax.ShapeDtypeStruct((6, columns, length)...  11.5 us
    ppermute x4, starting transfers between devices, shifted(): return lax.ppermute(block, axis, pairs)  10.4 us
    ppermute x3, waiting for transfers between devices, broadcast(): received = lax.ppermute(array, axis, pairs)  8.37 us
    ppermute x3, starting transfers between devices, broadcast(): received = lax.ppermute(array, axis, pairs)  3.23 us
    slice x1, local copies, waits for them, and re-layouts, shards(): from_high = shifted(pack(state[:, :HALO], shock_height[:HALO]), 'gx', False)  1.35 us
    dot_general x1, matrix products, replicate_lanes(): jnp.dot(small, pick, precision=lax.Precision.HIGHEST, preferred_element_t...  0.87 us
    select_n x1, other arithmetic, shards(): jnp.where(plane_lane < band, state[..., :PAD], top_block)  0.83 us
    select_n x1, other arithmetic, shards(): jnp.where(row_dev == row_devs - 1, top_block, jnp.where(row_dev == 0, bel...  0.83 us
  transfers between devices with their start and end apart: 7, of which 2 were waited for; matrix products, arithmetic and copies ran while one was open for 12% of the time, Pallas kernels for 0%

profile of v19, /device:TPU:40, one launch (start us, length us, event | category | flops | bytes accessed | tf_op | source)
XLA Modules:
  0.0 40.8 jit_solution(13500099341263387084)
XLA Ops:
  0.6 0.0 copy-start.4
  0.7 0.8 %slice_select_fusion = (f32[6,16,128]{2,1,0:T(8,128)S(1)}, f32[6,16,128]{2,1,0:T(8,128)S(1)}) fusion(f32[6,16,3072]{2,1,0:T(8,128)} %state_ref.1, pred[128]{0:T(512)(128)(4,1)S(1)} %iota_compare_fusion.5), kind=kLoop, calls=%fused_computation.5 | loop fusion | flops 12288 | bytes 196736 | tf_op jit(solution)/shard_map/jit(_where)/select_n | solution.py:397
  1.5 1.9 %collective-permute-start.3 = (f32[6,16,128]{2,1,0:T(8,128)S(1)}, f32[6,16,128]{2,1,0:T(8,128)S(1)}, u32[]{:S(2)}, u32[]{:S(2)}) collective-permute-start(f32[6,16,128]{2,1,0:T(8,128)S(1)} %get-tuple-element.8), channel_id=1, source_target_pairs={{1,0},{2,1},{3,2},{4,3},{5,4},{6,5},{7,6},{8,7},{9,8},{10,9},{11,1... | collective-permute-start | bytes 147464 | tf_op jit(solution)/shard_map/ppermute | solution.py:250
  3.4 0.0 copy-start.7
  3.4 0.0 copy-start.8
  3.4 0.5 %collective-permute-start.2 = (f32[6,16,128]{2,1,0:T(8,128)S(1)}, f32[6,16,128]{2,1,0:T(8,128)S(1)}, u32[]{:S(2)}, u32[]{:S(2)}) collective-permute-start(f32[6,16,128]{2,1,0:T(8,128)S(1)} %get-tuple-element.9), channel_id=1, source_target_pairs={{0,1},{1,2},{2,3},{3,4},{4,5},{5,6},{6,7},{7,8},{8,9},{9,10},{10,1... | collective-permute-start | bytes 147464 | tf_op jit(solution)/shard_map/ppermute | solution.py:250
  4.0 1.3 %fusion.12 = (f32[6,3,3072]{2,1,0:T(4,128)S(1)}, f32[6,3,3072]{2,1,0:T(4,128)S(1)}) fusion(f32[6,16,3072]{2,1,0:T(8,128)} %state_ref.1), kind=kLoop, calls=%fused_computation.40 | loop fusion | bytes 884736 | tf_op jit(solution)/shard_map/slice | solution.py:393
  5.3 0.1 select_maximum_fusion.1
  5.4 3.4 %collective-permute-start = (f32[7,3,3072]{2,1,0:T(4,128)S(1)}, f32[7,3,3072]{2,1,0:T(4,128)S(1)}, u32[]{:S(2)}, u32[]{:S(2)}) collective-permute-start(f32[7,3,3072]{2,1,0:T(4,128)S(1)} %select_maximum_fusion.1), channel_id=1, source_target_pairs={{0,16},{16,32},{32,48},{48,64},{64,80},{80,96},{96,112},{112,128},... | collective-permute-start | bytes 774152 | tf_op jit(solution)/shard_map/ppermute | solution.py:250
  8.8 0.1 select_maximum_fusion
  8.9 4.6 %collective-permute-start.1 = (f32[7,3,3072]{2,1,0:T(4,128)S(1)}, f32[7,3,3072]{2,1,0:T(4,128)S(1)}, u32[]{:S(2)}, u32[]{:S(2)}) collective-permute-start(f32[7,3,3072]{2,1,0:T(4,128)S(1)} %select_maximum_fusion), channel_id=1, source_target_pairs={{16,0},{32,16},{48,32},{64,48},{80,64},{96,80},{112,96},{128,112},... | collective-permute-start | bytes 774152 | tf_op jit(solution)/shard_map/ppermute | solution.py:250
  13.5 0.1 copy.36
  13.6 0.2 select_reduce_fusion.1
  13.8 0.1 iota_compare_fusion.3
  13.9 0.1 select_reduce_fusion
  14.0 0.8 %select_select_fusion = f32[6,16,128]{2,1,0:T(8,128)S(1)} fusion(f32[6,16,128]{2,1,0:T(8,128)S(1)} %collective-permute-done.2.below_ref, f32[6,16,128]{2,1,0:T(8,128)S(1)} %collective-permute-done.3.above_ref, pred[]{:T(512)S(6)} %eq.90, pred[]{:T(512)S(6)} %eq.89, f32[6,16,3072]{2,1,0:T(8,128)} %state_ref.1), kind=kLoop, calls=%fused_computation.4 | loop fusion | flops 24576 | bytes 196610 | tf_op jit(solution)/shard_map/jit(_where)/select_n | solution.py:409
  14.9 1.3 %collective-permute-start.4 = (f32[6,16,128]{2,1,0:T(8,128)S(1)}, f32[6,16,128]{2,1,0:T(8,128)S(1)}, u32[]{:S(2)}, u32[]{:S(2)}) collective-permute-start(f32[6,16,128]{2,1,0:T(8,128)S(1)} %select_select_fusion), channel_id=1, source_target_pairs={{15,1},{14,2},{0,3},{31,17},{30,18},{16,19},{47,33},{46,34},{32,35... | collective-permute-start | bytes 147464 | tf_op jit(solution)/shard_map/ppermute | solution.py:269
  16.2 7.4 %collective-permute-done.4 = f32[6,16,128]{2,1,0:T(8,128)S(1)} collective-permute-done((f32[6,16,128]{2,1,0:T(8,128)S(1)}, f32[6,16,128]{2,1,0:T(8,128)S(1)}, u32[]{:S(2)}, u32[]{:S(2)}) %collective-permute-start.4) | collective-permute-done | bytes 49184 | tf_op jit(solution)/shard_map/ppermute | solution.py:269
  23.6 1.3 %collective-permute-start.5 = (f32[6,16,128]{2,1,0:T(8,128)S(1)}, f32[6,16,128]{2,1,0:T(8,128)S(1)}, u32[]{:S(2)}, u32[]{:S(2)}) collective-permute-start(f32[6,16,128]{2,1,0:T(8,128)S(1)} %broadcast_select_fusion), channel_id=1, source_target_pairs={{15,4},{14,5},{0,6},{1,7},{2,8},{3,9},{31,20},{30,21},{16,22},{17,... | collective-permute-start | bytes 147464 | tf_op jit(solution)/shard_map/ppermute | solution.py:269
  24.9 0.1 copy.39
  25.0 0.7 %collective-permute-start.6 = (f32[6,16,128]{2,1,0:T(8,128)S(1)}, f32[6,16,128]{2,1,0:T(8,128)S(1)}, u32[]{:S(2)}, u32[]{:S(2)}) collective-permute-start(f32[6,16,128]{2,1,0:T(8,128)S(1)} %broadcast_select_fusion), channel_id=1, source_target_pairs={{15,10},{14,11},{0,12},{1,13},{31,26},{30,27},{16,28},{17,29},{47,... | collective-permute-start | bytes 147464 | tf_op jit(solution)/shard_map/ppermute | solution.py:269
  25.7 1.0 %collective-permute-done.5 = f32[6,16,128]{2,1,0:T(8,128)S(1)} collective-permute-done((f32[6,16,128]{2,1,0:T(8,128)S(1)}, f32[6,16,128]{2,1,0:T(8,128)S(1)}, u32[]{:S(2)}, u32[]{:S(2)}) %collective-permute-start.5) | collective-permute-done | bytes 49184 | tf_op jit(solution)/shard_map/ppermute | solution.py:269
  26.6 0.6 %broadcast_select_fusion.1.before_ref = f32[6,16,128]{2,1,0:T(8,128)} fusion(f32[6,16,128]{2,1,0:T(8,128)S(1)} %collective-permute-done.5, f32[6,16,128]{2,1,0:T(8,128)S(1)} %broadcast_select_fusion, pred[]{:T(512)S(6)} %or.25), kind=kLoop, calls=%fused_computation.7 | loop fusion | flops 12288 | bytes 147457 | tf_op jit(solution)/shard_map/jit(_where)/select_n | solution.py:274
  27.3 0.1 copy.35
  27.4 0.1 copy.37
  27.5 0.1 fusion.1
  27.6 0.1 broadcast_in_dim.95
  27.7 0.1 broadcast_in_dim.99
  27.7 0.1 concatenate.51
  27.8 0.9 %fusion.8.geo_ref = f32[96,128]{1,0:T(8,128)} fusion(f32[96,32]{0,1:T(8,128)S(1)} %concatenate.51, s32[128]{0:T(128)S(1)} %and_select_fusion), kind=kOutput, calls=%fused_computation.23 | convolution fusion | flops 4722688 | bytes 61952 | tf_op jit(solution)/shard_map/dot_general | solution.py:372
  28.8 0.6 %copy-done.5 = f32[6,16,128]{2,1,0:T(8,128)} copy-done((f32[6,16,128]{2,1,0:T(8,128)}, f32[6,16,128]{2,1,0:T(8,128)S(1)}, u32[]{:S(2)}) %copy-start.5) | copy-done | bytes 49176
  29.4 11.5 %shard_map.68 = (f32[6,16,3072]{2,1,0:T(8,128)}, f32[16,32]{1,0:T(8,128)}) custom-call(f32[6,16,3072]{2,1,0:T(8,128)} %state_ref.1, f32[7,3,3072]{2,1,0:T(4,128)} %copy-done, f32[7,3,3072]{2,1,0:T(4,128)} %copy-done.1, f32[6,16,128]{2,1,0:T(8,128)} %copy-done.3, f32[6,16,128]{2,1,0:T(8,128)} %copy-done.2, f32[96,128]{1,0:T(8,128)} %fusion.8.geo_ref, ...), custom_call_target="tpu_custom_call" | custom-call | tf_op jit(solution)/shard_map/pallas_call | solution.py:227
  (33 shorter events, 0.1 us)
Async XLA Ops:
  0.6 4.7 %copy-start.4 = (f32[16,32]{1,0:T(8,128)S(1)}, f32[16,32]{1,0:T(8,128)}, u32[]{:S(2)}) copy-start(f32[16,32]{1,0:T(8,128)} %height_ref.1) | copy-start | bytes 6148
  1.5 12.5 %collective-permute-start.3 = (f32[6,16,128]{2,1,0:T(8,128)S(1)}, f32[6,16,128]{2,1,0:T(8,128)S(1)}, u32[]{:S(2)}, u32[]{:S(2)}) collective-permute-start(f32[6,16,128]{2,1,0:T(8,128)S(1)} %get-tuple-element.8), channel_id=1, source_target_pairs={{1,0},{2,1},{3,2},{4,3},{5,4},{6,5},{7,6},{8,7},{9,8},{10,9},{11,1... | collective-permute-start | bytes 147464 | tf_op jit(solution)/shard_map/ppermute | solution.py:250
  3.4 10.2 %copy-start.7 = (s32[16]{0:T(128)S(1)}, s32[16]{0:T(128)}, u32[]{:S(2)}) copy-start(s32[16]{0:T(128)} %param.8) | copy-start | bytes 196
  3.4 10.2 %copy-start.8 = (s32[16]{0:T(128)S(1)}, s32[16]{0:T(128)}, u32[]{:S(2)}) copy-start(s32[16]{0:T(128)} %param.7) | copy-start | bytes 196
  3.4 10.4 %copy-start.6 = (f32[16,32]{1,0:T(8,128)S(1)}, f32[16,32]{1,0:T(8,128)}, u32[]{:S(2)}) copy-start(f32[16,32]{1,0:T(8,128)} %param.9) | copy-start | bytes 6148
  3.4 10.6 %collective-permute-start.2 = (f32[6,16,128]{2,1,0:T(8,128)S(1)}, f32[6,16,128]{2,1,0:T(8,128)S(1)}, u32[]{:S(2)}, u32[]{:S(2)}) collective-permute-start(f32[6,16,128]{2,1,0:T(8,128)S(1)} %get-tuple-element.9), channel_id=1, source_target_pairs={{0,1},{1,2},{2,3},{3,4},{4,5},{5,6},{6,7},{7,8},{8,9},{9,10},{10,1... | collective-permute-start | bytes 147464 | tf_op jit(solution)/shard_map/ppermute | solution.py:250
  5.4 21.9 %collective-permute-start = (f32[7,3,3072]{2,1,0:T(4,128)S(1)}, f32[7,3,3072]{2,1,0:T(4,128)S(1)}, u32[]{:S(2)}, u32[]{:S(2)}) collective-permute-start(f32[7,3,3072]{2,1,0:T(4,128)S(1)} %select_maximum_fusion.1), channel_id=1, source_target_pairs={{0,16},{16,32},{32,48},{48,64},{64,80},{80,96},{96,112},{112,128},... | collective-permute-start | bytes 774152 | tf_op jit(solution)/shard_map/ppermute | solution.py:250
  8.9 18.5 %collective-permute-start.1 = (f32[7,3,3072]{2,1,0:T(4,128)S(1)}, f32[7,3,3072]{2,1,0:T(4,128)S(1)}, u32[]{:S(2)}, u32[]{:S(2)}) collective-permute-start(f32[7,3,3072]{2,1,0:T(4,128)S(1)} %select_maximum_fusion), channel_id=1, source_target_pairs={{16,0},{32,16},{48,32},{64,48},{80,64},{96,80},{112,96},{128,112},... | collective-permute-start | bytes 774152 | tf_op jit(solution)/shard_map/ppermute | solution.py:250
  14.0 14.7 %copy-start.2 = (f32[6,16,128]{2,1,0:T(8,128)}, f32[6,16,128]{2,1,0:T(8,128)S(1)}, u32[]{:S(2)}) copy-start(f32[6,16,128]{2,1,0:T(8,128)S(1)} %collective-permute-done.3.above_ref) | copy-start | bytes 147460
  14.0 14.7 %copy-start.3 = (f32[6,16,128]{2,1,0:T(8,128)}, f32[6,16,128]{2,1,0:T(8,128)S(1)}, u32[]{:S(2)}) copy-start(f32[6,16,128]{2,1,0:T(8,128)S(1)} %collective-permute-done.2.below_ref) | copy-start | bytes 147460
  14.9 8.7 %collective-permute-start.4 = (f32[6,16,128]{2,1,0:T(8,128)S(1)}, f32[6,16,128]{2,1,0:T(8,128)S(1)}, u32[]{:S(2)}, u32[]{:S(2)}) collective-permute-start(f32[6,16,128]{2,1,0:T(8,128)S(1)} %select_select_fusion), channel_id=1, source_target_pairs={{15,1},{14,2},{0,3},{31,17},{30,18},{16,19},{47,33},{46,34},{32,35... | collective-permute-start | bytes 147464 | tf_op jit(solution)/shard_map/ppermute | solution.py:269
  23.6 3.0 %collective-permute-start.5 = (f32[6,16,128]{2,1,0:T(8,128)S(1)}, f32[6,16,128]{2,1,0:T(8,128)S(1)}, u32[]{:S(2)}, u32[]{:S(2)}) collective-permute-start(f32[6,16,128]{2,1,0:T(8,128)S(1)} %broadcast_select_fusion), channel_id=1, source_target_pairs={{15,4},{14,5},{0,6},{1,7},{2,8},{3,9},{31,20},{30,21},{16,22},{17,... | collective-permute-start | bytes 147464 | tf_op jit(solution)/shard_map/ppermute | solution.py:269
  25.0 3.7 %collective-permute-start.6 = (f32[6,16,128]{2,1,0:T(8,128)S(1)}, f32[6,16,128]{2,1,0:T(8,128)S(1)}, u32[]{:S(2)}, u32[]{:S(2)}) collective-permute-start(f32[6,16,128]{2,1,0:T(8,128)S(1)} %broadcast_select_fusion), channel_id=1, source_target_pairs={{15,10},{14,11},{0,12},{1,13},{31,26},{30,27},{16,28},{17,29},{47,... | collective-permute-start | bytes 147464 | tf_op jit(solution)/shard_map/ppermute | solution.py:269
  27.3 1.4 %copy-start = (f32[7,3,3072]{2,1,0:T(4,128)}, f32[7,3,3072]{2,1,0:T(4,128)S(1)}, u32[]{:S(2)}) copy-start(f32[7,3,3072]{2,1,0:T(4,128)S(1)} %collective-permute-done.xlo_ref) | copy-start | bytes 774148
  27.4 1.4 %copy-start.1 = (f32[7,3,3072]{2,1,0:T(4,128)}, f32[7,3,3072]{2,1,0:T(4,128)S(1)}, u32[]{:S(2)}) copy-start(f32[7,3,3072]{2,1,0:T(4,128)S(1)} %collective-permute-done.1.xhi_ref) | copy-start | bytes 774148
  28.7 0.6 %copy-start.5 = (f32[6,16,128]{2,1,0:T(8,128)}, f32[6,16,128]{2,1,0:T(8,128)S(1)}, u32[]{:S(2)}) copy-start(f32[6,16,128]{2,1,0:T(8,128)S(1)} %collective-permute-done.6.last_ref) | copy-start | bytes 147460

commit v20 on v19

--- a/solution.py
+++ b/solution.py
@@ -20,7 +20,7 @@
 
 FLUX_WEIGHTS = (45.0, -9.0, 1.0)
 SPEED_WEIGHTS = (20.0, -15.0, 6.0, -1.0)
-CHUNK = 512
+CHUNK = 384
 PAD = 128
 HALO = 3
 XPAD = 8

time: 41.2 us -> 40.6 us (0.985)
  Pallas kernels: 11.5 us -> 10.9 us
    pallas_call x1, Pallas kernels: 11.5 us -> 10.9 us  [update(): pl.pallas_call(kern, out_shape=(jax.ShapeDtypeStruct((6, columns, length)...]
where the time goes in v20:
time: 40.6 us; the launch traced here: 40.2 us
  starting transfers between devices  13.6 us (33%)
  Pallas kernels  10.9 us (27%)
  waiting for transfers between devices  8.38 us (21%)
  other arithmetic  2.95 us (7%)
  local copies, waits for them, and re-layouts  2.59 us (6%)
  between operations  0.96 us (2%)
  matrix products  0.87 us (2%)
    pallas_call x1, Pallas kernels, update(): pl.pallas_call(kern, out_shape=(jax.ShapeDtypeStruct((6, columns, length)...  10.9 us
    ppermute x4, starting transfers between devices, shifted(): return lax.ppermute(block, axis, pairs)  10.4 us
    ppermute x3, waiting for transfers between devices, broadcast(): received = lax.ppermute(array, axis, pairs)  8.37 us
    ppermute x3, starting transfers between devices, broadcast(): received = lax.ppermute(array, axis, pairs)  3.23 us
    slice x1, local copies, waits for them, and re-layouts, shards(): from_high = shifted(pack(state[:, :HALO], shock_height[:HALO]), 'gx', False)  1.35 us
    dot_general x1, matrix products, replicate_lanes(): jnp.dot(small, pick, precision=lax.Precision.HIGHEST, preferred_element_t...  0.87 us
    select_n x1, other arithmetic, shards(): jnp.where(plane_lane < band, state[..., :PAD], top_block)  0.83 us
    select_n x1, other arithmetic, shards(): jnp.where(row_dev == row_devs - 1, top_block, jnp.where(row_dev == 0, bel...  0.83 us
  transfers between devices with their start and end apart: 7, of which 2 were waited for; matrix products, arithmetic and copies ran while one was open for 12% of the time, Pallas kernels for 0%

profile of v20, /device:TPU:40, one launch (start us, length us, event | category | flops | bytes accessed | tf_op | source)
XLA Modules:
  0.0 40.2 jit_solution(15680494156403036618)
XLA Ops:
  0.6 0.0 copy-start.4
  0.7 0.8 %slice_select_fusion = (f32[6,16,128]{2,1,0:T(8,128)S(1)}, f32[6,16,128]{2,1,0:T(8,128)S(1)}) fusion(f32[6,16,3072]{2,1,0:T(8,128)} %state_ref.1, pred[128]{0:T(512)(128)(4,1)S(1)} %iota_compare_fusion.5), kind=kLoop, calls=%fused_computation.5 | loop fusion | flops 12288 | bytes 196736 | tf_op jit(solution)/shard_map/jit(_where)/select_n | solution.py:397
  1.5 1.9 %collective-permute-start.3 = (f32[6,16,128]{2,1,0:T(8,128)S(1)}, f32[6,16,128]{2,1,0:T(8,128)S(1)}, u32[]{:S(2)}, u32[]{:S(2)}) collective-permute-start(f32[6,16,128]{2,1,0:T(8,128)S(1)} %get-tuple-element.8), channel_id=1, source_target_pairs={{1,0},{2,1},{3,2},{4,3},{5,4},{6,5},{7,6},{8,7},{9,8},{10,9},{11,1... | collective-permute-start | bytes 147464 | tf_op jit(solution)/shard_map/ppermute | solution.py:250
  3.4 0.0 copy-start.7
  3.4 0.0 copy-start.8
  3.4 0.5 %collective-permute-start.2 = (f32[6,16,128]{2,1,0:T(8,128)S(1)}, f32[6,16,128]{2,1,0:T(8,128)S(1)}, u32[]{:S(2)}, u32[]{:S(2)}) collective-permute-start(f32[6,16,128]{2,1,0:T(8,128)S(1)} %get-tuple-element.9), channel_id=1, source_target_pairs={{0,1},{1,2},{2,3},{3,4},{4,5},{5,6},{6,7},{7,8},{8,9},{9,10},{10,1... | collective-permute-start | bytes 147464 | tf_op jit(solution)/shard_map/ppermute | solution.py:250
  4.0 1.3 %fusion.12 = (f32[6,3,3072]{2,1,0:T(4,128)S(1)}, f32[6,3,3072]{2,1,0:T(4,128)S(1)}) fusion(f32[6,16,3072]{2,1,0:T(8,128)} %state_ref.1), kind=kLoop, calls=%fused_computation.40 | loop fusion | bytes 884736 | tf_op jit(solution)/shard_map/slice | solution.py:393
  5.3 0.1 select_maximum_fusion.1
  5.4 3.4 %collective-permute-start = (f32[7,3,3072]{2,1,0:T(4,128)S(1)}, f32[7,3,3072]{2,1,0:T(4,128)S(1)}, u32[]{:S(2)}, u32[]{:S(2)}) collective-permute-start(f32[7,3,3072]{2,1,0:T(4,128)S(1)} %select_maximum_fusion.1), channel_id=1, source_target_pairs={{0,16},{16,32},{32,48},{48,64},{64,80},{80,96},{96,112},{112,128},... | collective-permute-start | bytes 774152 | tf_op jit(solution)/shard_map/ppermute | solution.py:250
  8.8 0.1 select_maximum_fusion
  8.9 4.6 %collective-permute-start.1 = (f32[7,3,3072]{2,1,0:T(4,128)S(1)}, f32[7,3,3072]{2,1,0:T(4,128)S(1)}, u32[]{:S(2)}, u32[]{:S(2)}) collective-permute-start(f32[7,3,3072]{2,1,0:T(4,128)S(1)} %select_maximum_fusion), channel_id=1, source_target_pairs={{16,0},{32,16},{48,32},{64,48},{80,64},{96,80},{112,96},{128,112},... | collective-permute-start | bytes 774152 | tf_op jit(solution)/shard_map/ppermute | solution.py:250
  13.5 0.1 copy.36
  13.6 0.2 select_reduce_fusion.1
  13.8 0.1 iota_compare_fusion.3
  13.9 0.1 select_reduce_fusion
  14.0 0.8 %select_select_fusion = f32[6,16,128]{2,1,0:T(8,128)S(1)} fusion(f32[6,16,128]{2,1,0:T(8,128)S(1)} %collective-permute-done.2.below_ref, f32[6,16,128]{2,1,0:T(8,128)S(1)} %collective-permute-done.3.above_ref, pred[]{:T(512)S(6)} %eq.90, pred[]{:T(512)S(6)} %eq.89, f32[6,16,3072]{2,1,0:T(8,128)} %state_ref.1), kind=kLoop, calls=%fused_computation.4 | loop fusion | flops 24576 | bytes 196610 | tf_op jit(solution)/shard_map/jit(_where)/select_n | solution.py:409
  14.9 1.3 %collective-permute-start.4 = (f32[6,16,128]{2,1,0:T(8,128)S(1)}, f32[6,16,128]{2,1,0:T(8,128)S(1)}, u32[]{:S(2)}, u32[]{:S(2)}) collective-permute-start(f32[6,16,128]{2,1,0:T(8,128)S(1)} %select_select_fusion), channel_id=1, source_target_pairs={{15,1},{14,2},{0,3},{31,17},{30,18},{16,19},{47,33},{46,34},{32,35... | collective-permute-start | bytes 147464 | tf_op jit(solution)/shard_map/ppermute | solution.py:269
  16.2 7.4 %collective-permute-done.4 = f32[6,16,128]{2,1,0:T(8,128)S(1)} collective-permute-done((f32[6,16,128]{2,1,0:T(8,128)S(1)}, f32[6,16,128]{2,1,0:T(8,128)S(1)}, u32[]{:S(2)}, u32[]{:S(2)}) %collective-permute-start.4) | collective-permute-done | bytes 49184 | tf_op jit(solution)/shard_map/ppermute | solution.py:269
  23.6 1.3 %collective-permute-start.5 = (f32[6,16,128]{2,1,0:T(8,128)S(1)}, f32[6,16,128]{2,1,0:T(8,128)S(1)}, u32[]{:S(2)}, u32[]{:S(2)}) collective-permute-start(f32[6,16,128]{2,1,0:T(8,128)S(1)} %broadcast_select_fusion), channel_id=1, source_target_pairs={{15,4},{14,5},{0,6},{1,7},{2,8},{3,9},{31,20},{30,21},{16,22},{17,... | collective-permute-start | bytes 147464 | tf_op jit(solution)/shard_map/ppermute | solution.py:269
  24.9 0.1 copy.39
  25.0 0.7 %collective-permute-start.6 = (f32[6,16,128]{2,1,0:T(8,128)S(1)}, f32[6,16,128]{2,1,0:T(8,128)S(1)}, u32[]{:S(2)}, u32[]{:S(2)}) collective-permute-start(f32[6,16,128]{2,1,0:T(8,128)S(1)} %broadcast_select_fusion), channel_id=1, source_target_pairs={{15,10},{14,11},{0,12},{1,13},{31,26},{30,27},{16,28},{17,29},{47,... | collective-permute-start | bytes 147464 | tf_op jit(solution)/shard_map/ppermute | solution.py:269
  25.7 1.0 %collective-permute-done.5 = f32[6,16,128]{2,1,0:T(8,128)S(1)} collective-permute-done((f32[6,16,128]{2,1,0:T(8,128)S(1)}, f32[6,16,128]{2,1,0:T(8,128)S(1)}, u32[]{:S(2)}, u32[]{:S(2)}) %collective-permute-start.5) | collective-permute-done | bytes 49184 | tf_op jit(solution)/shard_map/ppermute | solution.py:269
  26.6 0.6 %broadcast_select_fusion.1.before_ref = f32[6,16,128]{2,1,0:T(8,128)} fusion(f32[6,16,128]{2,1,0:T(8,128)S(1)} %collective-permute-done.5, f32[6,16,128]{2,1,0:T(8,128)S(1)} %broadcast_select_fusion, pred[]{:T(512)S(6)} %or.25), kind=kLoop, calls=%fused_computation.7 | loop fusion | flops 12288 | bytes 147457 | tf_op jit(solution)/shard_map/jit(_where)/select_n | solution.py:274
  27.3 0.1 copy.35
  27.4 0.1 copy.37
  27.5 0.1 fusion.1
  27.6 0.1 broadcast_in_dim.95
  27.7 0.1 broadcast_in_dim.99
  27.7 0.1 concatenate.51
  27.8 0.9 %fusion.8.geo_ref = f32[96,128]{1,0:T(8,128)} fusion(f32[96,32]{0,1:T(8,128)S(1)} %concatenate.51, s32[128]{0:T(128)S(1)} %and_select_fusion), kind=kOutput, calls=%fused_computation.23 | convolution fusion | flops 4722688 | bytes 61952 | tf_op jit(solution)/shard_map/dot_general | solution.py:372
  28.8 0.6 %copy-done.5 = f32[6,16,128]{2,1,0:T(8,128)} copy-done((f32[6,16,128]{2,1,0:T(8,128)}, f32[6,16,128]{2,1,0:T(8,128)S(1)}, u32[]{:S(2)}) %copy-start.5) | copy-done | bytes 49176
  29.4 10.9 %shard_map.68 = (f32[6,16,3072]{2,1,0:T(8,128)}, f32[16,32]{1,0:T(8,128)}) custom-call(f32[6,16,3072]{2,1,0:T(8,128)} %state_ref.1, f32[7,3,3072]{2,1,0:T(4,128)} %copy-done, f32[7,3,3072]{2,1,0:T(4,128)} %copy-done.1, f32[6,16,128]{2,1,0:T(8,128)} %copy-done.3, f32[6,16,128]{2,1,0:T(8,128)} %copy-done.2, f32[96,128]{1,0:T(8,128)} %fusion.8.geo_ref, ...), custom_call_target="tpu_custom_call" | custom-call | tf_op jit(solution)/shard_map/pallas_call | solution.py:227
  (33 shorter events, 0.1 us)
Async XLA Ops:
  0.6 4.7 %copy-start.4 = (f32[16,32]{1,0:T(8,128)S(1)}, f32[16,32]{1,0:T(8,128)}, u32[]{:S(2)}) copy-start(f32[16,32]{1,0:T(8,128)} %height_ref.1) | copy-start | bytes 6148
  1.5 12.5 %collective-permute-start.3 = (f32[6,16,128]{2,1,0:T(8,128)S(1)}, f32[6,16,128]{2,1,0:T(8,128)S(1)}, u32[]{:S(2)}, u32[]{:S(2)}) collective-permute-start(f32[6,16,128]{2,1,0:T(8,128)S(1)} %get-tuple-element.8), channel_id=1, source_target_pairs={{1,0},{2,1},{3,2},{4,3},{5,4},{6,5},{7,6},{8,7},{9,8},{10,9},{11,1... | collective-permute-start | bytes 147464 | tf_op jit(solution)/shard_map/ppermute | solution.py:250
  3.4 10.2 %copy-start.7 = (s32[16]{0:T(128)S(1)}, s32[16]{0:T(128)}, u32[]{:S(2)}) copy-start(s32[16]{0:T(128)} %param.8) | copy-start | bytes 196
  3.4 10.2 %copy-start.8 = (s32[16]{0:T(128)S(1)}, s32[16]{0:T(128)}, u32[]{:S(2)}) copy-start(s32[16]{0:T(128)} %param.7) | copy-start | bytes 196
  3.4 10.4 %copy-start.6 = (f32[16,32]{1,0:T(8,128)S(1)}, f32[16,32]{1,0:T(8,128)}, u32[]{:S(2)}) copy-start(f32[16,32]{1,0:T(8,128)} %param.9) | copy-start | bytes 6148
  3.4 10.6 %collective-permute-start.2 = (f32[6,16,128]{2,1,0:T(8,128)S(1)}, f32[6,16,128]{2,1,0:T(8,128)S(1)}, u32[]{:S(2)}, u32[]{:S(2)}) collective-permute-start(f32[6,16,128]{2,1,0:T(8,128)S(1)} %get-tuple-element.9), channel_id=1, source_target_pairs={{0,1},{1,2},{2,3},{3,4},{4,5},{5,6},{6,7},{7,8},{8,9},{9,10},{10,1... | collective-permute-start | bytes 147464 | tf_op jit(solution)/shard_map/ppermute | solution.py:250
  5.4 21.9 %collective-permute-start = (f32[7,3,3072]{2,1,0:T(4,128)S(1)}, f32[7,3,3072]{2,1,0:T(4,128)S(1)}, u32[]{:S(2)}, u32[]{:S(2)}) collective-permute-start(f32[7,3,3072]{2,1,0:T(4,128)S(1)} %select_maximum_fusion.1), channel_id=1, source_target_pairs={{0,16},{16,32},{32,48},{48,64},{64,80},{80,96},{96,112},{112,128},... | collective-permute-start | bytes 774152 | tf_op jit(solution)/shard_map/ppermute | solution.py:250
  8.9 18.5 %collective-permute-start.1 = (f32[7,3,3072]{2,1,0:T(4,128)S(1)}, f32[7,3,3072]{2,1,0:T(4,128)S(1)}, u32[]{:S(2)}, u32[]{:S(2)}) collective-permute-start(f32[7,3,3072]{2,1,0:T(4,128)S(1)} %select_maximum_fusion), channel_id=1, source_target_pairs={{16,0},{32,16},{48,32},{64,48},{80,64},{96,80},{112,96},{128,112},... | collective-permute-start | bytes 774152 | tf_op jit(solution)/shard_map/ppermute | solution.py:250
  14.0 14.7 %copy-start.2 = (f32[6,16,128]{2,1,0:T(8,128)}, f32[6,16,128]{2,1,0:T(8,128)S(1)}, u32[]{:S(2)}) copy-start(f32[6,16,128]{2,1,0:T(8,128)S(1)} %collective-permute-done.3.above_ref) | copy-start | bytes 147460
  14.0 14.7 %copy-start.3 = (f32[6,16,128]{2,1,0:T(8,128)}, f32[6,16,128]{2,1,0:T(8,128)S(1)}, u32[]{:S(2)}) copy-start(f32[6,16,128]{2,1,0:T(8,128)S(1)} %collective-permute-done.2.below_ref) | copy-start | bytes 147460
  14.9 8.7 %collective-permute-start.4 = (f32[6,16,128]{2,1,0:T(8,128)S(1)}, f32[6,16,128]{2,1,0:T(8,128)S(1)}, u32[]{:S(2)}, u32[]{:S(2)}) collective-permute-start(f32[6,16,128]{2,1,0:T(8,128)S(1)} %select_select_fusion), channel_id=1, source_target_pairs={{15,1},{14,2},{0,3},{31,17},{30,18},{16,19},{47,33},{46,34},{32,35... | collective-permute-start | bytes 147464 | tf_op jit(solution)/shard_map/ppermute | solution.py:269
  23.6 3.0 %collective-permute-start.5 = (f32[6,16,128]{2,1,0:T(8,128)S(1)}, f32[6,16,128]{2,1,0:T(8,128)S(1)}, u32[]{:S(2)}, u32[]{:S(2)}) collective-permute-start(f32[6,16,128]{2,1,0:T(8,128)S(1)} %broadcast_select_fusion), channel_id=1, source_target_pairs={{15,4},{14,5},{0,6},{1,7},{2,8},{3,9},{31,20},{30,21},{16,22},{17,... | collective-permute-start | bytes 147464 | tf_op jit(solution)/shard_map/ppermute | solution.py:269
  25.0 3.7 %collective-permute-start.6 = (f32[6,16,128]{2,1,0:T(8,128)S(1)}, f32[6,16,128]{2,1,0:T(8,128)S(1)}, u32[]{:S(2)}, u32[]{:S(2)}) collective-permute-start(f32[6,16,128]{2,1,0:T(8,128)S(1)} %broadcast_select_fusion), channel_id=1, source_target_pairs={{15,10},{14,11},{0,12},{1,13},{31,26},{30,27},{16,28},{17,29},{47,... | collective-permute-start | bytes 147464 | tf_op jit(solution)/shard_map/ppermute | solution.py:269
  27.3 1.4 %copy-start = (f32[7,3,3072]{2,1,0:T(4,128)}, f32[7,3,3072]{2,1,0:T(4,128)S(1)}, u32[]{:S(2)}) copy-start(f32[7,3,3072]{2,1,0:T(4,128)S(1)} %collective-permute-done.xlo_ref) | copy-start | bytes 774148
  27.4 1.4 %copy-start.1 = (f32[7,3,3072]{2,1,0:T(4,128)}, f32[7,3,3072]{2,1,0:T(4,128)S(1)}, u32[]{:S(2)}) copy-start(f32[7,3,3072]{2,1,0:T(4,128)S(1)} %collective-permute-done.1.xhi_ref) | copy-start | bytes 774148
  28.7 0.6 %copy-start.5 = (f32[6,16,128]{2,1,0:T(8,128)}, f32[6,16,128]{2,1,0:T(8,128)S(1)}, u32[]{:S(2)}) copy-start(f32[6,16,128]{2,1,0:T(8,128)S(1)} %collective-permute-done.6.last_ref) | copy-start | bytes 147460
